TPU v7x, 32 devices: a whole 2x2x4 slice. The times are simulated.
32 devices in a mesh: group: 2 (over y), sub: 4 (over z), tile: 2 (over x), rep: 2 (over core).
Axes of the slice: x: 2, y: 2, z: 4, core: 2. Of those that a mesh axis runs over, the one named last changes fastest.
Arguments:
- right_side: bfloat16 [16, 1024, 512], P(('group', 'sub', 'tile'), None, 'rep'), parts along dimension 0, may hold values from -6 to 6
- interface_inverse: bfloat16 [16, 1024, 1024], P(('group', 'sub', 'tile')), parts along dimension 0, may hold values from -0.1875 to 0.1875
- coupling: float32 [16, 2, 128], P(('group', 'sub', 'tile')), parts along dimension 0, may hold values from 0.5 to 2
- trace_rows: int32 [16, 2, 128], P(('group', 'sub', 'tile')), parts along dimension 0, may hold values from 0 to 1023
- deflation_basis: bfloat16 [16, 1024, 128], P(('group', 'sub', 'tile')), parts along dimension 0, may hold values from -0.375 to 0.375
- deflation_counts: int32 [16], P(('group', 'sub', 'tile')), parts along dimension 0, may hold values from 32 to 128, as said below
- coarse_inverse: bfloat16 [8, 2, 128, 4, 256], P('group', 'tile', 'rep', 'sub'), parts along dimension 0, may hold values from -0.25 to 0.25
Outputs:
- corrected_field: bfloat16 [16, 1024, 512], P(('group', 'sub', 'tile'), None, 'rep'), parts along dimension 0
There are 2 independent parts, one for each index of `group`. A program takes and returns all parts, laid end to end along the dimension named above; each array names one. Nothing has to cross between parts.
Inputs may be any that keep to these rules, and one draw needn't show every extreme that they name: `deflation_counts`: some subdomain has exactly 128 live deflation vectors.
All inputs are finite; a program needn't handle non-finite values.
Results may differ from a plain program's by a relative error of at most 0.035.
Values may be sent and summed in bfloat16 or wider, within the bound.
No kernel may reach another device: no remote copies, remote signals or barrier semaphores. Data moves between devices by JAX's collectives and lax.ppermute only.
A program may use at most 64 MiB of HBM per device.

v0:
```python
import jax
import jax.numpy as jnp
from jax import lax
from jax.sharding import PartitionSpec as P

ROUNDS = 2


def passed_along(shard, axis, by):
    peers = lax.axis_size(axis)
    pairs = [(i, i + by) for i in range(peers) if 0 <= i + by < peers]
    return lax.ppermute(shard, axis, pairs)


def add_columns(matrix, piece):
    return jnp.dot(matrix, piece, preferred_element_type=jnp.float32)


def local(
    right_side,
    interface_inverse,
    coupling,
    trace_rows,
    deflation_basis,
    deflation_counts,
    coarse_inverse,
):
    source = right_side[0].astype(jnp.float32)
    inverse = interface_inverse[0]
    iface_rows = inverse.shape[0]
    face_rows = coupling.shape[2]
    mode_cols = source.shape[1]
    slot_count = deflation_basis.shape[2]
    half_slots = coarse_inverse.shape[2]
    sub_count = lax.axis_size("sub")
    slot_ids = jnp.arange(slot_count, dtype=jnp.int32)
    masked_basis = jnp.where(
        slot_ids[None, :] < deflation_counts[0],
        deflation_basis[0],
        jnp.zeros((), deflation_basis.dtype),
    )
    coarse_block = coarse_inverse.reshape(sub_count * half_slots, coarse_inverse.shape[4])
    lower_gain = coupling[0, 0][:, None]
    upper_gain = coupling[0, 1][:, None]
    iterate = jnp.zeros((iface_rows, mode_cols), jnp.float32)
    for cycle_index in range(ROUNDS):
        lower_trace = iterate[trace_rows[0, 0]]
        upper_trace = iterate[trace_rows[0, 1]]
        from_lower = passed_along(upper_trace.astype(jnp.bfloat16), ("sub", "tile"), 1).astype(
            upper_trace.dtype
        )
        from_upper = passed_along(lower_trace.astype(jnp.bfloat16), ("sub", "tile"), -1).astype(
            lower_trace.dtype
        )
        lower_rows = source[:face_rows] + lower_gain * from_lower
        upper_rows = source[iface_rows - face_rows :] + upper_gain * from_upper
        boundary = jnp.concatenate(
            [lower_rows, source[face_rows : iface_rows - face_rows], upper_rows], axis=0
        ).astype(jnp.bfloat16)
        local_solve = jnp.dot(inverse, boundary, preferred_element_type=jnp.float32)
        defect = (local_solve - iterate).astype(jnp.bfloat16)
        projected = lax.dot_general(
            masked_basis, defect, (((0,), (0,)), ((), ())), preferred_element_type=jnp.float32
        ).astype(jnp.bfloat16)
        all_modes = lax.all_gather(projected, "rep", axis=1, tiled=True)
        partial_value = add_columns(
            coarse_block, lax.all_gather(all_modes, "tile", axis=0, tiled=True)
        )
        own_coarse = lax.psum_scatter(
            partial_value.astype(jnp.bfloat16), "sub", scatter_dimension=0, tiled=True
        )
        coarse_rows = lax.all_to_all(own_coarse, "rep", split_axis=1, concat_axis=0, tiled=True)
        iterate = local_solve + jnp.dot(
            masked_basis, coarse_rows, preferred_element_type=jnp.float32
        )
    return iterate.astype(jnp.bfloat16)[None]


def solution(mesh):
    placed = (
        P(("group", "sub", "tile"), None, "rep"),
        P(("group", "sub", "tile"), None, None),
        P(("group", "sub", "tile"), None, None),
        P(("group", "sub", "tile"), None, None),
        P(("group", "sub", "tile"), None, None),
        P(("group", "sub", "tile")),
        P("group", "tile", "rep", "sub", None),
    )
    return jax.shard_map(
        local,
        mesh=mesh,
        in_specs=placed,
        out_specs=P(("group", "sub", "tile"), None, "rep"),
        check_vma=False,
    )
```

profile of v0, /device:TPU:0, one launch (start us, length us, event | category | flops | bytes accessed | tf_op | source)
XLA Modules:
  0.0 124.2 jit_solution(14332137796741248323)
XLA Ops:
  8.3 4.8 %collective-permute-start = (bf16[128,256]{1,0:T(8,128)(2,1)S(1)}, bf16[128,256]{1,0:T(8,128)(2,1)S(1)}, u32[]{:S(2)}, u32[]{:S(2)}) collective-permute-start(bf16[128,256]{1,0:T(8,128)(2,1)S(1)} %gather_fusion), channel_id=1, source_target_pairs={{0,2},{2,4},{4,6},{6,8},{8,10},{10,12},{12,14},{1,3},{3,5},{5,7},{... | collective-permute-start | bytes 196616 | tf_op jit(solution)/shard_map/ppermute | solution.py:12
  14.0 1.3 %collective-permute-start.1 = (bf16[128,256]{1,0:T(8,128)(2,1)S(1)}, bf16[128,256]{1,0:T(8,128)(2,1)S(1)}, u32[]{:S(2)}, u32[]{:S(2)}) collective-permute-start(bf16[128,256]{1,0:T(8,128)(2,1)S(1)} %gather_fusion.1), channel_id=1, source_target_pairs={{2,0},{4,2},{6,4},{8,6},{10,8},{12,10},{14,12},{3,1},{5,3},{7,5},{... | collective-permute-start | bytes 196616 | tf_op jit(solution)/shard_map/ppermute | solution.py:12
  16.7 1.1 convert_element_type.57
  17.9 2.2 %collective-permute-done.1 = bf16[128,256]{1,0:T(8,128)(2,1)S(1)} collective-permute-done((bf16[128,256]{1,0:T(8,128)(2,1)S(1)}, bf16[128,256]{1,0:T(8,128)(2,1)S(1)}, u32[]{:S(2)}, u32[]{:S(2)}) %collective-permute-start.1) | collective-permute-done | bytes 65568 | tf_op jit(solution)/shard_map/ppermute | solution.py:12
  22.5 1.9 %all_gather.12 = bf16[128,512]{1,0:T(8,128)(2,1)S(1)} all-gather(bf16[128,256]{1,0:T(8,128)(2,1)S(1)} %convolution_convert_fusion.3), channel_id=1, replica_groups=mesh['group'=2,'sub'=4,'tile'=2,'rep'=2] {'rep'}, dimensions={1}, use_global_device_ids=true | all-gather | bytes 196608 | tf_op jit(solution)/shard_map/all_gather | solution.py:65
  24.4 6.9 %all_gather.13 = bf16[256,512]{1,0:T(8,128)(2,1)S(1)} all-gather(bf16[128,512]{1,0:T(8,128)(2,1)S(1)} %all_gather.12), channel_id=1, replica_groups=mesh['group'=2,'sub'=4,'tile'=2,'rep'=2] {'tile'}, dimensions={0}, use_global_device_ids=true | all-gather | bytes 393216 | tf_op jit(solution)/shard_map/all_gather | solution.py:67
  32.5 20.2 %reduce-scatter.7.cloned.1.call-done = bf16[64,512]{1,0:T(8,128)(2,1)} async-done(((bf16[256,512]{1,0:T(8,128)(2,1)}), bf16[64,512]{1,0:T(8,128)(2,1)}) %reduce-scatter.7.cloned.1.call-update) | async-done | bytes 65552
  53.7 3.8 %all_to_all.38 = bf16[64,2,256]{2,0,1:T(8,128)(2,1)S(1)} all-to-all(bf16[64,2,256]{2,0,1:T(8,128)(2,1)S(1)} %copy.35), channel_id=1, replica_groups=mesh['group'=2,'sub'=4,'tile'=2,'rep'=2] {'rep'}, dimensions={1} | all-to-all | bytes 131072 | tf_op jit(solution)/shard_map/all_to_all | solution.py:72
  57.5 1.6 %convolution_add_fusion.1 = f32[1024,256]{0,1:T(8,128)S(1)} fusion(f32[1024,256]{0,1:T(8,128)} %copy-done.1, bf16[128,256]{1,0:T(8,128)(2,1)S(1)} %bitcast.78, bf16[1,1024,128]{2,1,0:T(8,128)(2,1)S(1)} %copy-done.4, pred[128]{0:T(512)(128)(4,1)S(1)} %iota_compare_fusion), kind=kOutput, calls=%fused_computation.11 | convolution fusion | flops 67502080 | bytes 2424960 | tf_op jit(solution)/shard_map/dot_general | solution.py:73
  59.1 1.0 copy.37
  60.1 2.5 %gather_fusion.3 = bf16[128,256]{1,0:T(8,128)(2,1)} fusion(bf16[1024,256]{1,0:T(8,128)(2,1)} %copy.37, s32[1024]{0:T(1024)S(1)} %pad_clamp_fusion), kind=kCustom, calls=%fused_computation.3 | custom fusion | bytes 131584 | tf_op jit(solution)/shard_map/gather | solution.py:47
  62.6 2.5 %gather_fusion.2 = bf16[128,256]{1,0:T(8,128)(2,1)} fusion(bf16[1024,256]{1,0:T(8,128)(2,1)} %copy.37, s32[1024]{0:T(1024)S(1)} %pad_clamp_fusion.1), kind=kCustom, calls=%fused_computation.2 | custom fusion | bytes 131584 | tf_op jit(solution)/shard_map/gather | solution.py:48
  65.0 3.4 %collective-permute-start.2 = (bf16[128,256]{1,0:T(8,128)(2,1)}, bf16[128,256]{1,0:T(8,128)(2,1)S(1)}, u32[]{:S(2)}, u32[]{:S(2)}) collective-permute-start(bf16[128,256]{1,0:T(8,128)(2,1)} %gather_fusion.2), channel_id=1, source_target_pairs={{0,2},{2,4},{4,6},{6,8},{8,10},{10,12},{12,14},{1,3},{3,5},{5,7},{... | collective-permute-start | bytes 196616 | tf_op jit(solution)/shard_map/ppermute | solution.py:12
  68.5 1.3 %collective-permute-start.3 = (bf16[128,256]{1,0:T(8,128)(2,1)}, bf16[128,256]{1,0:T(8,128)(2,1)S(1)}, u32[]{:S(2)}, u32[]{:S(2)}) collective-permute-start(bf16[128,256]{1,0:T(8,128)(2,1)} %gather_fusion.3), channel_id=1, source_target_pairs={{2,0},{4,2},{6,4},{8,6},{10,8},{12,10},{14,12},{3,1},{5,3},{7,5},{... | collective-permute-start | bytes 196616 | tf_op jit(solution)/shard_map/ppermute | solution.py:12
  70.7 4.2 %collective-permute-done.3 = bf16[128,256]{1,0:T(8,128)(2,1)S(1)} collective-permute-done((bf16[128,256]{1,0:T(8,128)(2,1)}, bf16[128,256]{1,0:T(8,128)(2,1)S(1)}, u32[]{:S(2)}, u32[]{:S(2)}) %collective-permute-start.3) | collective-permute-done | bytes 65568 | tf_op jit(solution)/shard_map/ppermute | solution.py:12
  74.9 1.1 add_convert_fusion.1
  75.9 1.8 %fusion.7 = f32[1024,256]{0,1:T(8,128)S(1)} fusion(bf16[1,1024,1024]{2,1,0:T(8,128)(2,1)S(1)} %copy-done, bf16[768,256]{1,0:T(8,128)(2,1)} %copy-done.7, bf16[128,256]{1,0:T(8,128)(2,1)S(1)} %get-tuple-element.6, bf16[128,256]{1,0:T(8,128)(2,1)S(1)} %get-tuple-element.5), kind=kOutput, calls=%fused_computation.9 | convolution fusion | flops 538443776 | bytes 3670016 | tf_op jit(solution)/shard_map/dot_general | solution.py:60
  78.7 1.9 %all_gather.14 = bf16[128,512]{1,0:T(8,128)(2,1)S(1)} all-gather(bf16[128,256]{1,0:T(8,128)(2,1)S(1)} %convolution_convert_fusion.2), channel_id=1, replica_groups=mesh['group'=2,'sub'=4,'tile'=2,'rep'=2] {'rep'}, dimensions={1}, use_global_device_ids=true | all-gather | bytes 196608 | tf_op jit(solution)/shard_map/all_gather | solution.py:65
  80.6 6.4 %all_gather.15 = bf16[256,512]{1,0:T(8,128)(2,1)S(1)} all-gather(bf16[128,512]{1,0:T(8,128)(2,1)S(1)} %all_gather.14), channel_id=1, replica_groups=mesh['group'=2,'sub'=4,'tile'=2,'rep'=2] {'tile'}, dimensions={0}, use_global_device_ids=true | all-gather | bytes 393216 | tf_op jit(solution)/shard_map/all_gather | solution.py:67
  87.9 1.8 %copy.51 = bf16[256,512]{1,0:T(8,128)(2,1)} copy(bf16[256,512]{0,1:T(8,128)(2,1)} %fusion.13) | data formatting | bytes 524288
  89.7 18.1 %reduce-scatter.9.cloned.1.call-done = bf16[64,512]{1,0:T(8,128)(2,1)} async-done(((bf16[256,512]{1,0:T(8,128)(2,1)}), bf16[64,512]{1,0:T(8,128)(2,1)}) %reduce-scatter.9.cloned.1.call-update) | async-done | bytes 65552
  109.5 4.7 %all_to_all.39 = bf16[64,2,256]{2,0,1:T(8,128)(2,1)S(1)} all-to-all(bf16[64,2,256]{2,0,1:T(8,128)(2,1)} %copy.40), channel_id=1, replica_groups=mesh['group'=2,'sub'=4,'tile'=2,'rep'=2] {'rep'}, dimensions={1} | all-to-all | bytes 131072 | tf_op jit(solution)/shard_map/all_to_all | solution.py:72
  114.2 1.1 fusion.11
  115.3 2.0 %copy.42 = bf16[1,1024,256]{2,1,0:T(8,128)(2,1)} copy(bf16[1,1024,256]{1,2,0:T(8,128)(2,1)} %fusion.11) | data formatting | bytes 1048576 | tf_op jit(solution)/shard_map/broadcast_in_dim | solution.py:76
  (44 shorter events, 12.4 us)
Async XLA Ops:
  6.5 13.8 %copy-start = (bf16[1,1024,1024]{2,1,0:T(8,128)(2,1)S(1)}, bf16[1,1024,1024]{2,1,0:T(8,128)(2,1)}, u32[]{:S(2)}) copy-start(bf16[1,1024,1024]{2,1,0:T(8,128)(2,1)} %param.8) | copy-start | bytes 6291460
  6.5 46.1 %reduce-scatter.7.cloned.1.call-start = ((), (), s32[]{:S(2)}) async-start(), calls=%async_computation.4 | async-start | bytes 327680
  8.3 9.6 %collective-permute-start = (bf16[128,256]{1,0:T(8,128)(2,1)S(1)}, bf16[128,256]{1,0:T(8,128)(2,1)S(1)}, u32[]{:S(2)}, u32[]{:S(2)}) collective-permute-start(bf16[128,256]{1,0:T(8,128)(2,1)S(1)} %gather_fusion), channel_id=1, source_target_pairs={{0,2},{2,4},{4,6},{6,8},{8,10},{10,12},{12,14},{1,3},{3,5},{5,7},{... | collective-permute-start | bytes 196616 | tf_op jit(solution)/shard_map/ppermute | solution.py:12
  14.0 6.2 %collective-permute-start.1 = (bf16[128,256]{1,0:T(8,128)(2,1)S(1)}, bf16[128,256]{1,0:T(8,128)(2,1)S(1)}, u32[]{:S(2)}, u32[]{:S(2)}) collective-permute-start(bf16[128,256]{1,0:T(8,128)(2,1)S(1)} %gather_fusion.1), channel_id=1, source_target_pairs={{2,0},{4,2},{6,4},{8,6},{10,8},{12,10},{14,12},{3,1},{5,3},{7,5},{... | collective-permute-start | bytes 196616 | tf_op jit(solution)/shard_map/ppermute | solution.py:12
  16.7 3.6 %copy-start.8 = (f32[128]{0:T(128)}, f32[128]{0:T(128)S(1)}, u32[]{:S(2)}) copy-start(f32[128]{0:T(128)S(1)} %get-tuple-element.10) | copy-start | bytes 1540
  17.8 2.5 %copy-start.5 = (f32[1,1024,256]{2,1,0:T(8,128)}, f32[1,1024,256]{2,1,0:T(8,128)S(1)}, u32[]{:S(2)}) copy-start(f32[1,1024,256]{2,1,0:T(8,128)S(1)} %convert_element_type.57) | copy-start | bytes 3145732
  17.9 3.2 %copy-start.7 = (bf16[768,256]{1,0:T(8,128)(2,1)}, bf16[768,256]{1,0:T(8,128)(2,1)S(1)}, u32[]{:S(2)}) copy-start(bf16[768,256]{1,0:T(8,128)(2,1)S(1)} %fusion.23) | copy-start | bytes 1179652
  20.3 1.8 %copy-start.4 = (bf16[1,1024,128]{2,1,0:T(8,128)(2,1)S(1)}, bf16[1,1024,128]{2,1,0:T(8,128)(2,1)}, u32[]{:S(2)}) copy-start(bf16[1,1024,128]{2,1,0:T(8,128)(2,1)} %param.11) | copy-start | bytes 786436
  20.3 10.9 %copy-start.6 = (bf16[4,1,64,1,256]{4,2,3,1,0:T(8,128)(2,1)S(1)}, bf16[4,1,64,1,256]{4,2,3,1,0:T(8,128)(2,1)}, u32[]{:S(2)}) copy-start(bf16[4,1,64,1,256]{4,2,3,1,0:T(8,128)(2,1)} %param.13) | copy-start | bytes 393220
  21.1 1.0 copy-start.1
  32.4 75.4 %reduce-scatter.9.cloned.1.call-start = ((), (), s32[]{:S(2)}) async-start(), calls=%async_computation.5 | async-start | bytes 327680
  65.0 5.6 %collective-permute-start.2 = (bf16[128,256]{1,0:T(8,128)(2,1)}, bf16[128,256]{1,0:T(8,128)(2,1)S(1)}, u32[]{:S(2)}, u32[]{:S(2)}) collective-permute-start(bf16[128,256]{1,0:T(8,128)(2,1)} %gather_fusion.2), channel_id=1, source_target_pairs={{0,2},{2,4},{4,6},{6,8},{8,10},{10,12},{12,14},{1,3},{3,5},{5,7},{... | collective-permute-start | bytes 196616 | tf_op jit(solution)/shard_map/ppermute | solution.py:12
  68.5 6.4 %collective-permute-start.3 = (bf16[128,256]{1,0:T(8,128)(2,1)}, bf16[128,256]{1,0:T(8,128)(2,1)S(1)}, u32[]{:S(2)}, u32[]{:S(2)}) collective-permute-start(bf16[128,256]{1,0:T(8,128)(2,1)} %gather_fusion.3), channel_id=1, source_target_pairs={{2,0},{4,2},{6,4},{8,6},{10,8},{12,10},{14,12},{3,1},{5,3},{7,5},{... | collective-permute-start | bytes 196616 | tf_op jit(solution)/shard_map/ppermute | solution.py:12
  77.7 1.0 copy-start.2
  80.6 33.6 %copy-start.3 = (f32[1024,256]{0,1:T(8,128)S(1)}, f32[1024,256]{0,1:T(8,128)}, u32[]{:S(2)}) copy-start(f32[1024,256]{0,1:T(8,128)} %copy-done.2) | copy-start | bytes 3145732
Sparse Core Ops, SparseCore 0:
  32.5 20.0 reduce-scatter.6
  89.9 17.9 reduce-scatter.8
where the time goes:
time: 125 us; the launch traced here: 124 us
  waiting for transfers between devices  45.6 us (36%)
  blocking collectives  25.5 us (20%)
  local copies, waits for them, and re-layouts  17.6 us (14%)
  between operations  14.3 us (11%)
  starting transfers between devices  10.9 us (9%)
  matrix products  7.14 us (6%)
  other arithmetic  3.16 us (3%)
    unnamed x4, waiting for transfers between devices  38.3 us
    all_gather x2, blocking collectives, local(): lax.all_gather(all_modes, 'tile', axis=0, tiled=True)  13.3 us
    ppermute x4, starting transfers between devices, passed_along(): return lax.ppermute(shard, axis, pairs)  10.9 us
    all_to_all x2, blocking collectives, local(): lax.all_to_all(own_coarse, 'rep', split_axis=1, concat_axis=0, tiled=True)  8.49 us
    ppermute x4, waiting for transfers between devices, passed_along(): return lax.ppermute(shard, axis, pairs)  7.31 us
    unnamed x22, local copies, waits for them, and re-layouts  6.19 us
    all_gather x2, blocking collectives, local(): all_modes = lax.all_gather(projected, 'rep', axis=1, tiled=True)  3.79 us
    gather x2, local copies, waits for them, and re-layouts, local(): upper_trace = iterate[trace_rows[0, 1]]  3.33 us
  transfers between devices with their start and end apart: 6, of which 5 were waited for; matrix products, arithmetic and copies ran while one was open for 2% of the time, Pallas kernels for 0%

commit v1 on v0

v1 whole, which is shorter than its diff:
```python
import jax
import jax.numpy as jnp
from jax import lax
from jax.sharding import PartitionSpec as P

ROUNDS = 2
DUCT = ("sub", "tile")


def passed_along(shard, by):
    peers = lax.axis_size(DUCT)
    pairs = [(i, i + by) for i in range(peers) if 0 <= i + by < peers]
    return lax.ppermute(shard, DUCT, pairs)


def own_coarse_rows(coarse_inverse):
    rows = lax.all_to_all(coarse_inverse, "sub", split_axis=0, concat_axis=3, tiled=True)
    rows = lax.all_gather(rows, "rep", axis=2, tiled=True)
    return rows.reshape(rows.shape[2], rows.shape[3] * rows.shape[4])


def local(
    right_side,
    interface_inverse,
    coupling,
    trace_rows,
    deflation_basis,
    deflation_counts,
    coarse_inverse,
):
    source = right_side[0]
    inverse = interface_inverse[0]
    iface_rows = inverse.shape[0]
    face_rows = coupling.shape[2]
    slot_count = deflation_basis.shape[2]
    slot_ids = jnp.arange(slot_count, dtype=jnp.int32)
    masked_basis = jnp.where(
        slot_ids[None, :] < deflation_counts[0],
        deflation_basis[0],
        jnp.zeros((), deflation_basis.dtype),
    )
    coarse_rows = own_coarse_rows(coarse_inverse)
    lower_gain = coupling[0, 0][:, None]
    upper_gain = coupling[0, 1][:, None]

    def coarse_step(local_solve, defect):
        projected = lax.dot_general(
            masked_basis, defect, (((0,), (0,)), ((), ())), preferred_element_type=jnp.float32
        ).astype(jnp.bfloat16)
        vector = lax.all_gather(projected, DUCT, axis=0, tiled=True)
        coarse = jnp.dot(coarse_rows, vector, preferred_element_type=jnp.float32).astype(
            jnp.bfloat16
        )
        return local_solve + jnp.dot(masked_basis, coarse, preferred_element_type=jnp.float32)

    local_solve = jnp.dot(inverse, source, preferred_element_type=jnp.float32)
    iterate = coarse_step(local_solve, local_solve.astype(jnp.bfloat16))
    for cycle_index in range(1, ROUNDS):
        lower_trace = iterate[trace_rows[0, 0]]
        upper_trace = iterate[trace_rows[0, 1]]
        from_lower = passed_along(upper_trace.astype(jnp.bfloat16), 1).astype(jnp.float32)
        from_upper = passed_along(lower_trace.astype(jnp.bfloat16), -1).astype(jnp.float32)
        lower_rows = source[:face_rows].astype(jnp.float32) + lower_gain * from_lower
        upper_rows = source[iface_rows - face_rows :].astype(jnp.float32) + upper_gain * from_upper
        boundary = jnp.concatenate(
            [
                lower_rows.astype(jnp.bfloat16),
                source[face_rows : iface_rows - face_rows],
                upper_rows.astype(jnp.bfloat16),
            ],
            axis=0,
        )
        local_solve = jnp.dot(inverse, boundary, preferred_element_type=jnp.float32)
        iterate = coarse_step(local_solve, (local_solve - iterate).astype(jnp.bfloat16))
    return iterate.astype(jnp.bfloat16)[None]


def solution(mesh):
    placed = (
        P(("group", "sub", "tile"), None, "rep"),
        P(("group", "sub", "tile"), None, None),
        P(("group", "sub", "tile"), None, None),
        P(("group", "sub", "tile"), None, None),
        P(("group", "sub", "tile"), None, None),
        P(("group", "sub", "tile")),
        P("group", "tile", "rep", "sub", None),
    )
    return jax.shard_map(
        local,
        mesh=mesh,
        in_specs=placed,
        out_specs=P(("group", "sub", "tile"), None, "rep"),
        check_vma=False,
    )
```

time: 125 us -> 101 us (0.81)
  blocking collectives: 25.5 us -> 67.3 us
  waiting for transfers between devices: 45.6 us -> 4.84 us
  between operations: 14.3 us -> 0.77 us
  local copies, waits for them, and re-layouts: 17.6 us -> 5.93 us
  matrix products: 7.14 us -> 8.85 us
  other arithmetic: 3.16 us -> 1.75 us
    all_gather x4 -> x3, blocking collectives: 17.1 us -> 67.3 us  [the longest x2 65.3 us: coarse_step(): vector = lax.all_gather(projected, DUCT, axis=0, tiled=True)]
    unnamed x4 -> x0, waiting for transfers between devices: 38.3 us -> none
    all_to_all x2 -> x0, blocking collectives: 8.49 us -> none  [local(): lax.all_to_all(own_coarse, 'rep', split_axis=1, concat_axis=0, tiled=True)]
    all_to_all x0 -> x1, starting transfers between devices: none -> 6.45 us  [own_coarse_rows(): lax.all_to_all(coarse_inverse, 'sub', split_axis=0, concat_axis=3, tiled=...]
    ppermute x4 -> x2, starting transfers between devices: 10.9 us -> 4.83 us  [passed_along(): return lax.ppermute(shard, DUCT, pairs)]
    unnamed x22 -> x10, local copies, waits for them, and re-layouts: 6.19 us -> 1.64 us
    gather x2 -> x1, local copies, waits for them, and re-layouts: 3.33 us -> 0.76 us  [local(): upper_trace = iterate[trace_rows[0, 1]]]
    gather x2 -> x1, local copies, waits for them, and re-layouts: 3.33 us -> 0.76 us  [local(): lower_trace = iterate[trace_rows[0, 0]]]
  transfers between devices with their start and end apart: 6 -> 3, of which waited for: 5 -> 2; matrix products, arithmetic and copies ran while one was open for 2% -> 5% of each run, Pallas kernels for 0% -> 0%
where the time goes in v1:
time: 101 us
  blocking collectives  67.3 us (67%)
  starting transfers between devices  11.3 us (11%)
  matrix products  8.85 us (9%)
  local copies, waits for them, and re-layouts  5.93 us (6%)
  waiting for transfers between devices  4.84 us (5%)
  other arithmetic  1.75 us (2%)
    all_gather x2, blocking collectives, coarse_step(): vector = lax.all_gather(projected, DUCT, axis=0, tiled=True)  65.3 us
    all_to_all x1, starting transfers between devices, own_coarse_rows(): lax.all_to_all(coarse_inverse, 'sub', split_axis=0, concat_axis=3, tiled=...  6.45 us
    ppermute x2, waiting for transfers between devices, passed_along(): return lax.ppermute(shard, DUCT, pairs)  4.84 us
    ppermute x2, starting transfers between devices, passed_along(): return lax.ppermute(shard, DUCT, pairs)  4.83 us
    dot_general x2, matrix products, coarse_step(): jnp.dot(masked_basis, coarse, preferred_element_type=jnp.float32)  4.79 us
  transfers between devices with their start and end apart: 3, of which 2 were waited for; matrix products, arithmetic and copies ran while one was open for 5% of the time, Pallas kernels for 0%

profile of v1, /device:TPU:0, one launch (start us, length us, event | category | flops | bytes accessed | tf_op | source)
XLA Modules:
  0.0 100.7 jit_solution(9996963207697085527)
XLA Ops:
  0.0 6.4 %all-to-all-start = ((bf16[4,1,64,1,256]{4,2,3,1,0:T(8,128)(2,1)}), bf16[4,1,64,1,256]{4,2,3,1,0:T(8,128)(2,1)S(1)}, u32[]{:S(2)}, u32[]{:S(2)}) async-start(bf16[4,1,64,1,256]{4,2,3,1,0:T(8,128)(2,1)} %param.13), calls=%async_computation | async-start | bytes 262144 | tf_op jit(solution)/shard_map/all_to_all | solution.py:17
  7.1 0.8 fusion.22
  7.9 1.8 %slice_bitcast_fusion = bf16[768,256]{1,0:T(8,128)(2,1)} fusion(bf16[1,1024,256]{2,1,0:T(8,128)(2,1)} %param.7), kind=kLoop, calls=%fused_computation.23 | loop fusion | bytes 786432 | tf_op jit(solution)/shard_map/slice | solution.py:68
  9.7 1.8 %fusion.2 = f32[1024,256]{1,0:T(8,128)S(1)} fusion(bf16[1,1024,1024]{2,1,0:T(8,128)(2,1)S(1)} %copy-done, bf16[1,1024,256]{2,1,0:T(8,128)(2,1)} %param.7), kind=kOutput, calls=%fused_computation.4 | convolution fusion | flops 536870912 | bytes 3670016 | tf_op jit(solution)/shard_map/dot_general | solution.py:56
  11.5 1.0 copy-done.1
  12.4 0.3 convolution_convert_fusion.3
  12.7 34.0 %all_gather.9 = bf16[1024,256]{1,0:T(8,128)(2,1)} all-gather(bf16[128,256]{1,0:T(8,128)(2,1)S(1)} %convolution_convert_fusion.3), channel_id=1, replica_groups=mesh['group'=2,'sub'=4,'tile'=2,'rep'=2] {'sub','tile'}, dimensions={0}, use_global_device_ids=true | all-gather | bytes 589824 | tf_op jit(solution)/shard_map/all_gather | solution.py:50
  46.7 0.0 all-to-all-done
  46.7 0.1 copy.11
  46.8 2.0 %all-gather = bf16[1,1,128,4,1,256]{5,3,4,1,0,2:T(4,128)(2,1)S(1)} all-gather(bf16[1,1,64,4,1,256]{5,3,4,1,0,2:T(4,128)(2,1)S(1)} %copy.11), channel_id=2, replica_groups=mesh['group'=2,'sub'=4,'tile'=2,'rep'=2] {'rep'}, dimensions={2}, use_global_device_ids=true | all-gather | bytes 393216 | tf_op jit(solution)/shard_map/all_gather | solution.py:18
  48.8 0.9 copy.12
  49.7 2.1 %convolution_add_fusion.1 = f32[1024,256]{1,0:T(8,128)S(1)} fusion(f32[1024,256]{1,0:T(8,128)} %copy-done.1, bf16[1024,256]{1,0:T(8,128)(2,1)} %all_gather.9, bf16[128,1024]{0,1:T(8,128)(2,1)} %bitcast.50, bf16[1,1024,128]{2,1,0:T(8,128)(2,1)S(1)} %copy-done.3, pred[128]{0:T(512)(128)(4,1)S(1)} %iota_compare_fusion), kind=kOutput, calls=%fused_computation.8 | convolution fusion | flops 134643712 | bytes 3145856 | tf_op jit(solution)/shard_map/dot_general | solution.py:54
  51.8 0.8 gather_fusion.1
  52.5 0.8 gather_fusion
  53.3 3.5 %collective-permute-start = (bf16[128,256]{1,0:T(8,128)(2,1)S(1)}, bf16[128,256]{1,0:T(8,128)(2,1)S(1)}, u32[]{:S(2)}, u32[]{:S(2)}) collective-permute-start(bf16[128,256]{1,0:T(8,128)(2,1)S(1)} %gather_fusion), channel_id=1, source_target_pairs={{0,2},{2,4},{4,6},{6,8},{8,10},{10,12},{12,14},{1,3},{3,5},{5,7},{... | collective-permute-start | bytes 196616 | tf_op jit(solution)/shard_map/ppermute | solution.py:13
  56.9 1.3 %collective-permute-start.1 = (bf16[128,256]{1,0:T(8,128)(2,1)S(1)}, bf16[128,256]{1,0:T(8,128)(2,1)S(1)}, u32[]{:S(2)}, u32[]{:S(2)}) collective-permute-start(bf16[128,256]{1,0:T(8,128)(2,1)S(1)} %gather_fusion.1), channel_id=1, source_target_pairs={{2,0},{4,2},{6,4},{8,6},{10,8},{12,10},{14,12},{3,1},{5,3},{7,5},{... | collective-permute-start | bytes 196616 | tf_op jit(solution)/shard_map/ppermute | solution.py:13
  58.2 0.6 collective-permute-done
  58.7 4.3 %collective-permute-done.1 = bf16[128,256]{1,0:T(8,128)(2,1)S(1)} collective-permute-done((bf16[128,256]{1,0:T(8,128)(2,1)S(1)}, bf16[128,256]{1,0:T(8,128)(2,1)S(1)}, u32[]{:S(2)}, u32[]{:S(2)}) %collective-permute-start.1) | collective-permute-done | bytes 65568 | tf_op jit(solution)/shard_map/ppermute | solution.py:13
  63.0 1.0 fusion.17
  64.0 1.7 %fusion.4 = f32[1024,256]{1,0:T(8,128)S(1)} fusion(bf16[1,1024,1024]{2,1,0:T(8,128)(2,1)S(1)} %copy-done, bf16[128,256]{1,0:T(8,128)(2,1)S(1)} %get-tuple-element.6, bf16[768,256]{1,0:T(8,128)(2,1)} %slice_bitcast_fusion, bf16[128,256]{1,0:T(8,128)(2,1)S(1)} %get-tuple-element.5), kind=kOutput, calls=%fused_computation.6 | convolution fusion | flops 538443776 | bytes 3670016 | tf_op jit(solution)/shard_map/dot_general | solution.py:73
  65.7 0.3 convolution_convert_fusion.1
  66.0 0.7 copy-done.2
  66.7 31.3 %all_gather.11 = bf16[1024,256]{1,0:T(8,128)(2,1)S(1)} all-gather(bf16[128,256]{1,0:T(8,128)(2,1)S(1)} %convolution_convert_fusion.1), channel_id=1, replica_groups=mesh['group'=2,'sub'=4,'tile'=2,'rep'=2] {'sub','tile'}, dimensions={0}, use_global_device_ids=true | all-gather | bytes 589824 | tf_op jit(solution)/shard_map/all_gather | solution.py:50
  98.0 2.7 %fusion.8 = bf16[1,1024,256]{2,1,0:T(8,128)(2,1)} fusion(f32[1024,256]{1,0:T(8,128)} %copy-done.2, bf16[1024,256]{1,0:T(8,128)(2,1)S(1)} %all_gather.11, bf16[128,1024]{0,1:T(8,128)(2,1)} %bitcast.51, bf16[1,1024,128]{2,1,0:T(8,128)(2,1)S(1)} %copy-done.3, pred[128]{0:T(512)(128)(4,1)S(1)} %iota_compare_fusion), kind=kOutput, calls=%fused_computation.10 | convolution fusion | flops 134905856 | bytes 2621568 | tf_op jit(solution)/shard_map/dot_general | solution.py:54
  (12 shorter events, 0.0 us)
Async XLA Ops:
  0.0 9.7 %copy-start = (bf16[1,1024,1024]{2,1,0:T(8,128)(2,1)S(1)}, bf16[1,1024,1024]{2,1,0:T(8,128)(2,1)}, u32[]{:S(2)}) copy-start(bf16[1,1024,1024]{2,1,0:T(8,128)(2,1)} %param.8) | copy-start | bytes 6291460
  0.0 46.7 %all-to-all-start = ((bf16[4,1,64,1,256]{4,2,3,1,0:T(8,128)(2,1)}), bf16[4,1,64,1,256]{4,2,3,1,0:T(8,128)(2,1)S(1)}, u32[]{:S(2)}, u32[]{:S(2)}) async-start(bf16[4,1,64,1,256]{4,2,3,1,0:T(8,128)(2,1)} %param.13), calls=%async_computation | async-start | bytes 262144 | tf_op jit(solution)/shard_map/all_to_all | solution.py:17
  9.7 2.8 %copy-start.3 = (bf16[1,1024,128]{2,1,0:T(8,128)(2,1)S(1)}, bf16[1,1024,128]{2,1,0:T(8,128)(2,1)}, u32[]{:S(2)}) copy-start(bf16[1,1024,128]{2,1,0:T(8,128)(2,1)} %param.11) | copy-start | bytes 786436
  11.5 1.0 copy-start.1
  49.7 8.5 %copy-start.4 = (f32[1,2,128]{2,1,0:T(2,128)S(1)}, f32[1,2,128]{2,1,0:T(2,128)}, u32[]{:S(2)}) copy-start(f32[1,2,128]{2,1,0:T(2,128)} %param.9) | copy-start | bytes 3076
  53.3 5.4 %collective-permute-start = (bf16[128,256]{1,0:T(8,128)(2,1)S(1)}, bf16[128,256]{1,0:T(8,128)(2,1)S(1)}, u32[]{:S(2)}, u32[]{:S(2)}) collective-permute-start(bf16[128,256]{1,0:T(8,128)(2,1)S(1)} %gather_fusion), channel_id=1, source_target_pairs={{0,2},{2,4},{4,6},{6,8},{8,10},{10,12},{12,14},{1,3},{3,5},{5,7},{... | collective-permute-start | bytes 196616 | tf_op jit(solution)/shard_map/ppermute | solution.py:13
  56.9 6.2 %collective-permute-start.1 = (bf16[128,256]{1,0:T(8,128)(2,1)S(1)}, bf16[128,256]{1,0:T(8,128)(2,1)S(1)}, u32[]{:S(2)}, u32[]{:S(2)}) collective-permute-start(bf16[128,256]{1,0:T(8,128)(2,1)S(1)} %gather_fusion.1), channel_id=1, source_target_pairs={{2,0},{4,2},{6,4},{8,6},{10,8},{12,10},{14,12},{3,1},{5,3},{7,5},{... | collective-permute-start | bytes 196616 | tf_op jit(solution)/shard_map/ppermute | solution.py:13
  65.7 1.0 copy-start.2

commit v2 on v1

--- a/solution.py
+++ b/solution.py
@@ -5,6 +5,8 @@
 
 ROUNDS = 2
 DUCT = ("sub", "tile")
+OWNERS = ("sub", "rep")
+MAX_RING = 8
 
 
 def passed_along(shard, by):
@@ -13,10 +15,48 @@
     return lax.ppermute(shard, DUCT, pairs)
 
 
+def shifted_copies(pick, axes):
+    peers = lax.axis_size(axes)
+    parts = [pick(0)]
+    for k in range(1, peers):
+        parts.append(lax.ppermute(pick(k), axes, [(i, (i + k) % peers) for i in range(peers)]))
+    return jnp.stack(parts)
+
+
+def sources(axes):
+    peers = lax.axis_size(axes)
+    return (lax.axis_index(axes) - jnp.arange(peers)) % peers
+
+
 def own_coarse_rows(coarse_inverse):
-    rows = lax.all_to_all(coarse_inverse, "sub", split_axis=0, concat_axis=3, tiled=True)
-    rows = lax.all_gather(rows, "rep", axis=2, tiled=True)
-    return rows.reshape(rows.shape[2], rows.shape[3] * rows.shape[4])
+    out_sub, _, half_slots, _, in_cols = coarse_inverse.shape
+    if lax.axis_size(OWNERS) > MAX_RING:
+        rows = lax.all_to_all(coarse_inverse, "sub", split_axis=0, concat_axis=3, tiled=True)
+        rows = lax.all_gather(rows, "rep", axis=2, tiled=True)
+        return rows.reshape(rows.shape[2], rows.shape[3] * rows.shape[4])
+    reps = lax.axis_size("rep")
+    blocks = coarse_inverse[:, 0, :, 0, :]
+
+    def pick(k):
+        target = (lax.axis_index(OWNERS) + k) % lax.axis_size(OWNERS)
+        return lax.dynamic_index_in_dim(blocks, target // reps, 0, keepdims=False)
+
+    parts = shifted_copies(pick, OWNERS)
+    order = jnp.argsort(sources(OWNERS))
+    parts = jnp.take(parts, order, axis=0)
+    parts = parts.reshape(out_sub, reps, half_slots, in_cols).transpose(1, 2, 0, 3)
+    return parts.reshape(reps * half_slots, out_sub * in_cols)
+
+
+def gathered_product(coarse_rows, projected):
+    peers = lax.axis_size(DUCT)
+    if peers > MAX_RING:
+        vector = lax.all_gather(projected, DUCT, axis=0, tiled=True)
+        return jnp.dot(coarse_rows, vector, preferred_element_type=jnp.float32)
+    parts = shifted_copies(lambda k: projected, DUCT)
+    return jnp.dot(
+        coarse_rows, parts.reshape(-1, parts.shape[-1]), preferred_element_type=jnp.float32
+    )
 
 
 def local(
@@ -40,6 +80,11 @@
         jnp.zeros((), deflation_basis.dtype),
     )
     coarse_rows = own_coarse_rows(coarse_inverse)
+    peers = lax.axis_size(DUCT)
+    if peers <= MAX_RING:
+        coarse_rows = jnp.take(
+            coarse_rows.reshape(coarse_rows.shape[0], peers, -1), sources(DUCT), axis=1
+        ).reshape(coarse_rows.shape[0], -1)
     lower_gain = coupling[0, 0][:, None]
     upper_gain = coupling[0, 1][:, None]
 
@@ -47,10 +92,7 @@
         projected = lax.dot_general(
             masked_basis, defect, (((0,), (0,)), ((), ())), preferred_element_type=jnp.float32
         ).astype(jnp.bfloat16)
-        vector = lax.all_gather(projected, DUCT, axis=0, tiled=True)
-        coarse = jnp.dot(coarse_rows, vector, preferred_element_type=jnp.float32).astype(
-            jnp.bfloat16
-        )
+        coarse = gathered_product(coarse_rows, projected).astype(jnp.bfloat16)
         return local_solve + jnp.dot(masked_basis, coarse, preferred_element_type=jnp.float32)
 
     local_solve = jnp.dot(inverse, source, preferred_element_type=jnp.float32)

time: 101 us -> 94.4 us (0.935)
  blocking collectives: 67.3 us -> 0 us
  waiting for transfers between devices: 4.84 us -> 28.1 us
  starting transfers between devices: 11.3 us -> 31.9 us
  local copies, waits for them, and re-layouts: 5.93 us -> 19.3 us
  matrix products: 8.85 us -> 10.5 us
  other arithmetic: 1.75 us -> 3.31 us
    all_gather x3 -> x0, blocking collectives: 67.3 us -> none  [the longest x2 65.3 us: coarse_step(): vector = lax.all_gather(projected, DUCT, axis=0, tiled=True)]
    ppermute x0 -> x21, starting transfers between devices: none -> 26.5 us  [shifted_copies(): lax.ppermute(pick(k), axes, [(i, (i + k) % peers) for i in range(peers)])]
    ppermute x0 -> x21, waiting for transfers between devices: none -> 23.7 us  [shifted_copies(): lax.ppermute(pick(k), axes, [(i, (i + k) % peers) for i in range(peers)])]
    unnamed x10 -> x33, local copies, waits for them, and re-layouts: 1.64 us -> 10.2 us
    all_to_all x1 -> x0, starting transfers between devices: 6.45 us -> none  [own_coarse_rows(): lax.all_to_all(coarse_inverse, 'sub', split_axis=0, concat_axis=3, tiled=...]
    gather x0 -> x2, local copies, waits for them, and re-layouts: none -> 1.87 us  [the longest x1 1.31 us: local(): jnp.take(coarse_rows.reshape(coarse_rows.shape[0], peers, -1), sources(DU...]
    sort x0 -> x1, other arithmetic: none -> 1.59 us  [own_coarse_rows(): order = jnp.argsort(sources(OWNERS))]
    another operation x0 -> x5, local copies, waits for them, and re-layouts: none -> 1.41 us  [the longest x3 1.27 us: shifted_copies(): return jnp.stack(parts)]
  transfers between devices with their start and end apart: 3 -> 23, of which waited for: 2 -> 12; matrix products, arithmetic and copies ran while one was open for 5% -> 19% of each run, Pallas kernels for 0% -> 0%
where the time goes in v2:
time: 94.4 us; the launch traced here: 94 us
  starting transfers between devices  31.9 us (34%)
  waiting for transfers between devices  28.1 us (30%)
  local copies, waits for them, and re-layouts  19.3 us (20%)
  matrix products  10.5 us (11%)
  other arithmetic  3.31 us (4%)
  between operations  1.01 us (1%)
    ppermute x21, starting transfers between devices, shifted_copies(): lax.ppermute(pick(k), axes, [(i, (i + k) % peers) for i in range(peers)])  26.5 us
    ppermute x21, waiting for transfers between devices, shifted_copies(): lax.ppermute(pick(k), axes, [(i, (i + k) % peers) for i in range(peers)])  23.7 us
    unnamed x33, local copies, waits for them, and re-layouts  10.2 us
    ppermute x2, starting transfers between devices, passed_along(): return lax.ppermute(shard, DUCT, pairs)  5.35 us
    dot_general x2, matrix products, coarse_step(): jnp.dot(masked_basis, coarse, preferred_element_type=jnp.float32)  5.05 us
    ppermute x2, waiting for transfers between devices, passed_along(): return lax.ppermute(shard, DUCT, pairs)  4.31 us
    dot_general x2, matrix products, coarse_step(): lax.dot_general(masked_basis, defect, (((0,), (0,)), ((), ())), preferred...  1.9 us
  transfers between devices with their start and end apart: 23, of which 12 were waited for; matrix products, arithmetic and copies ran while one was open for 19% of the time, Pallas kernels for 0%

profile of v2, /device:TPU:0, one launch (start us, length us, event | category | flops | bytes accessed | tf_op | source)
XLA Modules:
  0.0 94.0 jit_solution(5636244710363063099)
XLA Ops:
  1.6 1.8 %fusion.2 = f32[1024,256]{1,0:T(8,128)S(1)} fusion(bf16[1,1024,1024]{2,1,0:T(8,128)(2,1)S(1)} %copy-done, bf16[1,1024,256]{2,1,0:T(8,128)(2,1)} %param.7), kind=kOutput, calls=%fused_computation.6 | convolution fusion | flops 536870912 | bytes 3670016 | tf_op jit(solution)/shard_map/dot_general | solution.py:98
  5.4 2.9 %collective-permute-start.7 = (bf16[128,256]{1,0:T(8,128)(2,1)S(1)}, bf16[128,256]{1,0:T(8,128)(2,1)S(1)}, u32[]{:S(2)}, u32[]{:S(2)}) collective-permute-start(bf16[128,256]{1,0:T(8,128)(2,1)S(1)} %get-tuple-element.21), channel_id=1, source_target_pairs={{0,2},{2,4},{4,6},{6,8},{8,10},{10,12},{12,14},{14,0},{1,3},{3,5},... | collective-permute-start | bytes 196616 | tf_op jit(solution)/shard_map/ppermute | solution.py:22
  8.3 1.6 %collective-permute-start.8 = (bf16[128,256]{1,0:T(8,128)(2,1)S(1)}, bf16[128,256]{1,0:T(8,128)(2,1)S(1)}, u32[]{:S(2)}, u32[]{:S(2)}) collective-permute-start(bf16[128,256]{1,0:T(8,128)(2,1)S(1)} %get-tuple-element.21), channel_id=1, source_target_pairs={{0,4},{2,6},{4,8},{6,10},{8,12},{10,14},{12,0},{14,2},{1,5},{3,7},... | collective-permute-start | bytes 196616 | tf_op jit(solution)/shard_map/ppermute | solution.py:22
  9.9 2.6 %collective-permute-start.9 = (bf16[128,256]{1,0:T(8,128)(2,1)S(1)}, bf16[128,256]{1,0:T(8,128)(2,1)S(1)}, u32[]{:S(2)}, u32[]{:S(2)}) collective-permute-start(bf16[128,256]{1,0:T(8,128)(2,1)S(1)} %get-tuple-element.21), channel_id=1, source_target_pairs={{0,6},{2,8},{4,10},{6,12},{8,14},{10,0},{12,2},{14,4},{1,7},{3,9},... | collective-permute-start | bytes 196616 | tf_op jit(solution)/shard_map/ppermute | solution.py:22
  14.8 1.6 %sort.17 = (s32[8]{0:T(128)}, s32[8]{0:T(128)S(1)}) sort(s32[8]{0:T(128)S(1)} %and_select_fusion.1, s32[8]{0:T(128)} %iota.21), dimensions={0}, to_apply=%region_0.1 | sort | flops 24 | bytes 128 | tf_op jit(solution)/shard_map/jit(argsort)/sort | solution.py:45
  21.0 4.4 %collective-permute-done.1 = bf16[64,256]{1,0:T(8,128)(2,1)S(1)} collective-permute-done((bf16[64,256]{1,0:T(8,128)(2,1)S(1)}, bf16[64,256]{1,0:T(8,128)(2,1)S(1)}, u32[]{:S(2)}, u32[]{:S(2)}) %collective-permute-start.1) | collective-permute-done | bytes 32800 | tf_op jit(solution)/shard_map/ppermute | solution.py:22
  25.5 4.2 %collective-permute-done.2 = bf16[64,256]{1,0:T(8,128)(2,1)S(1)} collective-permute-done((bf16[64,256]{1,0:T(8,128)(2,1)S(1)}, bf16[64,256]{1,0:T(8,128)(2,1)S(1)}, u32[]{:S(2)}, u32[]{:S(2)}) %collective-permute-start.2) | collective-permute-done | bytes 32800 | tf_op jit(solution)/shard_map/ppermute | solution.py:22
  29.7 4.8 %collective-permute-done.3 = bf16[64,256]{1,0:T(8,128)(2,1)S(1)} collective-permute-done((bf16[64,256]{1,0:T(8,128)(2,1)S(1)}, bf16[64,256]{1,0:T(8,128)(2,1)S(1)}, u32[]{:S(2)}, u32[]{:S(2)}) %collective-permute-start.3) | collective-permute-done | bytes 32800 | tf_op jit(solution)/shard_map/ppermute | solution.py:22
  34.5 3.3 %collective-permute-done.4 = bf16[64,256]{1,0:T(8,128)(2,1)S(1)} collective-permute-done((bf16[64,256]{1,0:T(8,128)(2,1)S(1)}, bf16[64,256]{1,0:T(8,128)(2,1)S(1)}, u32[]{:S(2)}, u32[]{:S(2)}) %collective-permute-start.4) | collective-permute-done | bytes 32800 | tf_op jit(solution)/shard_map/ppermute | solution.py:22
  37.9 2.1 %collective-permute-start.5 = (bf16[64,256]{1,0:T(8,128)(2,1)S(1)}, bf16[64,256]{1,0:T(8,128)(2,1)S(1)}, u32[]{:S(2)}, u32[]{:S(2)}) collective-permute-start(bf16[64,256]{1,0:T(8,128)(2,1)S(1)} %get-tuple-element.15), channel_id=1, source_target_pairs={{0,12},{1,13},{4,0},{5,1},{8,4},{9,5},{12,8},{13,9},{2,14},{3,15},... | collective-permute-start | bytes 98312 | tf_op jit(solution)/shard_map/ppermute | solution.py:22
  39.9 1.9 %collective-permute-done.5 = bf16[64,256]{1,0:T(8,128)(2,1)S(1)} collective-permute-done((bf16[64,256]{1,0:T(8,128)(2,1)S(1)}, bf16[64,256]{1,0:T(8,128)(2,1)S(1)}, u32[]{:S(2)}, u32[]{:S(2)}) %collective-permute-start.5) | collective-permute-done | bytes 32800 | tf_op jit(solution)/shard_map/ppermute | solution.py:22
  42.5 1.6 %collective-permute-done.6 = bf16[64,256]{1,0:T(8,128)(2,1)S(1)} collective-permute-done((bf16[64,256]{1,0:T(8,128)(2,1)S(1)}, bf16[64,256]{1,0:T(8,128)(2,1)S(1)}, u32[]{:S(2)}, u32[]{:S(2)}) %collective-permute-start.6) | collective-permute-done | bytes 32800 | tf_op jit(solution)/shard_map/ppermute | solution.py:22
  46.5 3.1 %collective-permute-start.12 = (bf16[128,256]{1,0:T(8,128)(2,1)S(1)}, bf16[128,256]{1,0:T(8,128)(2,1)S(1)}, u32[]{:S(2)}, u32[]{:S(2)}) collective-permute-start(bf16[128,256]{1,0:T(8,128)(2,1)S(1)} %get-tuple-element.21), channel_id=1, source_target_pairs={{0,12},{2,14},{4,0},{6,2},{8,4},{10,6},{12,8},{14,10},{1,13},{3,15... | collective-permute-start | bytes 196616 | tf_op jit(solution)/shard_map/ppermute | solution.py:22
  55.5 2.1 %convolution_add_fusion.1 = f32[1024,256]{1,0:T(8,128)S(1)} fusion(f32[1024,256]{1,0:T(8,128)} %copy-done.2, bf16[8,128,256]{2,1,0:T(8,128)(2,1)} %bitcast_dynamic-update-slice_fusion.8, bf16[1,1024,128]{2,1,0:T(8,128)(2,1)S(1)} %copy-done.3, pred[128]{0:T(512)(128)(4,1)S(1)} %iota_compare_fusion, bf16[8,128,128]{2,1,0:T(8,128)(2,1)} %gather_fusion.1, ...), kind=kOutput, calls=%fused_computation.10 | convolution fusion | flops 134774784 | bytes 3145864 | tf_op jit(solution)/shard_map/dot_general | solution.py:96
  58.4 4.1 %collective-permute-start.14 = (bf16[128,256]{1,0:T(8,128)(2,1)S(1)}, bf16[128,256]{1,0:T(8,128)(2,1)S(1)}, u32[]{:S(2)}, u32[]{:S(2)}) collective-permute-start(bf16[128,256]{1,0:T(8,128)(2,1)S(1)} %gather_fusion.2), channel_id=1, source_target_pairs={{0,2},{2,4},{4,6},{6,8},{8,10},{10,12},{12,14},{1,3},{3,5},{5,7},{... | collective-permute-start | bytes 196616 | tf_op jit(solution)/shard_map/ppermute | solution.py:15
  62.5 1.4 %gather_fusion.3 = bf16[128,256]{1,0:T(8,128)(2,1)} fusion(f32[1024,256]{1,0:T(8,128)S(1)} %convolution_add_fusion.1, s32[1024]{0:T(1024)S(1)} %pad_clamp_fusion), kind=kCustom, calls=%fused_computation.3 | custom fusion | bytes 131584 | tf_op jit(solution)/shard_map/gather | solution.py:101
  65.9 4.3 %collective-permute-done.15 = bf16[128,256]{1,0:T(8,128)(2,1)S(1)} collective-permute-done((bf16[128,256]{1,0:T(8,128)(2,1)}, bf16[128,256]{1,0:T(8,128)(2,1)S(1)}, u32[]{:S(2)}, u32[]{:S(2)}) %collective-permute-start.15) | collective-permute-done | bytes 65568 | tf_op jit(solution)/shard_map/ppermute | solution.py:15
  71.2 1.7 %fusion.4 = f32[1024,256]{1,0:T(8,128)S(1)} fusion(bf16[1,1024,1024]{2,1,0:T(8,128)(2,1)S(1)} %copy-done, bf16[128,256]{1,0:T(8,128)(2,1)S(1)} %get-tuple-element.8, bf16[768,256]{1,0:T(8,128)(2,1)} %slice_bitcast_fusion, bf16[128,256]{1,0:T(8,128)(2,1)S(1)} %get-tuple-element.7), kind=kOutput, calls=%fused_computation.8 | convolution fusion | flops 538443776 | bytes 3670016 | tf_op jit(solution)/shard_map/dot_general | solution.py:115
  73.9 2.4 %collective-permute-start.16 = (bf16[128,256]{1,0:T(8,128)(2,1)S(1)}, bf16[128,256]{1,0:T(8,128)(2,1)S(1)}, u32[]{:S(2)}, u32[]{:S(2)}) collective-permute-start(bf16[128,256]{1,0:T(8,128)(2,1)S(1)} %get-tuple-element.23), channel_id=1, source_target_pairs={{0,2},{2,4},{4,6},{6,8},{8,10},{10,12},{12,14},{14,0},{1,3},{3,5},... | collective-permute-start | bytes 196616 | tf_op jit(solution)/shard_map/ppermute | solution.py:22
  76.3 1.3 %collective-permute-start.17 = (bf16[128,256]{1,0:T(8,128)(2,1)S(1)}, bf16[128,256]{1,0:T(8,128)(2,1)S(1)}, u32[]{:S(2)}, u32[]{:S(2)}) collective-permute-start(bf16[128,256]{1,0:T(8,128)(2,1)S(1)} %get-tuple-element.23), channel_id=1, source_target_pairs={{0,4},{2,6},{4,8},{6,10},{8,12},{10,14},{12,0},{14,2},{1,5},{3,7},... | collective-permute-start | bytes 196616 | tf_op jit(solution)/shard_map/ppermute | solution.py:22
  77.8 3.3 %collective-permute-start.19 = (bf16[128,256]{1,0:T(8,128)(2,1)S(1)}, bf16[128,256]{1,0:T(8,128)(2,1)S(1)}, u32[]{:S(2)}, u32[]{:S(2)}) collective-permute-start(bf16[128,256]{1,0:T(8,128)(2,1)S(1)} %get-tuple-element.23), channel_id=1, source_target_pairs={{0,8},{2,10},{4,12},{6,14},{8,0},{10,2},{12,4},{14,6},{1,9},{3,11}... | collective-permute-start | bytes 196616 | tf_op jit(solution)/shard_map/ppermute | solution.py:22
  81.6 2.3 %collective-permute-start.21 = (bf16[128,256]{1,0:T(8,128)(2,1)S(1)}, bf16[128,256]{1,0:T(8,128)(2,1)S(1)}, u32[]{:S(2)}, u32[]{:S(2)}) collective-permute-start(bf16[128,256]{1,0:T(8,128)(2,1)S(1)} %get-tuple-element.23), channel_id=1, source_target_pairs={{0,12},{2,14},{4,0},{6,2},{8,4},{10,6},{12,8},{14,10},{1,13},{3,15... | collective-permute-start | bytes 196616 | tf_op jit(solution)/shard_map/ppermute | solution.py:22
  84.6 1.3 %collective-permute-start.22 = (bf16[128,256]{1,0:T(8,128)(2,1)S(1)}, bf16[128,256]{1,0:T(8,128)(2,1)S(1)}, u32[]{:S(2)}, u32[]{:S(2)}) collective-permute-start(bf16[128,256]{1,0:T(8,128)(2,1)S(1)} %get-tuple-element.23), channel_id=1, source_target_pairs={{0,14},{2,0},{4,2},{6,4},{8,6},{10,8},{12,10},{14,12},{1,15},{3,1}... | collective-permute-start | bytes 196616 | tf_op jit(solution)/shard_map/ppermute | solution.py:22
  91.0 2.9 %fusion.8 = bf16[1,1024,256]{2,1,0:T(8,128)(2,1)} fusion(f32[1024,256]{1,0:T(8,128)} %copy-done.1, bf16[8,128,256]{2,1,0:T(8,128)(2,1)} %bitcast_dynamic-update-slice_fusion, bf16[1,1024,128]{2,1,0:T(8,128)(2,1)S(1)} %copy-done.3, pred[128]{0:T(512)(128)(4,1)S(1)} %iota_compare_fusion, bf16[8,128,128]{2,1,0:T(8,128)(2,1)} %gather_fusion.1, ...), kind=kOutput, calls=%fused_computation.12 | convolution fusion | flops 135036928 | bytes 2621576 | tf_op jit(solution)/shard_map/dot_general | solution.py:96
  (90 shorter events, 29.9 us)
Async XLA Ops:
  4.4 13.4 %copy-start.6 = (s32[1,2,128]{2,1,0:T(2,128)S(1)}, s32[1,2,128]{2,1,0:T(2,128)}, u32[]{:S(2)}) copy-start(s32[1,2,128]{2,1,0:T(2,128)} %param.10) | copy-start | bytes 3076
  5.4 41.2 %collective-permute-start.7 = (bf16[128,256]{1,0:T(8,128)(2,1)S(1)}, bf16[128,256]{1,0:T(8,128)(2,1)S(1)}, u32[]{:S(2)}, u32[]{:S(2)}) collective-permute-start(bf16[128,256]{1,0:T(8,128)(2,1)S(1)} %get-tuple-element.21), channel_id=1, source_target_pairs={{0,2},{2,4},{4,6},{6,8},{8,10},{10,12},{12,14},{14,0},{1,3},{3,5},... | collective-permute-start | bytes 196616 | tf_op jit(solution)/shard_map/ppermute | solution.py:22
  8.3 42.0 %collective-permute-start.8 = (bf16[128,256]{1,0:T(8,128)(2,1)S(1)}, bf16[128,256]{1,0:T(8,128)(2,1)S(1)}, u32[]{:S(2)}, u32[]{:S(2)}) collective-permute-start(bf16[128,256]{1,0:T(8,128)(2,1)S(1)} %get-tuple-element.21), channel_id=1, source_target_pairs={{0,4},{2,6},{4,8},{6,10},{8,12},{10,14},{12,0},{14,2},{1,5},{3,7},... | collective-permute-start | bytes 196616 | tf_op jit(solution)/shard_map/ppermute | solution.py:22
  9.9 41.6 %collective-permute-start.9 = (bf16[128,256]{1,0:T(8,128)(2,1)S(1)}, bf16[128,256]{1,0:T(8,128)(2,1)S(1)}, u32[]{:S(2)}, u32[]{:S(2)}) collective-permute-start(bf16[128,256]{1,0:T(8,128)(2,1)S(1)} %get-tuple-element.21), channel_id=1, source_target_pairs={{0,6},{2,8},{4,10},{6,12},{8,14},{10,0},{12,2},{14,4},{1,7},{3,9},... | collective-permute-start | bytes 196616 | tf_op jit(solution)/shard_map/ppermute | solution.py:22
  12.4 39.7 %collective-permute-start.10 = (bf16[128,256]{1,0:T(8,128)(2,1)S(1)}, bf16[128,256]{1,0:T(8,128)(2,1)S(1)}, u32[]{:S(2)}, u32[]{:S(2)}) collective-permute-start(bf16[128,256]{1,0:T(8,128)(2,1)S(1)} %get-tuple-element.21), channel_id=1, source_target_pairs={{0,8},{2,10},{4,12},{6,14},{8,0},{10,2},{12,4},{14,6},{1,9},{3,11}... | collective-permute-start | bytes 196616 | tf_op jit(solution)/shard_map/ppermute | solution.py:22
  14.3 5.5 %collective-permute-start = (bf16[64,256]{1,0:T(8,128)(2,1)}, bf16[64,256]{1,0:T(8,128)(2,1)}, u32[]{:S(2)}, u32[]{:S(2)}) collective-permute-start(bf16[64,256]{1,0:T(8,128)(2,1)} %get-tuple-element.14), channel_id=1, source_target_pairs={{0,1},{1,4},{4,5},{5,8},{8,9},{9,12},{12,13},{13,0},{2,3},{3,6},{6... | collective-permute-start | bytes 98312 | tf_op jit(solution)/shard_map/ppermute | solution.py:22
  19.7 5.7 %collective-permute-start.1 = (bf16[64,256]{1,0:T(8,128)(2,1)S(1)}, bf16[64,256]{1,0:T(8,128)(2,1)S(1)}, u32[]{:S(2)}, u32[]{:S(2)}) collective-permute-start(bf16[64,256]{1,0:T(8,128)(2,1)S(1)} %get-tuple-element.13), channel_id=1, source_target_pairs={{0,4},{1,5},{4,8},{5,9},{8,12},{9,13},{12,0},{13,1},{2,6},{3,7},{6... | collective-permute-start | bytes 98312 | tf_op jit(solution)/shard_map/ppermute | solution.py:22
  25.5 4.2 %collective-permute-start.2 = (bf16[64,256]{1,0:T(8,128)(2,1)S(1)}, bf16[64,256]{1,0:T(8,128)(2,1)S(1)}, u32[]{:S(2)}, u32[]{:S(2)}) collective-permute-start(bf16[64,256]{1,0:T(8,128)(2,1)S(1)} %get-tuple-element.12), channel_id=1, source_target_pairs={{0,5},{1,8},{4,9},{5,12},{8,13},{9,0},{12,1},{13,4},{2,7},{3,10},{... | collective-permute-start | bytes 98312 | tf_op jit(solution)/shard_map/ppermute | solution.py:22
  29.7 4.8 %collective-permute-start.3 = (bf16[64,256]{1,0:T(8,128)(2,1)S(1)}, bf16[64,256]{1,0:T(8,128)(2,1)S(1)}, u32[]{:S(2)}, u32[]{:S(2)}) collective-permute-start(bf16[64,256]{1,0:T(8,128)(2,1)S(1)} %get-tuple-element.11), channel_id=1, source_target_pairs={{0,8},{1,9},{4,12},{5,13},{8,0},{9,1},{12,4},{13,5},{2,10},{3,11},... | collective-permute-start | bytes 98312 | tf_op jit(solution)/shard_map/ppermute | solution.py:22
  34.5 3.4 %collective-permute-start.4 = (bf16[64,256]{1,0:T(8,128)(2,1)S(1)}, bf16[64,256]{1,0:T(8,128)(2,1)S(1)}, u32[]{:S(2)}, u32[]{:S(2)}) collective-permute-start(bf16[64,256]{1,0:T(8,128)(2,1)S(1)} %get-tuple-element.10), channel_id=1, source_target_pairs={{0,9},{1,12},{4,13},{5,0},{8,1},{9,4},{12,5},{13,8},{2,11},{3,14},... | collective-permute-start | bytes 98312 | tf_op jit(solution)/shard_map/ppermute | solution.py:22
  37.9 3.9 %collective-permute-start.5 = (bf16[64,256]{1,0:T(8,128)(2,1)S(1)}, bf16[64,256]{1,0:T(8,128)(2,1)S(1)}, u32[]{:S(2)}, u32[]{:S(2)}) collective-permute-start(bf16[64,256]{1,0:T(8,128)(2,1)S(1)} %get-tuple-element.15), channel_id=1, source_target_pairs={{0,12},{1,13},{4,0},{5,1},{8,4},{9,5},{12,8},{13,9},{2,14},{3,15},... | collective-permute-start | bytes 98312 | tf_op jit(solution)/shard_map/ppermute | solution.py:22
  41.8 2.3 %collective-permute-start.6 = (bf16[64,256]{1,0:T(8,128)(2,1)S(1)}, bf16[64,256]{1,0:T(8,128)(2,1)S(1)}, u32[]{:S(2)}, u32[]{:S(2)}) collective-permute-start(bf16[64,256]{1,0:T(8,128)(2,1)S(1)} %get-tuple-element.9), channel_id=1, source_target_pairs={{0,13},{1,0},{4,1},{5,4},{8,5},{9,8},{12,9},{13,12},{2,15},{3,2},{... | collective-permute-start | bytes 98312 | tf_op jit(solution)/shard_map/ppermute | solution.py:22
  44.1 8.7 %collective-permute-start.11 = (bf16[128,256]{1,0:T(8,128)(2,1)S(1)}, bf16[128,256]{1,0:T(8,128)(2,1)S(1)}, u32[]{:S(2)}, u32[]{:S(2)}) collective-permute-start(bf16[128,256]{1,0:T(8,128)(2,1)S(1)} %get-tuple-element.21), channel_id=1, source_target_pairs={{0,10},{2,12},{4,14},{6,0},{8,2},{10,4},{12,6},{14,8},{1,11},{3,13... | collective-permute-start | bytes 196616 | tf_op jit(solution)/shard_map/ppermute | solution.py:22
  46.5 6.9 %collective-permute-start.12 = (bf16[128,256]{1,0:T(8,128)(2,1)S(1)}, bf16[128,256]{1,0:T(8,128)(2,1)S(1)}, u32[]{:S(2)}, u32[]{:S(2)}) collective-permute-start(bf16[128,256]{1,0:T(8,128)(2,1)S(1)} %get-tuple-element.21), channel_id=1, source_target_pairs={{0,12},{2,14},{4,0},{6,2},{8,4},{10,6},{12,8},{14,10},{1,13},{3,15... | collective-permute-start | bytes 196616 | tf_op jit(solution)/shard_map/ppermute | solution.py:22
  50.2 4.6 %collective-permute-start.13 = (bf16[128,256]{1,0:T(8,128)(2,1)S(1)}, bf16[128,256]{1,0:T(8,128)(2,1)S(1)}, u32[]{:S(2)}, u32[]{:S(2)}) collective-permute-start(bf16[128,256]{1,0:T(8,128)(2,1)S(1)} %get-tuple-element.21), channel_id=1, source_target_pairs={{0,14},{2,0},{4,2},{6,4},{8,6},{10,8},{12,10},{14,12},{1,15},{3,1}... | collective-permute-start | bytes 196616 | tf_op jit(solution)/shard_map/ppermute | solution.py:22
  58.4 7.5 %collective-permute-start.14 = (bf16[128,256]{1,0:T(8,128)(2,1)S(1)}, bf16[128,256]{1,0:T(8,128)(2,1)S(1)}, u32[]{:S(2)}, u32[]{:S(2)}) collective-permute-start(bf16[128,256]{1,0:T(8,128)(2,1)S(1)} %gather_fusion.2), channel_id=1, source_target_pairs={{0,2},{2,4},{4,6},{6,8},{8,10},{10,12},{12,14},{1,3},{3,5},{5,7},{... | collective-permute-start | bytes 196616 | tf_op jit(solution)/shard_map/ppermute | solution.py:15
  63.9 6.4 %collective-permute-start.15 = (bf16[128,256]{1,0:T(8,128)(2,1)}, bf16[128,256]{1,0:T(8,128)(2,1)S(1)}, u32[]{:S(2)}, u32[]{:S(2)}) collective-permute-start(bf16[128,256]{1,0:T(8,128)(2,1)} %gather_fusion.3), channel_id=1, source_target_pairs={{2,0},{4,2},{6,4},{8,6},{10,8},{12,10},{14,12},{3,1},{5,3},{7,5},{... | collective-permute-start | bytes 196616 | tf_op jit(solution)/shard_map/ppermute | solution.py:15
  73.9 7.7 %collective-permute-start.16 = (bf16[128,256]{1,0:T(8,128)(2,1)S(1)}, bf16[128,256]{1,0:T(8,128)(2,1)S(1)}, u32[]{:S(2)}, u32[]{:S(2)}) collective-permute-start(bf16[128,256]{1,0:T(8,128)(2,1)S(1)} %get-tuple-element.23), channel_id=1, source_target_pairs={{0,2},{2,4},{4,6},{6,8},{8,10},{10,12},{12,14},{14,0},{1,3},{3,5},... | collective-permute-start | bytes 196616 | tf_op jit(solution)/shard_map/ppermute | solution.py:22
  76.3 8.3 %collective-permute-start.17 = (bf16[128,256]{1,0:T(8,128)(2,1)S(1)}, bf16[128,256]{1,0:T(8,128)(2,1)S(1)}, u32[]{:S(2)}, u32[]{:S(2)}) collective-permute-start(bf16[128,256]{1,0:T(8,128)(2,1)S(1)} %get-tuple-element.23), channel_id=1, source_target_pairs={{0,4},{2,6},{4,8},{6,10},{8,12},{10,14},{12,0},{14,2},{1,5},{3,7},... | collective-permute-start | bytes 196616 | tf_op jit(solution)/shard_map/ppermute | solution.py:22
  77.7 8.9 %collective-permute-start.18 = (bf16[128,256]{1,0:T(8,128)(2,1)S(1)}, bf16[128,256]{1,0:T(8,128)(2,1)S(1)}, u32[]{:S(2)}, u32[]{:S(2)}) collective-permute-start(bf16[128,256]{1,0:T(8,128)(2,1)S(1)} %get-tuple-element.23), channel_id=1, source_target_pairs={{0,6},{2,8},{4,10},{6,12},{8,14},{10,0},{12,2},{14,4},{1,7},{3,9},... | collective-permute-start | bytes 196616 | tf_op jit(solution)/shard_map/ppermute | solution.py:22
  77.8 10.0 %collective-permute-start.19 = (bf16[128,256]{1,0:T(8,128)(2,1)S(1)}, bf16[128,256]{1,0:T(8,128)(2,1)S(1)}, u32[]{:S(2)}, u32[]{:S(2)}) collective-permute-start(bf16[128,256]{1,0:T(8,128)(2,1)S(1)} %get-tuple-element.23), channel_id=1, source_target_pairs={{0,8},{2,10},{4,12},{6,14},{8,0},{10,2},{12,4},{14,6},{1,9},{3,11}... | collective-permute-start | bytes 196616 | tf_op jit(solution)/shard_map/ppermute | solution.py:22
  81.1 7.3 %collective-permute-start.20 = (bf16[128,256]{1,0:T(8,128)(2,1)S(1)}, bf16[128,256]{1,0:T(8,128)(2,1)S(1)}, u32[]{:S(2)}, u32[]{:S(2)}) collective-permute-start(bf16[128,256]{1,0:T(8,128)(2,1)S(1)} %get-tuple-element.23), channel_id=1, source_target_pairs={{0,10},{2,12},{4,14},{6,0},{8,2},{10,4},{12,6},{14,8},{1,11},{3,13... | collective-permute-start | bytes 196616 | tf_op jit(solution)/shard_map/ppermute | solution.py:22
  81.6 8.1 %collective-permute-start.21 = (bf16[128,256]{1,0:T(8,128)(2,1)S(1)}, bf16[128,256]{1,0:T(8,128)(2,1)S(1)}, u32[]{:S(2)}, u32[]{:S(2)}) collective-permute-start(bf16[128,256]{1,0:T(8,128)(2,1)S(1)} %get-tuple-element.23), channel_id=1, source_target_pairs={{0,12},{2,14},{4,0},{6,2},{8,4},{10,6},{12,8},{14,10},{1,13},{3,15... | collective-permute-start | bytes 196616 | tf_op jit(solution)/shard_map/ppermute | solution.py:22
  84.6 5.8 %collective-permute-start.22 = (bf16[128,256]{1,0:T(8,128)(2,1)S(1)}, bf16[128,256]{1,0:T(8,128)(2,1)S(1)}, u32[]{:S(2)}, u32[]{:S(2)}) collective-permute-start(bf16[128,256]{1,0:T(8,128)(2,1)S(1)} %get-tuple-element.23), channel_id=1, source_target_pairs={{0,14},{2,0},{4,2},{6,4},{8,6},{10,8},{12,10},{14,12},{1,15},{3,1}... | collective-permute-start | bytes 196616 | tf_op jit(solution)/shard_map/ppermute | solution.py:22
  (6 other events, 31.1 us)

commit v3 on v1

--- a/solution.py
+++ b/solution.py
@@ -5,6 +5,7 @@
 
 ROUNDS = 2
 DUCT = ("sub", "tile")
+MAX_RING = 8
 
 
 def passed_along(shard, by):
@@ -17,6 +18,42 @@
     rows = lax.all_to_all(coarse_inverse, "sub", split_axis=0, concat_axis=3, tiled=True)
     rows = lax.all_gather(rows, "rep", axis=2, tiled=True)
     return rows.reshape(rows.shape[2], rows.shape[3] * rows.shape[4])
+
+
+def gathered(projected, up_trace, low_trace):
+    peers = lax.axis_size(DUCT)
+    rows = projected.shape[0]
+    if peers > MAX_RING:
+        vector = lax.all_gather(projected, DUCT, axis=0, tiled=True)
+        if up_trace is None:
+            return vector, None, None
+        return vector, passed_along(up_trace, 1), passed_along(low_trace, -1)
+    parts = [projected]
+    extras = {}
+    if up_trace is not None:
+        extras.setdefault(1, []).append(up_trace)
+        extras.setdefault(peers - 1, []).append(low_trace)
+    came = {}
+    for k in range(1, peers):
+        piece = jnp.concatenate([projected] + extras.get(k, []), axis=0)
+        got = lax.ppermute(piece, DUCT, [(i, (i + k) % peers) for i in range(peers)])
+        parts.append(got[:rows])
+        came[k] = got[rows:]
+    vector = jnp.concatenate(parts, axis=0)
+    if up_trace is None:
+        return vector, None, None
+    from_lower = came[1][: up_trace.shape[0]]
+    from_upper = came[peers - 1][came[peers - 1].shape[0] - low_trace.shape[0] :]
+    return vector, from_lower, from_upper
+
+
+def block_order(matrix):
+    peers = lax.axis_size(DUCT)
+    if peers > MAX_RING:
+        return matrix
+    came_from = (lax.axis_index(DUCT) - jnp.arange(peers)) % peers
+    blocks = matrix.reshape(matrix.shape[0], peers, -1)
+    return jnp.take(blocks, came_from, axis=1).reshape(matrix.shape)
 
 
 def local(
@@ -33,33 +70,68 @@
     iface_rows = inverse.shape[0]
     face_rows = coupling.shape[2]
     slot_count = deflation_basis.shape[2]
+    peers = lax.axis_size(DUCT)
+    position = lax.axis_index(DUCT)
     slot_ids = jnp.arange(slot_count, dtype=jnp.int32)
     masked_basis = jnp.where(
         slot_ids[None, :] < deflation_counts[0],
         deflation_basis[0],
         jnp.zeros((), deflation_basis.dtype),
     )
+    lower_rows_at = trace_rows[0, 0]
+    upper_rows_at = trace_rows[0, 1]
     coarse_rows = own_coarse_rows(coarse_inverse)
+    width = coarse_rows.shape[1]
+    below = passed_along(jnp.concatenate([coarse_rows, masked_basis[upper_rows_at]], axis=1), 1)
+    above = passed_along(jnp.concatenate([coarse_rows, masked_basis[lower_rows_at]], axis=1), -1)
+    coarse_all = block_order(
+        jnp.concatenate([coarse_rows, below[:, :width], above[:, :width]], axis=0)
+    )
+    below_basis = below[:, width:]
+    above_basis = above[:, width:]
+    has_lower = position > 0
+    has_upper = position < peers - 1
     lower_gain = coupling[0, 0][:, None]
     upper_gain = coupling[0, 1][:, None]
+    block = coarse_rows.shape[0]
 
-    def coarse_step(local_solve, defect):
+    iterate = None
+    boundary = source
+    for cycle_index in range(ROUNDS):
+        local_solve = jnp.dot(inverse, boundary, preferred_element_type=jnp.float32)
+        if iterate is None:
+            defect = local_solve.astype(jnp.bfloat16)
+        else:
+            defect = (local_solve - iterate).astype(jnp.bfloat16)
         projected = lax.dot_general(
             masked_basis, defect, (((0,), (0,)), ((), ())), preferred_element_type=jnp.float32
         ).astype(jnp.bfloat16)
-        vector = lax.all_gather(projected, DUCT, axis=0, tiled=True)
-        coarse = jnp.dot(coarse_rows, vector, preferred_element_type=jnp.float32).astype(
+        last = cycle_index == ROUNDS - 1
+        if last:
+            vector = gathered(projected, None, None)[0]
+            coarse = jnp.dot(coarse_all[:block], vector, preferred_element_type=jnp.float32)
+            coarse = coarse.astype(jnp.bfloat16)
+            iterate = local_solve + jnp.dot(masked_basis, coarse, preferred_element_type=jnp.float32)
+            break
+        vector, solve_lower, solve_upper = gathered(
+            projected,
+            local_solve[upper_rows_at].astype(jnp.bfloat16),
+            local_solve[lower_rows_at].astype(jnp.bfloat16),
+        )
+        coarse = jnp.dot(coarse_all, vector, preferred_element_type=jnp.float32).astype(
             jnp.bfloat16
         )
-        return local_solve + jnp.dot(masked_basis, coarse, preferred_element_type=jnp.float32)
-
-    local_solve = jnp.dot(inverse, source, preferred_element_type=jnp.float32)
-    iterate = coarse_step(local_solve, local_solve.astype(jnp.bfloat16))
-    for cycle_index in range(1, ROUNDS):
-        lower_trace = iterate[trace_rows[0, 0]]
-        upper_trace = iterate[trace_rows[0, 1]]
-        from_lower = passed_along(upper_trace.astype(jnp.bfloat16), 1).astype(jnp.float32)
-        from_upper = passed_along(lower_trace.astype(jnp.bfloat16), -1).astype(jnp.float32)
+        iterate = local_solve + jnp.dot(
+            masked_basis, coarse[:block], preferred_element_type=jnp.float32
+        )
+        from_lower = solve_lower.astype(jnp.float32) + jnp.dot(
+            below_basis, coarse[block : 2 * block], preferred_element_type=jnp.float32
+        )
+        from_upper = solve_upper.astype(jnp.float32) + jnp.dot(
+            above_basis, coarse[2 * block :], preferred_element_type=jnp.float32
+        )
+        from_lower = jnp.where(has_lower, from_lower, 0.0)
+        from_upper = jnp.where(has_upper, from_upper, 0.0)
         lower_rows = source[:face_rows].astype(jnp.float32) + lower_gain * from_lower
         upper_rows = source[iface_rows - face_rows :].astype(jnp.float32) + upper_gain * from_upper
         boundary = jnp.concatenate(
@@ -70,8 +142,6 @@
             ],
             axis=0,
         )
-        local_solve = jnp.dot(inverse, boundary, preferred_element_type=jnp.float32)
-        iterate = coarse_step(local_solve, (local_solve - iterate).astype(jnp.bfloat16))
     return iterate.astype(jnp.bfloat16)[None]
 
 

time: 101 us -> 116 us (1.15); the launches traced: 101 us -> 114 us
  blocking collectives: 67.3 us -> 2.13 us
  local copies, waits for them, and re-layouts: 5.93 us -> 46.3 us
  starting transfers between devices: 11.3 us -> 39.9 us
  other arithmetic: 1.75 us -> 9.73 us
  matrix products: 8.85 us -> 13.1 us
  waiting for transfers between devices: 4.84 us -> 1.85 us
    all_gather x2 -> x0, blocking collectives: 65.3 us -> none  [coarse_step(): vector = lax.all_gather(projected, DUCT, axis=0, tiled=True)]
    ppermute x0 -> x14, starting transfers between devices: none -> 30 us  [gathered(): lax.ppermute(piece, DUCT, [(i, (i + k) % peers) for i in range(peers)])]
    unnamed x10 -> x32, local copies, waits for them, and re-layouts: 1.64 us -> 16 us
    gather x2 -> x8, local copies, waits for them, and re-layouts: 1.51 us -> 13.3 us  [the longest x2 4.98 us: block_order(): return jnp.take(blocks, came_from, axis=1).reshape(matrix.shape)]
    concatenate x0 -> x5, local copies, waits for them, and re-layouts: none -> 7.46 us  [the longest x3 5.36 us: local(): jnp.concatenate([coarse_rows, below[:, :width], above[:, :width]], axis=0)]
    concatenate x0 -> x3, other arithmetic: none -> 5.56 us  [the longest x1 2.07 us: local(): jnp.concatenate([coarse_rows, below[:, :width], above[:, :width]], axis=0)]
    slice x0 -> x3, local copies, waits for them, and re-layouts: none -> 5.12 us  [the longest x1 1.79 us: local(): coarse_all[:block]]
    select_n x1 -> x5, other arithmetic: 0.76 us -> 4.13 us  [the longest x3 3.15 us: block_order(): return jnp.take(blocks, came_from, axis=1).reshape(matrix.shape)]
  transfers between devices with their start and end apart: 3 -> 17, of which waited for: 2 -> 1; matrix products, arithmetic and copies ran while one was open for 5% -> 37% of each run, Pallas kernels for 0% -> 0%
where the time goes in v3:
time: 116 us; the launch traced here: 114 us
  local copies, waits for them, and re-layouts  46.3 us (40%)
  starting transfers between devices  39.9 us (34%)
  matrix products  13.1 us (11%)
  other arithmetic  9.73 us (8%)
  blocking collectives  2.13 us (2%)
  waiting for transfers between devices  1.85 us (2%)
    ppermute x14, starting transfers between devices, gathered(): lax.ppermute(piece, DUCT, [(i, (i + k) % peers) for i in range(peers)])  30 us
    unnamed x32, local copies, waits for them, and re-layouts  16 us
    ppermute x2, starting transfers between devices, passed_along(): return lax.ppermute(shard, DUCT, pairs)  6.56 us
    concatenate x3, local copies, waits for them, and re-layouts, local(): jnp.concatenate([coarse_rows, below[:, :width], above[:, :width]], axis=0)  5.36 us
    gather x2, local copies, waits for them, and re-layouts, block_order(): return jnp.take(blocks, came_from, axis=1).reshape(matrix.shape)  4.98 us
    dot_general x2, matrix products, local(): local_solve = jnp.dot(inverse, boundary, preferred_element_type=jnp.float32)  3.46 us
    dot_general x2, matrix products, local(): lax.dot_general(masked_basis, defect, (((0,), (0,)), ((), ())), preferred...  3.35 us
    all_to_all x1, starting transfers between devices, own_coarse_rows(): lax.all_to_all(coarse_inverse, 'sub', split_axis=0, concat_axis=3, tiled=...  3.33 us
  transfers between devices with their start and end apart: 17, of which 1 were waited for; matrix products, arithmetic and copies ran while one was open for 37% of the time, Pallas kernels for 0%

profile of v3, /device:TPU:0, one launch (start us, length us, event | category | flops | bytes accessed | tf_op | source)
XLA Modules:
  0.0 113.9 jit_solution(484941452803717135)
XLA Ops:
  4.5 3.0 %collective-permute-start.3 = (bf16[128,256]{1,0:T(8,128)(2,1)}, bf16[128,256]{1,0:T(8,128)(2,1)}, u32[]{:S(2)}, u32[]{:S(2)}) collective-permute-start(bf16[128,256]{1,0:T(8,128)(2,1)} %get-tuple-element.14), channel_id=1, source_target_pairs={{0,4},{2,6},{4,8},{6,10},{8,12},{10,14},{12,0},{14,2},{1,5},{3,7},... | collective-permute-start | bytes 196616 | tf_op jit(solution)/shard_map/ppermute | solution.py:39
  7.5 2.5 %collective-permute-start.4 = (bf16[128,256]{1,0:T(8,128)(2,1)}, bf16[128,256]{1,0:T(8,128)(2,1)}, u32[]{:S(2)}, u32[]{:S(2)}) collective-permute-start(bf16[128,256]{1,0:T(8,128)(2,1)} %get-tuple-element.14), channel_id=1, source_target_pairs={{0,6},{2,8},{4,10},{6,12},{8,14},{10,0},{12,2},{14,4},{1,7},{3,9},... | collective-permute-start | bytes 196616 | tf_op jit(solution)/shard_map/ppermute | solution.py:39
  11.3 2.7 %collective-permute-start.6 = (bf16[128,256]{1,0:T(8,128)(2,1)}, bf16[128,256]{1,0:T(8,128)(2,1)}, u32[]{:S(2)}, u32[]{:S(2)}) collective-permute-start(bf16[128,256]{1,0:T(8,128)(2,1)} %get-tuple-element.14), channel_id=1, source_target_pairs={{0,10},{2,12},{4,14},{6,0},{8,2},{10,4},{12,6},{14,8},{1,11},{3,13... | collective-permute-start | bytes 196616 | tf_op jit(solution)/shard_map/ppermute | solution.py:39
  14.0 3.3 %all-to-all-start = ((bf16[4,1,64,1,256]{4,2,3,1,0:T(8,128)(2,1)}), bf16[4,1,64,1,256]{4,2,3,1,0:T(8,128)(2,1)S(1)}, u32[]{:S(2)}, u32[]{:S(2)}) async-start(bf16[4,1,64,1,256]{4,2,3,1,0:T(8,128)(2,1)} %param.13), calls=%async_computation | async-start | bytes 262144 | tf_op jit(solution)/shard_map/all_to_all | solution.py:18
  31.3 3.8 %collective-permute-start.7 = (bf16[128,256]{1,0:T(8,128)(2,1)}, bf16[128,256]{1,0:T(8,128)(2,1)}, u32[]{:S(2)}, u32[]{:S(2)}) collective-permute-start(bf16[128,256]{1,0:T(8,128)(2,1)} %get-tuple-element.14), channel_id=1, source_target_pairs={{0,12},{2,14},{4,0},{6,2},{8,4},{10,6},{12,8},{14,10},{1,13},{3,15... | collective-permute-start | bytes 196616 | tf_op jit(solution)/shard_map/ppermute | solution.py:39
  44.0 2.1 %all-gather = bf16[1,1,128,4,1,256]{5,3,4,1,0,2:T(4,128)(2,1)} all-gather(bf16[1,1,64,4,1,256]{5,3,4,1,0,2:T(4,128)(2,1)S(1)} %copy.23), channel_id=2, replica_groups=mesh['group'=2,'sub'=4,'tile'=2,'rep'=2] {'rep'}, dimensions={2}, use_global_device_ids=true | all-gather | bytes 393216 | tf_op jit(solution)/shard_map/all_gather | solution.py:19
  46.2 1.8 %copy.24 = bf16[1,1,128,4,1,256]{2,5,3,4,1,0:T(8,128)(2,1)} copy(bf16[1,1,128,4,1,256]{5,3,4,1,0,2:T(4,128)(2,1)} %all-gather) | data formatting | bytes 524288 | tf_op jit(solution)/shard_map/all_gather | solution.py:19
  48.0 1.9 %pad_maximum_fusion.1 = (bf16[128,1152]{0,1:T(8,128)(2,1)}, bf16[128,1152]{0,1:T(8,128)(2,1)}) fusion(bf16[128,128]{0,1:T(8,128)(2,1)} %copy.25, bf16[128,1024]{0,1:T(8,128)(2,1)} %bitcast.63, bf16[128,128]{0,1:T(8,128)(2,1)} %copy.27), kind=kLoop, calls=%fused_computation.31 | loop fusion | flops 1032192 | bytes 917504 | tf_op jit(solution)/shard_map/concatenate | solution.py:85
  51.1 5.3 %collective-permute-start.1 = (bf16[128,1152]{0,1:T(8,128)(2,1)}, bf16[128,1152]{0,1:T(8,128)(2,1)}, u32[]{:S(2)}, u32[]{:S(2)}) collective-permute-start(bf16[128,1152]{0,1:T(8,128)(2,1)} %get-tuple-element.5), channel_id=1, source_target_pairs={{0,2},{2,4},{4,6},{6,8},{8,10},{10,12},{12,14},{1,3},{3,5},{5,7},{... | collective-permute-start | bytes 884744 | tf_op jit(solution)/shard_map/ppermute | solution.py:14
  59.4 1.8 %copy.28 = bf16[128,8,128]{2,0,1:T(8,128)(2,1)} copy(bf16[128,8,128]{0,2,1:T(8,128)(2,1)} %bitcast.64) | data formatting | bytes 524288 | tf_op jit(solution)/shard_map/concatenate | solution.py:88
  62.8 1.8 %copy.30 = bf16[128,8,128]{2,0,1:T(8,128)(2,1)} copy(bf16[128,8,128]{0,2,1:T(8,128)(2,1)} %bitcast.66) | data formatting | bytes 524288 | tf_op jit(solution)/shard_map/concatenate | solution.py:88
  64.6 1.8 %collective-permute-done.1 = bf16[128,1152]{0,1:T(8,128)(2,1)} collective-permute-done((bf16[128,1152]{0,1:T(8,128)(2,1)}, bf16[128,1152]{0,1:T(8,128)(2,1)}, u32[]{:S(2)}, u32[]{:S(2)}) %collective-permute-start.1) | collective-permute-done | bytes 294944 | tf_op jit(solution)/shard_map/ppermute | solution.py:14
  68.1 1.8 %copy.29 = bf16[128,8,128]{2,0,1:T(8,128)(2,1)} copy(bf16[128,8,128]{0,2,1:T(8,128)(2,1)} %bitcast.67) | data formatting | bytes 524288 | tf_op jit(solution)/shard_map/concatenate | solution.py:88
  69.9 2.1 %pad_maximum_fusion = bf16[384,8,128]{2,0,1:T(8,128)(2,1)} fusion(bf16[128,8,128]{2,0,1:T(8,128)(2,1)} %copy.30, bf16[128,8,128]{2,0,1:T(8,128)(2,1)} %copy.29, bf16[128,8,128]{2,0,1:T(8,128)(2,1)} %copy.28), kind=kLoop, calls=%fused_computation.21 | loop fusion | flops 2359296 | bytes 1572864 | tf_op jit(solution)/shard_map/concatenate | solution.py:88
  71.9 2.7 %gather_fusion.3 = bf16[8,384,128]{2,1,0:T(8,128)(2,1)} fusion(bf16[384,8,128]{2,0,1:T(8,128)(2,1)} %pad_maximum_fusion, s32[1024]{0:T(1024)S(1)} %pad_clamp_fusion), kind=kCustom, calls=%fused_computation.3 | custom fusion | bytes 1572896 | tf_op jit(solution)/shard_map/jit(_take)/gather | solution.py:56
  74.6 2.3 %copy.31 = bf16[384,8,128]{0,2,1:T(8,128)(2,1)} copy(bf16[384,8,128]{2,0,1:T(8,128)(2,1)} %bitcast.61) | data formatting | bytes 1572864 | tf_op jit(solution)/shard_map/jit(_take)/gather | solution.py:56
  83.8 2.4 %constant_dynamic-update-slice_fusion.13 = (bf16[1024,256]{1,0:T(8,128)(2,1)}, bf16[128,256]{1,0:T(8,128)(2,1)S(1)}) fusion(bf16[1024,128]{1,0:T(8,128)(2,1)S(1)} %bitcast_select_fusion.1, f32[1024,256]{1,0:T(8,128)} %fusion.4, f32[1024,256]{1,0:T(8,128)S(1)} %fusion.2, bf16[384,256]{1,0:T(8,128)(2,1)} %copy-done.3), kind=kOutput, calls=%fused_computation.63 | convolution fusion | flops 135036928 | bytes 2818048 | tf_op jit(solution)/shard_map/dot_general | solution.py:106
  86.2 2.5 %collective-permute-start.9 = (bf16[128,256]{1,0:T(8,128)(2,1)S(1)}, bf16[128,256]{1,0:T(8,128)(2,1)}, u32[]{:S(2)}, u32[]{:S(2)}) collective-permute-start(bf16[128,256]{1,0:T(8,128)(2,1)S(1)} %get-tuple-element.16), channel_id=1, source_target_pairs={{0,2},{2,4},{4,6},{6,8},{8,10},{10,12},{12,14},{14,0},{1,3},{3,5},... | collective-permute-start | bytes 196616 | tf_op jit(solution)/shard_map/ppermute | solution.py:39
  90.5 2.1 %collective-permute-start.10 = (bf16[128,256]{1,0:T(8,128)(2,1)S(1)}, bf16[128,256]{1,0:T(8,128)(2,1)}, u32[]{:S(2)}, u32[]{:S(2)}) collective-permute-start(bf16[128,256]{1,0:T(8,128)(2,1)S(1)} %get-tuple-element.16), channel_id=1, source_target_pairs={{0,4},{2,6},{4,8},{6,10},{8,12},{10,14},{12,0},{14,2},{1,5},{3,7},... | collective-permute-start | bytes 196616 | tf_op jit(solution)/shard_map/ppermute | solution.py:39
  92.6 2.4 %collective-permute-start.11 = (bf16[128,256]{1,0:T(8,128)(2,1)S(1)}, bf16[128,256]{1,0:T(8,128)(2,1)}, u32[]{:S(2)}, u32[]{:S(2)}) collective-permute-start(bf16[128,256]{1,0:T(8,128)(2,1)S(1)} %get-tuple-element.16), channel_id=1, source_target_pairs={{0,6},{2,8},{4,10},{6,12},{8,14},{10,0},{12,2},{14,4},{1,7},{3,9},... | collective-permute-start | bytes 196616 | tf_op jit(solution)/shard_map/ppermute | solution.py:39
  95.0 2.7 %collective-permute-start.12 = (bf16[128,256]{1,0:T(8,128)(2,1)S(1)}, bf16[128,256]{1,0:T(8,128)(2,1)}, u32[]{:S(2)}, u32[]{:S(2)}) collective-permute-start(bf16[128,256]{1,0:T(8,128)(2,1)S(1)} %get-tuple-element.16), channel_id=1, source_target_pairs={{0,8},{2,10},{4,12},{6,14},{8,0},{10,2},{12,4},{14,6},{1,9},{3,11}... | collective-permute-start | bytes 196616 | tf_op jit(solution)/shard_map/ppermute | solution.py:39
  97.8 1.8 %copy.33 = bf16[128,8,128]{0,2,1:T(8,128)(2,1)} copy(bf16[128,8,128]{2,0,1:T(8,128)(2,1)} %slice_select_fusion) | data formatting | bytes 524288 | tf_op jit(solution)/shard_map/slice | solution.py:112
  99.6 2.4 %collective-permute-start.14 = (bf16[128,256]{1,0:T(8,128)(2,1)S(1)}, bf16[128,256]{1,0:T(8,128)(2,1)S(1)}, u32[]{:S(2)}, u32[]{:S(2)}) collective-permute-start(bf16[128,256]{1,0:T(8,128)(2,1)S(1)} %get-tuple-element.16), channel_id=1, source_target_pairs={{0,12},{2,14},{4,0},{6,2},{8,4},{10,6},{12,8},{14,10},{1,13},{3,15... | collective-permute-start | bytes 196616 | tf_op jit(solution)/shard_map/ppermute | solution.py:39
  111.4 2.6 %fusion.10 = bf16[1,1024,256]{2,1,0:T(8,128)(2,1)} fusion(f32[1024,256]{1,0:T(8,128)S(1)} %copy-done.1, bf16[1024,128]{1,0:T(8,128)(2,1)S(1)} %bitcast_select_fusion.1, bf16[128,1024]{0,1:T(8,128)(2,1)} %bitcast.65, bf16[1024,256]{1,0:T(8,128)(2,1)} %constant_dynamic-update-slice_fusion.6), kind=kOutput, calls=%fused_computation.15 | convolution fusion | flops 134774784 | bytes 2621440 | tf_op jit(solution)/shard_map/dot_general | solution.py:114
  (84 shorter events, 53.3 us)
Async XLA Ops:
  1.8 15.5 %copy-start.4 = (s32[1,2,128]{2,1,0:T(2,128)S(1)}, s32[1,2,128]{2,1,0:T(2,128)}, u32[]{:S(2)}) copy-start(s32[1,2,128]{2,1,0:T(2,128)} %param.10) | copy-start | bytes 3076
  3.6 21.5 %copy-start.5 = (f32[1,2,128]{2,1,0:T(2,128)S(1)}, f32[1,2,128]{2,1,0:T(2,128)}, u32[]{:S(2)}) copy-start(f32[1,2,128]{2,1,0:T(2,128)} %param.9) | copy-start | bytes 3076
  4.5 32.0 %collective-permute-start.3 = (bf16[128,256]{1,0:T(8,128)(2,1)}, bf16[128,256]{1,0:T(8,128)(2,1)}, u32[]{:S(2)}, u32[]{:S(2)}) collective-permute-start(bf16[128,256]{1,0:T(8,128)(2,1)} %get-tuple-element.14), channel_id=1, source_target_pairs={{0,4},{2,6},{4,8},{6,10},{8,12},{10,14},{12,0},{14,2},{1,5},{3,7},... | collective-permute-start | bytes 196616 | tf_op jit(solution)/shard_map/ppermute | solution.py:39
  7.5 31.9 %collective-permute-start.4 = (bf16[128,256]{1,0:T(8,128)(2,1)}, bf16[128,256]{1,0:T(8,128)(2,1)}, u32[]{:S(2)}, u32[]{:S(2)}) collective-permute-start(bf16[128,256]{1,0:T(8,128)(2,1)} %get-tuple-element.14), channel_id=1, source_target_pairs={{0,6},{2,8},{4,10},{6,12},{8,14},{10,0},{12,2},{14,4},{1,7},{3,9},... | collective-permute-start | bytes 196616 | tf_op jit(solution)/shard_map/ppermute | solution.py:39
  10.1 30.9 %collective-permute-start.5 = (bf16[128,256]{1,0:T(8,128)(2,1)}, bf16[128,256]{1,0:T(8,128)(2,1)}, u32[]{:S(2)}, u32[]{:S(2)}) collective-permute-start(bf16[128,256]{1,0:T(8,128)(2,1)} %get-tuple-element.14), channel_id=1, source_target_pairs={{0,8},{2,10},{4,12},{6,14},{8,0},{10,2},{12,4},{14,6},{1,9},{3,11}... | collective-permute-start | bytes 196616 | tf_op jit(solution)/shard_map/ppermute | solution.py:39
  11.3 31.2 %collective-permute-start.6 = (bf16[128,256]{1,0:T(8,128)(2,1)}, bf16[128,256]{1,0:T(8,128)(2,1)}, u32[]{:S(2)}, u32[]{:S(2)}) collective-permute-start(bf16[128,256]{1,0:T(8,128)(2,1)} %get-tuple-element.14), channel_id=1, source_target_pairs={{0,10},{2,12},{4,14},{6,0},{8,2},{10,4},{12,6},{14,8},{1,11},{3,13... | collective-permute-start | bytes 196616 | tf_op jit(solution)/shard_map/ppermute | solution.py:39
  14.0 30.0 %all-to-all-start = ((bf16[4,1,64,1,256]{4,2,3,1,0:T(8,128)(2,1)}), bf16[4,1,64,1,256]{4,2,3,1,0:T(8,128)(2,1)S(1)}, u32[]{:S(2)}, u32[]{:S(2)}) async-start(bf16[4,1,64,1,256]{4,2,3,1,0:T(8,128)(2,1)} %param.13), calls=%async_computation | async-start | bytes 262144 | tf_op jit(solution)/shard_map/all_to_all | solution.py:18
  21.7 9.5 %collective-permute-start = (bf16[256,256]{1,0:T(8,128)(2,1)}, bf16[256,256]{1,0:T(8,128)(2,1)}, u32[]{:S(2)}, u32[]{:S(2)}) collective-permute-start(bf16[256,256]{1,0:T(8,128)(2,1)} %get-tuple-element.8), channel_id=1, source_target_pairs={{0,2},{2,4},{4,6},{6,8},{8,10},{10,12},{12,14},{14,0},{1,3},{3,5},... | collective-permute-start | bytes 393224 | tf_op jit(solution)/shard_map/ppermute | solution.py:39
  31.3 25.2 %collective-permute-start.7 = (bf16[128,256]{1,0:T(8,128)(2,1)}, bf16[128,256]{1,0:T(8,128)(2,1)}, u32[]{:S(2)}, u32[]{:S(2)}) collective-permute-start(bf16[128,256]{1,0:T(8,128)(2,1)} %get-tuple-element.14), channel_id=1, source_target_pairs={{0,12},{2,14},{4,0},{6,2},{8,4},{10,6},{12,8},{14,10},{1,13},{3,15... | collective-permute-start | bytes 196616 | tf_op jit(solution)/shard_map/ppermute | solution.py:39
  36.6 21.3 %collective-permute-start.8 = (bf16[256,256]{1,0:T(8,128)(2,1)}, bf16[256,256]{1,0:T(8,128)(2,1)}, u32[]{:S(2)}, u32[]{:S(2)}) collective-permute-start(bf16[256,256]{1,0:T(8,128)(2,1)} %get-tuple-element.7), channel_id=1, source_target_pairs={{0,14},{2,0},{4,2},{6,4},{8,6},{10,8},{12,10},{14,12},{1,15},{3,1}... | collective-permute-start | bytes 393224 | tf_op jit(solution)/shard_map/ppermute | solution.py:39
  49.8 11.3 %collective-permute-start.2 = (bf16[128,1152]{0,1:T(8,128)(2,1)}, bf16[128,1152]{0,1:T(8,128)(2,1)}, u32[]{:S(2)}, u32[]{:S(2)}) collective-permute-start(bf16[128,1152]{0,1:T(8,128)(2,1)} %get-tuple-element.6), channel_id=1, source_target_pairs={{2,0},{4,2},{6,4},{8,6},{10,8},{12,10},{14,12},{3,1},{5,3},{7,5},{... | collective-permute-start | bytes 884744 | tf_op jit(solution)/shard_map/ppermute | solution.py:14
  51.1 15.3 %collective-permute-start.1 = (bf16[128,1152]{0,1:T(8,128)(2,1)}, bf16[128,1152]{0,1:T(8,128)(2,1)}, u32[]{:S(2)}, u32[]{:S(2)}) collective-permute-start(bf16[128,1152]{0,1:T(8,128)(2,1)} %get-tuple-element.5), channel_id=1, source_target_pairs={{0,2},{2,4},{4,6},{6,8},{8,10},{10,12},{12,14},{1,3},{3,5},{5,7},{... | collective-permute-start | bytes 884744 | tf_op jit(solution)/shard_map/ppermute | solution.py:14
  76.9 2.9 %copy-start.9 = (f32[128]{0:T(128)S(1)}, f32[128]{0:T(128)}, u32[]{:S(2)}) copy-start(f32[128]{0:T(128)} %get-tuple-element.10) | copy-start | bytes 1540
  76.9 4.1 %copy-start.8 = (f32[128]{0:T(128)S(1)}, f32[128]{0:T(128)}, u32[]{:S(2)}) copy-start(f32[128]{0:T(128)} %get-tuple-element.9) | copy-start | bytes 1540
  76.9 5.2 %copy-start.2 = (bf16[768,256]{1,0:T(8,128)(2,1)S(1)}, bf16[768,256]{1,0:T(8,128)(2,1)}, u32[]{:S(2)}) copy-start(bf16[768,256]{1,0:T(8,128)(2,1)} %slice_bitcast_fusion) | copy-start | bytes 1179652
  83.8 4.9 %copy-start.7 = (pred[8]{0:T(512)(128)(4,1)S(1)}, pred[8]{0:T(512)(128)(4,1)}, u32[]{:S(2)}) copy-start(pred[8]{0:T(512)(128)(4,1)} %copy-done.6) | copy-start | bytes 28
  86.2 25.1 %copy-start.1 = (f32[1024,256]{1,0:T(8,128)S(1)}, f32[1024,256]{1,0:T(8,128)}, u32[]{:S(2)}) copy-start(f32[1024,256]{1,0:T(8,128)} %fusion.4) | copy-start | bytes 3145732
  86.2 13.3 %collective-permute-start.9 = (bf16[128,256]{1,0:T(8,128)(2,1)S(1)}, bf16[128,256]{1,0:T(8,128)(2,1)}, u32[]{:S(2)}, u32[]{:S(2)}) collective-permute-start(bf16[128,256]{1,0:T(8,128)(2,1)S(1)} %get-tuple-element.16), channel_id=1, source_target_pairs={{0,2},{2,4},{4,6},{6,8},{8,10},{10,12},{12,14},{14,0},{1,3},{3,5},... | collective-permute-start | bytes 196616 | tf_op jit(solution)/shard_map/ppermute | solution.py:39
  90.5 12.9 %collective-permute-start.10 = (bf16[128,256]{1,0:T(8,128)(2,1)S(1)}, bf16[128,256]{1,0:T(8,128)(2,1)}, u32[]{:S(2)}, u32[]{:S(2)}) collective-permute-start(bf16[128,256]{1,0:T(8,128)(2,1)S(1)} %get-tuple-element.16), channel_id=1, source_target_pairs={{0,4},{2,6},{4,8},{6,10},{8,12},{10,14},{12,0},{14,2},{1,5},{3,7},... | collective-permute-start | bytes 196616 | tf_op jit(solution)/shard_map/ppermute | solution.py:39
  92.6 13.9 %collective-permute-start.11 = (bf16[128,256]{1,0:T(8,128)(2,1)S(1)}, bf16[128,256]{1,0:T(8,128)(2,1)}, u32[]{:S(2)}, u32[]{:S(2)}) collective-permute-start(bf16[128,256]{1,0:T(8,128)(2,1)S(1)} %get-tuple-element.16), channel_id=1, source_target_pairs={{0,6},{2,8},{4,10},{6,12},{8,14},{10,0},{12,2},{14,4},{1,7},{3,9},... | collective-permute-start | bytes 196616 | tf_op jit(solution)/shard_map/ppermute | solution.py:39
  95.0 12.9 %collective-permute-start.12 = (bf16[128,256]{1,0:T(8,128)(2,1)S(1)}, bf16[128,256]{1,0:T(8,128)(2,1)}, u32[]{:S(2)}, u32[]{:S(2)}) collective-permute-start(bf16[128,256]{1,0:T(8,128)(2,1)S(1)} %get-tuple-element.16), channel_id=1, source_target_pairs={{0,8},{2,10},{4,12},{6,14},{8,0},{10,2},{12,4},{14,6},{1,9},{3,11}... | collective-permute-start | bytes 196616 | tf_op jit(solution)/shard_map/ppermute | solution.py:39
  97.8 11.7 %collective-permute-start.13 = (bf16[128,256]{1,0:T(8,128)(2,1)S(1)}, bf16[128,256]{1,0:T(8,128)(2,1)S(1)}, u32[]{:S(2)}, u32[]{:S(2)}) collective-permute-start(bf16[128,256]{1,0:T(8,128)(2,1)S(1)} %get-tuple-element.16), channel_id=1, source_target_pairs={{0,10},{2,12},{4,14},{6,0},{8,2},{10,4},{12,6},{14,8},{1,11},{3,13... | collective-permute-start | bytes 196616 | tf_op jit(solution)/shard_map/ppermute | solution.py:39
  99.6 10.5 %collective-permute-start.14 = (bf16[128,256]{1,0:T(8,128)(2,1)S(1)}, bf16[128,256]{1,0:T(8,128)(2,1)S(1)}, u32[]{:S(2)}, u32[]{:S(2)}) collective-permute-start(bf16[128,256]{1,0:T(8,128)(2,1)S(1)} %get-tuple-element.16), channel_id=1, source_target_pairs={{0,12},{2,14},{4,0},{6,2},{8,4},{10,6},{12,8},{14,10},{1,13},{3,15... | collective-permute-start | bytes 196616 | tf_op jit(solution)/shard_map/ppermute | solution.py:39
  103.4 7.3 %collective-permute-start.15 = (bf16[128,256]{1,0:T(8,128)(2,1)S(1)}, bf16[128,256]{1,0:T(8,128)(2,1)S(1)}, u32[]{:S(2)}, u32[]{:S(2)}) collective-permute-start(bf16[128,256]{1,0:T(8,128)(2,1)S(1)} %get-tuple-element.16), channel_id=1, source_target_pairs={{0,14},{2,0},{4,2},{6,4},{8,6},{10,8},{12,10},{14,12},{1,15},{3,1}... | collective-permute-start | bytes 196616 | tf_op jit(solution)/shard_map/ppermute | solution.py:39
  (3 other events, 3.7 us)

commit v4 on v1

--- a/solution.py
+++ b/solution.py
@@ -13,10 +13,18 @@
     return lax.ppermute(shard, DUCT, pairs)
 
 
-def own_coarse_rows(coarse_inverse):
-    rows = lax.all_to_all(coarse_inverse, "sub", split_axis=0, concat_axis=3, tiled=True)
-    rows = lax.all_gather(rows, "rep", axis=2, tiled=True)
-    return rows.reshape(rows.shape[2], rows.shape[3] * rows.shape[4])
+def swapped(shard, axis):
+    return lax.ppermute(shard, axis, [(0, 1), (1, 0)])
+
+
+def gathered(shard, axis, dim):
+    if lax.axis_size(axis) != 2:
+        return lax.all_gather(shard, axis, axis=dim, tiled=True)
+    other = swapped(shard, axis)
+    first = lax.axis_index(axis) == 0
+    return jnp.concatenate(
+        [jnp.where(first, shard, other), jnp.where(first, other, shard)], axis=dim
+    )
 
 
 def local(
@@ -33,13 +41,16 @@
     iface_rows = inverse.shape[0]
     face_rows = coupling.shape[2]
     slot_count = deflation_basis.shape[2]
+    sub_count = lax.axis_size("sub")
+    sub_index = lax.axis_index("sub")
     slot_ids = jnp.arange(slot_count, dtype=jnp.int32)
     masked_basis = jnp.where(
         slot_ids[None, :] < deflation_counts[0],
         deflation_basis[0],
         jnp.zeros((), deflation_basis.dtype),
     )
-    coarse_rows = own_coarse_rows(coarse_inverse)
+    half_block = coarse_inverse[:, 0, :, 0, :]
+    columns = gathered(half_block, "rep", 1)
     lower_gain = coupling[0, 0][:, None]
     upper_gain = coupling[0, 1][:, None]
 
@@ -47,10 +58,19 @@
         projected = lax.dot_general(
             masked_basis, defect, (((0,), (0,)), ((), ())), preferred_element_type=jnp.float32
         ).astype(jnp.bfloat16)
-        vector = lax.all_gather(projected, DUCT, axis=0, tiled=True)
-        coarse = jnp.dot(coarse_rows, vector, preferred_element_type=jnp.float32).astype(
-            jnp.bfloat16
+        inputs = gathered(projected, "tile", 0)
+        partial = jnp.einsum(
+            "jsc,cm->jsm", columns, inputs, preferred_element_type=jnp.float32
+        ).astype(jnp.bfloat16)
+        total = lax.dynamic_index_in_dim(partial, sub_index, 0, keepdims=False).astype(
+            jnp.float32
         )
+        for k in range(1, sub_count):
+            piece = lax.dynamic_index_in_dim(partial, (sub_index + k) % sub_count, 0, keepdims=False)
+            total = total + lax.ppermute(
+                piece, "sub", [(i, (i + k) % sub_count) for i in range(sub_count)]
+            ).astype(jnp.float32)
+        coarse = total.astype(jnp.bfloat16)
         return local_solve + jnp.dot(masked_basis, coarse, preferred_element_type=jnp.float32)
 
     local_solve = jnp.dot(inverse, source, preferred_element_type=jnp.float32)

time: 101 us -> 51.3 us (0.51)
  blocking collectives: 67.3 us -> 0 us
  waiting for transfers between devices: 4.84 us -> 19.9 us
  starting transfers between devices: 11.3 us -> 18.2 us
  matrix products: 8.85 us -> 5.94 us
    all_gather x3 -> x0, blocking collectives: 67.3 us -> none  [the longest x2 65.3 us: coarse_step(): vector = lax.all_gather(projected, DUCT, axis=0, tiled=True)]
    ppermute x0 -> x9, waiting for transfers between devices: none -> 14.8 us  [the longest x6 10 us: coarse_step(): lax.ppermute(piece, 'sub', [(i, (i + k) % sub_count) for i in range(sub_c...]
    ppermute x0 -> x9, starting transfers between devices: none -> 13.5 us  [the longest x6 9.07 us: coarse_step(): lax.ppermute(piece, 'sub', [(i, (i + k) % sub_count) for i in range(sub_c...]
    all_to_all x1 -> x0, starting transfers between devices: 6.45 us -> none  [own_coarse_rows(): lax.all_to_all(coarse_inverse, 'sub', split_axis=0, concat_axis=3, tiled=...]
    dot_general x2, matrix products: 4.79 us -> 1.39 us  [coarse_step(): jnp.dot(masked_basis, coarse, preferred_element_type=jnp.float32)]
  transfers between devices with their start and end apart: 3 -> 11, of which waited for: 2 -> 8; matrix products, arithmetic and copies ran while one was open for 5% -> 6% of each run, Pallas kernels for 0% -> 0%
where the time goes in v4:
time: 51.3 us; the launch traced here: 51 us
  waiting for transfers between devices  19.9 us (39%)
  starting transfers between devices  18.2 us (35%)
  matrix products  5.94 us (12%)
  local copies, waits for them, and re-layouts  4.93 us (10%)
  other arithmetic  1.05 us (2%)
  between operations  1.05 us (2%)
    ppermute x6, waiting for transfers between devices, coarse_step(): lax.ppermute(piece, 'sub', [(i, (i + k) % sub_count) for i in range(sub_c...  10 us
    ppermute x6, starting transfers between devices, coarse_step(): lax.ppermute(piece, 'sub', [(i, (i + k) % sub_count) for i in range(sub_c...  9.07 us
    ppermute x2, waiting for transfers between devices, passed_along(): return lax.ppermute(shard, DUCT, pairs)  5.05 us
    ppermute x3, waiting for transfers between devices, swapped(): return lax.ppermute(shard, axis, [(0, 1), (1, 0)])  4.8 us
    ppermute x2, starting transfers between devices, passed_along(): return lax.ppermute(shard, DUCT, pairs)  4.68 us
    ppermute x3, starting transfers between devices, swapped(): return lax.ppermute(shard, axis, [(0, 1), (1, 0)])  4.45 us
    dot_general x1, matrix products, local(): local_solve = jnp.dot(inverse, source, preferred_element_type=jnp.float32)  1.82 us
    dot_general x1, matrix products, local(): local_solve = jnp.dot(inverse, boundary, preferred_element_type=jnp.float32)  1.71 us
  transfers between devices with their start and end apart: 11, of which 8 were waited for; matrix products, arithmetic and copies ran while one was open for 6% of the time, Pallas kernels for 0%

profile of v4, /device:TPU:0, one launch (start us, length us, event | category | flops | bytes accessed | tf_op | source)
XLA Modules:
  0.0 51.0 jit_solution(1242618658419223209)
XLA Ops:
  1.6 1.8 %fusion.2 = f32[1024,256]{1,0:T(8,128)S(1)} fusion(bf16[1,1024,1024]{2,1,0:T(8,128)(2,1)S(1)} %copy-done, bf16[1,1024,256]{2,1,0:T(8,128)(2,1)} %param.7), kind=kOutput, calls=%fused_computation.4 | convolution fusion | flops 536870912 | bytes 3670016 | tf_op jit(solution)/shard_map/dot_general | solution.py:76
  3.4 1.0 %copy-done.1 = f32[1024,256]{1,0:T(8,128)} copy-done((f32[1024,256]{1,0:T(8,128)}, f32[1024,256]{1,0:T(8,128)S(1)}, u32[]{:S(2)}) %copy-start.1) | copy-done | bytes 1048600
  4.7 3.0 %collective-permute-start.1 = (bf16[128,256]{1,0:T(8,128)(2,1)S(1)}, bf16[128,256]{1,0:T(8,128)(2,1)S(1)}, u32[]{:S(2)}, u32[]{:S(2)}) collective-permute-start(bf16[128,256]{1,0:T(8,128)(2,1)S(1)} %convolution_convert_fusion.3), channel_id=1, source_target_pairs={{0,2},{2,0},{1,3},{3,1},{4,6},{6,4},{5,7},{7,5},{8,10},{10,8},{9,1... | collective-permute-start | bytes 196616 | tf_op jit(solution)/shard_map/ppermute | solution.py:17
  7.7 0.8 %slice_bitcast_fusion = bf16[768,256]{1,0:T(8,128)(2,1)} fusion(bf16[1,1024,256]{2,1,0:T(8,128)(2,1)S(1)} %copy-done.4), kind=kLoop, calls=%fused_computation.23 | loop fusion | bytes 786432 | tf_op jit(solution)/shard_map/slice | solution.py:88
  8.5 1.4 %collective-permute-done.1 = bf16[128,256]{1,0:T(8,128)(2,1)S(1)} collective-permute-done((bf16[128,256]{1,0:T(8,128)(2,1)S(1)}, bf16[128,256]{1,0:T(8,128)(2,1)S(1)}, u32[]{:S(2)}, u32[]{:S(2)}) %collective-permute-start.1) | collective-permute-done | bytes 65568 | tf_op jit(solution)/shard_map/ppermute | solution.py:17
  10.4 2.2 %collective-permute-start.2 = (bf16[128,256]{1,0:T(8,128)(2,1)S(1)}, bf16[128,256]{1,0:T(8,128)(2,1)S(1)}, u32[]{:S(2)}, u32[]{:S(2)}) collective-permute-start(bf16[128,256]{1,0:T(8,128)(2,1)S(1)} %get-tuple-element.10), channel_id=1, source_target_pairs={{0,4},{4,8},{8,12},{12,0},{1,5},{5,9},{9,13},{13,1},{2,6},{6,10},{... | collective-permute-start | bytes 196616 | tf_op jit(solution)/shard_map/ppermute | solution.py:70
  12.5 2.1 %collective-permute-start.4 = (bf16[128,256]{1,0:T(8,128)(2,1)S(1)}, bf16[128,256]{1,0:T(8,128)(2,1)S(1)}, u32[]{:S(2)}, u32[]{:S(2)}) collective-permute-start(bf16[128,256]{1,0:T(8,128)(2,1)S(1)} %get-tuple-element.11), channel_id=1, source_target_pairs={{0,12},{4,0},{8,4},{12,8},{1,13},{5,1},{9,5},{13,9},{2,14},{6,2},{... | collective-permute-start | bytes 196616 | tf_op jit(solution)/shard_map/ppermute | solution.py:70
  14.6 1.0 %collective-permute-start.3 = (bf16[128,256]{1,0:T(8,128)(2,1)S(1)}, bf16[128,256]{1,0:T(8,128)(2,1)S(1)}, u32[]{:S(2)}, u32[]{:S(2)}) collective-permute-start(bf16[128,256]{1,0:T(8,128)(2,1)S(1)} %get-tuple-element.12), channel_id=1, source_target_pairs={{0,8},{4,12},{8,0},{12,4},{1,9},{5,13},{9,1},{13,5},{2,10},{6,14},... | collective-permute-start | bytes 196616 | tf_op jit(solution)/shard_map/ppermute | solution.py:70
  15.6 1.9 %collective-permute-done.2 = bf16[128,256]{1,0:T(8,128)(2,1)S(1)} collective-permute-done((bf16[128,256]{1,0:T(8,128)(2,1)S(1)}, bf16[128,256]{1,0:T(8,128)(2,1)S(1)}, u32[]{:S(2)}, u32[]{:S(2)}) %collective-permute-start.2) | collective-permute-done | bytes 65568 | tf_op jit(solution)/shard_map/ppermute | solution.py:70
  17.6 2.9 %collective-permute-done.3 = bf16[128,256]{1,0:T(8,128)(2,1)S(1)} collective-permute-done((bf16[128,256]{1,0:T(8,128)(2,1)S(1)}, bf16[128,256]{1,0:T(8,128)(2,1)S(1)}, u32[]{:S(2)}, u32[]{:S(2)}) %collective-permute-start.3) | collective-permute-done | bytes 65568 | tf_op jit(solution)/shard_map/ppermute | solution.py:70
  20.7 1.4 %gather_fusion.1 = bf16[128,256]{1,0:T(8,128)(2,1)} fusion(f32[1024,256]{1,0:T(8,128)S(1)} %convolution_add_fusion.1, s32[1024]{0:T(1024)S(1)} %pad_clamp_fusion), kind=kCustom, calls=%fused_computation.1 | custom fusion | bytes 131584 | tf_op jit(solution)/shard_map/gather | solution.py:79
  22.1 1.4 %gather_fusion = bf16[128,256]{1,0:T(8,128)(2,1)} fusion(f32[1024,256]{1,0:T(8,128)S(1)} %convolution_add_fusion.1, s32[1024]{0:T(1024)S(1)} %pad_clamp_fusion.1), kind=kCustom, calls=%fused_computation | custom fusion | bytes 131584 | tf_op jit(solution)/shard_map/gather | solution.py:80
  23.5 3.4 %collective-permute-start.5 = (bf16[128,256]{1,0:T(8,128)(2,1)}, bf16[128,256]{1,0:T(8,128)(2,1)S(1)}, u32[]{:S(2)}, u32[]{:S(2)}) collective-permute-start(bf16[128,256]{1,0:T(8,128)(2,1)} %gather_fusion), channel_id=1, source_target_pairs={{0,2},{2,4},{4,6},{6,8},{8,10},{10,12},{12,14},{1,3},{3,5},{5,7},{... | collective-permute-start | bytes 196616 | tf_op jit(solution)/shard_map/ppermute | solution.py:13
  26.9 1.3 %collective-permute-start.6 = (bf16[128,256]{1,0:T(8,128)(2,1)}, bf16[128,256]{1,0:T(8,128)(2,1)S(1)}, u32[]{:S(2)}, u32[]{:S(2)}) collective-permute-start(bf16[128,256]{1,0:T(8,128)(2,1)} %gather_fusion.1), channel_id=1, source_target_pairs={{2,0},{4,2},{6,4},{8,6},{10,8},{12,10},{14,12},{3,1},{5,3},{7,5},{... | collective-permute-start | bytes 196616 | tf_op jit(solution)/shard_map/ppermute | solution.py:13
  28.2 0.9 %collective-permute-done.5 = bf16[128,256]{1,0:T(8,128)(2,1)S(1)} collective-permute-done((bf16[128,256]{1,0:T(8,128)(2,1)}, bf16[128,256]{1,0:T(8,128)(2,1)S(1)}, u32[]{:S(2)}, u32[]{:S(2)}) %collective-permute-start.5) | collective-permute-done | bytes 65568 | tf_op jit(solution)/shard_map/ppermute | solution.py:13
  29.1 4.2 %collective-permute-done.6 = bf16[128,256]{1,0:T(8,128)(2,1)S(1)} collective-permute-done((bf16[128,256]{1,0:T(8,128)(2,1)}, bf16[128,256]{1,0:T(8,128)(2,1)S(1)}, u32[]{:S(2)}, u32[]{:S(2)}) %collective-permute-start.6) | collective-permute-done | bytes 65568 | tf_op jit(solution)/shard_map/ppermute | solution.py:13
  33.3 1.0 %fusion.27 = (bf16[128,256]{1,0:T(8,128)(2,1)S(1)}, bf16[128,256]{1,0:T(8,128)(2,1)S(1)}) fusion(bf16[128,256]{1,0:T(8,128)(2,1)S(1)} %collective-permute-done.5, f32[128]{0:T(128)S(1)} %get-tuple-element.19, bf16[1,1024,256]{2,1,0:T(8,128)(2,1)} %param.7, bf16[128,256]{1,0:T(8,128)(2,1)S(1)} %collective-permute-done.6, f32[128]{0:T(128)S(1)} %get-tuple-element.20), kind=kLoop, calls=%fused_computation.43 | loop fusion | flops 327680 | bytes 394240 | tf_op jit(solution)/shard_map/convert_element_type | solution.py:87
  34.3 1.7 %fusion.4 = f32[1024,256]{1,0:T(8,128)S(1)} fusion(bf16[1,1024,1024]{2,1,0:T(8,128)(2,1)S(1)} %copy-done, bf16[128,256]{1,0:T(8,128)(2,1)S(1)} %get-tuple-element.6, bf16[768,256]{1,0:T(8,128)(2,1)} %slice_bitcast_fusion, bf16[128,256]{1,0:T(8,128)(2,1)S(1)} %get-tuple-element.5), kind=kOutput, calls=%fused_computation.6 | convolution fusion | flops 538443776 | bytes 3670016 | tf_op jit(solution)/shard_map/dot_general | solution.py:93
  36.3 1.0 %collective-permute-start.7 = (bf16[128,256]{1,0:T(8,128)(2,1)S(1)}, bf16[128,256]{1,0:T(8,128)(2,1)S(1)}, u32[]{:S(2)}, u32[]{:S(2)}) collective-permute-start(bf16[128,256]{1,0:T(8,128)(2,1)S(1)} %convolution_convert_fusion.2), channel_id=1, source_target_pairs={{0,2},{2,0},{1,3},{3,1},{4,6},{6,4},{5,7},{7,5},{8,10},{10,8},{9,1... | collective-permute-start | bytes 196616 | tf_op jit(solution)/shard_map/ppermute | solution.py:17
  37.3 3.4 %collective-permute-done.7 = bf16[128,256]{1,0:T(8,128)(2,1)S(1)} collective-permute-done((bf16[128,256]{1,0:T(8,128)(2,1)S(1)}, bf16[128,256]{1,0:T(8,128)(2,1)S(1)}, u32[]{:S(2)}, u32[]{:S(2)}) %collective-permute-start.7) | collective-permute-done | bytes 65568 | tf_op jit(solution)/shard_map/ppermute | solution.py:17
  41.0 3.8 %collective-permute-start.10 = (bf16[128,256]{1,0:T(8,128)(2,1)S(1)}, bf16[128,256]{1,0:T(8,128)(2,1)S(1)}, u32[]{:S(2)}, u32[]{:S(2)}) collective-permute-start(bf16[128,256]{1,0:T(8,128)(2,1)S(1)} %get-tuple-element.8), channel_id=1, source_target_pairs={{0,12},{4,0},{8,4},{12,8},{1,13},{5,1},{9,5},{13,9},{2,14},{6,2},{... | collective-permute-start | bytes 196616 | tf_op jit(solution)/shard_map/ppermute | solution.py:70
  44.8 2.3 %collective-permute-done.8 = bf16[128,256]{1,0:T(8,128)(2,1)S(1)} collective-permute-done((bf16[128,256]{1,0:T(8,128)(2,1)S(1)}, bf16[128,256]{1,0:T(8,128)(2,1)S(1)}, u32[]{:S(2)}, u32[]{:S(2)}) %collective-permute-start.8) | collective-permute-done | bytes 65568 | tf_op jit(solution)/shard_map/ppermute | solution.py:70
  47.1 2.8 %collective-permute-done.9 = bf16[128,256]{1,0:T(8,128)(2,1)S(1)} collective-permute-done((bf16[128,256]{1,0:T(8,128)(2,1)S(1)}, bf16[128,256]{1,0:T(8,128)(2,1)S(1)}, u32[]{:S(2)}, u32[]{:S(2)}) %collective-permute-start.9) | collective-permute-done | bytes 65568 | tf_op jit(solution)/shard_map/ppermute | solution.py:70
  50.0 1.1 %fusion.8 = bf16[1,1024,256]{2,1,0:T(8,128)(2,1)} fusion(f32[1024,256]{1,0:T(8,128)S(1)} %fusion.4, bf16[1,1024,128]{2,1,0:T(8,128)(2,1)S(1)} %copy-done.3, pred[128]{0:T(512)(128)(4,1)S(1)} %iota_compare_fusion, bf16[128,256]{1,0:T(8,128)(2,1)S(1)} %collective-permute-done.10, bf16[128,256]{1,0:T(8,128)(2,1)S(1)} %collective-permute-done.9, ...), kind=kOutput, calls=%fused_computation.10 | convolution fusion | flops 68026368 | bytes 2097668 | tf_op jit(solution)/shard_map/dot_general | solution.py:74
  (40 shorter events, 2.3 us)
Async XLA Ops:
  0.0 1.6 %copy-start = (bf16[1,1024,1024]{2,1,0:T(8,128)(2,1)S(1)}, bf16[1,1024,1024]{2,1,0:T(8,128)(2,1)}, u32[]{:S(2)}) copy-start(bf16[1,1024,1024]{2,1,0:T(8,128)(2,1)} %param.8) | copy-start | bytes 6291460
  0.0 10.0 %collective-permute-start = (bf16[4,64,256]{2,1,0:T(8,128)(2,1)}, bf16[4,64,256]{2,1,0:T(8,128)(2,1)S(1)}, u32[]{:S(2)}, u32[]{:S(2)}) collective-permute-start(bf16[4,64,256]{2,1,0:T(8,128)(2,1)} %bitcast.75), channel_id=1, source_target_pairs={{0,1},{1,0},{2,3},{3,2},{4,5},{5,4},{6,7},{7,6},{8,9},{9,8},{10,11... | collective-permute-start | bytes 393224 | tf_op jit(solution)/shard_map/ppermute | solution.py:17
  1.6 2.9 %copy-start.3 = (bf16[1,1024,128]{2,1,0:T(8,128)(2,1)S(1)}, bf16[1,1024,128]{2,1,0:T(8,128)(2,1)}, u32[]{:S(2)}) copy-start(bf16[1,1024,128]{2,1,0:T(8,128)(2,1)} %param.11) | copy-start | bytes 786436
  1.6 6.2 %copy-start.4 = (bf16[1,1024,256]{2,1,0:T(8,128)(2,1)S(1)}, bf16[1,1024,256]{2,1,0:T(8,128)(2,1)}, u32[]{:S(2)}) copy-start(bf16[1,1024,256]{2,1,0:T(8,128)(2,1)} %param.7) | copy-start | bytes 1572868
  3.4 1.0 %copy-start.1 = (f32[1024,256]{1,0:T(8,128)}, f32[1024,256]{1,0:T(8,128)S(1)}, u32[]{:S(2)}) copy-start(f32[1024,256]{1,0:T(8,128)S(1)} %fusion.2) | copy-start | bytes 3145732
  4.4 4.1 %copy-start.8 = (s32[1,2,128]{2,1,0:T(2,128)S(1)}, s32[1,2,128]{2,1,0:T(2,128)}, u32[]{:S(2)}) copy-start(s32[1,2,128]{2,1,0:T(2,128)} %param.10) | copy-start | bytes 3076
  4.4 5.6 %copy-start.5 = (bf16[4,1,64,1,256]{4,2,3,1,0:T(8,128)(2,1)S(1)}, bf16[4,1,64,1,256]{4,2,3,1,0:T(8,128)(2,1)}, u32[]{:S(2)}) copy-start(bf16[4,1,64,1,256]{4,2,3,1,0:T(8,128)(2,1)} %param.13) | copy-start | bytes 393220
  4.7 5.3 %collective-permute-start.1 = (bf16[128,256]{1,0:T(8,128)(2,1)S(1)}, bf16[128,256]{1,0:T(8,128)(2,1)S(1)}, u32[]{:S(2)}, u32[]{:S(2)}) collective-permute-start(bf16[128,256]{1,0:T(8,128)(2,1)S(1)} %convolution_convert_fusion.3), channel_id=1, source_target_pairs={{0,2},{2,0},{1,3},{3,1},{4,6},{6,4},{5,7},{7,5},{8,10},{10,8},{9,1... | collective-permute-start | bytes 196616 | tf_op jit(solution)/shard_map/ppermute | solution.py:17
  8.5 11.9 %copy-start.2 = (f32[1024,256]{1,0:T(8,128)S(1)}, f32[1024,256]{1,0:T(8,128)}, u32[]{:S(2)}) copy-start(f32[1024,256]{1,0:T(8,128)} %copy-done.1) | copy-start | bytes 3145732
  10.1 7.5 %copy-start.6 = (bf16[4,64,256]{2,1,0:T(8,128)(2,1)}, bf16[4,64,256]{2,1,0:T(8,128)(2,1)S(1)}, u32[]{:S(2)}) copy-start(bf16[4,64,256]{2,1,0:T(8,128)(2,1)S(1)} %get-tuple-element.14) | copy-start | bytes 393220
  10.3 17.9 %copy-start.9 = (f32[1,2,128]{2,1,0:T(2,128)S(1)}, f32[1,2,128]{2,1,0:T(2,128)}, u32[]{:S(2)}) copy-start(f32[1,2,128]{2,1,0:T(2,128)} %param.9) | copy-start | bytes 3076
  10.4 7.2 %collective-permute-start.2 = (bf16[128,256]{1,0:T(8,128)(2,1)S(1)}, bf16[128,256]{1,0:T(8,128)(2,1)S(1)}, u32[]{:S(2)}, u32[]{:S(2)}) collective-permute-start(bf16[128,256]{1,0:T(8,128)(2,1)S(1)} %get-tuple-element.10), channel_id=1, source_target_pairs={{0,4},{4,8},{8,12},{12,0},{1,5},{5,9},{9,13},{13,1},{2,6},{6,10},{... | collective-permute-start | bytes 196616 | tf_op jit(solution)/shard_map/ppermute | solution.py:70
  12.5 5.0 %collective-permute-start.4 = (bf16[128,256]{1,0:T(8,128)(2,1)S(1)}, bf16[128,256]{1,0:T(8,128)(2,1)S(1)}, u32[]{:S(2)}, u32[]{:S(2)}) collective-permute-start(bf16[128,256]{1,0:T(8,128)(2,1)S(1)} %get-tuple-element.11), channel_id=1, source_target_pairs={{0,12},{4,0},{8,4},{12,8},{1,13},{5,1},{9,5},{13,9},{2,14},{6,2},{... | collective-permute-start | bytes 196616 | tf_op jit(solution)/shard_map/ppermute | solution.py:70
  14.6 5.8 %collective-permute-start.3 = (bf16[128,256]{1,0:T(8,128)(2,1)S(1)}, bf16[128,256]{1,0:T(8,128)(2,1)S(1)}, u32[]{:S(2)}, u32[]{:S(2)}) collective-permute-start(bf16[128,256]{1,0:T(8,128)(2,1)S(1)} %get-tuple-element.12), channel_id=1, source_target_pairs={{0,8},{4,12},{8,0},{12,4},{1,9},{5,13},{9,1},{13,5},{2,10},{6,14},... | collective-permute-start | bytes 196616 | tf_op jit(solution)/shard_map/ppermute | solution.py:70
  23.5 5.6 %collective-permute-start.5 = (bf16[128,256]{1,0:T(8,128)(2,1)}, bf16[128,256]{1,0:T(8,128)(2,1)S(1)}, u32[]{:S(2)}, u32[]{:S(2)}) collective-permute-start(bf16[128,256]{1,0:T(8,128)(2,1)} %gather_fusion), channel_id=1, source_target_pairs={{0,2},{2,4},{4,6},{6,8},{8,10},{10,12},{12,14},{1,3},{3,5},{5,7},{... | collective-permute-start | bytes 196616 | tf_op jit(solution)/shard_map/ppermute | solution.py:13
  26.9 6.4 %collective-permute-start.6 = (bf16[128,256]{1,0:T(8,128)(2,1)}, bf16[128,256]{1,0:T(8,128)(2,1)S(1)}, u32[]{:S(2)}, u32[]{:S(2)}) collective-permute-start(bf16[128,256]{1,0:T(8,128)(2,1)} %gather_fusion.1), channel_id=1, source_target_pairs={{2,0},{4,2},{6,4},{8,6},{10,8},{12,10},{14,12},{3,1},{5,3},{7,5},{... | collective-permute-start | bytes 196616 | tf_op jit(solution)/shard_map/ppermute | solution.py:13
  36.0 4.7 %copy-start.7 = (bf16[4,64,256]{2,1,0:T(8,128)(2,1)S(1)}, bf16[4,64,256]{2,1,0:T(8,128)(2,1)}, u32[]{:S(2)}) copy-start(bf16[4,64,256]{2,1,0:T(8,128)(2,1)} %copy-done.6) | copy-start | bytes 393220
  36.3 4.3 %collective-permute-start.7 = (bf16[128,256]{1,0:T(8,128)(2,1)S(1)}, bf16[128,256]{1,0:T(8,128)(2,1)S(1)}, u32[]{:S(2)}, u32[]{:S(2)}) collective-permute-start(bf16[128,256]{1,0:T(8,128)(2,1)S(1)} %convolution_convert_fusion.2), channel_id=1, source_target_pairs={{0,2},{2,0},{1,3},{3,1},{4,6},{6,4},{5,7},{7,5},{8,10},{10,8},{9,1... | collective-permute-start | bytes 196616 | tf_op jit(solution)/shard_map/ppermute | solution.py:17
  40.9 6.2 %collective-permute-start.8 = (bf16[128,256]{1,0:T(8,128)(2,1)S(1)}, bf16[128,256]{1,0:T(8,128)(2,1)S(1)}, u32[]{:S(2)}, u32[]{:S(2)}) collective-permute-start(bf16[128,256]{1,0:T(8,128)(2,1)S(1)} %get-tuple-element.7), channel_id=1, source_target_pairs={{0,4},{4,8},{8,12},{12,0},{1,5},{5,9},{9,13},{13,1},{2,6},{6,10},{... | collective-permute-start | bytes 196616 | tf_op jit(solution)/shard_map/ppermute | solution.py:70
  41.0 6.2 %collective-permute-start.10 = (bf16[128,256]{1,0:T(8,128)(2,1)S(1)}, bf16[128,256]{1,0:T(8,128)(2,1)S(1)}, u32[]{:S(2)}, u32[]{:S(2)}) collective-permute-start(bf16[128,256]{1,0:T(8,128)(2,1)S(1)} %get-tuple-element.8), channel_id=1, source_target_pairs={{0,12},{4,0},{8,4},{12,8},{1,13},{5,1},{9,5},{13,9},{2,14},{6,2},{... | collective-permute-start | bytes 196616 | tf_op jit(solution)/shard_map/ppermute | solution.py:70
  44.8 5.2 %collective-permute-start.9 = (bf16[128,256]{1,0:T(8,128)(2,1)S(1)}, bf16[128,256]{1,0:T(8,128)(2,1)S(1)}, u32[]{:S(2)}, u32[]{:S(2)}) collective-permute-start(bf16[128,256]{1,0:T(8,128)(2,1)S(1)} %get-tuple-element.9), channel_id=1, source_target_pairs={{0,8},{4,12},{8,0},{12,4},{1,9},{5,13},{9,1},{13,5},{2,10},{6,14},... | collective-permute-start | bytes 196616 | tf_op jit(solution)/shard_map/ppermute | solution.py:70

commit v5 on v4

--- a/solution.py
+++ b/solution.py
@@ -54,7 +54,15 @@
     lower_gain = coupling[0, 0][:, None]
     upper_gain = coupling[0, 1][:, None]
 
-    def coarse_step(local_solve, defect):
+    lower_at = trace_rows[0, 0]
+    upper_at = trace_rows[0, 1]
+    lower_basis = masked_basis[lower_at]
+    upper_basis = masked_basis[upper_at]
+    face_inverse = jnp.concatenate(
+        [inverse[:, :face_rows], inverse[:, iface_rows - face_rows :]], axis=1
+    )
+
+    def coarse_of(defect):
         projected = lax.dot_general(
             masked_basis, defect, (((0,), (0,)), ((), ())), preferred_element_type=jnp.float32
         ).astype(jnp.bfloat16)
@@ -70,28 +78,34 @@
             total = total + lax.ppermute(
                 piece, "sub", [(i, (i + k) % sub_count) for i in range(sub_count)]
             ).astype(jnp.float32)
-        coarse = total.astype(jnp.bfloat16)
-        return local_solve + jnp.dot(masked_basis, coarse, preferred_element_type=jnp.float32)
+        return total.astype(jnp.bfloat16)
 
-    local_solve = jnp.dot(inverse, source, preferred_element_type=jnp.float32)
-    iterate = coarse_step(local_solve, local_solve.astype(jnp.bfloat16))
-    for cycle_index in range(1, ROUNDS):
-        lower_trace = iterate[trace_rows[0, 0]]
-        upper_trace = iterate[trace_rows[0, 1]]
+    base_solve = jnp.dot(inverse, source, preferred_element_type=jnp.float32)
+    local_solve = base_solve
+    defect = local_solve.astype(jnp.bfloat16)
+    earlier = None
+    for cycle_index in range(ROUNDS):
+        coarse = coarse_of(defect)
+        correction = jnp.dot(masked_basis, coarse, preferred_element_type=jnp.float32)
+        iterate = local_solve + correction
+        if cycle_index == ROUNDS - 1:
+            break
+        lower_trace = local_solve[lower_at] + jnp.dot(
+            lower_basis, coarse, preferred_element_type=jnp.float32
+        )
+        upper_trace = local_solve[upper_at] + jnp.dot(
+            upper_basis, coarse, preferred_element_type=jnp.float32
+        )
         from_lower = passed_along(upper_trace.astype(jnp.bfloat16), 1).astype(jnp.float32)
         from_upper = passed_along(lower_trace.astype(jnp.bfloat16), -1).astype(jnp.float32)
-        lower_rows = source[:face_rows].astype(jnp.float32) + lower_gain * from_lower
-        upper_rows = source[iface_rows - face_rows :].astype(jnp.float32) + upper_gain * from_upper
-        boundary = jnp.concatenate(
-            [
-                lower_rows.astype(jnp.bfloat16),
-                source[face_rows : iface_rows - face_rows],
-                upper_rows.astype(jnp.bfloat16),
-            ],
-            axis=0,
-        )
-        local_solve = jnp.dot(inverse, boundary, preferred_element_type=jnp.float32)
-        iterate = coarse_step(local_solve, (local_solve - iterate).astype(jnp.bfloat16))
+        faces = jnp.concatenate(
+            [lower_gain * from_lower, upper_gain * from_upper], axis=0
+        ).astype(jnp.bfloat16)
+        change = jnp.dot(face_inverse, faces, preferred_element_type=jnp.float32)
+        local_solve = base_solve + change
+        step = change if earlier is None else change - earlier
+        defect = (step - correction).astype(jnp.bfloat16)
+        earlier = change
     return iterate.astype(jnp.bfloat16)[None]
 
 

time: 51.3 us -> 48 us (0.936)
  waiting for transfers between devices: 19.9 us -> 17 us
  starting transfers between devices: 18.2 us -> 17.6 us
    ppermute x6, waiting for transfers between devices: 10 us -> 7.33 us  [coarse_of(): lax.ppermute(piece, 'sub', [(i, (i + k) % sub_count) for i in range(sub_c...]
    select_n x1 -> x2, other arithmetic: 0.01 us -> 0.98 us  [the longest x1 0.97 us: local(): jnp.where(slot_ids[None, :] < deflation_counts[0], deflation_basis[0], jn...]
    convert_element_type x1, other arithmetic: 0.97 us -> 0.04 us  [coarse_of(): return total.astype(jnp.bfloat16)]
    unnamed x20 -> x12, local copies, waits for them, and re-layouts: 1.34 us -> 0.65 us
    dot_general x8 -> x9, matrix products: 5.94 us -> 6.23 us  [the longest x1 2.31 us: local(): base_solve = jnp.dot(inverse, source, preferred_element_type=jnp.float32)]
    gather x2 -> x4, local copies, waits for them, and re-layouts: 2.77 us -> 2.93 us  [the longest x1 0.75 us: local(): local_solve[upper_at]]
  transfers between devices with their start and end apart: 11 -> 11, of which waited for: 8 -> 7; matrix products, arithmetic and copies ran while one was open for 6% -> 16% of each run, Pallas kernels for 0% -> 0%
where the time goes in v5:
time: 48 us; the launch traced here: 47.8 us
  starting transfers between devices  17.6 us (37%)
  waiting for transfers between devices  17 us (35%)
  matrix products  6.23 us (13%)
  local copies, waits for them, and re-layouts  4.7 us (10%)
  other arithmetic  1.25 us (3%)
  between operations  0.96 us (2%)
    ppermute x6, starting transfers between devices, coarse_of(): lax.ppermute(piece, 'sub', [(i, (i + k) % sub_count) for i in range(sub_c...  8.78 us
    ppermute x6, waiting for transfers between devices, coarse_of(): lax.ppermute(piece, 'sub', [(i, (i + k) % sub_count) for i in range(sub_c...  7.33 us
    ppermute x3, waiting for transfers between devices, swapped(): return lax.ppermute(shard, axis, [(0, 1), (1, 0)])  4.91 us
    ppermute x2, starting transfers between devices, passed_along(): return lax.ppermute(shard, DUCT, pairs)  4.82 us
    ppermute x2, waiting for transfers between devices, passed_along(): return lax.ppermute(shard, DUCT, pairs)  4.77 us
    ppermute x3, starting transfers between devices, swapped(): return lax.ppermute(shard, axis, [(0, 1), (1, 0)])  4.04 us
    dot_general x1, matrix products, local(): base_solve = jnp.dot(inverse, source, preferred_element_type=jnp.float32)  2.31 us
    dot_general x2, matrix products, coarse_of(): jnp.einsum('jsc,cm->jsm', columns, inputs, preferred_element_type=jnp.flo...  1.42 us
  transfers between devices with their start and end apart: 11, of which 7 were waited for; matrix products, arithmetic and copies ran while one was open for 16% of the time, Pallas kernels for 0%

profile of v5, /device:TPU:0, one launch (start us, length us, event | category | flops | bytes accessed | tf_op | source)
XLA Modules:
  0.0 47.8 jit_solution(7384480254159493578)
XLA Ops:
  1.1 1.0 %bitcast_select_fusion = bf16[1024,128]{1,0:T(8,128)(2,1)S(1)} fusion(bf16[1,1024,128]{2,1,0:T(8,128)(2,1)} %param.11, pred[128]{0:T(512)(128)(4,1)S(1)} %iota_compare_fusion), kind=kLoop, calls=%fused_computation.26 | loop fusion | flops 131072 | bytes 524416 | tf_op jit(solution)/shard_map/jit(_where)/select_n | solution.py:47
  2.1 2.3 %fusion.11 = f32[1024,256]{1,0:T(8,128)S(1)} fusion(bf16[1,1024,256]{2,1,0:T(8,128)(2,1)S(1)} %copy-done, bf16[1,1024,1024]{2,1,0:T(8,128)(2,1)} %param.8), kind=kOutput, calls=%fused_computation.22 | convolution fusion | flops 536870912 | bytes 3670016 | tf_op jit(solution)/shard_map/dot_general | solution.py:83
  4.7 2.6 %collective-permute-start.1 = (bf16[128,256]{1,0:T(8,128)(2,1)S(1)}, bf16[128,256]{1,0:T(8,128)(2,1)S(1)}, u32[]{:S(2)}, u32[]{:S(2)}) collective-permute-start(bf16[128,256]{1,0:T(8,128)(2,1)S(1)} %convolution_convert_fusion.2), channel_id=1, source_target_pairs={{0,2},{2,0},{1,3},{3,1},{4,6},{6,4},{5,7},{7,5},{8,10},{10,8},{9,1... | collective-permute-start | bytes 196616 | tf_op jit(solution)/shard_map/ppermute | solution.py:17
  7.4 1.1 %fusion.37 = (bf16[1024,128]{1,0:T(8,128)(2,1)S(1)}, bf16[1024,128]{1,0:T(8,128)(2,1)S(1)}) fusion(bf16[1024,1024]{1,0:T(8,128)(2,1)} %bitcast.64), kind=kLoop, calls=%fused_computation.74 | loop fusion | bytes 1048576 | tf_op jit(solution)/shard_map/slice | solution.py:62
  8.5 1.5 %collective-permute-done.1 = bf16[128,256]{1,0:T(8,128)(2,1)S(1)} collective-permute-done((bf16[128,256]{1,0:T(8,128)(2,1)S(1)}, bf16[128,256]{1,0:T(8,128)(2,1)S(1)}, u32[]{:S(2)}, u32[]{:S(2)}) %collective-permute-start.1) | collective-permute-done | bytes 65568 | tf_op jit(solution)/shard_map/ppermute | solution.py:17
  10.1 0.6 %copy-done.2 = bf16[4,64,256]{2,1,0:T(8,128)(2,1)} copy-done((bf16[4,64,256]{2,1,0:T(8,128)(2,1)}, bf16[4,64,256]{2,1,0:T(8,128)(2,1)S(1)}, u32[]{:S(2)}) %copy-start.2) | copy-done | bytes 131096
  11.0 1.9 %collective-permute-start.2 = (bf16[128,256]{1,0:T(8,128)(2,1)S(1)}, bf16[128,256]{1,0:T(8,128)(2,1)S(1)}, u32[]{:S(2)}, u32[]{:S(2)}) collective-permute-start(bf16[128,256]{1,0:T(8,128)(2,1)S(1)} %get-tuple-element.10), channel_id=1, source_target_pairs={{0,4},{4,8},{8,12},{12,0},{1,5},{5,9},{9,13},{13,1},{2,6},{6,10},{... | collective-permute-start | bytes 196616 | tf_op jit(solution)/shard_map/ppermute | solution.py:78
  12.9 2.1 %collective-permute-start.4 = (bf16[128,256]{1,0:T(8,128)(2,1)S(1)}, bf16[128,256]{1,0:T(8,128)(2,1)S(1)}, u32[]{:S(2)}, u32[]{:S(2)}) collective-permute-start(bf16[128,256]{1,0:T(8,128)(2,1)S(1)} %get-tuple-element.11), channel_id=1, source_target_pairs={{0,12},{4,0},{8,4},{12,8},{1,13},{5,1},{9,5},{13,9},{2,14},{6,2},{... | collective-permute-start | bytes 196616 | tf_op jit(solution)/shard_map/ppermute | solution.py:78
  15.0 0.9 %collective-permute-start.3 = (bf16[128,256]{1,0:T(8,128)(2,1)S(1)}, bf16[128,256]{1,0:T(8,128)(2,1)S(1)}, u32[]{:S(2)}, u32[]{:S(2)}) collective-permute-start(bf16[128,256]{1,0:T(8,128)(2,1)S(1)} %get-tuple-element.12), channel_id=1, source_target_pairs={{0,8},{4,12},{8,0},{12,4},{1,9},{5,13},{9,1},{13,5},{2,10},{6,14},... | collective-permute-start | bytes 196616 | tf_op jit(solution)/shard_map/ppermute | solution.py:78
  16.0 0.7 %gather_fusion.3 = bf16[128,128]{1,0:T(8,128)(2,1)S(1)} fusion(bf16[1024,128]{1,0:T(8,128)(2,1)S(1)} %bitcast_select_fusion, s32[1024]{0:T(1024)S(1)} %get-tuple-element.23), kind=kCustom, calls=%fused_computation.3 | custom fusion | bytes 66048 | tf_op jit(solution)/shard_map/gather | solution.py:59
  16.7 0.8 %gather_fusion.2 = f32[128,256]{1,0:T(8,128)S(1)} fusion(f32[1024,256]{1,0:T(8,128)S(1)} %fusion.11, s32[1024]{0:T(1024)S(1)} %get-tuple-element.23), kind=kCustom, calls=%fused_computation.2 | custom fusion | bytes 262656 | tf_op jit(solution)/shard_map/gather | solution.py:93
  17.4 0.7 %gather_fusion.1 = bf16[128,128]{1,0:T(8,128)(2,1)S(1)} fusion(bf16[1024,128]{1,0:T(8,128)(2,1)S(1)} %bitcast_select_fusion, s32[1024]{0:T(1024)S(1)} %get-tuple-element.24), kind=kCustom, calls=%fused_computation.1 | custom fusion | bytes 66048 | tf_op jit(solution)/shard_map/gather | solution.py:60
  18.1 0.8 %gather_fusion = f32[128,256]{1,0:T(8,128)S(1)} fusion(f32[1024,256]{1,0:T(8,128)S(1)} %fusion.11, s32[1024]{0:T(1024)S(1)} %get-tuple-element.24), kind=kCustom, calls=%fused_computation | custom fusion | bytes 262656 | tf_op jit(solution)/shard_map/gather | solution.py:96
  18.9 2.2 %collective-permute-done.3 = bf16[128,256]{1,0:T(8,128)(2,1)S(1)} collective-permute-done((bf16[128,256]{1,0:T(8,128)(2,1)S(1)}, bf16[128,256]{1,0:T(8,128)(2,1)S(1)}, u32[]{:S(2)}, u32[]{:S(2)}) %collective-permute-start.3) | collective-permute-done | bytes 65568 | tf_op jit(solution)/shard_map/ppermute | solution.py:78
  21.3 3.5 %collective-permute-start.5 = (bf16[128,256]{1,0:T(8,128)(2,1)S(1)}, bf16[128,256]{1,0:T(8,128)(2,1)S(1)}, u32[]{:S(2)}, u32[]{:S(2)}) collective-permute-start(bf16[128,256]{1,0:T(8,128)(2,1)S(1)} %fusion.5), channel_id=1, source_target_pairs={{0,2},{2,4},{4,6},{6,8},{8,10},{10,12},{12,14},{1,3},{3,5},{5,7},{... | collective-permute-start | bytes 196616 | tf_op jit(solution)/shard_map/ppermute | solution.py:13
  25.0 1.3 %collective-permute-start.6 = (bf16[128,256]{1,0:T(8,128)(2,1)S(1)}, bf16[128,256]{1,0:T(8,128)(2,1)S(1)}, u32[]{:S(2)}, u32[]{:S(2)}) collective-permute-start(bf16[128,256]{1,0:T(8,128)(2,1)S(1)} %fusion.6), channel_id=1, source_target_pairs={{2,0},{4,2},{6,4},{8,6},{10,8},{12,10},{14,12},{3,1},{5,3},{7,5},{... | collective-permute-start | bytes 196616 | tf_op jit(solution)/shard_map/ppermute | solution.py:13
  26.8 4.3 %collective-permute-done.6 = bf16[128,256]{1,0:T(8,128)(2,1)S(1)} collective-permute-done((bf16[128,256]{1,0:T(8,128)(2,1)S(1)}, bf16[128,256]{1,0:T(8,128)(2,1)S(1)}, u32[]{:S(2)}, u32[]{:S(2)}) %collective-permute-start.6) | collective-permute-done | bytes 65568 | tf_op jit(solution)/shard_map/ppermute | solution.py:13
  32.0 1.0 %collective-permute-start.7 = (bf16[128,256]{1,0:T(8,128)(2,1)S(1)}, bf16[128,256]{1,0:T(8,128)(2,1)S(1)}, u32[]{:S(2)}, u32[]{:S(2)}) collective-permute-start(bf16[128,256]{1,0:T(8,128)(2,1)S(1)} %fusion.4), channel_id=1, source_target_pairs={{0,2},{2,0},{1,3},{3,1},{4,6},{6,4},{5,7},{7,5},{8,10},{10,8},{9,1... | collective-permute-start | bytes 196616 | tf_op jit(solution)/shard_map/ppermute | solution.py:17
  33.0 3.4 %collective-permute-done.7 = bf16[128,256]{1,0:T(8,128)(2,1)S(1)} collective-permute-done((bf16[128,256]{1,0:T(8,128)(2,1)S(1)}, bf16[128,256]{1,0:T(8,128)(2,1)S(1)}, u32[]{:S(2)}, u32[]{:S(2)}) %collective-permute-start.7) | collective-permute-done | bytes 65568 | tf_op jit(solution)/shard_map/ppermute | solution.py:17
  36.4 1.2 %convolution_convert_fusion = bf16[4,128,256]{2,1,0:T(8,128)(2,1)S(1)} fusion(bf16[4,64,256]{2,1,0:T(8,128)(2,1)} %copy-done.3, bf16[4,64,256]{2,1,0:T(8,128)(2,1)} %copy-done.2, bf16[128,256]{1,0:T(8,128)(2,1)S(1)} %get-tuple-element.16, bf16[128,256]{1,0:T(8,128)(2,1)S(1)} %get-tuple-element.15), kind=kOutput, calls=%fused_computation.10 | convolution fusion | flops 68026368 | bytes 655360 | tf_op jit(solution)/shard_map/jsc,cm->jsm/dot_general | solution.py:70
  37.7 3.8 %collective-permute-start.10 = (bf16[128,256]{1,0:T(8,128)(2,1)S(1)}, bf16[128,256]{1,0:T(8,128)(2,1)S(1)}, u32[]{:S(2)}, u32[]{:S(2)}) collective-permute-start(bf16[128,256]{1,0:T(8,128)(2,1)S(1)} %get-tuple-element.8), channel_id=1, source_target_pairs={{0,12},{4,0},{8,4},{12,8},{1,13},{5,1},{9,5},{13,9},{2,14},{6,2},{... | collective-permute-start | bytes 196616 | tf_op jit(solution)/shard_map/ppermute | solution.py:78
  41.5 2.3 %collective-permute-done.8 = bf16[128,256]{1,0:T(8,128)(2,1)S(1)} collective-permute-done((bf16[128,256]{1,0:T(8,128)(2,1)S(1)}, bf16[128,256]{1,0:T(8,128)(2,1)S(1)}, u32[]{:S(2)}, u32[]{:S(2)}) %collective-permute-start.8) | collective-permute-done | bytes 65568 | tf_op jit(solution)/shard_map/ppermute | solution.py:78
  43.9 2.8 %collective-permute-done.9 = bf16[128,256]{1,0:T(8,128)(2,1)S(1)} collective-permute-done((bf16[128,256]{1,0:T(8,128)(2,1)S(1)}, bf16[128,256]{1,0:T(8,128)(2,1)S(1)}, u32[]{:S(2)}, u32[]{:S(2)}) %collective-permute-start.9) | collective-permute-done | bytes 65568 | tf_op jit(solution)/shard_map/ppermute | solution.py:78
  46.7 1.1 %fusion.2 = bf16[1,1024,256]{2,1,0:T(8,128)(2,1)} fusion(bf16[1024,128]{1,0:T(8,128)(2,1)S(1)} %bitcast_select_fusion, f32[1024,256]{1,0:T(8,128)S(1)} %fusion.11, f32[1024,256]{1,0:T(8,128)S(1)} %fusion.7, bf16[128,256]{1,0:T(8,128)(2,1)S(1)} %collective-permute-done.10, bf16[128,256]{1,0:T(8,128)(2,1)S(1)} %collective-permute-done.9, ...), kind=kOutput, calls=%fused_computation.8 | convolution fusion | flops 68157440 | bytes 3145732 | tf_op jit(solution)/shard_map/dot_general | solution.py:89
  (37 shorter events, 2.9 us)
Async XLA Ops:
  0.0 2.1 %copy-start = (bf16[1,1024,256]{2,1,0:T(8,128)(2,1)S(1)}, bf16[1,1024,256]{2,1,0:T(8,128)(2,1)}, u32[]{:S(2)}) copy-start(bf16[1,1024,256]{2,1,0:T(8,128)(2,1)} %param.7) | copy-start | bytes 1572868
  0.0 10.1 %collective-permute-start = (bf16[4,64,256]{2,1,0:T(8,128)(2,1)}, bf16[4,64,256]{2,1,0:T(8,128)(2,1)S(1)}, u32[]{:S(2)}, u32[]{:S(2)}) collective-permute-start(bf16[4,64,256]{2,1,0:T(8,128)(2,1)} %bitcast.63), channel_id=1, source_target_pairs={{0,1},{1,0},{2,3},{3,2},{4,5},{5,4},{6,7},{7,6},{8,9},{9,8},{10,11... | collective-permute-start | bytes 393224 | tf_op jit(solution)/shard_map/ppermute | solution.py:17
  2.1 5.2 %copy-start.4 = (f32[1,2,128]{2,1,0:T(2,128)S(1)}, f32[1,2,128]{2,1,0:T(2,128)}, u32[]{:S(2)}) copy-start(f32[1,2,128]{2,1,0:T(2,128)} %param.9) | copy-start | bytes 3076
  4.4 4.0 %copy-start.5 = (s32[1,2,128]{2,1,0:T(2,128)S(1)}, s32[1,2,128]{2,1,0:T(2,128)}, u32[]{:S(2)}) copy-start(s32[1,2,128]{2,1,0:T(2,128)} %param.10) | copy-start | bytes 3076
  4.5 5.6 %copy-start.1 = (bf16[4,1,64,1,256]{4,2,3,1,0:T(8,128)(2,1)S(1)}, bf16[4,1,64,1,256]{4,2,3,1,0:T(8,128)(2,1)}, u32[]{:S(2)}) copy-start(bf16[4,1,64,1,256]{4,2,3,1,0:T(8,128)(2,1)} %param.13) | copy-start | bytes 393220
  4.7 5.3 %collective-permute-start.1 = (bf16[128,256]{1,0:T(8,128)(2,1)S(1)}, bf16[128,256]{1,0:T(8,128)(2,1)S(1)}, u32[]{:S(2)}, u32[]{:S(2)}) collective-permute-start(bf16[128,256]{1,0:T(8,128)(2,1)S(1)} %convolution_convert_fusion.2), channel_id=1, source_target_pairs={{0,2},{2,0},{1,3},{3,1},{4,6},{6,4},{5,7},{7,5},{8,10},{10,8},{9,1... | collective-permute-start | bytes 196616 | tf_op jit(solution)/shard_map/ppermute | solution.py:17
  10.1 0.6 %copy-start.2 = (bf16[4,64,256]{2,1,0:T(8,128)(2,1)}, bf16[4,64,256]{2,1,0:T(8,128)(2,1)S(1)}, u32[]{:S(2)}) copy-start(bf16[4,64,256]{2,1,0:T(8,128)(2,1)S(1)} %get-tuple-element.13) | copy-start | bytes 393220
  10.1 0.9 %copy-start.3 = (bf16[4,64,256]{2,1,0:T(8,128)(2,1)}, bf16[4,64,256]{2,1,0:T(8,128)(2,1)S(1)}, u32[]{:S(2)}) copy-start(bf16[4,64,256]{2,1,0:T(8,128)(2,1)S(1)} %get-tuple-element.14) | copy-start | bytes 393220
  11.0 7.9 %collective-permute-start.2 = (bf16[128,256]{1,0:T(8,128)(2,1)S(1)}, bf16[128,256]{1,0:T(8,128)(2,1)S(1)}, u32[]{:S(2)}, u32[]{:S(2)}) collective-permute-start(bf16[128,256]{1,0:T(8,128)(2,1)S(1)} %get-tuple-element.10), channel_id=1, source_target_pairs={{0,4},{4,8},{8,12},{12,0},{1,5},{5,9},{9,13},{13,1},{2,6},{6,10},{... | collective-permute-start | bytes 196616 | tf_op jit(solution)/shard_map/ppermute | solution.py:78
  12.9 6.0 %collective-permute-start.4 = (bf16[128,256]{1,0:T(8,128)(2,1)S(1)}, bf16[128,256]{1,0:T(8,128)(2,1)S(1)}, u32[]{:S(2)}, u32[]{:S(2)}) collective-permute-start(bf16[128,256]{1,0:T(8,128)(2,1)S(1)} %get-tuple-element.11), channel_id=1, source_target_pairs={{0,12},{4,0},{8,4},{12,8},{1,13},{5,1},{9,5},{13,9},{2,14},{6,2},{... | collective-permute-start | bytes 196616 | tf_op jit(solution)/shard_map/ppermute | solution.py:78
  15.0 6.1 %collective-permute-start.3 = (bf16[128,256]{1,0:T(8,128)(2,1)S(1)}, bf16[128,256]{1,0:T(8,128)(2,1)S(1)}, u32[]{:S(2)}, u32[]{:S(2)}) collective-permute-start(bf16[128,256]{1,0:T(8,128)(2,1)S(1)} %get-tuple-element.12), channel_id=1, source_target_pairs={{0,8},{4,12},{8,0},{12,4},{1,9},{5,13},{9,1},{13,5},{2,10},{6,14},... | collective-permute-start | bytes 196616 | tf_op jit(solution)/shard_map/ppermute | solution.py:78
  21.3 5.4 %collective-permute-start.5 = (bf16[128,256]{1,0:T(8,128)(2,1)S(1)}, bf16[128,256]{1,0:T(8,128)(2,1)S(1)}, u32[]{:S(2)}, u32[]{:S(2)}) collective-permute-start(bf16[128,256]{1,0:T(8,128)(2,1)S(1)} %fusion.5), channel_id=1, source_target_pairs={{0,2},{2,4},{4,6},{6,8},{8,10},{10,12},{12,14},{1,3},{3,5},{5,7},{... | collective-permute-start | bytes 196616 | tf_op jit(solution)/shard_map/ppermute | solution.py:13
  25.0 6.2 %collective-permute-start.6 = (bf16[128,256]{1,0:T(8,128)(2,1)S(1)}, bf16[128,256]{1,0:T(8,128)(2,1)S(1)}, u32[]{:S(2)}, u32[]{:S(2)}) collective-permute-start(bf16[128,256]{1,0:T(8,128)(2,1)S(1)} %fusion.6), channel_id=1, source_target_pairs={{2,0},{4,2},{6,4},{8,6},{10,8},{12,10},{14,12},{3,1},{5,3},{7,5},{... | collective-permute-start | bytes 196616 | tf_op jit(solution)/shard_map/ppermute | solution.py:13
  32.0 4.3 %collective-permute-start.7 = (bf16[128,256]{1,0:T(8,128)(2,1)S(1)}, bf16[128,256]{1,0:T(8,128)(2,1)S(1)}, u32[]{:S(2)}, u32[]{:S(2)}) collective-permute-start(bf16[128,256]{1,0:T(8,128)(2,1)S(1)} %fusion.4), channel_id=1, source_target_pairs={{0,2},{2,0},{1,3},{3,1},{4,6},{6,4},{5,7},{7,5},{8,10},{10,8},{9,1... | collective-permute-start | bytes 196616 | tf_op jit(solution)/shard_map/ppermute | solution.py:17
  37.6 6.2 %collective-permute-start.8 = (bf16[128,256]{1,0:T(8,128)(2,1)S(1)}, bf16[128,256]{1,0:T(8,128)(2,1)S(1)}, u32[]{:S(2)}, u32[]{:S(2)}) collective-permute-start(bf16[128,256]{1,0:T(8,128)(2,1)S(1)} %get-tuple-element.7), channel_id=1, source_target_pairs={{0,4},{4,8},{8,12},{12,0},{1,5},{5,9},{9,13},{13,1},{2,6},{6,10},{... | collective-permute-start | bytes 196616 | tf_op jit(solution)/shard_map/ppermute | solution.py:78
  37.7 6.2 %collective-permute-start.10 = (bf16[128,256]{1,0:T(8,128)(2,1)S(1)}, bf16[128,256]{1,0:T(8,128)(2,1)S(1)}, u32[]{:S(2)}, u32[]{:S(2)}) collective-permute-start(bf16[128,256]{1,0:T(8,128)(2,1)S(1)} %get-tuple-element.8), channel_id=1, source_target_pairs={{0,12},{4,0},{8,4},{12,8},{1,13},{5,1},{9,5},{13,9},{2,14},{6,2},{... | collective-permute-start | bytes 196616 | tf_op jit(solution)/shard_map/ppermute | solution.py:78
  41.5 5.2 %collective-permute-start.9 = (bf16[128,256]{1,0:T(8,128)(2,1)S(1)}, bf16[128,256]{1,0:T(8,128)(2,1)S(1)}, u32[]{:S(2)}, u32[]{:S(2)}) collective-permute-start(bf16[128,256]{1,0:T(8,128)(2,1)S(1)} %get-tuple-element.9), channel_id=1, source_target_pairs={{0,8},{4,12},{8,0},{12,4},{1,9},{5,13},{9,1},{13,5},{2,10},{6,14},... | collective-permute-start | bytes 196616 | tf_op jit(solution)/shard_map/ppermute | solution.py:78

commit v6 on v5

--- a/solution.py
+++ b/solution.py
@@ -62,11 +62,12 @@
         [inverse[:, :face_rows], inverse[:, iface_rows - face_rows :]], axis=1
     )
 
-    def coarse_of(defect):
-        projected = lax.dot_general(
+    def coarse_input(defect):
+        return lax.dot_general(
             masked_basis, defect, (((0,), (0,)), ((), ())), preferred_element_type=jnp.float32
         ).astype(jnp.bfloat16)
-        inputs = gathered(projected, "tile", 0)
+
+    def coarse_of(inputs):
         partial = jnp.einsum(
             "jsc,cm->jsm", columns, inputs, preferred_element_type=jnp.float32
         ).astype(jnp.bfloat16)
@@ -80,31 +81,78 @@
             ).astype(jnp.float32)
         return total.astype(jnp.bfloat16)
 
+    pairwise = lax.axis_size("tile") == 2 and ROUNDS == 2
+    tile_index = lax.axis_index("tile")
+    gains = coupling[0]
+    if pairwise:
+        sends = jnp.dot(masked_basis.T, face_inverse, preferred_element_type=jnp.float32)
+        keeps = jnp.dot(masked_basis.T, masked_basis, preferred_element_type=jnp.float32)
+        mine = jnp.concatenate([sends, keeps], axis=1).astype(jnp.bfloat16)
+        theirs = swapped(mine, "tile")
+        partner_gains = swapped(gains, "tile")
+        duct_pairs = []
+        peers = lax.axis_size(DUCT)
+        for i in range(peers):
+            target = i - 2 if i % 2 == 0 else i + 2
+            if 0 <= target < peers:
+                duct_pairs.append((i, target))
+
+    def projection_of(mix, faces, coarse):
+        return (
+            jnp.dot(mix[:, : faces.shape[0]], faces, preferred_element_type=jnp.float32)
+            - jnp.dot(mix[:, faces.shape[0] :], coarse, preferred_element_type=jnp.float32)
+        ).astype(jnp.bfloat16)
+
+    def face_rows_of(gain, lower, upper):
+        return jnp.concatenate(
+            [gain[0][:, None] * lower, gain[1][:, None] * upper], axis=0
+        ).astype(jnp.bfloat16)
+
     base_solve = jnp.dot(inverse, source, preferred_element_type=jnp.float32)
     local_solve = base_solve
-    defect = local_solve.astype(jnp.bfloat16)
+    inputs = gathered(coarse_input(local_solve.astype(jnp.bfloat16)), "tile", 0)
     earlier = None
     for cycle_index in range(ROUNDS):
-        coarse = coarse_of(defect)
+        coarse = coarse_of(inputs)
         correction = jnp.dot(masked_basis, coarse, preferred_element_type=jnp.float32)
         iterate = local_solve + correction
         if cycle_index == ROUNDS - 1:
             break
-        lower_trace = local_solve[lower_at] + jnp.dot(
-            lower_basis, coarse, preferred_element_type=jnp.float32
-        )
-        upper_trace = local_solve[upper_at] + jnp.dot(
-            upper_basis, coarse, preferred_element_type=jnp.float32
-        )
-        from_lower = passed_along(upper_trace.astype(jnp.bfloat16), 1).astype(jnp.float32)
-        from_upper = passed_along(lower_trace.astype(jnp.bfloat16), -1).astype(jnp.float32)
-        faces = jnp.concatenate(
-            [lower_gain * from_lower, upper_gain * from_upper], axis=0
+        lower_trace = (
+            local_solve[lower_at] + jnp.dot(lower_basis, coarse, preferred_element_type=jnp.float32)
         ).astype(jnp.bfloat16)
+        upper_trace = (
+            local_solve[upper_at] + jnp.dot(upper_basis, coarse, preferred_element_type=jnp.float32)
+        ).astype(jnp.bfloat16)
+        rows = lower_trace.shape[0]
+        if pairwise:
+            got_lower = passed_along(jnp.concatenate([upper_trace, coarse], axis=0), 1)
+            got_upper = passed_along(jnp.concatenate([lower_trace, coarse], axis=0), -1)
+            crossing = lax.ppermute(
+                jnp.where(tile_index == 0, lower_trace, upper_trace), DUCT, duct_pairs
+            )
+            from_lower = got_lower[:rows].astype(jnp.float32)
+            from_upper = got_upper[:rows].astype(jnp.float32)
+            faces = face_rows_of(gains, from_lower, from_upper)
+            first = tile_index == 0
+            partner_lower = jnp.where(first, upper_trace, crossing).astype(jnp.float32)
+            partner_upper = jnp.where(first, crossing, lower_trace).astype(jnp.float32)
+            partner_coarse = jnp.where(first, got_upper[rows:], got_lower[rows:])
+            partner_faces = face_rows_of(partner_gains, partner_lower, partner_upper)
+            own = projection_of(mine, faces, coarse)
+            other = projection_of(theirs, partner_faces, partner_coarse)
+            inputs = jnp.concatenate(
+                [jnp.where(first, own, other), jnp.where(first, other, own)], axis=0
+            )
+        else:
+            from_lower = passed_along(upper_trace, 1).astype(jnp.float32)
+            from_upper = passed_along(lower_trace, -1).astype(jnp.float32)
+            faces = face_rows_of(gains, from_lower, from_upper)
         change = jnp.dot(face_inverse, faces, preferred_element_type=jnp.float32)
         local_solve = base_solve + change
-        step = change if earlier is None else change - earlier
-        defect = (step - correction).astype(jnp.bfloat16)
+        if not pairwise:
+            step = change if earlier is None else change - earlier
+            inputs = gathered(coarse_input((step - correction).astype(jnp.bfloat16)), "tile", 0)
         earlier = change
     return iterate.astype(jnp.bfloat16)[None]
 

time: 48 us -> 47.8 us (level)
  starting transfers between devices: 17.6 us -> 24 us
  waiting for transfers between devices: 17 us -> 12.1 us
  other arithmetic: 1.25 us -> 0.42 us
  local copies, waits for them, and re-layouts: 4.7 us -> 4.09 us
    ppermute x3 -> x4, waiting for transfers between devices: 4.91 us -> 0.01 us  [swapped(): return lax.ppermute(shard, axis, [(0, 1), (1, 0)])]
    ppermute x6, starting transfers between devices: 8.78 us -> 11.4 us  [coarse_of(): lax.ppermute(piece, 'sub', [(i, (i + k) % sub_count) for i in range(sub_c...]
    ppermute x2, waiting for transfers between devices: 4.77 us -> 3.18 us  [passed_along(): return lax.ppermute(shard, DUCT, pairs)]
    ppermute x6, waiting for transfers between devices: 7.33 us -> 8.9 us  [coarse_of(): lax.ppermute(piece, 'sub', [(i, (i + k) % sub_count) for i in range(sub_c...]
    ppermute x3 -> x4, starting transfers between devices: 4.04 us -> 5.47 us  [swapped(): return lax.ppermute(shard, axis, [(0, 1), (1, 0)])]
    ppermute x0 -> x1, starting transfers between devices: none -> 1.29 us  [local(): lax.ppermute(jnp.where(tile_index == 0, lower_trace, upper_trace), DUCT,...]
    ppermute x2, starting transfers between devices: 4.82 us -> 5.85 us  [passed_along(): return lax.ppermute(shard, DUCT, pairs)]
    dot_general x2, matrix products: 1.42 us -> 0.44 us  [coarse_of(): jnp.einsum('jsc,cm->jsm', columns, inputs, preferred_element_type=jnp.flo...]
  transfers between devices with their start and end apart: 11 -> 13, of which waited for: 7 -> 7; matrix products, arithmetic and copies ran while one was open for 16% -> 18% of each run, Pallas kernels for 0% -> 0%
where the time goes in v6:
time: 47.8 us; the launch traced here: 47.5 us
  starting transfers between devices  24 us (50%)
  waiting for transfers between devices  12.1 us (25%)
  matrix products  5.89 us (12%)
  local copies, waits for them, and re-layouts  4.09 us (9%)
  between operations  1 us (2%)
    ppermute x6, starting transfers between devices, coarse_of(): lax.ppermute(piece, 'sub', [(i, (i + k) % sub_count) for i in range(sub_c...  11.4 us
    ppermute x6, waiting for transfers between devices, coarse_of(): lax.ppermute(piece, 'sub', [(i, (i + k) % sub_count) for i in range(sub_c...  8.9 us
    ppermute x2, starting transfers between devices, passed_along(): return lax.ppermute(shard, DUCT, pairs)  5.85 us
    ppermute x4, starting transfers between devices, swapped(): return lax.ppermute(shard, axis, [(0, 1), (1, 0)])  5.47 us
    ppermute x2, waiting for transfers between devices, passed_along(): return lax.ppermute(shard, DUCT, pairs)  3.18 us
    dot_general x1, matrix products, local(): base_solve = jnp.dot(inverse, source, preferred_element_type=jnp.float32)  2.34 us
    ppermute x1, starting transfers between devices, local(): lax.ppermute(jnp.where(tile_index == 0, lower_trace, upper_trace), DUCT,...  1.29 us
    dot_general x1, matrix products, local(): jnp.dot(masked_basis, coarse, preferred_element_type=jnp.float32)  1.09 us
  transfers between devices with their start and end apart: 13, of which 7 were waited for; matrix products, arithmetic and copies ran while one was open for 18% of the time, Pallas kernels for 0%

profile of v6, /device:TPU:0, one launch (start us, length us, event | category | flops | bytes accessed | tf_op | source)
XLA Modules:
  0.0 47.5 jit_solution(2217217959957680973)
XLA Ops:
  0.0 0.5 collective-permute-start
  1.1 2.3 %fusion.6 = f32[1024,256]{1,0:T(8,128)S(1)} fusion(bf16[1,1024,256]{2,1,0:T(8,128)(2,1)S(1)} %copy-done, bf16[1,1024,1024]{2,1,0:T(8,128)(2,1)} %param.8), kind=kOutput, calls=%fused_computation.22 | convolution fusion | flops 536870912 | bytes 3670016 | tf_op jit(solution)/shard_map/dot_general | solution.py:111
  3.8 2.9 %collective-permute-start.1 = (bf16[128,256]{1,0:T(8,128)(2,1)S(1)}, bf16[128,256]{1,0:T(8,128)(2,1)S(1)}, u32[]{:S(2)}, u32[]{:S(2)}) collective-permute-start(bf16[128,256]{1,0:T(8,128)(2,1)S(1)} %convolution_convert_fusion.3), channel_id=1, source_target_pairs={{0,2},{2,0},{1,3},{3,1},{4,6},{6,4},{5,7},{7,5},{8,10},{10,8},{9,1... | collective-permute-start | bytes 196616 | tf_op jit(solution)/shard_map/ppermute | solution.py:17
  7.0 1.1 %fusion.46 = (bf16[1024,128]{1,0:T(8,128)(2,1)S(1)}, bf16[1024,128]{1,0:T(8,128)(2,1)S(1)}) fusion(bf16[1024,1024]{1,0:T(8,128)(2,1)} %bitcast.73), kind=kLoop, calls=%fused_computation.98 | loop fusion | bytes 1048576 | tf_op jit(solution)/shard_map/slice | solution.py:62
  8.5 2.0 %collective-permute-start.8 = (f32[2,128]{1,0:T(2,128)S(1)}, f32[2,128]{1,0:T(2,128)S(1)}, u32[]{:S(2)}, u32[]{:S(2)}) collective-permute-start(f32[2,128]{1,0:T(2,128)S(1)} %bitcast.74), channel_id=1, source_target_pairs={{0,2},{2,0},{1,3},{3,1},{4,6},{6,4},{5,7},{7,5},{8,10},{10,8},{9,1... | collective-permute-start | bytes 3080 | tf_op jit(solution)/shard_map/ppermute | solution.py:17
  10.6 0.8 %gather_fusion = f32[128,256]{1,0:T(8,128)S(1)} fusion(f32[1024,256]{1,0:T(8,128)S(1)} %fusion.6, s32[1024]{0:T(1024)S(1)} %get-tuple-element.32), kind=kCustom, calls=%fused_computation | custom fusion | bytes 262656 | tf_op jit(solution)/shard_map/gather | solution.py:125
  11.3 0.7 %gather_fusion.1 = bf16[128,128]{1,0:T(8,128)(2,1)S(1)} fusion(bf16[1024,128]{1,0:T(8,128)(2,1)S(1)} %bitcast_select_fusion, s32[1024]{0:T(1024)S(1)} %get-tuple-element.32), kind=kCustom, calls=%fused_computation.1 | custom fusion | bytes 66048 | tf_op jit(solution)/shard_map/gather | solution.py:60
  12.0 0.8 %gather_fusion.2 = f32[128,256]{1,0:T(8,128)S(1)} fusion(f32[1024,256]{1,0:T(8,128)S(1)} %fusion.6, s32[1024]{0:T(1024)S(1)} %get-tuple-element.31), kind=kCustom, calls=%fused_computation.2 | custom fusion | bytes 262656 | tf_op jit(solution)/shard_map/gather | solution.py:122
  12.8 0.7 %gather_fusion.3 = bf16[128,128]{1,0:T(8,128)(2,1)S(1)} fusion(bf16[1024,128]{1,0:T(8,128)(2,1)S(1)} %bitcast_select_fusion, s32[1024]{0:T(1024)S(1)} %get-tuple-element.31), kind=kCustom, calls=%fused_computation.3 | custom fusion | bytes 66048 | tf_op jit(solution)/shard_map/gather | solution.py:59
  13.9 3.6 %collective-permute-start.4 = (bf16[128,256]{1,0:T(8,128)(2,1)S(1)}, bf16[128,256]{1,0:T(8,128)(2,1)S(1)}, u32[]{:S(2)}, u32[]{:S(2)}) collective-permute-start(bf16[128,256]{1,0:T(8,128)(2,1)S(1)} %get-tuple-element.11), channel_id=1, source_target_pairs={{0,12},{4,0},{8,4},{12,8},{1,13},{5,1},{9,5},{13,9},{2,14},{6,2},{... | collective-permute-start | bytes 196616 | tf_op jit(solution)/shard_map/ppermute | solution.py:79
  17.5 1.0 %collective-permute-start.2 = (bf16[128,256]{1,0:T(8,128)(2,1)S(1)}, bf16[128,256]{1,0:T(8,128)(2,1)S(1)}, u32[]{:S(2)}, u32[]{:S(2)}) collective-permute-start(bf16[128,256]{1,0:T(8,128)(2,1)S(1)} %get-tuple-element.10), channel_id=1, source_target_pairs={{0,4},{4,8},{8,12},{12,0},{1,5},{5,9},{9,13},{13,1},{2,6},{6,10},{... | collective-permute-start | bytes 196616 | tf_op jit(solution)/shard_map/ppermute | solution.py:79
  18.5 1.2 %collective-permute-done.4 = bf16[128,256]{1,0:T(8,128)(2,1)S(1)} collective-permute-done((bf16[128,256]{1,0:T(8,128)(2,1)S(1)}, bf16[128,256]{1,0:T(8,128)(2,1)S(1)}, u32[]{:S(2)}, u32[]{:S(2)}) %collective-permute-start.4) | collective-permute-done | bytes 65568 | tf_op jit(solution)/shard_map/ppermute | solution.py:79
  19.7 3.1 %collective-permute-done.3 = bf16[128,256]{1,0:T(8,128)(2,1)S(1)} collective-permute-done((bf16[128,256]{1,0:T(8,128)(2,1)S(1)}, bf16[128,256]{1,0:T(8,128)(2,1)S(1)}, u32[]{:S(2)}, u32[]{:S(2)}) %collective-permute-start.3) | collective-permute-done | bytes 65568 | tf_op jit(solution)/shard_map/ppermute | solution.py:79
  22.8 0.8 %collective-permute-done.2 = bf16[128,256]{1,0:T(8,128)(2,1)S(1)} collective-permute-done((bf16[128,256]{1,0:T(8,128)(2,1)S(1)}, bf16[128,256]{1,0:T(8,128)(2,1)S(1)}, u32[]{:S(2)}, u32[]{:S(2)}) %collective-permute-start.2) | collective-permute-done | bytes 65568 | tf_op jit(solution)/shard_map/ppermute | solution.py:79
  23.9 1.3 %collective-permute-start.9 = (bf16[128,256]{1,0:T(8,128)(2,1)S(1)}, bf16[128,256]{1,0:T(8,128)(2,1)S(1)}, u32[]{:S(2)}, u32[]{:S(2)}) collective-permute-start(bf16[128,256]{1,0:T(8,128)(2,1)S(1)} %get-tuple-element.29), channel_id=1, source_target_pairs={{2,6},{4,0},{6,10},{8,4},{10,14},{12,8},{3,7},{5,1},{7,11},{9,5},{... | collective-permute-start | bytes 196616 | tf_op jit(solution)/shard_map/ppermute | solution.py:131
  25.3 1.3 %collective-permute-start.6 = (bf16[256,256]{1,0:T(8,128)(2,1)S(1)}, bf16[256,256]{1,0:T(8,128)(2,1)S(1)}, u32[]{:S(2)}, u32[]{:S(2)}) collective-permute-start(bf16[256,256]{1,0:T(8,128)(2,1)S(1)} %get-tuple-element.22), channel_id=1, source_target_pairs={{2,0},{4,2},{6,4},{8,6},{10,8},{12,10},{14,12},{3,1},{5,3},{7,5},{... | collective-permute-start | bytes 393224 | tf_op jit(solution)/shard_map/ppermute | solution.py:13
  26.6 4.6 %collective-permute-start.5 = (bf16[256,256]{1,0:T(8,128)(2,1)S(1)}, bf16[256,256]{1,0:T(8,128)(2,1)S(1)}, u32[]{:S(2)}, u32[]{:S(2)}) collective-permute-start(bf16[256,256]{1,0:T(8,128)(2,1)S(1)} %get-tuple-element.21), channel_id=1, source_target_pairs={{0,2},{2,4},{4,6},{6,8},{8,10},{10,12},{12,14},{1,3},{3,5},{5,7},{... | collective-permute-start | bytes 393224 | tf_op jit(solution)/shard_map/ppermute | solution.py:13
  31.2 0.9 %collective-permute-done.6 = bf16[256,256]{1,0:T(8,128)(2,1)S(1)} collective-permute-done((bf16[256,256]{1,0:T(8,128)(2,1)S(1)}, bf16[256,256]{1,0:T(8,128)(2,1)S(1)}, u32[]{:S(2)}, u32[]{:S(2)}) %collective-permute-start.6) | collective-permute-done | bytes 131104 | tf_op jit(solution)/shard_map/ppermute | solution.py:13
  32.2 2.3 %collective-permute-done.5 = bf16[256,256]{1,0:T(8,128)(2,1)S(1)} collective-permute-done((bf16[256,256]{1,0:T(8,128)(2,1)S(1)}, bf16[256,256]{1,0:T(8,128)(2,1)S(1)}, u32[]{:S(2)}, u32[]{:S(2)}) %collective-permute-start.5) | collective-permute-done | bytes 131104 | tf_op jit(solution)/shard_map/ppermute | solution.py:13
  35.5 4.9 %collective-permute-start.12 = (bf16[128,256]{1,0:T(8,128)(2,1)S(1)}, bf16[128,256]{1,0:T(8,128)(2,1)S(1)}, u32[]{:S(2)}, u32[]{:S(2)}) collective-permute-start(bf16[128,256]{1,0:T(8,128)(2,1)S(1)} %get-tuple-element.8), channel_id=1, source_target_pairs={{0,12},{4,0},{8,4},{12,8},{1,13},{5,1},{9,5},{13,9},{2,14},{6,2},{... | collective-permute-start | bytes 196616 | tf_op jit(solution)/shard_map/ppermute | solution.py:79
  40.4 1.9 %collective-permute-start.10 = (bf16[128,256]{1,0:T(8,128)(2,1)S(1)}, bf16[128,256]{1,0:T(8,128)(2,1)S(1)}, u32[]{:S(2)}, u32[]{:S(2)}) collective-permute-start(bf16[128,256]{1,0:T(8,128)(2,1)S(1)} %get-tuple-element.7), channel_id=1, source_target_pairs={{0,4},{4,8},{8,12},{12,0},{1,5},{5,9},{9,13},{13,1},{2,6},{6,10},{... | collective-permute-start | bytes 196616 | tf_op jit(solution)/shard_map/ppermute | solution.py:79
  42.6 3.0 %collective-permute-done.11 = bf16[128,256]{1,0:T(8,128)(2,1)S(1)} collective-permute-done((bf16[128,256]{1,0:T(8,128)(2,1)S(1)}, bf16[128,256]{1,0:T(8,128)(2,1)S(1)}, u32[]{:S(2)}, u32[]{:S(2)}) %collective-permute-start.11) | collective-permute-done | bytes 65568 | tf_op jit(solution)/shard_map/ppermute | solution.py:79
  45.5 0.9 %collective-permute-done.10 = bf16[128,256]{1,0:T(8,128)(2,1)S(1)} collective-permute-done((bf16[128,256]{1,0:T(8,128)(2,1)S(1)}, bf16[128,256]{1,0:T(8,128)(2,1)S(1)}, u32[]{:S(2)}, u32[]{:S(2)}) %collective-permute-start.10) | collective-permute-done | bytes 65568 | tf_op jit(solution)/shard_map/ppermute | solution.py:79
  46.5 1.1 %fusion.1 = bf16[1,1024,256]{2,1,0:T(8,128)(2,1)} fusion(f32[1024,256]{1,0:T(8,128)S(1)} %convolution_add_fusion, bf16[1024,128]{1,0:T(8,128)(2,1)S(1)} %bitcast_select_fusion, bf16[128,256]{1,0:T(8,128)(2,1)S(1)} %collective-permute-done.12, bf16[128,256]{1,0:T(8,128)(2,1)S(1)} %collective-permute-done.11, ...), kind=kOutput, calls=%fused_computation.7 | convolution fusion | flops 67895296 | bytes 2097156 | tf_op jit(solution)/shard_map/dot_general | solution.py:117
  (47 shorter events, 3.1 us)
Async XLA Ops:
  0.0 1.1 %copy-start = (bf16[1,1024,256]{2,1,0:T(8,128)(2,1)S(1)}, bf16[1,1024,256]{2,1,0:T(8,128)(2,1)}, u32[]{:S(2)}) copy-start(bf16[1,1024,256]{2,1,0:T(8,128)(2,1)} %param.7) | copy-start | bytes 1572868
  0.0 13.5 %collective-permute-start = (bf16[4,64,256]{2,1,0:T(8,128)(2,1)}, bf16[4,64,256]{2,1,0:T(8,128)(2,1)S(1)}, u32[]{:S(2)}, u32[]{:S(2)}) collective-permute-start(bf16[4,64,256]{2,1,0:T(8,128)(2,1)} %bitcast.72), channel_id=1, source_target_pairs={{0,1},{1,0},{2,3},{3,2},{4,5},{5,4},{6,7},{7,6},{8,9},{9,8},{10,11... | collective-permute-start | bytes 393224 | tf_op jit(solution)/shard_map/ppermute | solution.py:17
  1.1 2.4 %copy-start.1 = (bf16[1,1024,128]{2,1,0:T(8,128)(2,1)S(1)}, bf16[1,1024,128]{2,1,0:T(8,128)(2,1)}, u32[]{:S(2)}) copy-start(bf16[1,1024,128]{2,1,0:T(8,128)(2,1)} %param.11) | copy-start | bytes 786436
  3.5 5.0 %copy-start.4 = (f32[1,2,128]{2,1,0:T(2,128)S(1)}, f32[1,2,128]{2,1,0:T(2,128)}, u32[]{:S(2)}) copy-start(f32[1,2,128]{2,1,0:T(2,128)} %param.9) | copy-start | bytes 3076
  3.5 7.0 %copy-start.3 = (s32[1,2,128]{2,1,0:T(2,128)S(1)}, s32[1,2,128]{2,1,0:T(2,128)}, u32[]{:S(2)}) copy-start(s32[1,2,128]{2,1,0:T(2,128)} %param.10) | copy-start | bytes 3076
  3.8 9.7 %collective-permute-start.1 = (bf16[128,256]{1,0:T(8,128)(2,1)S(1)}, bf16[128,256]{1,0:T(8,128)(2,1)S(1)}, u32[]{:S(2)}, u32[]{:S(2)}) collective-permute-start(bf16[128,256]{1,0:T(8,128)(2,1)S(1)} %convolution_convert_fusion.3), channel_id=1, source_target_pairs={{0,2},{2,0},{1,3},{3,1},{4,6},{6,4},{5,7},{7,5},{8,10},{10,8},{9,1... | collective-permute-start | bytes 196616 | tf_op jit(solution)/shard_map/ppermute | solution.py:17
  8.1 5.4 %copy-start.2 = (bf16[4,1,64,1,256]{4,2,3,1,0:T(8,128)(2,1)S(1)}, bf16[4,1,64,1,256]{4,2,3,1,0:T(8,128)(2,1)}, u32[]{:S(2)}) copy-start(bf16[4,1,64,1,256]{4,2,3,1,0:T(8,128)(2,1)} %param.13) | copy-start | bytes 393220
  8.4 26.3 %collective-permute-start.7 = (bf16[128,384]{1,0:T(8,128)(2,1)S(1)}, bf16[128,384]{1,0:T(8,128)(2,1)S(1)}, u32[]{:S(2)}, u32[]{:S(2)}) collective-permute-start(bf16[128,384]{1,0:T(8,128)(2,1)S(1)} %pad_maximum_fusion.9), channel_id=1, source_target_pairs={{0,2},{2,0},{1,3},{3,1},{4,6},{6,4},{5,7},{7,5},{8,10},{10,8},{9,1... | collective-permute-start | bytes 294920 | tf_op jit(solution)/shard_map/ppermute | solution.py:17
  8.5 10.0 %collective-permute-start.8 = (f32[2,128]{1,0:T(2,128)S(1)}, f32[2,128]{1,0:T(2,128)S(1)}, u32[]{:S(2)}, u32[]{:S(2)}) collective-permute-start(f32[2,128]{1,0:T(2,128)S(1)} %bitcast.74), channel_id=1, source_target_pairs={{0,2},{2,0},{1,3},{3,1},{4,6},{6,4},{5,7},{7,5},{8,10},{10,8},{9,1... | collective-permute-start | bytes 3080 | tf_op jit(solution)/shard_map/ppermute | solution.py:17
  13.9 5.9 %collective-permute-start.4 = (bf16[128,256]{1,0:T(8,128)(2,1)S(1)}, bf16[128,256]{1,0:T(8,128)(2,1)S(1)}, u32[]{:S(2)}, u32[]{:S(2)}) collective-permute-start(bf16[128,256]{1,0:T(8,128)(2,1)S(1)} %get-tuple-element.11), channel_id=1, source_target_pairs={{0,12},{4,0},{8,4},{12,8},{1,13},{5,1},{9,5},{13,9},{2,14},{6,2},{... | collective-permute-start | bytes 196616 | tf_op jit(solution)/shard_map/ppermute | solution.py:79
  17.5 5.3 %collective-permute-start.3 = (bf16[128,256]{1,0:T(8,128)(2,1)S(1)}, bf16[128,256]{1,0:T(8,128)(2,1)S(1)}, u32[]{:S(2)}, u32[]{:S(2)}) collective-permute-start(bf16[128,256]{1,0:T(8,128)(2,1)S(1)} %get-tuple-element.12), channel_id=1, source_target_pairs={{0,8},{4,12},{8,0},{12,4},{1,9},{5,13},{9,1},{13,5},{2,10},{6,14},... | collective-permute-start | bytes 196616 | tf_op jit(solution)/shard_map/ppermute | solution.py:79
  17.5 6.1 %collective-permute-start.2 = (bf16[128,256]{1,0:T(8,128)(2,1)S(1)}, bf16[128,256]{1,0:T(8,128)(2,1)S(1)}, u32[]{:S(2)}, u32[]{:S(2)}) collective-permute-start(bf16[128,256]{1,0:T(8,128)(2,1)S(1)} %get-tuple-element.10), channel_id=1, source_target_pairs={{0,4},{4,8},{8,12},{12,0},{1,5},{5,9},{9,13},{13,1},{2,6},{6,10},{... | collective-permute-start | bytes 196616 | tf_op jit(solution)/shard_map/ppermute | solution.py:79
  23.9 7.2 %collective-permute-start.9 = (bf16[128,256]{1,0:T(8,128)(2,1)S(1)}, bf16[128,256]{1,0:T(8,128)(2,1)S(1)}, u32[]{:S(2)}, u32[]{:S(2)}) collective-permute-start(bf16[128,256]{1,0:T(8,128)(2,1)S(1)} %get-tuple-element.29), channel_id=1, source_target_pairs={{2,6},{4,0},{6,10},{8,4},{10,14},{12,8},{3,7},{5,1},{7,11},{9,5},{... | collective-permute-start | bytes 196616 | tf_op jit(solution)/shard_map/ppermute | solution.py:131
  25.3 6.9 %collective-permute-start.6 = (bf16[256,256]{1,0:T(8,128)(2,1)S(1)}, bf16[256,256]{1,0:T(8,128)(2,1)S(1)}, u32[]{:S(2)}, u32[]{:S(2)}) collective-permute-start(bf16[256,256]{1,0:T(8,128)(2,1)S(1)} %get-tuple-element.22), channel_id=1, source_target_pairs={{2,0},{4,2},{6,4},{8,6},{10,8},{12,10},{14,12},{3,1},{5,3},{7,5},{... | collective-permute-start | bytes 393224 | tf_op jit(solution)/shard_map/ppermute | solution.py:13
  26.6 8.0 %collective-permute-start.5 = (bf16[256,256]{1,0:T(8,128)(2,1)S(1)}, bf16[256,256]{1,0:T(8,128)(2,1)S(1)}, u32[]{:S(2)}, u32[]{:S(2)}) collective-permute-start(bf16[256,256]{1,0:T(8,128)(2,1)S(1)} %get-tuple-element.21), channel_id=1, source_target_pairs={{0,2},{2,4},{4,6},{6,8},{8,10},{10,12},{12,14},{1,3},{3,5},{5,7},{... | collective-permute-start | bytes 393224 | tf_op jit(solution)/shard_map/ppermute | solution.py:13
  35.5 7.1 %collective-permute-start.12 = (bf16[128,256]{1,0:T(8,128)(2,1)S(1)}, bf16[128,256]{1,0:T(8,128)(2,1)S(1)}, u32[]{:S(2)}, u32[]{:S(2)}) collective-permute-start(bf16[128,256]{1,0:T(8,128)(2,1)S(1)} %get-tuple-element.8), channel_id=1, source_target_pairs={{0,12},{4,0},{8,4},{12,8},{1,13},{5,1},{9,5},{13,9},{2,14},{6,2},{... | collective-permute-start | bytes 196616 | tf_op jit(solution)/shard_map/ppermute | solution.py:79
  40.4 5.2 %collective-permute-start.11 = (bf16[128,256]{1,0:T(8,128)(2,1)S(1)}, bf16[128,256]{1,0:T(8,128)(2,1)S(1)}, u32[]{:S(2)}, u32[]{:S(2)}) collective-permute-start(bf16[128,256]{1,0:T(8,128)(2,1)S(1)} %get-tuple-element.9), channel_id=1, source_target_pairs={{0,8},{4,12},{8,0},{12,4},{1,9},{5,13},{9,1},{13,5},{2,10},{6,14},... | collective-permute-start | bytes 196616 | tf_op jit(solution)/shard_map/ppermute | solution.py:79
  40.4 6.1 %collective-permute-start.10 = (bf16[128,256]{1,0:T(8,128)(2,1)S(1)}, bf16[128,256]{1,0:T(8,128)(2,1)S(1)}, u32[]{:S(2)}, u32[]{:S(2)}) collective-permute-start(bf16[128,256]{1,0:T(8,128)(2,1)S(1)} %get-tuple-element.7), channel_id=1, source_target_pairs={{0,4},{4,8},{8,12},{12,0},{1,5},{5,9},{9,13},{13,1},{2,6},{6,10},{... | collective-permute-start | bytes 196616 | tf_op jit(solution)/shard_map/ppermute | solution.py:79

commit v7 on v6

--- a/solution.py
+++ b/solution.py
@@ -88,8 +88,9 @@
         sends = jnp.dot(masked_basis.T, face_inverse, preferred_element_type=jnp.float32)
         keeps = jnp.dot(masked_basis.T, masked_basis, preferred_element_type=jnp.float32)
         mine = jnp.concatenate([sends, keeps], axis=1).astype(jnp.bfloat16)
-        theirs = swapped(mine, "tile")
-        partner_gains = swapped(gains, "tile")
+        gains_high = gains.T.astype(jnp.bfloat16)
+        gains_low = (gains.T - gains_high.astype(jnp.float32)).astype(jnp.bfloat16)
+        extra = jnp.concatenate([mine, gains_high, gains_low], axis=1)
         duct_pairs = []
         peers = lax.axis_size(DUCT)
         for i in range(peers):
@@ -110,7 +111,24 @@
 
     base_solve = jnp.dot(inverse, source, preferred_element_type=jnp.float32)
     local_solve = base_solve
-    inputs = gathered(coarse_input(local_solve.astype(jnp.bfloat16)), "tile", 0)
+    projected = coarse_input(local_solve.astype(jnp.bfloat16))
+    if pairwise:
+        width = projected.shape[1]
+        got = swapped(jnp.concatenate([projected, extra], axis=1), "tile")
+        first = tile_index == 0
+        inputs = jnp.concatenate(
+            [
+                jnp.where(first, projected, got[:, :width]),
+                jnp.where(first, got[:, :width], projected),
+            ],
+            axis=0,
+        )
+        theirs = got[:, width : width + mine.shape[1]]
+        tail = got[:, width + mine.shape[1] :].astype(jnp.float32)
+        pair = gains.shape[0]
+        partner_gains = (tail[:, :pair] + tail[:, pair:]).T
+    else:
+        inputs = gathered(projected, "tile", 0)
     earlier = None
     for cycle_index in range(ROUNDS):
         coarse = coarse_of(inputs)

time: 47.8 us -> 51.8 us (1.084)
  waiting for transfers between devices: 12.1 us -> 14.7 us
  starting transfers between devices: 24 us -> 22.8 us
  other arithmetic: 0.42 us -> 1.45 us
  matrix products: 5.89 us -> 6.9 us
  local copies, waits for them, and re-layouts: 4.09 us -> 4.63 us
    ppermute x4 -> x2, waiting for transfers between devices: 0.01 us -> 2.48 us  [swapped(): return lax.ppermute(shard, axis, [(0, 1), (1, 0)])]
    ppermute x4 -> x2, starting transfers between devices: 5.47 us -> 3.06 us  [swapped(): return lax.ppermute(shard, axis, [(0, 1), (1, 0)])]
    dot_general x1, matrix products: 0.27 us -> 1.3 us  [local(): jnp.dot(masked_basis.T, masked_basis, preferred_element_type=jnp.float32)]
    select_n x1, other arithmetic: 0.02 us -> 0.97 us  [local(): jnp.where(slot_ids[None, :] < deflation_counts[0], deflation_basis[0], jn...]
    ppermute x6, starting transfers between devices: 11.4 us -> 12.3 us  [coarse_of(): lax.ppermute(piece, 'sub', [(i, (i + k) % sub_count) for i in range(sub_c...]
  transfers between devices with their start and end apart: 13 -> 11, of which waited for: 7 -> 7; matrix products, arithmetic and copies ran while one was open for 18% -> 20% of each run, Pallas kernels for 0% -> 0%
where the time goes in v7:
time: 51.8 us; the launch traced here: 51.5 us
  starting transfers between devices  22.8 us (44%)
  waiting for transfers between devices  14.7 us (28%)
  matrix products  6.9 us (13%)
  local copies, waits for them, and re-layouts  4.63 us (9%)
  other arithmetic  1.45 us (3%)
  between operations  0.98 us (2%)
    ppermute x6, starting transfers between devices, coarse_of(): lax.ppermute(piece, 'sub', [(i, (i + k) % sub_count) for i in range(sub_c...  12.3 us
    ppermute x6, waiting for transfers between devices, coarse_of(): lax.ppermute(piece, 'sub', [(i, (i + k) % sub_count) for i in range(sub_c...  8.91 us
    ppermute x2, starting transfers between devices, passed_along(): return lax.ppermute(shard, DUCT, pairs)  6.1 us
    ppermute x2, waiting for transfers between devices, passed_along(): return lax.ppermute(shard, DUCT, pairs)  3.33 us
    ppermute x2, starting transfers between devices, swapped(): return lax.ppermute(shard, axis, [(0, 1), (1, 0)])  3.06 us
    ppermute x2, waiting for transfers between devices, swapped(): return lax.ppermute(shard, axis, [(0, 1), (1, 0)])  2.48 us
    dot_general x1, matrix products, local(): base_solve = jnp.dot(inverse, source, preferred_element_type=jnp.float32)  2.31 us
    dot_general x1, matrix products, local(): jnp.dot(masked_basis.T, masked_basis, preferred_element_type=jnp.float32)  1.3 us
  transfers between devices with their start and end apart: 11, of which 7 were waited for; matrix products, arithmetic and copies ran while one was open for 20% of the time, Pallas kernels for 0%

profile of v7, /device:TPU:0, one launch (start us, length us, event | category | flops | bytes accessed | tf_op | source)
XLA Modules:
  0.0 51.5 jit_solution(11441045970805621935)
XLA Ops:
  1.1 1.0 %bitcast_select_fusion = bf16[1024,128]{1,0:T(8,128)(2,1)S(1)} fusion(bf16[1,1024,128]{2,1,0:T(8,128)(2,1)} %param.11, pred[128]{0:T(512)(128)(4,1)S(1)} %iota_compare_fusion), kind=kLoop, calls=%fused_computation.27 | loop fusion | flops 131072 | bytes 524416 | tf_op jit(solution)/shard_map/jit(_where)/select_n | solution.py:47
  2.1 1.3 %convolution_convert_fusion.4 = bf16[128,128]{1,0:T(8,128)(2,1)S(1)} fusion(bf16[1,1024,128]{2,1,0:T(8,128)(2,1)} %param.11, pred[128]{0:T(512)(128)(4,1)S(1)} %iota_compare_fusion), kind=kOutput, calls=%fused_computation.20 | convolution fusion | flops 33701888 | bytes 295040 | tf_op jit(solution)/shard_map/dot_general | solution.py:89
  3.4 2.3 %fusion.6 = f32[1024,256]{1,0:T(8,128)S(1)} fusion(bf16[1,1024,256]{2,1,0:T(8,128)(2,1)S(1)} %copy-done, bf16[1,1024,1024]{2,1,0:T(8,128)(2,1)} %param.8), kind=kOutput, calls=%fused_computation.22 | convolution fusion | flops 536870912 | bytes 3670016 | tf_op jit(solution)/shard_map/dot_general | solution.py:112
  5.8 1.1 %fusion.48 = (bf16[1024,128]{1,0:T(8,128)(2,1)S(1)}, bf16[1024,128]{1,0:T(8,128)(2,1)S(1)}) fusion(bf16[1024,1024]{1,0:T(8,128)(2,1)} %bitcast.78), kind=kLoop, calls=%fused_computation.103 | loop fusion | bytes 1048576 | tf_op jit(solution)/shard_map/slice | solution.py:62
  7.8 2.6 %collective-permute-start.1 = (bf16[128,644]{1,0:T(8,128)(2,1)S(1)}, bf16[128,644]{1,0:T(8,128)(2,1)S(1)}, u32[]{:S(2)}, u32[]{:S(2)}) collective-permute-start(bf16[128,644]{1,0:T(8,128)(2,1)S(1)} %concatenate.34), channel_id=1, source_target_pairs={{0,2},{2,0},{1,3},{3,1},{4,6},{6,4},{5,7},{7,5},{8,10},{10,8},{9,1... | collective-permute-start | bytes 494600 | tf_op jit(solution)/shard_map/ppermute | solution.py:17
  10.4 0.8 %gather_fusion = f32[128,256]{1,0:T(8,128)S(1)} fusion(f32[1024,256]{1,0:T(8,128)S(1)} %fusion.6, s32[1024]{0:T(1024)S(1)} %get-tuple-element.34), kind=kCustom, calls=%fused_computation | custom fusion | bytes 262656 | tf_op jit(solution)/shard_map/gather | solution.py:143
  11.2 0.7 %gather_fusion.1 = bf16[128,128]{1,0:T(8,128)(2,1)S(1)} fusion(bf16[1024,128]{1,0:T(8,128)(2,1)S(1)} %bitcast_select_fusion, s32[1024]{0:T(1024)S(1)} %get-tuple-element.34), kind=kCustom, calls=%fused_computation.1 | custom fusion | bytes 66048 | tf_op jit(solution)/shard_map/gather | solution.py:60
  11.9 0.8 %gather_fusion.2 = f32[128,256]{1,0:T(8,128)S(1)} fusion(f32[1024,256]{1,0:T(8,128)S(1)} %fusion.6, s32[1024]{0:T(1024)S(1)} %get-tuple-element.33), kind=kCustom, calls=%fused_computation.2 | custom fusion | bytes 262656 | tf_op jit(solution)/shard_map/gather | solution.py:140
  12.7 0.7 %gather_fusion.3 = bf16[128,128]{1,0:T(8,128)(2,1)S(1)} fusion(bf16[1024,128]{1,0:T(8,128)(2,1)S(1)} %bitcast_select_fusion, s32[1024]{0:T(1024)S(1)} %get-tuple-element.33), kind=kCustom, calls=%fused_computation.3 | custom fusion | bytes 66048 | tf_op jit(solution)/shard_map/gather | solution.py:59
  13.5 2.5 %collective-permute-done.1 = bf16[128,644]{1,0:T(8,128)(2,1)S(1)} collective-permute-done((bf16[128,644]{1,0:T(8,128)(2,1)S(1)}, bf16[128,644]{1,0:T(8,128)(2,1)S(1)}, u32[]{:S(2)}, u32[]{:S(2)}) %collective-permute-start.1) | collective-permute-done | bytes 164896 | tf_op jit(solution)/shard_map/ppermute | solution.py:17
  16.2 3.9 %collective-permute-start.4 = (bf16[128,256]{1,0:T(8,128)(2,1)S(1)}, bf16[128,256]{1,0:T(8,128)(2,1)S(1)}, u32[]{:S(2)}, u32[]{:S(2)}) collective-permute-start(bf16[128,256]{1,0:T(8,128)(2,1)S(1)} %get-tuple-element.15), channel_id=1, source_target_pairs={{0,12},{4,0},{8,4},{12,8},{1,13},{5,1},{9,5},{13,9},{2,14},{6,2},{... | collective-permute-start | bytes 196616 | tf_op jit(solution)/shard_map/ppermute | solution.py:79
  20.1 1.0 %collective-permute-start.2 = (bf16[128,256]{1,0:T(8,128)(2,1)S(1)}, bf16[128,256]{1,0:T(8,128)(2,1)S(1)}, u32[]{:S(2)}, u32[]{:S(2)}) collective-permute-start(bf16[128,256]{1,0:T(8,128)(2,1)S(1)} %get-tuple-element.14), channel_id=1, source_target_pairs={{0,4},{4,8},{8,12},{12,0},{1,5},{5,9},{9,13},{13,1},{2,6},{6,10},{... | collective-permute-start | bytes 196616 | tf_op jit(solution)/shard_map/ppermute | solution.py:79
  21.4 1.2 %collective-permute-done.4 = bf16[128,256]{1,0:T(8,128)(2,1)S(1)} collective-permute-done((bf16[128,256]{1,0:T(8,128)(2,1)S(1)}, bf16[128,256]{1,0:T(8,128)(2,1)S(1)}, u32[]{:S(2)}, u32[]{:S(2)}) %collective-permute-start.4) | collective-permute-done | bytes 65568 | tf_op jit(solution)/shard_map/ppermute | solution.py:79
  22.6 3.8 %collective-permute-done.3 = bf16[128,256]{1,0:T(8,128)(2,1)S(1)} collective-permute-done((bf16[128,256]{1,0:T(8,128)(2,1)S(1)}, bf16[128,256]{1,0:T(8,128)(2,1)S(1)}, u32[]{:S(2)}, u32[]{:S(2)}) %collective-permute-start.3) | collective-permute-done | bytes 65568 | tf_op jit(solution)/shard_map/ppermute | solution.py:79
  26.8 1.3 %collective-permute-start.7 = (bf16[128,256]{1,0:T(8,128)(2,1)S(1)}, bf16[128,256]{1,0:T(8,128)(2,1)S(1)}, u32[]{:S(2)}, u32[]{:S(2)}) collective-permute-start(bf16[128,256]{1,0:T(8,128)(2,1)S(1)} %get-tuple-element.31), channel_id=1, source_target_pairs={{2,6},{4,0},{6,10},{8,4},{10,14},{12,8},{3,7},{5,1},{7,11},{9,5},{... | collective-permute-start | bytes 196616 | tf_op jit(solution)/shard_map/ppermute | solution.py:149
  28.1 1.3 %collective-permute-start.6 = (bf16[256,256]{1,0:T(8,128)(2,1)S(1)}, bf16[256,256]{1,0:T(8,128)(2,1)S(1)}, u32[]{:S(2)}, u32[]{:S(2)}) collective-permute-start(bf16[256,256]{1,0:T(8,128)(2,1)S(1)} %get-tuple-element.26), channel_id=1, source_target_pairs={{2,0},{4,2},{6,4},{8,6},{10,8},{12,10},{14,12},{3,1},{5,3},{7,5},{... | collective-permute-start | bytes 393224 | tf_op jit(solution)/shard_map/ppermute | solution.py:13
  29.4 4.8 %collective-permute-start.5 = (bf16[256,256]{1,0:T(8,128)(2,1)S(1)}, bf16[256,256]{1,0:T(8,128)(2,1)S(1)}, u32[]{:S(2)}, u32[]{:S(2)}) collective-permute-start(bf16[256,256]{1,0:T(8,128)(2,1)S(1)} %get-tuple-element.25), channel_id=1, source_target_pairs={{0,2},{2,4},{4,6},{6,8},{8,10},{10,12},{12,14},{1,3},{3,5},{5,7},{... | collective-permute-start | bytes 393224 | tf_op jit(solution)/shard_map/ppermute | solution.py:13
  34.3 0.9 %collective-permute-done.6 = bf16[256,256]{1,0:T(8,128)(2,1)S(1)} collective-permute-done((bf16[256,256]{1,0:T(8,128)(2,1)S(1)}, bf16[256,256]{1,0:T(8,128)(2,1)S(1)}, u32[]{:S(2)}, u32[]{:S(2)}) %collective-permute-start.6) | collective-permute-done | bytes 131104 | tf_op jit(solution)/shard_map/ppermute | solution.py:13
  35.3 2.5 %collective-permute-done.5 = bf16[256,256]{1,0:T(8,128)(2,1)S(1)} collective-permute-done((bf16[256,256]{1,0:T(8,128)(2,1)S(1)}, bf16[256,256]{1,0:T(8,128)(2,1)S(1)}, u32[]{:S(2)}, u32[]{:S(2)}) %collective-permute-start.5) | collective-permute-done | bytes 131104 | tf_op jit(solution)/shard_map/ppermute | solution.py:13
  38.8 5.5 %collective-permute-start.10 = (bf16[128,256]{1,0:T(8,128)(2,1)S(1)}, bf16[128,256]{1,0:T(8,128)(2,1)S(1)}, u32[]{:S(2)}, u32[]{:S(2)}) collective-permute-start(bf16[128,256]{1,0:T(8,128)(2,1)S(1)} %get-tuple-element.12), channel_id=1, source_target_pairs={{0,12},{4,0},{8,4},{12,8},{1,13},{5,1},{9,5},{13,9},{2,14},{6,2},{... | collective-permute-start | bytes 196616 | tf_op jit(solution)/shard_map/ppermute | solution.py:79
  44.3 1.9 %collective-permute-start.8 = (bf16[128,256]{1,0:T(8,128)(2,1)S(1)}, bf16[128,256]{1,0:T(8,128)(2,1)S(1)}, u32[]{:S(2)}, u32[]{:S(2)}) collective-permute-start(bf16[128,256]{1,0:T(8,128)(2,1)S(1)} %get-tuple-element.11), channel_id=1, source_target_pairs={{0,4},{4,8},{8,12},{12,0},{1,5},{5,9},{9,13},{13,1},{2,6},{6,10},{... | collective-permute-start | bytes 196616 | tf_op jit(solution)/shard_map/ppermute | solution.py:79
  46.5 3.0 %collective-permute-done.9 = bf16[128,256]{1,0:T(8,128)(2,1)S(1)} collective-permute-done((bf16[128,256]{1,0:T(8,128)(2,1)S(1)}, bf16[128,256]{1,0:T(8,128)(2,1)S(1)}, u32[]{:S(2)}, u32[]{:S(2)}) %collective-permute-start.9) | collective-permute-done | bytes 65568 | tf_op jit(solution)/shard_map/ppermute | solution.py:79
  49.5 0.9 %collective-permute-done.8 = bf16[128,256]{1,0:T(8,128)(2,1)S(1)} collective-permute-done((bf16[128,256]{1,0:T(8,128)(2,1)S(1)}, bf16[128,256]{1,0:T(8,128)(2,1)S(1)}, u32[]{:S(2)}, u32[]{:S(2)}) %collective-permute-start.8) | collective-permute-done | bytes 65568 | tf_op jit(solution)/shard_map/ppermute | solution.py:79
  50.4 1.1 %fusion.1 = bf16[1,1024,256]{2,1,0:T(8,128)(2,1)} fusion(f32[1024,256]{1,0:T(8,128)S(1)} %convolution_add_fusion, bf16[1024,128]{1,0:T(8,128)(2,1)S(1)} %bitcast_select_fusion, bf16[128,256]{1,0:T(8,128)(2,1)S(1)} %collective-permute-done.10, bf16[128,256]{1,0:T(8,128)(2,1)S(1)} %collective-permute-done.9, bf16[128,256]{1,0:T(8,128)(2,1)S(1)} %collective-permute-done.8, ...), kind=kOutput, calls=%fused_computation.7 | convolution fusion | flops 67895296 | bytes 2097156 | tf_op jit(solution)/shard_map/dot_general | solution.py:135
  (46 shorter events, 3.8 us)
Async XLA Ops:
  0.0 3.4 %copy-start = (bf16[1,1024,256]{2,1,0:T(8,128)(2,1)S(1)}, bf16[1,1024,256]{2,1,0:T(8,128)(2,1)}, u32[]{:S(2)}) copy-start(bf16[1,1024,256]{2,1,0:T(8,128)(2,1)} %param.7) | copy-start | bytes 1572868
  0.0 13.4 %collective-permute-start = (bf16[4,64,256]{2,1,0:T(8,128)(2,1)}, bf16[4,64,256]{2,1,0:T(8,128)(2,1)S(1)}, u32[]{:S(2)}, u32[]{:S(2)}) collective-permute-start(bf16[4,64,256]{2,1,0:T(8,128)(2,1)} %bitcast.77), channel_id=1, source_target_pairs={{0,1},{1,0},{2,3},{3,2},{4,5},{5,4},{6,7},{7,6},{8,9},{9,8},{10,11... | collective-permute-start | bytes 393224 | tf_op jit(solution)/shard_map/ppermute | solution.py:17
  3.4 3.4 %copy-start.2 = (f32[1,2,128]{2,1,0:T(2,128)S(1)}, f32[1,2,128]{2,1,0:T(2,128)}, u32[]{:S(2)}) copy-start(f32[1,2,128]{2,1,0:T(2,128)} %param.9) | copy-start | bytes 3076
  5.7 4.7 %copy-start.3 = (s32[1,2,128]{2,1,0:T(2,128)S(1)}, s32[1,2,128]{2,1,0:T(2,128)}, u32[]{:S(2)}) copy-start(s32[1,2,128]{2,1,0:T(2,128)} %param.10) | copy-start | bytes 3076
  7.4 6.0 %copy-start.1 = (bf16[4,1,64,1,256]{4,2,3,1,0:T(8,128)(2,1)S(1)}, bf16[4,1,64,1,256]{4,2,3,1,0:T(8,128)(2,1)}, u32[]{:S(2)}) copy-start(bf16[4,1,64,1,256]{4,2,3,1,0:T(8,128)(2,1)} %param.13) | copy-start | bytes 393220
  7.8 8.1 %collective-permute-start.1 = (bf16[128,644]{1,0:T(8,128)(2,1)S(1)}, bf16[128,644]{1,0:T(8,128)(2,1)S(1)}, u32[]{:S(2)}, u32[]{:S(2)}) collective-permute-start(bf16[128,644]{1,0:T(8,128)(2,1)S(1)} %concatenate.34), channel_id=1, source_target_pairs={{0,2},{2,0},{1,3},{3,1},{4,6},{6,4},{5,7},{7,5},{8,10},{10,8},{9,1... | collective-permute-start | bytes 494600 | tf_op jit(solution)/shard_map/ppermute | solution.py:17
  16.2 6.4 %collective-permute-start.4 = (bf16[128,256]{1,0:T(8,128)(2,1)S(1)}, bf16[128,256]{1,0:T(8,128)(2,1)S(1)}, u32[]{:S(2)}, u32[]{:S(2)}) collective-permute-start(bf16[128,256]{1,0:T(8,128)(2,1)S(1)} %get-tuple-element.15), channel_id=1, source_target_pairs={{0,12},{4,0},{8,4},{12,8},{1,13},{5,1},{9,5},{13,9},{2,14},{6,2},{... | collective-permute-start | bytes 196616 | tf_op jit(solution)/shard_map/ppermute | solution.py:79
  20.1 6.3 %collective-permute-start.3 = (bf16[128,256]{1,0:T(8,128)(2,1)S(1)}, bf16[128,256]{1,0:T(8,128)(2,1)S(1)}, u32[]{:S(2)}, u32[]{:S(2)}) collective-permute-start(bf16[128,256]{1,0:T(8,128)(2,1)S(1)} %get-tuple-element.16), channel_id=1, source_target_pairs={{0,8},{4,12},{8,0},{12,4},{1,9},{5,13},{9,1},{13,5},{2,10},{6,14},... | collective-permute-start | bytes 196616 | tf_op jit(solution)/shard_map/ppermute | solution.py:79
  20.1 6.3 %collective-permute-start.2 = (bf16[128,256]{1,0:T(8,128)(2,1)S(1)}, bf16[128,256]{1,0:T(8,128)(2,1)S(1)}, u32[]{:S(2)}, u32[]{:S(2)}) collective-permute-start(bf16[128,256]{1,0:T(8,128)(2,1)S(1)} %get-tuple-element.14), channel_id=1, source_target_pairs={{0,4},{4,8},{8,12},{12,0},{1,5},{5,9},{9,13},{13,1},{2,6},{6,10},{... | collective-permute-start | bytes 196616 | tf_op jit(solution)/shard_map/ppermute | solution.py:79
  26.8 7.4 %collective-permute-start.7 = (bf16[128,256]{1,0:T(8,128)(2,1)S(1)}, bf16[128,256]{1,0:T(8,128)(2,1)S(1)}, u32[]{:S(2)}, u32[]{:S(2)}) collective-permute-start(bf16[128,256]{1,0:T(8,128)(2,1)S(1)} %get-tuple-element.31), channel_id=1, source_target_pairs={{2,6},{4,0},{6,10},{8,4},{10,14},{12,8},{3,7},{5,1},{7,11},{9,5},{... | collective-permute-start | bytes 196616 | tf_op jit(solution)/shard_map/ppermute | solution.py:149
  28.1 7.1 %collective-permute-start.6 = (bf16[256,256]{1,0:T(8,128)(2,1)S(1)}, bf16[256,256]{1,0:T(8,128)(2,1)S(1)}, u32[]{:S(2)}, u32[]{:S(2)}) collective-permute-start(bf16[256,256]{1,0:T(8,128)(2,1)S(1)} %get-tuple-element.26), channel_id=1, source_target_pairs={{2,0},{4,2},{6,4},{8,6},{10,8},{12,10},{14,12},{3,1},{5,3},{7,5},{... | collective-permute-start | bytes 393224 | tf_op jit(solution)/shard_map/ppermute | solution.py:13
  29.4 8.4 %collective-permute-start.5 = (bf16[256,256]{1,0:T(8,128)(2,1)S(1)}, bf16[256,256]{1,0:T(8,128)(2,1)S(1)}, u32[]{:S(2)}, u32[]{:S(2)}) collective-permute-start(bf16[256,256]{1,0:T(8,128)(2,1)S(1)} %get-tuple-element.25), channel_id=1, source_target_pairs={{0,2},{2,4},{4,6},{6,8},{8,10},{10,12},{12,14},{1,3},{3,5},{5,7},{... | collective-permute-start | bytes 393224 | tf_op jit(solution)/shard_map/ppermute | solution.py:13
  38.8 7.7 %collective-permute-start.10 = (bf16[128,256]{1,0:T(8,128)(2,1)S(1)}, bf16[128,256]{1,0:T(8,128)(2,1)S(1)}, u32[]{:S(2)}, u32[]{:S(2)}) collective-permute-start(bf16[128,256]{1,0:T(8,128)(2,1)S(1)} %get-tuple-element.12), channel_id=1, source_target_pairs={{0,12},{4,0},{8,4},{12,8},{1,13},{5,1},{9,5},{13,9},{2,14},{6,2},{... | collective-permute-start | bytes 196616 | tf_op jit(solution)/shard_map/ppermute | solution.py:79
  44.3 5.2 %collective-permute-start.9 = (bf16[128,256]{1,0:T(8,128)(2,1)S(1)}, bf16[128,256]{1,0:T(8,128)(2,1)S(1)}, u32[]{:S(2)}, u32[]{:S(2)}) collective-permute-start(bf16[128,256]{1,0:T(8,128)(2,1)S(1)} %get-tuple-element.13), channel_id=1, source_target_pairs={{0,8},{4,12},{8,0},{12,4},{1,9},{5,13},{9,1},{13,5},{2,10},{6,14},... | collective-permute-start | bytes 196616 | tf_op jit(solution)/shard_map/ppermute | solution.py:79
  44.3 6.1 %collective-permute-start.8 = (bf16[128,256]{1,0:T(8,128)(2,1)S(1)}, bf16[128,256]{1,0:T(8,128)(2,1)S(1)}, u32[]{:S(2)}, u32[]{:S(2)}) collective-permute-start(bf16[128,256]{1,0:T(8,128)(2,1)S(1)} %get-tuple-element.11), channel_id=1, source_target_pairs={{0,4},{4,8},{8,12},{12,0},{1,5},{5,9},{9,13},{13,1},{2,6},{6,10},{... | collective-permute-start | bytes 196616 | tf_op jit(solution)/shard_map/ppermute | solution.py:79

commit v8 on v6

--- a/solution.py
+++ b/solution.py
@@ -88,8 +88,15 @@
         sends = jnp.dot(masked_basis.T, face_inverse, preferred_element_type=jnp.float32)
         keeps = jnp.dot(masked_basis.T, masked_basis, preferred_element_type=jnp.float32)
         mine = jnp.concatenate([sends, keeps], axis=1).astype(jnp.bfloat16)
-        theirs = swapped(mine, "tile")
-        partner_gains = swapped(gains, "tile")
+        gains_high = gains.T.astype(jnp.bfloat16)
+        gains_low = (gains.T - gains_high.astype(jnp.float32)).astype(jnp.bfloat16)
+        message = jnp.concatenate([mine, gains_high, gains_low], axis=1)
+        message, source = lax.optimization_barrier((message, source))
+        got = swapped(message, "tile")
+        theirs = got[:, : mine.shape[1]]
+        tail = got[:, mine.shape[1] :].astype(jnp.float32)
+        pair = gains.shape[0]
+        partner_gains = (tail[:, :pair] + tail[:, pair:]).T
         duct_pairs = []
         peers = lax.axis_size(DUCT)
         for i in range(peers):

time: 47.8 us -> 57.8 us (1.21)
  other arithmetic: 0.42 us -> 5 us
  matrix products: 5.89 us -> 8.51 us
  local copies, waits for them, and re-layouts: 4.09 us -> 6.04 us
  waiting for transfers between devices: 12.1 us -> 14 us
  starting transfers between devices: 24 us -> 22.7 us
    ppermute x4 -> x3, starting transfers between devices: 5.47 us -> 2.97 us  [swapped(): return lax.ppermute(shard, axis, [(0, 1), (1, 0)])]
    select_n x2, other arithmetic: 0.04 us -> 1.88 us  [gathered(): jnp.where(first, shard, other)]
    ppermute x2, starting transfers between devices: 5.85 us -> 7.58 us  [passed_along(): return lax.ppermute(shard, DUCT, pairs)]
    slice x0 -> x1, other arithmetic: none -> 1.19 us  [local(): inverse[:, :face_rows]]
    dot_general x1, matrix products: 0.27 us -> 1.3 us  [local(): jnp.dot(masked_basis.T, masked_basis, preferred_element_type=jnp.float32)]
    ppermute x2, waiting for transfers between devices: 3.18 us -> 4.2 us  [passed_along(): return lax.ppermute(shard, DUCT, pairs)]
    broadcast_in_dim x0 -> x1, local copies, waits for them, and re-layouts: none -> 1 us  [local(): return iterate.astype(jnp.bfloat16)[None]]
    slice x1, local copies, waits for them, and re-layouts: 1.08 us -> 0.17 us  [face_rows_of(): gain[0][:, None] * lower]
  transfers between devices with their start and end apart: 13 -> 12, of which waited for: 7 -> 9; matrix products, arithmetic and copies ran while one was open for 18% -> 12% of each run, Pallas kernels for 0% -> 0%
where the time goes in v8:
time: 57.8 us; the launch traced here: 57.3 us
  starting transfers between devices  22.7 us (39%)
  waiting for transfers between devices  14 us (24%)
  matrix products  8.51 us (15%)
  local copies, waits for them, and re-layouts  6.04 us (10%)
  other arithmetic  5 us (9%)
  between operations  1.1 us (2%)
    ppermute x6, starting transfers between devices, coarse_of(): lax.ppermute(piece, 'sub', [(i, (i + k) % sub_count) for i in range(sub_c...  10.9 us
    ppermute x6, waiting for transfers between devices, coarse_of(): lax.ppermute(piece, 'sub', [(i, (i + k) % sub_count) for i in range(sub_c...  9.04 us
    ppermute x2, starting transfers between devices, passed_along(): return lax.ppermute(shard, DUCT, pairs)  7.58 us
    ppermute x2, waiting for transfers between devices, passed_along(): return lax.ppermute(shard, DUCT, pairs)  4.2 us
    ppermute x3, starting transfers between devices, swapped(): return lax.ppermute(shard, axis, [(0, 1), (1, 0)])  2.97 us
    dot_general x1, matrix products, local(): base_solve = jnp.dot(inverse, source, preferred_element_type=jnp.float32)  2.34 us
    select_n x2, other arithmetic, gathered(): jnp.where(first, shard, other)  1.88 us
    gather x1, local copies, waits for them, and re-layouts, local(): local_solve[lower_at]  1.4 us
  transfers between devices with their start and end apart: 12, of which 9 were waited for; matrix products, arithmetic and copies ran while one was open for 12% of the time, Pallas kernels for 0%

profile of v8, /device:TPU:0, one launch (start us, length us, event | category | flops | bytes accessed | tf_op | source)
XLA Modules:
  0.0 57.3 jit_solution(2178277435789043529)
XLA Ops:
  0.7 1.3 %convolution_convert_fusion.4 = bf16[128,128]{1,0:T(8,128)(2,1)S(1)} fusion(bf16[1,1024,128]{2,1,0:T(8,128)(2,1)} %param.11, pred[128]{0:T(512)(128)(4,1)S(1)} %iota_compare_fusion), kind=kOutput, calls=%fused_computation.21 | convolution fusion | flops 33701888 | bytes 295040 | tf_op jit(solution)/shard_map/dot_general | solution.py:89
  2.1 1.2 %fusion.46 = (bf16[1024,128]{1,0:T(8,128)(2,1)S(1)}, bf16[1024,128]{1,0:T(8,128)(2,1)S(1)}, bf16[1024,128]{1,0:T(8,128)(2,1)S(1)}) fusion(bf16[1024,1024]{1,0:T(8,128)(2,1)} %bitcast.79, bf16[1,1024,128]{2,1,0:T(8,128)(2,1)} %param.11, pred[128]{0:T(512)(128)(4,1)S(1)} %iota_compare_fusion), kind=kLoop, calls=%fused_computation.103 | loop fusion | flops 131072 | bytes 1572992 | tf_op jit(solution)/shard_map/slice | solution.py:62
  4.6 2.3 %convolution_bitcast_fusion = f32[1024,256]{0,1:T(8,128)S(1)} fusion(bf16[1024,256]{1,0:T(8,128)(2,1)S(1)} %bitcast.78, bf16[1,1024,1024]{2,1,0:T(8,128)(2,1)} %param.8), kind=kOutput, calls=%fused_computation.4 | convolution fusion | flops 536870912 | bytes 3670016 | tf_op jit(solution)/shard_map/dot_general | solution.py:118
  6.9 1.0 %convolution_convert_fusion.2 = bf16[128,256]{1,0:T(8,128)(2,1)} fusion(bf16[1024,128]{1,0:T(8,128)(2,1)S(1)} %get-tuple-element.37, f32[1024,256]{0,1:T(8,128)S(1)} %convolution_bitcast_fusion), kind=kOutput, calls=%fused_computation.15 | convolution fusion | flops 67403776 | bytes 1376256 | tf_op jit(solution)/shard_map/dot_general | solution.py:66
  7.9 2.9 %collective-permute-start.1 = (bf16[128,256]{1,0:T(8,128)(2,1)}, bf16[128,256]{1,0:T(8,128)(2,1)}, u32[]{:S(2)}, u32[]{:S(2)}) collective-permute-start(bf16[128,256]{1,0:T(8,128)(2,1)} %convolution_convert_fusion.2), channel_id=1, source_target_pairs={{0,2},{2,0},{1,3},{3,1},{4,6},{6,4},{5,7},{7,5},{8,10},{10,8},{9,1... | collective-permute-start | bytes 196616 | tf_op jit(solution)/shard_map/ppermute | solution.py:17
  11.3 1.3 %gather_fusion.1 = bf16[128,128]{1,0:T(8,128)(2,1)} fusion(bf16[1024,128]{1,0:T(8,128)(2,1)S(1)} %get-tuple-element.37, s32[1024]{0:T(1024)S(1)} %get-tuple-element.39), kind=kCustom, calls=%fused_computation.1 | custom fusion | bytes 66048 | tf_op jit(solution)/shard_map/gather | solution.py:60
  13.3 1.4 %gather_fusion.2 = f32[128,256]{1,0:T(8,128)} fusion(f32[1024,256]{1,0:T(8,128)S(1)} %copy.25, s32[1024]{0:T(1024)S(1)} %get-tuple-element.38), kind=kCustom, calls=%fused_computation.2 | custom fusion | bytes 262656 | tf_op jit(solution)/shard_map/gather | solution.py:129
  15.5 0.9 %broadcast_select_fusion.6 = (bf16[128,256]{1,0:T(8,128)(2,1)S(1)}, bf16[128,256]{1,0:T(8,128)(2,1)S(1)}) fusion(bf16[128,256]{1,0:T(8,128)(2,1)} %convolution_convert_fusion.2, bf16[128,256]{1,0:T(8,128)(2,1)} %collective-permute-done.1, pred[]{:T(512)S(6)} %eq.16), kind=kLoop, calls=%fused_computation.79 | loop fusion | flops 65536 | bytes 262145 | tf_op jit(solution)/shard_map/jit(_where)/select_n | solution.py:26
  17.9 1.0 %broadcast_select_fusion.1 = (bf16[4,64,256]{2,1,0:T(8,128)(2,1)S(1)}, bf16[4,64,256]{2,1,0:T(8,128)(2,1)S(1)}) fusion(bf16[4,64,256]{2,1,0:T(8,128)(2,1)} %collective-permute-done, pred[]{:T(512)S(6)} %eq.15, bf16[4,1,64,1,256]{4,2,3,1,0:T(8,128)(2,1)} %param.13), kind=kLoop, calls=%fused_computation.56 | loop fusion | flops 131072 | bytes 524289 | tf_op jit(solution)/shard_map/jit(_where)/select_n | solution.py:26
  19.2 1.6 %collective-permute-start.2 = (bf16[128,256]{1,0:T(8,128)(2,1)S(1)}, bf16[128,256]{1,0:T(8,128)(2,1)S(1)}, u32[]{:S(2)}, u32[]{:S(2)}) collective-permute-start(bf16[128,256]{1,0:T(8,128)(2,1)S(1)} %get-tuple-element.18), channel_id=1, source_target_pairs={{0,4},{4,8},{8,12},{12,0},{1,5},{5,9},{9,13},{13,1},{2,6},{6,10},{... | collective-permute-start | bytes 196616 | tf_op jit(solution)/shard_map/ppermute | solution.py:79
  20.8 2.6 %collective-permute-start.3 = (bf16[128,256]{1,0:T(8,128)(2,1)S(1)}, bf16[128,256]{1,0:T(8,128)(2,1)S(1)}, u32[]{:S(2)}, u32[]{:S(2)}) collective-permute-start(bf16[128,256]{1,0:T(8,128)(2,1)S(1)} %get-tuple-element.20), channel_id=1, source_target_pairs={{0,8},{4,12},{8,0},{12,4},{1,9},{5,13},{9,1},{13,5},{2,10},{6,14},... | collective-permute-start | bytes 196616 | tf_op jit(solution)/shard_map/ppermute | solution.py:79
  23.4 1.3 %collective-permute-start.4 = (bf16[128,256]{1,0:T(8,128)(2,1)S(1)}, bf16[128,256]{1,0:T(8,128)(2,1)S(1)}, u32[]{:S(2)}, u32[]{:S(2)}) collective-permute-start(bf16[128,256]{1,0:T(8,128)(2,1)S(1)} %get-tuple-element.19), channel_id=1, source_target_pairs={{0,12},{4,0},{8,4},{12,8},{1,13},{5,1},{9,5},{13,9},{2,14},{6,2},{... | collective-permute-start | bytes 196616 | tf_op jit(solution)/shard_map/ppermute | solution.py:79
  25.6 2.5 %collective-permute-done.3 = bf16[128,256]{1,0:T(8,128)(2,1)S(1)} collective-permute-done((bf16[128,256]{1,0:T(8,128)(2,1)S(1)}, bf16[128,256]{1,0:T(8,128)(2,1)S(1)}, u32[]{:S(2)}, u32[]{:S(2)}) %collective-permute-start.3) | collective-permute-done | bytes 65568 | tf_op jit(solution)/shard_map/ppermute | solution.py:79
  28.6 1.3 %collective-permute-start.8 = (bf16[128,256]{1,0:T(8,128)(2,1)S(1)}, bf16[128,256]{1,0:T(8,128)(2,1)S(1)}, u32[]{:S(2)}, u32[]{:S(2)}) collective-permute-start(bf16[128,256]{1,0:T(8,128)(2,1)S(1)} %get-tuple-element.35), channel_id=1, source_target_pairs={{2,6},{4,0},{6,10},{8,4},{10,14},{12,8},{3,7},{5,1},{7,11},{9,5},{... | collective-permute-start | bytes 196616 | tf_op jit(solution)/shard_map/ppermute | solution.py:138
  30.0 1.3 %collective-permute-start.6 = (bf16[256,256]{1,0:T(8,128)(2,1)S(1)}, bf16[256,256]{1,0:T(8,128)(2,1)S(1)}, u32[]{:S(2)}, u32[]{:S(2)}) collective-permute-start(bf16[256,256]{1,0:T(8,128)(2,1)S(1)} %get-tuple-element.30), channel_id=1, source_target_pairs={{2,0},{4,2},{6,4},{8,6},{10,8},{12,10},{14,12},{3,1},{5,3},{7,5},{... | collective-permute-start | bytes 393224 | tf_op jit(solution)/shard_map/ppermute | solution.py:13
  31.3 6.3 %collective-permute-start.5 = (bf16[256,256]{1,0:T(8,128)(2,1)S(1)}, bf16[256,256]{1,0:T(8,128)(2,1)S(1)}, u32[]{:S(2)}, u32[]{:S(2)}) collective-permute-start(bf16[256,256]{1,0:T(8,128)(2,1)S(1)} %get-tuple-element.29), channel_id=1, source_target_pairs={{0,2},{2,4},{4,6},{6,8},{8,10},{10,12},{12,14},{1,3},{3,5},{5,7},{... | collective-permute-start | bytes 393224 | tf_op jit(solution)/shard_map/ppermute | solution.py:13
  37.7 1.3 %collective-permute-done.6 = bf16[256,256]{1,0:T(8,128)(2,1)S(1)} collective-permute-done((bf16[256,256]{1,0:T(8,128)(2,1)S(1)}, bf16[256,256]{1,0:T(8,128)(2,1)S(1)}, u32[]{:S(2)}, u32[]{:S(2)}) %collective-permute-start.6) | collective-permute-done | bytes 131104 | tf_op jit(solution)/shard_map/ppermute | solution.py:13
  39.1 2.9 %collective-permute-done.5 = bf16[256,256]{1,0:T(8,128)(2,1)S(1)} collective-permute-done((bf16[256,256]{1,0:T(8,128)(2,1)S(1)}, bf16[256,256]{1,0:T(8,128)(2,1)S(1)}, u32[]{:S(2)}, u32[]{:S(2)}) %collective-permute-start.5) | collective-permute-done | bytes 131104 | tf_op jit(solution)/shard_map/ppermute | solution.py:13
  42.2 0.9 %fusion.26 = f32[128,256]{1,0:T(8,128)S(1)} fusion(bf16[256,256]{1,0:T(8,128)(2,1)S(1)} %collective-permute-done.5, bf16[256,256]{1,0:T(8,128)(2,1)S(1)} %collective-permute-done.6, pred[]{:T(512)S(6)} %eq.16, bf16[128,388]{1,0:T(8,128)(2,1)} %collective-permute-done.7), kind=kOutput, calls=%fused_computation.59 | convolution fusion | flops 8421376 | bytes 294913 | tf_op jit(solution)/shard_map/dot_general | solution.py:110
  43.2 1.0 %fusion.5 = bf16[128,256]{1,0:T(8,128)(2,1)S(1)} fusion(f32[128,256]{1,0:T(8,128)S(1)} %fusion.26, bf16[128,256]{1,0:T(8,128)(2,1)S(1)} %get-tuple-element.28, bf16[128,256]{1,0:T(8,128)(2,1)S(1)} %get-tuple-element.27, bf16[128,388]{1,0:T(8,128)(2,1)} %collective-permute-done.7), kind=kOutput, calls=%fused_computation.20 | convolution fusion | flops 17104896 | bytes 393216 | tf_op jit(solution)/shard_map/dot_general | solution.py:109
  44.6 2.6 %collective-permute-start.10 = (bf16[128,256]{1,0:T(8,128)(2,1)S(1)}, bf16[128,256]{1,0:T(8,128)(2,1)S(1)}, u32[]{:S(2)}, u32[]{:S(2)}) collective-permute-start(bf16[128,256]{1,0:T(8,128)(2,1)S(1)} %get-tuple-element.17), channel_id=1, source_target_pairs={{0,8},{4,12},{8,0},{12,4},{1,9},{5,13},{9,1},{13,5},{2,10},{6,14},... | collective-permute-start | bytes 196616 | tf_op jit(solution)/shard_map/ppermute | solution.py:79
  47.2 2.7 %collective-permute-start.11 = (bf16[128,256]{1,0:T(8,128)(2,1)S(1)}, bf16[128,256]{1,0:T(8,128)(2,1)S(1)}, u32[]{:S(2)}, u32[]{:S(2)}) collective-permute-start(bf16[128,256]{1,0:T(8,128)(2,1)S(1)} %get-tuple-element.16), channel_id=1, source_target_pairs={{0,12},{4,0},{8,4},{12,8},{1,13},{5,1},{9,5},{13,9},{2,14},{6,2},{... | collective-permute-start | bytes 196616 | tf_op jit(solution)/shard_map/ppermute | solution.py:79
  51.8 4.2 %collective-permute-done.9 = bf16[128,256]{1,0:T(8,128)(2,1)S(1)} collective-permute-done((bf16[128,256]{1,0:T(8,128)(2,1)S(1)}, bf16[128,256]{1,0:T(8,128)(2,1)S(1)}, u32[]{:S(2)}, u32[]{:S(2)}) %collective-permute-start.9) | collective-permute-done | bytes 65568 | tf_op jit(solution)/shard_map/ppermute | solution.py:79
  56.3 1.0 %copy.29 = bf16[1,1024,256]{2,1,0:T(8,128)(2,1)} copy(bf16[1,1024,256]{1,2,0:T(8,128)(2,1)S(1)} %fusion.1) | data formatting | bytes 1048576 | tf_op jit(solution)/shard_map/broadcast_in_dim | solution.py:164
  (59 shorter events, 9.4 us)
Async XLA Ops:
  0.0 4.6 %copy-start = (bf16[1,1024,256]{2,1,0:T(8,128)(2,1)S(1)}, bf16[1,1024,256]{2,1,0:T(8,128)(2,1)}, u32[]{:S(2)}) copy-start(bf16[1,1024,256]{2,1,0:T(8,128)(2,1)} %param.7) | copy-start | bytes 1572868
  0.0 3.3 %copy-start.7 = (f32[1,2,128]{2,1,0:T(2,128)S(1)}, f32[1,2,128]{2,1,0:T(2,128)}, u32[]{:S(2)}) copy-start(f32[1,2,128]{2,1,0:T(2,128)} %param.9) | copy-start | bytes 3076
  2.0 2.5 %copy-start.5 = (bf16[128,128]{1,0:T(8,128)(2,1)}, bf16[128,128]{1,0:T(8,128)(2,1)S(1)}, u32[]{:S(2)}) copy-start(bf16[128,128]{1,0:T(8,128)(2,1)S(1)} %convolution_convert_fusion.4) | copy-start | bytes 98308
  3.8 0.8 %copy-start.2 = (bf16[128,256]{1,0:T(8,128)(2,1)}, bf16[128,256]{1,0:T(8,128)(2,1)S(1)}, u32[]{:S(2)}) copy-start(bf16[128,256]{1,0:T(8,128)(2,1)S(1)} %convolution_convert_fusion.3) | copy-start | bytes 196612
  6.9 4.3 %copy-start.8 = (s32[1,2,128]{2,1,0:T(2,128)S(1)}, s32[1,2,128]{2,1,0:T(2,128)}, u32[]{:S(2)}) copy-start(s32[1,2,128]{2,1,0:T(2,128)} %param.10) | copy-start | bytes 3076
  7.9 7.6 %collective-permute-start.1 = (bf16[128,256]{1,0:T(8,128)(2,1)}, bf16[128,256]{1,0:T(8,128)(2,1)}, u32[]{:S(2)}, u32[]{:S(2)}) collective-permute-start(bf16[128,256]{1,0:T(8,128)(2,1)} %convolution_convert_fusion.2), channel_id=1, source_target_pairs={{0,2},{2,0},{1,3},{3,1},{4,6},{6,4},{5,7},{7,5},{8,10},{10,8},{9,1... | collective-permute-start | bytes 196616 | tf_op jit(solution)/shard_map/ppermute | solution.py:17
  10.8 7.1 %collective-permute-start = (bf16[4,64,256]{2,1,0:T(8,128)(2,1)}, bf16[4,64,256]{2,1,0:T(8,128)(2,1)}, u32[]{:S(2)}, u32[]{:S(2)}) collective-permute-start(bf16[4,64,256]{2,1,0:T(8,128)(2,1)} %bitcast.12), channel_id=1, source_target_pairs={{0,1},{1,0},{2,3},{3,2},{4,5},{5,4},{6,7},{7,6},{8,9},{9,8},{10,11... | collective-permute-start | bytes 393224 | tf_op jit(solution)/shard_map/ppermute | solution.py:17
  10.8 6.2 %collective-permute-start.7 = (bf16[128,388]{1,0:T(8,128)(2,1)}, bf16[128,388]{1,0:T(8,128)(2,1)}, u32[]{:S(2)}, u32[]{:S(2)}) collective-permute-start(bf16[128,388]{1,0:T(8,128)(2,1)} %pad_maximum_fusion.8), channel_id=1, source_target_pairs={{0,2},{2,0},{1,3},{3,1},{4,6},{6,4},{5,7},{7,5},{8,10},{10,8},{9,1... | collective-permute-start | bytes 297992 | tf_op jit(solution)/shard_map/ppermute | solution.py:17
  14.7 13.6 %copy-start.4 = (bf16[128,128]{1,0:T(8,128)(2,1)S(1)}, bf16[128,128]{1,0:T(8,128)(2,1)}, u32[]{:S(2)}) copy-start(bf16[128,128]{1,0:T(8,128)(2,1)} %gather_fusion.1) | copy-start | bytes 98308
  14.7 13.8 %copy-start.1 = (f32[128,256]{1,0:T(8,128)S(1)}, f32[128,256]{1,0:T(8,128)}, u32[]{:S(2)}) copy-start(f32[128,256]{1,0:T(8,128)} %gather_fusion.2) | copy-start | bytes 393220
  17.8 24.3 %copy-start.3 = (bf16[128,256]{1,0:T(8,128)(2,1)S(1)}, bf16[128,256]{1,0:T(8,128)(2,1)}, u32[]{:S(2)}) copy-start(bf16[128,256]{1,0:T(8,128)(2,1)} %copy-done.2) | copy-start | bytes 196612
  18.9 25.3 %copy-start.6 = (bf16[128,128]{1,0:T(8,128)(2,1)S(1)}, bf16[128,128]{1,0:T(8,128)(2,1)}, u32[]{:S(2)}) copy-start(bf16[128,128]{1,0:T(8,128)(2,1)} %copy-done.5) | copy-start | bytes 98308
  19.2 6.4 %collective-permute-start.2 = (bf16[128,256]{1,0:T(8,128)(2,1)S(1)}, bf16[128,256]{1,0:T(8,128)(2,1)S(1)}, u32[]{:S(2)}, u32[]{:S(2)}) collective-permute-start(bf16[128,256]{1,0:T(8,128)(2,1)S(1)} %get-tuple-element.18), channel_id=1, source_target_pairs={{0,4},{4,8},{8,12},{12,0},{1,5},{5,9},{9,13},{13,1},{2,6},{6,10},{... | collective-permute-start | bytes 196616 | tf_op jit(solution)/shard_map/ppermute | solution.py:79
  20.8 7.3 %collective-permute-start.3 = (bf16[128,256]{1,0:T(8,128)(2,1)S(1)}, bf16[128,256]{1,0:T(8,128)(2,1)S(1)}, u32[]{:S(2)}, u32[]{:S(2)}) collective-permute-start(bf16[128,256]{1,0:T(8,128)(2,1)S(1)} %get-tuple-element.20), channel_id=1, source_target_pairs={{0,8},{4,12},{8,0},{12,4},{1,9},{5,13},{9,1},{13,5},{2,10},{6,14},... | collective-permute-start | bytes 196616 | tf_op jit(solution)/shard_map/ppermute | solution.py:79
  23.4 4.9 %collective-permute-start.4 = (bf16[128,256]{1,0:T(8,128)(2,1)S(1)}, bf16[128,256]{1,0:T(8,128)(2,1)S(1)}, u32[]{:S(2)}, u32[]{:S(2)}) collective-permute-start(bf16[128,256]{1,0:T(8,128)(2,1)S(1)} %get-tuple-element.19), channel_id=1, source_target_pairs={{0,12},{4,0},{8,4},{12,8},{1,13},{5,1},{9,5},{13,9},{2,14},{6,2},{... | collective-permute-start | bytes 196616 | tf_op jit(solution)/shard_map/ppermute | solution.py:79
  28.6 8.9 %collective-permute-start.8 = (bf16[128,256]{1,0:T(8,128)(2,1)S(1)}, bf16[128,256]{1,0:T(8,128)(2,1)S(1)}, u32[]{:S(2)}, u32[]{:S(2)}) collective-permute-start(bf16[128,256]{1,0:T(8,128)(2,1)S(1)} %get-tuple-element.35), channel_id=1, source_target_pairs={{2,6},{4,0},{6,10},{8,4},{10,14},{12,8},{3,7},{5,1},{7,11},{9,5},{... | collective-permute-start | bytes 196616 | tf_op jit(solution)/shard_map/ppermute | solution.py:138
  30.0 9.0 %collective-permute-start.6 = (bf16[256,256]{1,0:T(8,128)(2,1)S(1)}, bf16[256,256]{1,0:T(8,128)(2,1)S(1)}, u32[]{:S(2)}, u32[]{:S(2)}) collective-permute-start(bf16[256,256]{1,0:T(8,128)(2,1)S(1)} %get-tuple-element.30), channel_id=1, source_target_pairs={{2,0},{4,2},{6,4},{8,6},{10,8},{12,10},{14,12},{3,1},{5,3},{7,5},{... | collective-permute-start | bytes 393224 | tf_op jit(solution)/shard_map/ppermute | solution.py:13
  31.3 10.7 %collective-permute-start.5 = (bf16[256,256]{1,0:T(8,128)(2,1)S(1)}, bf16[256,256]{1,0:T(8,128)(2,1)S(1)}, u32[]{:S(2)}, u32[]{:S(2)}) collective-permute-start(bf16[256,256]{1,0:T(8,128)(2,1)S(1)} %get-tuple-element.29), channel_id=1, source_target_pairs={{0,2},{2,4},{4,6},{6,8},{8,10},{10,12},{12,14},{1,3},{3,5},{5,7},{... | collective-permute-start | bytes 393224 | tf_op jit(solution)/shard_map/ppermute | solution.py:13
  44.6 6.4 %collective-permute-start.10 = (bf16[128,256]{1,0:T(8,128)(2,1)S(1)}, bf16[128,256]{1,0:T(8,128)(2,1)S(1)}, u32[]{:S(2)}, u32[]{:S(2)}) collective-permute-start(bf16[128,256]{1,0:T(8,128)(2,1)S(1)} %get-tuple-element.17), channel_id=1, source_target_pairs={{0,8},{4,12},{8,0},{12,4},{1,9},{5,13},{9,1},{13,5},{2,10},{6,14},... | collective-permute-start | bytes 196616 | tf_op jit(solution)/shard_map/ppermute | solution.py:79
  47.2 4.6 %collective-permute-start.11 = (bf16[128,256]{1,0:T(8,128)(2,1)S(1)}, bf16[128,256]{1,0:T(8,128)(2,1)S(1)}, u32[]{:S(2)}, u32[]{:S(2)}) collective-permute-start(bf16[128,256]{1,0:T(8,128)(2,1)S(1)} %get-tuple-element.16), channel_id=1, source_target_pairs={{0,12},{4,0},{8,4},{12,8},{1,13},{5,1},{9,5},{13,9},{2,14},{6,2},{... | collective-permute-start | bytes 196616 | tf_op jit(solution)/shard_map/ppermute | solution.py:79
  49.9 6.1 %collective-permute-start.9 = (bf16[128,256]{1,0:T(8,128)(2,1)S(1)}, bf16[128,256]{1,0:T(8,128)(2,1)S(1)}, u32[]{:S(2)}, u32[]{:S(2)}) collective-permute-start(bf16[128,256]{1,0:T(8,128)(2,1)S(1)} %get-tuple-element.15), channel_id=1, source_target_pairs={{0,4},{4,8},{8,12},{12,0},{1,5},{5,9},{9,13},{13,1},{2,6},{6,10},{... | collective-permute-start | bytes 196616 | tf_op jit(solution)/shard_map/ppermute | solution.py:79

commit v9 on v7

--- a/solution.py
+++ b/solution.py
@@ -90,13 +90,17 @@
         mine = jnp.concatenate([sends, keeps], axis=1).astype(jnp.bfloat16)
         gains_high = gains.T.astype(jnp.bfloat16)
         gains_low = (gains.T - gains_high.astype(jnp.float32)).astype(jnp.bfloat16)
-        extra = jnp.concatenate([mine, gains_high, gains_low], axis=1)
-        duct_pairs = []
+        gains_pair = jnp.concatenate([gains_high, gains_low], axis=1)
         peers = lax.axis_size(DUCT)
+        diagonal_pairs = []
+        crossing_pairs = []
         for i in range(peers):
+            target = i - 1 if i % 2 == 0 else i + 1
+            if 0 <= target < peers:
+                diagonal_pairs.append((i, target))
             target = i - 2 if i % 2 == 0 else i + 2
             if 0 <= target < peers:
-                duct_pairs.append((i, target))
+                crossing_pairs.append((i, target))
 
     def projection_of(mix, faces, coarse):
         return (
@@ -114,7 +118,7 @@
     projected = coarse_input(local_solve.astype(jnp.bfloat16))
     if pairwise:
         width = projected.shape[1]
-        got = swapped(jnp.concatenate([projected, extra], axis=1), "tile")
+        got = swapped(jnp.concatenate([projected, gains_pair], axis=1), "tile")
         first = tile_index == 0
         inputs = jnp.concatenate(
             [
@@ -123,8 +127,7 @@
             ],
             axis=0,
         )
-        theirs = got[:, width : width + mine.shape[1]]
-        tail = got[:, width + mine.shape[1] :].astype(jnp.float32)
+        tail = got[:, width:].astype(jnp.float32)
         pair = gains.shape[0]
         partner_gains = (tail[:, :pair] + tail[:, pair:]).T
     else:
@@ -144,18 +147,20 @@
         ).astype(jnp.bfloat16)
         rows = lower_trace.shape[0]
         if pairwise:
-            got_lower = passed_along(jnp.concatenate([upper_trace, coarse], axis=0), 1)
-            got_upper = passed_along(jnp.concatenate([lower_trace, coarse], axis=0), -1)
-            crossing = lax.ppermute(
-                jnp.where(tile_index == 0, lower_trace, upper_trace), DUCT, duct_pairs
-            )
-            from_lower = got_lower[:rows].astype(jnp.float32)
-            from_upper = got_upper[:rows].astype(jnp.float32)
+            toward_partner = jnp.where(first, upper_trace, lower_trace)
+            toward_diagonal = jnp.where(first, lower_trace, upper_trace)
+            width = toward_partner.shape[1]
+            got = swapped(jnp.concatenate([toward_partner, coarse, mine], axis=1), "tile")
+            from_diagonal = lax.ppermute(toward_diagonal, DUCT, diagonal_pairs)
+            crossing = lax.ppermute(toward_diagonal, DUCT, crossing_pairs)
+            from_partner = got[:, :width]
+            from_lower = jnp.where(first, from_diagonal, from_partner).astype(jnp.float32)
+            from_upper = jnp.where(first, from_partner, from_diagonal).astype(jnp.float32)
             faces = face_rows_of(gains, from_lower, from_upper)
-            first = tile_index == 0
             partner_lower = jnp.where(first, upper_trace, crossing).astype(jnp.float32)
             partner_upper = jnp.where(first, crossing, lower_trace).astype(jnp.float32)
-            partner_coarse = jnp.where(first, got_upper[rows:], got_lower[rows:])
+            partner_coarse = got[:, width : 2 * width]
+            theirs = got[:, 2 * width :]
             partner_faces = face_rows_of(partner_gains, partner_lower, partner_upper)
             own = projection_of(mine, faces, coarse)
             other = projection_of(theirs, partner_faces, partner_coarse)

time: 51.8 us -> 47.4 us (0.915)
  starting transfers between devices: 22.8 us -> 19.5 us
  matrix products: 6.9 us -> 5.9 us
  other arithmetic: 1.45 us -> 2.15 us
  waiting for transfers between devices: 14.7 us -> 14 us
    ppermute x3 -> x2, starting transfers between devices: 7.39 us -> 1.96 us  [the longest x1 1.29 us: local(): crossing = lax.ppermute(toward_diagonal, DUCT, crossing_pairs)]
    ppermute x2 -> x3, starting transfers between devices: 3.06 us -> 7.56 us  [swapped(): return lax.ppermute(shard, axis, [(0, 1), (1, 0)])]
    ppermute x6, starting transfers between devices: 12.3 us -> 10 us  [coarse_of(): lax.ppermute(piece, 'sub', [(i, (i + k) % sub_count) for i in range(sub_c...]
    ppermute x3 -> x2, waiting for transfers between devices: 3.34 us -> 1.49 us  [the longest x1 1.49 us: local(): crossing = lax.ppermute(toward_diagonal, DUCT, crossing_pairs)]
    ppermute x2 -> x3, waiting for transfers between devices: 2.48 us -> 3.77 us  [swapped(): return lax.ppermute(shard, axis, [(0, 1), (1, 0)])]
    dot_general x1, matrix products: 1.3 us -> 0.27 us  [local(): jnp.dot(masked_basis.T, masked_basis, preferred_element_type=jnp.float32)]
    convert_element_type x1, other arithmetic: 0.01 us -> 0.69 us  [local(): gains_low = (gains.T - gains_high.astype(jnp.float32)).astype(jnp.bfloat16)]
  transfers between devices with their start and end apart: 11 -> 11, of which waited for: 7 -> 7; matrix products, arithmetic and copies ran while one was open for 20% -> 11% of each run, Pallas kernels for 0% -> 0%
where the time goes in v9:
time: 47.4 us; the launch traced here: 47.1 us
  starting transfers between devices  19.5 us (41%)
  waiting for transfers between devices  14 us (30%)
  matrix products  5.9 us (12%)
  local copies, waits for them, and re-layouts  4.53 us (10%)
  other arithmetic  2.15 us (5%)
  between operations  1.06 us (2%)
    ppermute x6, starting transfers between devices, coarse_of(): lax.ppermute(piece, 'sub', [(i, (i + k) % sub_count) for i in range(sub_c...  10 us
    ppermute x6, waiting for transfers between devices, coarse_of(): lax.ppermute(piece, 'sub', [(i, (i + k) % sub_count) for i in range(sub_c...  8.7 us
    ppermute x3, starting transfers between devices, swapped(): return lax.ppermute(shard, axis, [(0, 1), (1, 0)])  7.56 us
    ppermute x3, waiting for transfers between devices, swapped(): return lax.ppermute(shard, axis, [(0, 1), (1, 0)])  3.77 us
    dot_general x1, matrix products, local(): base_solve = jnp.dot(inverse, source, preferred_element_type=jnp.float32)  2.35 us
    ppermute x1, waiting for transfers between devices, local(): crossing = lax.ppermute(toward_diagonal, DUCT, crossing_pairs)  1.49 us
    ppermute x1, starting transfers between devices, local(): crossing = lax.ppermute(toward_diagonal, DUCT, crossing_pairs)  1.29 us
    dot_general x1, matrix products, local(): jnp.dot(masked_basis, coarse, preferred_element_type=jnp.float32)  1.09 us
  transfers between devices with their start and end apart: 11, of which 7 were waited for; matrix products, arithmetic and copies ran while one was open for 11% of the time, Pallas kernels for 0%

profile of v9, /device:TPU:0, one launch (start us, length us, event | category | flops | bytes accessed | tf_op | source)
XLA Modules:
  0.0 47.1 jit_solution(15865872473684301960)
XLA Ops:
  0.7 0.7 %fusion.36 = (bf16[128,2]{0,1:T(2,128)(2,1)S(1)}, bf16[128,2]{0,1:T(2,128)(2,1)S(1)}) fusion(f32[1,2,128]{2,1,0:T(2,128)} %param.9), kind=kLoop, calls=%fused_computation.88 | loop fusion | flops 1024 | bytes 2048 | tf_op jit(solution)/shard_map/convert_element_type | solution.py:92
  1.7 1.0 %bitcast_select_fusion = bf16[1024,128]{1,0:T(8,128)(2,1)S(1)} fusion(bf16[1,1024,128]{2,1,0:T(8,128)(2,1)} %param.11, pred[128]{0:T(512)(128)(4,1)S(1)} %iota_compare_fusion), kind=kLoop, calls=%fused_computation.27 | loop fusion | flops 131072 | bytes 524416 | tf_op jit(solution)/shard_map/jit(_where)/select_n | solution.py:47
  2.7 2.4 %fusion.6 = f32[1024,256]{1,0:T(8,128)S(1)} fusion(bf16[1,1024,256]{2,1,0:T(8,128)(2,1)S(1)} %copy-done, bf16[1,1024,1024]{2,1,0:T(8,128)(2,1)} %param.8), kind=kOutput, calls=%fused_computation.22 | convolution fusion | flops 536870912 | bytes 3670016 | tf_op jit(solution)/shard_map/dot_general | solution.py:116
  5.4 3.0 %collective-permute-start.1 = (bf16[128,260]{1,0:T(8,128)(2,1)S(1)}, bf16[128,260]{1,0:T(8,128)(2,1)S(1)}, u32[]{:S(2)}, u32[]{:S(2)}) collective-permute-start(bf16[128,260]{1,0:T(8,128)(2,1)S(1)} %pad_maximum_fusion.8), channel_id=1, source_target_pairs={{0,2},{2,0},{1,3},{3,1},{4,6},{6,4},{5,7},{7,5},{8,10},{10,8},{9,1... | collective-permute-start | bytes 199688 | tf_op jit(solution)/shard_map/ppermute | solution.py:17
  8.8 1.1 %fusion.47 = (bf16[1024,128]{1,0:T(8,128)(2,1)S(1)}, bf16[1024,128]{1,0:T(8,128)(2,1)S(1)}) fusion(bf16[1024,1024]{1,0:T(8,128)(2,1)} %bitcast.78), kind=kLoop, calls=%fused_computation.102 | loop fusion | bytes 1048576 | tf_op jit(solution)/shard_map/slice | solution.py:62
  10.2 0.7 %gather_fusion.1 = bf16[128,128]{1,0:T(8,128)(2,1)S(1)} fusion(bf16[1024,128]{1,0:T(8,128)(2,1)S(1)} %bitcast_select_fusion, s32[1024]{0:T(1024)S(1)} %get-tuple-element.35), kind=kCustom, calls=%fused_computation.1 | custom fusion | bytes 66048 | tf_op jit(solution)/shard_map/gather | solution.py:59
  10.9 0.8 %gather_fusion = f32[128,256]{1,0:T(8,128)S(1)} fusion(f32[1024,256]{1,0:T(8,128)S(1)} %fusion.6, s32[1024]{0:T(1024)S(1)} %get-tuple-element.35), kind=kCustom, calls=%fused_computation | custom fusion | bytes 262656 | tf_op jit(solution)/shard_map/gather | solution.py:143
  11.6 0.7 %gather_fusion.3 = bf16[128,128]{1,0:T(8,128)(2,1)S(1)} fusion(bf16[1024,128]{1,0:T(8,128)(2,1)S(1)} %bitcast_select_fusion, s32[1024]{0:T(1024)S(1)} %get-tuple-element.34), kind=kCustom, calls=%fused_computation.3 | custom fusion | bytes 66048 | tf_op jit(solution)/shard_map/gather | solution.py:60
  12.3 0.8 %gather_fusion.2 = f32[128,256]{1,0:T(8,128)S(1)} fusion(f32[1024,256]{1,0:T(8,128)S(1)} %fusion.6, s32[1024]{0:T(1024)S(1)} %get-tuple-element.34), kind=kCustom, calls=%fused_computation.2 | custom fusion | bytes 262656 | tf_op jit(solution)/shard_map/gather | solution.py:146
  13.6 1.6 %collective-permute-start.2 = (bf16[128,256]{1,0:T(8,128)(2,1)S(1)}, bf16[128,256]{1,0:T(8,128)(2,1)S(1)}, u32[]{:S(2)}, u32[]{:S(2)}) collective-permute-start(bf16[128,256]{1,0:T(8,128)(2,1)S(1)} %get-tuple-element.16), channel_id=1, source_target_pairs={{0,4},{4,8},{8,12},{12,0},{1,5},{5,9},{9,13},{13,1},{2,6},{6,10},{... | collective-permute-start | bytes 196616 | tf_op jit(solution)/shard_map/ppermute | solution.py:79
  15.2 2.6 %collective-permute-start.3 = (bf16[128,256]{1,0:T(8,128)(2,1)S(1)}, bf16[128,256]{1,0:T(8,128)(2,1)S(1)}, u32[]{:S(2)}, u32[]{:S(2)}) collective-permute-start(bf16[128,256]{1,0:T(8,128)(2,1)S(1)} %get-tuple-element.18), channel_id=1, source_target_pairs={{0,8},{4,12},{8,0},{12,4},{1,9},{5,13},{9,1},{13,5},{2,10},{6,14},... | collective-permute-start | bytes 196616 | tf_op jit(solution)/shard_map/ppermute | solution.py:79
  17.8 1.3 %collective-permute-start.4 = (bf16[128,256]{1,0:T(8,128)(2,1)S(1)}, bf16[128,256]{1,0:T(8,128)(2,1)S(1)}, u32[]{:S(2)}, u32[]{:S(2)}) collective-permute-start(bf16[128,256]{1,0:T(8,128)(2,1)S(1)} %get-tuple-element.17), channel_id=1, source_target_pairs={{0,12},{4,0},{8,4},{12,8},{1,13},{5,1},{9,5},{13,9},{2,14},{6,2},{... | collective-permute-start | bytes 196616 | tf_op jit(solution)/shard_map/ppermute | solution.py:79
  19.3 0.8 %collective-permute-done.2 = bf16[128,256]{1,0:T(8,128)(2,1)S(1)} collective-permute-done((bf16[128,256]{1,0:T(8,128)(2,1)S(1)}, bf16[128,256]{1,0:T(8,128)(2,1)S(1)}, u32[]{:S(2)}, u32[]{:S(2)}) %collective-permute-start.2) | collective-permute-done | bytes 65568 | tf_op jit(solution)/shard_map/ppermute | solution.py:79
  20.2 2.7 %collective-permute-done.3 = bf16[128,256]{1,0:T(8,128)(2,1)S(1)} collective-permute-done((bf16[128,256]{1,0:T(8,128)(2,1)S(1)}, bf16[128,256]{1,0:T(8,128)(2,1)S(1)}, u32[]{:S(2)}, u32[]{:S(2)}) %collective-permute-start.3) | collective-permute-done | bytes 65568 | tf_op jit(solution)/shard_map/ppermute | solution.py:79
  23.5 0.7 %collective-permute-start.5 = (bf16[128,256]{1,0:T(8,128)(2,1)S(1)}, bf16[128,256]{1,0:T(8,128)(2,1)S(1)}, u32[]{:S(2)}, u32[]{:S(2)}) collective-permute-start(bf16[128,256]{1,0:T(8,128)(2,1)S(1)} %get-tuple-element.26), channel_id=1, source_target_pairs={{2,4},{4,2},{6,8},{8,6},{10,12},{12,10},{3,5},{5,3},{7,9},{9,7},{1... | collective-permute-start | bytes 196616 | tf_op jit(solution)/shard_map/ppermute | solution.py:154
  24.2 1.3 %collective-permute-start.7 = (bf16[128,256]{1,0:T(8,128)(2,1)S(1)}, bf16[128,256]{1,0:T(8,128)(2,1)S(1)}, u32[]{:S(2)}, u32[]{:S(2)}) collective-permute-start(bf16[128,256]{1,0:T(8,128)(2,1)S(1)} %get-tuple-element.26), channel_id=1, source_target_pairs={{2,6},{4,0},{6,10},{8,4},{10,14},{12,8},{3,7},{5,1},{7,11},{9,5},{... | collective-permute-start | bytes 196616 | tf_op jit(solution)/shard_map/ppermute | solution.py:155
  25.5 4.6 %collective-permute-start.6 = (bf16[128,896]{1,0:T(8,128)(2,1)S(1)}, bf16[128,896]{1,0:T(8,128)(2,1)S(1)}, u32[]{:S(2)}, u32[]{:S(2)}) collective-permute-start(bf16[128,896]{1,0:T(8,128)(2,1)S(1)} %pad_maximum_fusion.4), channel_id=1, source_target_pairs={{0,2},{2,0},{1,3},{3,1},{4,6},{6,4},{5,7},{7,5},{8,10},{10,8},{9,1... | collective-permute-start | bytes 688136 | tf_op jit(solution)/shard_map/ppermute | solution.py:17
  30.1 1.5 %collective-permute-done.7 = bf16[128,256]{1,0:T(8,128)(2,1)S(1)} collective-permute-done((bf16[128,256]{1,0:T(8,128)(2,1)S(1)}, bf16[128,256]{1,0:T(8,128)(2,1)S(1)}, u32[]{:S(2)}, u32[]{:S(2)}) %collective-permute-start.7) | collective-permute-done | bytes 65568 | tf_op jit(solution)/shard_map/ppermute | solution.py:155
  31.7 3.8 %collective-permute-done.6 = bf16[128,896]{1,0:T(8,128)(2,1)S(1)} collective-permute-done((bf16[128,896]{1,0:T(8,128)(2,1)S(1)}, bf16[128,896]{1,0:T(8,128)(2,1)S(1)}, u32[]{:S(2)}, u32[]{:S(2)}) %collective-permute-start.6) | collective-permute-done | bytes 229408 | tf_op jit(solution)/shard_map/ppermute | solution.py:17
  36.4 3.5 %collective-permute-start.10 = (bf16[128,256]{1,0:T(8,128)(2,1)S(1)}, bf16[128,256]{1,0:T(8,128)(2,1)S(1)}, u32[]{:S(2)}, u32[]{:S(2)}) collective-permute-start(bf16[128,256]{1,0:T(8,128)(2,1)S(1)} %get-tuple-element.14), channel_id=1, source_target_pairs={{0,12},{4,0},{8,4},{12,8},{1,13},{5,1},{9,5},{13,9},{2,14},{6,2},{... | collective-permute-start | bytes 196616 | tf_op jit(solution)/shard_map/ppermute | solution.py:79
  40.0 0.9 %collective-permute-start.9 = (bf16[128,256]{1,0:T(8,128)(2,1)S(1)}, bf16[128,256]{1,0:T(8,128)(2,1)S(1)}, u32[]{:S(2)}, u32[]{:S(2)}) collective-permute-start(bf16[128,256]{1,0:T(8,128)(2,1)S(1)} %get-tuple-element.15), channel_id=1, source_target_pairs={{0,8},{4,12},{8,0},{12,4},{1,9},{5,13},{9,1},{13,5},{2,10},{6,14},... | collective-permute-start | bytes 196616 | tf_op jit(solution)/shard_map/ppermute | solution.py:79
  41.2 0.7 %collective-permute-done.10 = bf16[128,256]{1,0:T(8,128)(2,1)S(1)} collective-permute-done((bf16[128,256]{1,0:T(8,128)(2,1)S(1)}, bf16[128,256]{1,0:T(8,128)(2,1)S(1)}, u32[]{:S(2)}, u32[]{:S(2)}) %collective-permute-start.10) | collective-permute-done | bytes 65568 | tf_op jit(solution)/shard_map/ppermute | solution.py:79
  41.9 4.2 %collective-permute-done.8 = bf16[128,256]{1,0:T(8,128)(2,1)S(1)} collective-permute-done((bf16[128,256]{1,0:T(8,128)(2,1)S(1)}, bf16[128,256]{1,0:T(8,128)(2,1)S(1)}, u32[]{:S(2)}, u32[]{:S(2)}) %collective-permute-start.8) | collective-permute-done | bytes 65568 | tf_op jit(solution)/shard_map/ppermute | solution.py:79
  46.0 1.1 %fusion.1 = bf16[1,1024,256]{2,1,0:T(8,128)(2,1)} fusion(f32[1024,256]{1,0:T(8,128)S(1)} %convolution_add_fusion, bf16[1024,128]{1,0:T(8,128)(2,1)S(1)} %bitcast_select_fusion, bf16[128,256]{1,0:T(8,128)(2,1)S(1)} %collective-permute-done.10, bf16[128,256]{1,0:T(8,128)(2,1)S(1)} %collective-permute-done.9, bf16[128,256]{1,0:T(8,128)(2,1)S(1)} %collective-permute-done.8, ...), kind=kOutput, calls=%fused_computation.7 | convolution fusion | flops 67895296 | bytes 2097156 | tf_op jit(solution)/shard_map/dot_general | solution.py:138
  (47 shorter events, 3.7 us)
Async XLA Ops:
  0.0 2.7 %copy-start = (bf16[1,1024,256]{2,1,0:T(8,128)(2,1)S(1)}, bf16[1,1024,256]{2,1,0:T(8,128)(2,1)}, u32[]{:S(2)}) copy-start(bf16[1,1024,256]{2,1,0:T(8,128)(2,1)} %param.7) | copy-start | bytes 1572868
  2.7 5.8 %copy-start.2 = (bf16[4,1,64,1,256]{4,2,3,1,0:T(8,128)(2,1)S(1)}, bf16[4,1,64,1,256]{4,2,3,1,0:T(8,128)(2,1)}, u32[]{:S(2)}) copy-start(bf16[4,1,64,1,256]{4,2,3,1,0:T(8,128)(2,1)} %param.13) | copy-start | bytes 393220
  2.7 5.8 %copy-start.1 = (bf16[1,1024,128]{2,1,0:T(8,128)(2,1)S(1)}, bf16[1,1024,128]{2,1,0:T(8,128)(2,1)}, u32[]{:S(2)}) copy-start(bf16[1,1024,128]{2,1,0:T(8,128)(2,1)} %param.11) | copy-start | bytes 786436
  5.1 3.7 %copy-start.3 = (f32[1,2,128]{2,1,0:T(2,128)S(1)}, f32[1,2,128]{2,1,0:T(2,128)}, u32[]{:S(2)}) copy-start(f32[1,2,128]{2,1,0:T(2,128)} %param.9) | copy-start | bytes 3076
  5.1 3.7 %copy-start.4 = (s32[1,2,128]{2,1,0:T(2,128)S(1)}, s32[1,2,128]{2,1,0:T(2,128)}, u32[]{:S(2)}) copy-start(s32[1,2,128]{2,1,0:T(2,128)} %param.10) | copy-start | bytes 3076
  5.4 7.7 %collective-permute-start.1 = (bf16[128,260]{1,0:T(8,128)(2,1)S(1)}, bf16[128,260]{1,0:T(8,128)(2,1)S(1)}, u32[]{:S(2)}, u32[]{:S(2)}) collective-permute-start(bf16[128,260]{1,0:T(8,128)(2,1)S(1)} %pad_maximum_fusion.8), channel_id=1, source_target_pairs={{0,2},{2,0},{1,3},{3,1},{4,6},{6,4},{5,7},{7,5},{8,10},{10,8},{9,1... | collective-permute-start | bytes 199688 | tf_op jit(solution)/shard_map/ppermute | solution.py:17
  8.5 4.8 %collective-permute-start = (bf16[4,64,256]{2,1,0:T(8,128)(2,1)S(1)}, bf16[4,64,256]{2,1,0:T(8,128)(2,1)S(1)}, u32[]{:S(2)}, u32[]{:S(2)}) collective-permute-start(bf16[4,64,256]{2,1,0:T(8,128)(2,1)S(1)} %bitcast.77), channel_id=1, source_target_pairs={{0,1},{1,0},{2,3},{3,2},{4,5},{5,4},{6,7},{7,6},{8,9},{9,8},{10,11... | collective-permute-start | bytes 393224 | tf_op jit(solution)/shard_map/ppermute | solution.py:17
  13.6 6.6 %collective-permute-start.2 = (bf16[128,256]{1,0:T(8,128)(2,1)S(1)}, bf16[128,256]{1,0:T(8,128)(2,1)S(1)}, u32[]{:S(2)}, u32[]{:S(2)}) collective-permute-start(bf16[128,256]{1,0:T(8,128)(2,1)S(1)} %get-tuple-element.16), channel_id=1, source_target_pairs={{0,4},{4,8},{8,12},{12,0},{1,5},{5,9},{9,13},{13,1},{2,6},{6,10},{... | collective-permute-start | bytes 196616 | tf_op jit(solution)/shard_map/ppermute | solution.py:79
  15.2 7.7 %collective-permute-start.3 = (bf16[128,256]{1,0:T(8,128)(2,1)S(1)}, bf16[128,256]{1,0:T(8,128)(2,1)S(1)}, u32[]{:S(2)}, u32[]{:S(2)}) collective-permute-start(bf16[128,256]{1,0:T(8,128)(2,1)S(1)} %get-tuple-element.18), channel_id=1, source_target_pairs={{0,8},{4,12},{8,0},{12,4},{1,9},{5,13},{9,1},{13,5},{2,10},{6,14},... | collective-permute-start | bytes 196616 | tf_op jit(solution)/shard_map/ppermute | solution.py:79
  17.8 5.4 %collective-permute-start.4 = (bf16[128,256]{1,0:T(8,128)(2,1)S(1)}, bf16[128,256]{1,0:T(8,128)(2,1)S(1)}, u32[]{:S(2)}, u32[]{:S(2)}) collective-permute-start(bf16[128,256]{1,0:T(8,128)(2,1)S(1)} %get-tuple-element.17), channel_id=1, source_target_pairs={{0,12},{4,0},{8,4},{12,8},{1,13},{5,1},{9,5},{13,9},{2,14},{6,2},{... | collective-permute-start | bytes 196616 | tf_op jit(solution)/shard_map/ppermute | solution.py:79
  23.5 8.2 %collective-permute-start.5 = (bf16[128,256]{1,0:T(8,128)(2,1)S(1)}, bf16[128,256]{1,0:T(8,128)(2,1)S(1)}, u32[]{:S(2)}, u32[]{:S(2)}) collective-permute-start(bf16[128,256]{1,0:T(8,128)(2,1)S(1)} %get-tuple-element.26), channel_id=1, source_target_pairs={{2,4},{4,2},{6,8},{8,6},{10,12},{12,10},{3,5},{5,3},{7,9},{9,7},{1... | collective-permute-start | bytes 196616 | tf_op jit(solution)/shard_map/ppermute | solution.py:154
  24.2 7.4 %collective-permute-start.7 = (bf16[128,256]{1,0:T(8,128)(2,1)S(1)}, bf16[128,256]{1,0:T(8,128)(2,1)S(1)}, u32[]{:S(2)}, u32[]{:S(2)}) collective-permute-start(bf16[128,256]{1,0:T(8,128)(2,1)S(1)} %get-tuple-element.26), channel_id=1, source_target_pairs={{2,6},{4,0},{6,10},{8,4},{10,14},{12,8},{3,7},{5,1},{7,11},{9,5},{... | collective-permute-start | bytes 196616 | tf_op jit(solution)/shard_map/ppermute | solution.py:155
  25.5 9.9 %collective-permute-start.6 = (bf16[128,896]{1,0:T(8,128)(2,1)S(1)}, bf16[128,896]{1,0:T(8,128)(2,1)S(1)}, u32[]{:S(2)}, u32[]{:S(2)}) collective-permute-start(bf16[128,896]{1,0:T(8,128)(2,1)S(1)} %pad_maximum_fusion.4), channel_id=1, source_target_pairs={{0,2},{2,0},{1,3},{3,1},{4,6},{6,4},{5,7},{7,5},{8,10},{10,8},{9,1... | collective-permute-start | bytes 688136 | tf_op jit(solution)/shard_map/ppermute | solution.py:17
  36.4 5.4 %collective-permute-start.10 = (bf16[128,256]{1,0:T(8,128)(2,1)S(1)}, bf16[128,256]{1,0:T(8,128)(2,1)S(1)}, u32[]{:S(2)}, u32[]{:S(2)}) collective-permute-start(bf16[128,256]{1,0:T(8,128)(2,1)S(1)} %get-tuple-element.14), channel_id=1, source_target_pairs={{0,12},{4,0},{8,4},{12,8},{1,13},{5,1},{9,5},{13,9},{2,14},{6,2},{... | collective-permute-start | bytes 196616 | tf_op jit(solution)/shard_map/ppermute | solution.py:79
  40.0 6.1 %collective-permute-start.8 = (bf16[128,256]{1,0:T(8,128)(2,1)S(1)}, bf16[128,256]{1,0:T(8,128)(2,1)S(1)}, u32[]{:S(2)}, u32[]{:S(2)}) collective-permute-start(bf16[128,256]{1,0:T(8,128)(2,1)S(1)} %get-tuple-element.13), channel_id=1, source_target_pairs={{0,4},{4,8},{8,12},{12,0},{1,5},{5,9},{9,13},{13,1},{2,6},{6,10},{... | collective-permute-start | bytes 196616 | tf_op jit(solution)/shard_map/ppermute | solution.py:79
  40.0 6.1 %collective-permute-start.9 = (bf16[128,256]{1,0:T(8,128)(2,1)S(1)}, bf16[128,256]{1,0:T(8,128)(2,1)S(1)}, u32[]{:S(2)}, u32[]{:S(2)}) collective-permute-start(bf16[128,256]{1,0:T(8,128)(2,1)S(1)} %get-tuple-element.15), channel_id=1, source_target_pairs={{0,8},{4,12},{8,0},{12,4},{1,9},{5,13},{9,1},{13,5},{2,10},{6,14},... | collective-permute-start | bytes 196616 | tf_op jit(solution)/shard_map/ppermute | solution.py:79

commit v10 on v6

--- a/solution.py
+++ b/solution.py
@@ -88,8 +88,9 @@
         sends = jnp.dot(masked_basis.T, face_inverse, preferred_element_type=jnp.float32)
         keeps = jnp.dot(masked_basis.T, masked_basis, preferred_element_type=jnp.float32)
         mine = jnp.concatenate([sends, keeps], axis=1).astype(jnp.bfloat16)
-        theirs = swapped(mine, "tile")
-        partner_gains = swapped(gains, "tile")
+        gains_high = gains.T.astype(jnp.bfloat16)
+        gains_low = (gains.T - gains_high.astype(jnp.float32)).astype(jnp.bfloat16)
+        message = jnp.concatenate([mine, gains_high, gains_low], axis=1)
         duct_pairs = []
         peers = lax.axis_size(DUCT)
         for i in range(peers):
@@ -111,6 +112,13 @@
     base_solve = jnp.dot(inverse, source, preferred_element_type=jnp.float32)
     local_solve = base_solve
     inputs = gathered(coarse_input(local_solve.astype(jnp.bfloat16)), "tile", 0)
+    if pairwise:
+        message, inputs = lax.optimization_barrier((message, inputs))
+        got = swapped(message, "tile")
+        theirs = got[:, : mine.shape[1]]
+        tail = got[:, mine.shape[1] :].astype(jnp.float32)
+        pair = gains.shape[0]
+        partner_gains = (tail[:, :pair] + tail[:, pair:]).T
     earlier = None
     for cycle_index in range(ROUNDS):
         coarse = coarse_of(inputs)

time: 47.8 us -> 47.9 us (level)
  starting transfers between devices: 24 us -> 23.5 us
    ppermute x4 -> x3, starting transfers between devices: 5.47 us -> 3.47 us  [swapped(): return lax.ppermute(shard, axis, [(0, 1), (1, 0)])]
    ppermute x6, starting transfers between devices: 11.4 us -> 12.6 us  [coarse_of(): lax.ppermute(piece, 'sub', [(i, (i + k) % sub_count) for i in range(sub_c...]
  transfers between devices with their start and end apart: 13 -> 12, of which waited for: 7 -> 6; matrix products, arithmetic and copies ran while one was open for 18% -> 18% of each run, Pallas kernels for 0% -> 0%
where the time goes in v10:
time: 47.9 us; the launch traced here: 47.7 us
  starting transfers between devices  23.5 us (49%)
  waiting for transfers between devices  12.1 us (25%)
  matrix products  5.89 us (12%)
  local copies, waits for them, and re-layouts  4.53 us (9%)
  between operations  1.06 us (2%)
  other arithmetic  0.61 us (1%)
    ppermute x6, starting transfers between devices, coarse_of(): lax.ppermute(piece, 'sub', [(i, (i + k) % sub_count) for i in range(sub_c...  12.6 us
    ppermute x6, waiting for transfers between devices, coarse_of(): lax.ppermute(piece, 'sub', [(i, (i + k) % sub_count) for i in range(sub_c...  8.79 us
    ppermute x2, starting transfers between devices, passed_along(): return lax.ppermute(shard, DUCT, pairs)  6.11 us
    ppermute x3, starting transfers between devices, swapped(): return lax.ppermute(shard, axis, [(0, 1), (1, 0)])  3.47 us
    ppermute x2, waiting for transfers between devices, passed_along(): return lax.ppermute(shard, DUCT, pairs)  3.33 us
    dot_general x1, matrix products, local(): base_solve = jnp.dot(inverse, source, preferred_element_type=jnp.float32)  2.34 us
    ppermute x1, starting transfers between devices, local(): lax.ppermute(jnp.where(tile_index == 0, lower_trace, upper_trace), DUCT,...  1.29 us
    dot_general x1, matrix products, local(): jnp.dot(masked_basis, coarse, preferred_element_type=jnp.float32)  1.09 us
  transfers between devices with their start and end apart: 12, of which 6 were waited for; matrix products, arithmetic and copies ran while one was open for 18% of the time, Pallas kernels for 0%

profile of v10, /device:TPU:0, one launch (start us, length us, event | category | flops | bytes accessed | tf_op | source)
XLA Modules:
  0.0 47.7 jit_solution(13497151863194026525)
XLA Ops:
  0.0 0.5 collective-permute-start
  1.1 2.3 %fusion.6 = f32[1024,256]{1,0:T(8,128)S(1)} fusion(bf16[1,1024,256]{2,1,0:T(8,128)(2,1)S(1)} %copy-done, bf16[1,1024,1024]{2,1,0:T(8,128)(2,1)} %param.8), kind=kOutput, calls=%fused_computation.22 | convolution fusion | flops 536870912 | bytes 3670016 | tf_op jit(solution)/shard_map/dot_general | solution.py:112
  3.8 2.9 %collective-permute-start.1 = (bf16[128,256]{1,0:T(8,128)(2,1)S(1)}, bf16[128,256]{1,0:T(8,128)(2,1)S(1)}, u32[]{:S(2)}, u32[]{:S(2)}) collective-permute-start(bf16[128,256]{1,0:T(8,128)(2,1)S(1)} %convolution_convert_fusion.2), channel_id=1, source_target_pairs={{0,2},{2,0},{1,3},{3,1},{4,6},{6,4},{5,7},{7,5},{8,10},{10,8},{9,1... | collective-permute-start | bytes 196616 | tf_op jit(solution)/shard_map/ppermute | solution.py:17
  7.1 0.8 %gather_fusion = f32[128,256]{1,0:T(8,128)S(1)} fusion(f32[1024,256]{1,0:T(8,128)S(1)} %fusion.6, s32[1024]{0:T(1024)S(1)} %get-tuple-element.38), kind=kCustom, calls=%fused_computation | custom fusion | bytes 262656 | tf_op jit(solution)/shard_map/gather | solution.py:133
  7.9 0.7 %gather_fusion.1 = bf16[128,128]{1,0:T(8,128)(2,1)S(1)} fusion(bf16[1024,128]{1,0:T(8,128)(2,1)S(1)} %bitcast_select_fusion, s32[1024]{0:T(1024)S(1)} %get-tuple-element.38), kind=kCustom, calls=%fused_computation.1 | custom fusion | bytes 66048 | tf_op jit(solution)/shard_map/gather | solution.py:60
  8.6 0.8 %gather_fusion.2 = f32[128,256]{1,0:T(8,128)S(1)} fusion(f32[1024,256]{1,0:T(8,128)S(1)} %fusion.6, s32[1024]{0:T(1024)S(1)} %get-tuple-element.37), kind=kCustom, calls=%fused_computation.2 | custom fusion | bytes 262656 | tf_op jit(solution)/shard_map/gather | solution.py:130
  9.4 0.7 %gather_fusion.3 = bf16[128,128]{1,0:T(8,128)(2,1)S(1)} fusion(bf16[1024,128]{1,0:T(8,128)(2,1)S(1)} %bitcast_select_fusion, s32[1024]{0:T(1024)S(1)} %get-tuple-element.37), kind=kCustom, calls=%fused_computation.3 | custom fusion | bytes 66048 | tf_op jit(solution)/shard_map/gather | solution.py:59
  10.1 1.1 %fusion.47 = (bf16[1024,128]{1,0:T(8,128)(2,1)S(1)}, bf16[1024,128]{1,0:T(8,128)(2,1)S(1)}) fusion(bf16[1024,1024]{1,0:T(8,128)(2,1)} %bitcast.78), kind=kLoop, calls=%fused_computation.103 | loop fusion | bytes 1048576 | tf_op jit(solution)/shard_map/slice | solution.py:62
  11.4 0.3 convolution_convert_fusion.3
  12.3 4.2 %collective-permute-start.4 = (bf16[128,256]{1,0:T(8,128)(2,1)S(1)}, bf16[128,256]{1,0:T(8,128)(2,1)S(1)}, u32[]{:S(2)}, u32[]{:S(2)}) collective-permute-start(bf16[128,256]{1,0:T(8,128)(2,1)S(1)} %get-tuple-element.19), channel_id=1, source_target_pairs={{0,12},{4,0},{8,4},{12,8},{1,13},{5,1},{9,5},{13,9},{2,14},{6,2},{... | collective-permute-start | bytes 196616 | tf_op jit(solution)/shard_map/ppermute | solution.py:79
  16.4 1.0 %collective-permute-start.2 = (bf16[128,256]{1,0:T(8,128)(2,1)S(1)}, bf16[128,256]{1,0:T(8,128)(2,1)S(1)}, u32[]{:S(2)}, u32[]{:S(2)}) collective-permute-start(bf16[128,256]{1,0:T(8,128)(2,1)S(1)} %get-tuple-element.18), channel_id=1, source_target_pairs={{0,4},{4,8},{8,12},{12,0},{1,5},{5,9},{9,13},{13,1},{2,6},{6,10},{... | collective-permute-start | bytes 196616 | tf_op jit(solution)/shard_map/ppermute | solution.py:79
  17.7 1.2 %collective-permute-done.4 = bf16[128,256]{1,0:T(8,128)(2,1)S(1)} collective-permute-done((bf16[128,256]{1,0:T(8,128)(2,1)S(1)}, bf16[128,256]{1,0:T(8,128)(2,1)S(1)}, u32[]{:S(2)}, u32[]{:S(2)}) %collective-permute-start.4) | collective-permute-done | bytes 65568 | tf_op jit(solution)/shard_map/ppermute | solution.py:79
  18.9 3.7 %collective-permute-done.3 = bf16[128,256]{1,0:T(8,128)(2,1)S(1)} collective-permute-done((bf16[128,256]{1,0:T(8,128)(2,1)S(1)}, bf16[128,256]{1,0:T(8,128)(2,1)S(1)}, u32[]{:S(2)}, u32[]{:S(2)}) %collective-permute-start.3) | collective-permute-done | bytes 65568 | tf_op jit(solution)/shard_map/ppermute | solution.py:79
  23.0 1.3 %collective-permute-start.8 = (bf16[128,256]{1,0:T(8,128)(2,1)S(1)}, bf16[128,256]{1,0:T(8,128)(2,1)S(1)}, u32[]{:S(2)}, u32[]{:S(2)}) collective-permute-start(bf16[128,256]{1,0:T(8,128)(2,1)S(1)} %get-tuple-element.35), channel_id=1, source_target_pairs={{2,6},{4,0},{6,10},{8,4},{10,14},{12,8},{3,7},{5,1},{7,11},{9,5},{... | collective-permute-start | bytes 196616 | tf_op jit(solution)/shard_map/ppermute | solution.py:139
  24.3 1.3 %collective-permute-start.6 = (bf16[256,256]{1,0:T(8,128)(2,1)S(1)}, bf16[256,256]{1,0:T(8,128)(2,1)S(1)}, u32[]{:S(2)}, u32[]{:S(2)}) collective-permute-start(bf16[256,256]{1,0:T(8,128)(2,1)S(1)} %get-tuple-element.30), channel_id=1, source_target_pairs={{2,0},{4,2},{6,4},{8,6},{10,8},{12,10},{14,12},{3,1},{5,3},{7,5},{... | collective-permute-start | bytes 393224 | tf_op jit(solution)/shard_map/ppermute | solution.py:13
  25.6 4.8 %collective-permute-start.5 = (bf16[256,256]{1,0:T(8,128)(2,1)S(1)}, bf16[256,256]{1,0:T(8,128)(2,1)S(1)}, u32[]{:S(2)}, u32[]{:S(2)}) collective-permute-start(bf16[256,256]{1,0:T(8,128)(2,1)S(1)} %get-tuple-element.29), channel_id=1, source_target_pairs={{0,2},{2,4},{4,6},{6,8},{8,10},{10,12},{12,14},{1,3},{3,5},{5,7},{... | collective-permute-start | bytes 393224 | tf_op jit(solution)/shard_map/ppermute | solution.py:13
  30.6 0.9 %collective-permute-done.6 = bf16[256,256]{1,0:T(8,128)(2,1)S(1)} collective-permute-done((bf16[256,256]{1,0:T(8,128)(2,1)S(1)}, bf16[256,256]{1,0:T(8,128)(2,1)S(1)}, u32[]{:S(2)}, u32[]{:S(2)}) %collective-permute-start.6) | collective-permute-done | bytes 131104 | tf_op jit(solution)/shard_map/ppermute | solution.py:13
  31.5 2.4 %collective-permute-done.5 = bf16[256,256]{1,0:T(8,128)(2,1)S(1)} collective-permute-done((bf16[256,256]{1,0:T(8,128)(2,1)S(1)}, bf16[256,256]{1,0:T(8,128)(2,1)S(1)}, u32[]{:S(2)}, u32[]{:S(2)}) %collective-permute-start.5) | collective-permute-done | bytes 131104 | tf_op jit(solution)/shard_map/ppermute | solution.py:13
  35.0 5.5 %collective-permute-start.11 = (bf16[128,256]{1,0:T(8,128)(2,1)S(1)}, bf16[128,256]{1,0:T(8,128)(2,1)S(1)}, u32[]{:S(2)}, u32[]{:S(2)}) collective-permute-start(bf16[128,256]{1,0:T(8,128)(2,1)S(1)} %get-tuple-element.16), channel_id=1, source_target_pairs={{0,12},{4,0},{8,4},{12,8},{1,13},{5,1},{9,5},{13,9},{2,14},{6,2},{... | collective-permute-start | bytes 196616 | tf_op jit(solution)/shard_map/ppermute | solution.py:79
  40.5 1.9 %collective-permute-start.9 = (bf16[128,256]{1,0:T(8,128)(2,1)S(1)}, bf16[128,256]{1,0:T(8,128)(2,1)S(1)}, u32[]{:S(2)}, u32[]{:S(2)}) collective-permute-start(bf16[128,256]{1,0:T(8,128)(2,1)S(1)} %get-tuple-element.15), channel_id=1, source_target_pairs={{0,4},{4,8},{8,12},{12,0},{1,5},{5,9},{9,13},{13,1},{2,6},{6,10},{... | collective-permute-start | bytes 196616 | tf_op jit(solution)/shard_map/ppermute | solution.py:79
  42.4 0.3 convolution_add_fusion
  42.7 3.0 %collective-permute-done.10 = bf16[128,256]{1,0:T(8,128)(2,1)S(1)} collective-permute-done((bf16[128,256]{1,0:T(8,128)(2,1)S(1)}, bf16[128,256]{1,0:T(8,128)(2,1)S(1)}, u32[]{:S(2)}, u32[]{:S(2)}) %collective-permute-start.10) | collective-permute-done | bytes 65568 | tf_op jit(solution)/shard_map/ppermute | solution.py:79
  45.7 0.9 %collective-permute-done.9 = bf16[128,256]{1,0:T(8,128)(2,1)S(1)} collective-permute-done((bf16[128,256]{1,0:T(8,128)(2,1)S(1)}, bf16[128,256]{1,0:T(8,128)(2,1)S(1)}, u32[]{:S(2)}, u32[]{:S(2)}) %collective-permute-start.9) | collective-permute-done | bytes 65568 | tf_op jit(solution)/shard_map/ppermute | solution.py:79
  46.6 1.1 %fusion.1 = bf16[1,1024,256]{2,1,0:T(8,128)(2,1)} fusion(f32[1024,256]{1,0:T(8,128)S(1)} %convolution_add_fusion, bf16[1024,128]{1,0:T(8,128)(2,1)S(1)} %bitcast_select_fusion, bf16[128,256]{1,0:T(8,128)(2,1)S(1)} %collective-permute-done.11, bf16[128,256]{1,0:T(8,128)(2,1)S(1)} %collective-permute-done.10, bf16[128,256]{1,0:T(8,128)(2,1)S(1)} %collective-permute-done.9, ...), kind=kOutput, calls=%fused_computation.7 | convolution fusion | flops 67895296 | bytes 2097156 | tf_op jit(solution)/shard_map/dot_general | solution.py:125
  (51 shorter events, 3.1 us)
Async XLA Ops:
  0.0 1.1 %copy-start = (bf16[1,1024,256]{2,1,0:T(8,128)(2,1)S(1)}, bf16[1,1024,256]{2,1,0:T(8,128)(2,1)}, u32[]{:S(2)}) copy-start(bf16[1,1024,256]{2,1,0:T(8,128)(2,1)} %param.7) | copy-start | bytes 1572868
  0.0 12.0 %collective-permute-start = (bf16[4,64,256]{2,1,0:T(8,128)(2,1)}, bf16[4,64,256]{2,1,0:T(8,128)(2,1)S(1)}, u32[]{:S(2)}, u32[]{:S(2)}) collective-permute-start(bf16[4,64,256]{2,1,0:T(8,128)(2,1)} %bitcast.77), channel_id=1, source_target_pairs={{0,1},{1,0},{2,3},{3,2},{4,5},{5,4},{6,7},{7,6},{8,9},{9,8},{10,11... | collective-permute-start | bytes 393224 | tf_op jit(solution)/shard_map/ppermute | solution.py:17
  1.1 2.4 %copy-start.1 = (bf16[1,1024,128]{2,1,0:T(8,128)(2,1)S(1)}, bf16[1,1024,128]{2,1,0:T(8,128)(2,1)}, u32[]{:S(2)}) copy-start(bf16[1,1024,128]{2,1,0:T(8,128)(2,1)} %param.11) | copy-start | bytes 786436
  3.5 3.6 %copy-start.4 = (s32[1,2,128]{2,1,0:T(2,128)S(1)}, s32[1,2,128]{2,1,0:T(2,128)}, u32[]{:S(2)}) copy-start(s32[1,2,128]{2,1,0:T(2,128)} %param.10) | copy-start | bytes 3076
  3.8 6.2 %copy-start.3 = (f32[1,2,128]{2,1,0:T(2,128)S(1)}, f32[1,2,128]{2,1,0:T(2,128)}, u32[]{:S(2)}) copy-start(f32[1,2,128]{2,1,0:T(2,128)} %param.9) | copy-start | bytes 3076
  3.8 8.0 %collective-permute-start.1 = (bf16[128,256]{1,0:T(8,128)(2,1)S(1)}, bf16[128,256]{1,0:T(8,128)(2,1)S(1)}, u32[]{:S(2)}, u32[]{:S(2)}) collective-permute-start(bf16[128,256]{1,0:T(8,128)(2,1)S(1)} %convolution_convert_fusion.2), channel_id=1, source_target_pairs={{0,2},{2,0},{1,3},{3,1},{4,6},{6,4},{5,7},{7,5},{8,10},{10,8},{9,1... | collective-permute-start | bytes 196616 | tf_op jit(solution)/shard_map/ppermute | solution.py:17
  8.6 3.4 %copy-start.2 = (bf16[4,1,64,1,256]{4,2,3,1,0:T(8,128)(2,1)S(1)}, bf16[4,1,64,1,256]{4,2,3,1,0:T(8,128)(2,1)}, u32[]{:S(2)}) copy-start(bf16[4,1,64,1,256]{4,2,3,1,0:T(8,128)(2,1)} %param.13) | copy-start | bytes 393220
  11.9 5.6 %collective-permute-start.7 = (bf16[128,388]{1,0:T(8,128)(2,1)S(1)}, bf16[128,388]{1,0:T(8,128)(2,1)S(1)}, u32[]{:S(2)}, u32[]{:S(2)}) collective-permute-start(bf16[128,388]{1,0:T(8,128)(2,1)S(1)} %pad_maximum_fusion.8), channel_id=1, source_target_pairs={{0,2},{2,0},{1,3},{3,1},{4,6},{6,4},{5,7},{7,5},{8,10},{10,8},{9,1... | collective-permute-start | bytes 297992 | tf_op jit(solution)/shard_map/ppermute | solution.py:17
  12.3 6.7 %collective-permute-start.4 = (bf16[128,256]{1,0:T(8,128)(2,1)S(1)}, bf16[128,256]{1,0:T(8,128)(2,1)S(1)}, u32[]{:S(2)}, u32[]{:S(2)}) collective-permute-start(bf16[128,256]{1,0:T(8,128)(2,1)S(1)} %get-tuple-element.19), channel_id=1, source_target_pairs={{0,12},{4,0},{8,4},{12,8},{1,13},{5,1},{9,5},{13,9},{2,14},{6,2},{... | collective-permute-start | bytes 196616 | tf_op jit(solution)/shard_map/ppermute | solution.py:79
  16.4 6.2 %collective-permute-start.3 = (bf16[128,256]{1,0:T(8,128)(2,1)S(1)}, bf16[128,256]{1,0:T(8,128)(2,1)S(1)}, u32[]{:S(2)}, u32[]{:S(2)}) collective-permute-start(bf16[128,256]{1,0:T(8,128)(2,1)S(1)} %get-tuple-element.20), channel_id=1, source_target_pairs={{0,8},{4,12},{8,0},{12,4},{1,9},{5,13},{9,1},{13,5},{2,10},{6,14},... | collective-permute-start | bytes 196616 | tf_op jit(solution)/shard_map/ppermute | solution.py:79
  16.4 6.2 %collective-permute-start.2 = (bf16[128,256]{1,0:T(8,128)(2,1)S(1)}, bf16[128,256]{1,0:T(8,128)(2,1)S(1)}, u32[]{:S(2)}, u32[]{:S(2)}) collective-permute-start(bf16[128,256]{1,0:T(8,128)(2,1)S(1)} %get-tuple-element.18), channel_id=1, source_target_pairs={{0,4},{4,8},{8,12},{12,0},{1,5},{5,9},{9,13},{13,1},{2,6},{6,10},{... | collective-permute-start | bytes 196616 | tf_op jit(solution)/shard_map/ppermute | solution.py:79
  23.0 7.5 %collective-permute-start.8 = (bf16[128,256]{1,0:T(8,128)(2,1)S(1)}, bf16[128,256]{1,0:T(8,128)(2,1)S(1)}, u32[]{:S(2)}, u32[]{:S(2)}) collective-permute-start(bf16[128,256]{1,0:T(8,128)(2,1)S(1)} %get-tuple-element.35), channel_id=1, source_target_pairs={{2,6},{4,0},{6,10},{8,4},{10,14},{12,8},{3,7},{5,1},{7,11},{9,5},{... | collective-permute-start | bytes 196616 | tf_op jit(solution)/shard_map/ppermute | solution.py:139
  24.3 7.1 %collective-permute-start.6 = (bf16[256,256]{1,0:T(8,128)(2,1)S(1)}, bf16[256,256]{1,0:T(8,128)(2,1)S(1)}, u32[]{:S(2)}, u32[]{:S(2)}) collective-permute-start(bf16[256,256]{1,0:T(8,128)(2,1)S(1)} %get-tuple-element.30), channel_id=1, source_target_pairs={{2,0},{4,2},{6,4},{8,6},{10,8},{12,10},{14,12},{3,1},{5,3},{7,5},{... | collective-permute-start | bytes 393224 | tf_op jit(solution)/shard_map/ppermute | solution.py:13
  25.6 8.4 %collective-permute-start.5 = (bf16[256,256]{1,0:T(8,128)(2,1)S(1)}, bf16[256,256]{1,0:T(8,128)(2,1)S(1)}, u32[]{:S(2)}, u32[]{:S(2)}) collective-permute-start(bf16[256,256]{1,0:T(8,128)(2,1)S(1)} %get-tuple-element.29), channel_id=1, source_target_pairs={{0,2},{2,4},{4,6},{6,8},{8,10},{10,12},{12,14},{1,3},{3,5},{5,7},{... | collective-permute-start | bytes 393224 | tf_op jit(solution)/shard_map/ppermute | solution.py:13
  35.0 7.7 %collective-permute-start.11 = (bf16[128,256]{1,0:T(8,128)(2,1)S(1)}, bf16[128,256]{1,0:T(8,128)(2,1)S(1)}, u32[]{:S(2)}, u32[]{:S(2)}) collective-permute-start(bf16[128,256]{1,0:T(8,128)(2,1)S(1)} %get-tuple-element.16), channel_id=1, source_target_pairs={{0,12},{4,0},{8,4},{12,8},{1,13},{5,1},{9,5},{13,9},{2,14},{6,2},{... | collective-permute-start | bytes 196616 | tf_op jit(solution)/shard_map/ppermute | solution.py:79
  40.5 5.2 %collective-permute-start.10 = (bf16[128,256]{1,0:T(8,128)(2,1)S(1)}, bf16[128,256]{1,0:T(8,128)(2,1)S(1)}, u32[]{:S(2)}, u32[]{:S(2)}) collective-permute-start(bf16[128,256]{1,0:T(8,128)(2,1)S(1)} %get-tuple-element.17), channel_id=1, source_target_pairs={{0,8},{4,12},{8,0},{12,4},{1,9},{5,13},{9,1},{13,5},{2,10},{6,14},... | collective-permute-start | bytes 196616 | tf_op jit(solution)/shard_map/ppermute | solution.py:79
  40.5 6.1 %collective-permute-start.9 = (bf16[128,256]{1,0:T(8,128)(2,1)S(1)}, bf16[128,256]{1,0:T(8,128)(2,1)S(1)}, u32[]{:S(2)}, u32[]{:S(2)}) collective-permute-start(bf16[128,256]{1,0:T(8,128)(2,1)S(1)} %get-tuple-element.15), channel_id=1, source_target_pairs={{0,4},{4,8},{8,12},{12,0},{1,5},{5,9},{9,13},{13,1},{2,6},{6,10},{... | collective-permute-start | bytes 196616 | tf_op jit(solution)/shard_map/ppermute | solution.py:79

commit v11 on v10

--- a/solution.py
+++ b/solution.py
@@ -56,8 +56,13 @@
 
     lower_at = trace_rows[0, 0]
     upper_at = trace_rows[0, 1]
-    lower_basis = masked_basis[lower_at]
-    upper_basis = masked_basis[upper_at]
+    trace_at = jnp.concatenate([lower_at, upper_at])
+    trace_basis = jnp.take(masked_basis, trace_at, axis=0)
+    lower_basis = trace_basis[: lower_at.shape[0]]
+    upper_basis = trace_basis[lower_at.shape[0] :]
+    trace_solve = jnp.dot(
+        jnp.take(inverse, trace_at, axis=0), source, preferred_element_type=jnp.float32
+    )
     face_inverse = jnp.concatenate(
         [inverse[:, :face_rows], inverse[:, iface_rows - face_rows :]], axis=1
     )
@@ -126,13 +131,16 @@
         iterate = local_solve + correction
         if cycle_index == ROUNDS - 1:
             break
-        lower_trace = (
-            local_solve[lower_at] + jnp.dot(lower_basis, coarse, preferred_element_type=jnp.float32)
+        if cycle_index == 0:
+            solve_rows = trace_solve
+        else:
+            solve_rows = jnp.take(local_solve, trace_at, axis=0)
+        traces = (
+            solve_rows + jnp.dot(trace_basis, coarse, preferred_element_type=jnp.float32)
         ).astype(jnp.bfloat16)
-        upper_trace = (
-            local_solve[upper_at] + jnp.dot(upper_basis, coarse, preferred_element_type=jnp.float32)
-        ).astype(jnp.bfloat16)
-        rows = lower_trace.shape[0]
+        rows = lower_at.shape[0]
+        lower_trace = traces[:rows]
+        upper_trace = traces[rows:]
         if pairwise:
             got_lower = passed_along(jnp.concatenate([upper_trace, coarse], axis=0), 1)
             got_upper = passed_along(jnp.concatenate([lower_trace, coarse], axis=0), -1)

time: 47.9 us -> 51.2 us (1.069)
  other arithmetic: 0.61 us -> 2.37 us
  matrix products: 5.89 us -> 7.24 us
    select_n x2, other arithmetic: 0.04 us -> 1.78 us  [gathered(): jnp.where(first, shard, other)]
    dot_general x2, matrix products: 0.29 us -> 1.62 us  [the longest x1 1.39 us: local(): jnp.dot(jnp.take(inverse, trace_at, axis=0), source, preferred_element_ty...]
    slice x1, local copies, waits for them, and re-layouts: 1.08 us -> 0.07 us  [local(): inverse[:, :face_rows]]
    unnamed x10 -> x16, local copies, waits for them, and re-layouts: 0.03 us -> 0.99 us
    gather x4 -> x2, local copies, waits for them, and re-layouts: 2.93 us -> 2.81 us  [the longest x1 1.96 us: local(): jnp.take(inverse, trace_at, axis=0)]
  transfers between devices with their start and end apart: 12 -> 12, of which waited for: 6 -> 6; matrix products, arithmetic and copies ran while one was open for 18% -> 21% of each run, Pallas kernels for 0% -> 0%
where the time goes in v11:
time: 51.2 us; the launch traced here: 50.8 us
  starting transfers between devices  23.6 us (46%)
  waiting for transfers between devices  12.2 us (24%)
  matrix products  7.24 us (14%)
  local copies, waits for them, and re-layouts  4.37 us (9%)
  other arithmetic  2.37 us (5%)
  between operations  1.1 us (2%)
    ppermute x6, starting transfers between devices, coarse_of(): lax.ppermute(piece, 'sub', [(i, (i + k) % sub_count) for i in range(sub_c...  12.3 us
    ppermute x6, waiting for transfers between devices, coarse_of(): lax.ppermute(piece, 'sub', [(i, (i + k) % sub_count) for i in range(sub_c...  8.83 us
    ppermute x2, starting transfers between devices, passed_along(): return lax.ppermute(shard, DUCT, pairs)  6.07 us
    ppermute x3, starting transfers between devices, swapped(): return lax.ppermute(shard, axis, [(0, 1), (1, 0)])  3.75 us
    ppermute x2, waiting for transfers between devices, passed_along(): return lax.ppermute(shard, DUCT, pairs)  3.33 us
    dot_general x1, matrix products, local(): base_solve = jnp.dot(inverse, source, preferred_element_type=jnp.float32)  2.34 us
    gather x1, local copies, waits for them, and re-layouts, local(): jnp.take(inverse, trace_at, axis=0)  1.96 us
    select_n x2, other arithmetic, gathered(): jnp.where(first, shard, other)  1.78 us
  transfers between devices with their start and end apart: 12, of which 6 were waited for; matrix products, arithmetic and copies ran while one was open for 21% of the time, Pallas kernels for 0%

profile of v11, /device:TPU:0, one launch (start us, length us, event | category | flops | bytes accessed | tf_op | source)
XLA Modules:
  0.0 50.8 jit_solution(403889877759496248)
XLA Ops:
  0.0 0.5 collective-permute-start
  1.1 2.3 %fusion.7 = f32[1024,256]{1,0:T(8,128)S(1)} fusion(bf16[1,1024,256]{2,1,0:T(8,128)(2,1)S(1)} %copy-done, bf16[1,1024,1024]{2,1,0:T(8,128)(2,1)} %param.8), kind=kOutput, calls=%fused_computation.20 | convolution fusion | flops 536870912 | bytes 3670016 | tf_op jit(solution)/shard_map/dot_general | solution.py:117
  3.6 0.9 %copy-done.2 = f32[1024,256]{1,0:T(8,128)} copy-done((f32[1024,256]{1,0:T(8,128)}, f32[1024,256]{1,0:T(8,128)S(1)}, u32[]{:S(2)}) %copy-start.2) | copy-done | bytes 1048600
  4.8 2.9 %collective-permute-start.1 = (bf16[128,256]{1,0:T(8,128)(2,1)S(1)}, bf16[128,256]{1,0:T(8,128)(2,1)}, u32[]{:S(2)}, u32[]{:S(2)}) collective-permute-start(bf16[128,256]{1,0:T(8,128)(2,1)S(1)} %convolution_convert_fusion.2), channel_id=1, source_target_pairs={{0,2},{2,0},{1,3},{3,1},{4,6},{6,4},{5,7},{7,5},{8,10},{10,8},{9,1... | collective-permute-start | bytes 196616 | tf_op jit(solution)/shard_map/ppermute | solution.py:17
  8.2 2.0 %gather_fusion = bf16[256,1024]{1,0:T(8,128)(2,1)} fusion(bf16[1024,1024]{1,0:T(8,128)(2,1)S(1)} %bitcast.78, s32[1024]{0:T(1024)S(1)} %pad_clamp_fusion), kind=kCustom, calls=%fused_computation | custom fusion | bytes 1049600 | tf_op jit(solution)/shard_map/jit(_take)/gather | solution.py:64
  10.1 0.9 %gather_fusion.1 = bf16[256,128]{1,0:T(8,128)(2,1)S(1)} fusion(bf16[1024,128]{1,0:T(8,128)(2,1)S(1)} %bitcast_select_fusion, s32[1024]{0:T(1024)S(1)} %pad_clamp_fusion), kind=kCustom, calls=%fused_computation.1 | custom fusion | bytes 132096 | tf_op jit(solution)/shard_map/jit(_take)/gather | solution.py:60
  11.6 1.4 %fusion.5 = f32[256,256]{1,0:T(8,128)S(1)} fusion(bf16[1,1024,256]{2,1,0:T(8,128)(2,1)S(1)} %copy-done, bf16[256,1024]{1,0:T(8,128)(2,1)} %gather_fusion, pred[256]{0:T(512)(128)(4,1)S(1)} %compare_and_fusion), kind=kOutput, calls=%fused_computation.18 | convolution fusion | flops 134479872 | bytes 1310976 | tf_op jit(solution)/shard_map/dot_general | solution.py:63
  13.1 0.9 %broadcast_select_fusion.6 = (bf16[128,256]{1,0:T(8,128)(2,1)S(1)}, bf16[128,256]{1,0:T(8,128)(2,1)S(1)}) fusion(bf16[128,256]{1,0:T(8,128)(2,1)S(1)} %convolution_convert_fusion.2, bf16[128,256]{1,0:T(8,128)(2,1)} %collective-permute-done.1, pred[]{:T(512)S(6)} %eq.16), kind=kLoop, calls=%fused_computation.82 | loop fusion | flops 65536 | bytes 262145 | tf_op jit(solution)/shard_map/jit(_where)/select_n | solution.py:26
  14.0 0.4 collective-permute-start.7
  14.4 0.9 %broadcast_select_fusion.1 = (bf16[4,64,256]{2,1,0:T(8,128)(2,1)S(1)}, bf16[4,64,256]{2,1,0:T(8,128)(2,1)S(1)}) fusion(bf16[4,64,256]{2,1,0:T(8,128)(2,1)} %collective-permute-done, pred[]{:T(512)S(6)} %eq.15, bf16[4,1,64,1,256]{4,2,3,1,0:T(8,128)(2,1)S(1)} %copy-done.5), kind=kLoop, calls=%fused_computation.57 | loop fusion | flops 131072 | bytes 524289 | tf_op jit(solution)/shard_map/jit(_where)/select_n | solution.py:26
  15.6 3.9 %collective-permute-start.4 = (bf16[128,256]{1,0:T(8,128)(2,1)S(1)}, bf16[128,256]{1,0:T(8,128)(2,1)S(1)}, u32[]{:S(2)}, u32[]{:S(2)}) collective-permute-start(bf16[128,256]{1,0:T(8,128)(2,1)S(1)} %get-tuple-element.19), channel_id=1, source_target_pairs={{0,12},{4,0},{8,4},{12,8},{1,13},{5,1},{9,5},{13,9},{2,14},{6,2},{... | collective-permute-start | bytes 196616 | tf_op jit(solution)/shard_map/ppermute | solution.py:84
  19.4 1.0 %collective-permute-start.2 = (bf16[128,256]{1,0:T(8,128)(2,1)S(1)}, bf16[128,256]{1,0:T(8,128)(2,1)S(1)}, u32[]{:S(2)}, u32[]{:S(2)}) collective-permute-start(bf16[128,256]{1,0:T(8,128)(2,1)S(1)} %get-tuple-element.18), channel_id=1, source_target_pairs={{0,4},{4,8},{8,12},{12,0},{1,5},{5,9},{9,13},{13,1},{2,6},{6,10},{... | collective-permute-start | bytes 196616 | tf_op jit(solution)/shard_map/ppermute | solution.py:84
  20.7 1.2 %collective-permute-done.4 = bf16[128,256]{1,0:T(8,128)(2,1)S(1)} collective-permute-done((bf16[128,256]{1,0:T(8,128)(2,1)S(1)}, bf16[128,256]{1,0:T(8,128)(2,1)S(1)}, u32[]{:S(2)}, u32[]{:S(2)}) %collective-permute-start.4) | collective-permute-done | bytes 65568 | tf_op jit(solution)/shard_map/ppermute | solution.py:84
  22.0 3.7 %collective-permute-done.3 = bf16[128,256]{1,0:T(8,128)(2,1)S(1)} collective-permute-done((bf16[128,256]{1,0:T(8,128)(2,1)S(1)}, bf16[128,256]{1,0:T(8,128)(2,1)S(1)}, u32[]{:S(2)}, u32[]{:S(2)}) %collective-permute-start.3) | collective-permute-done | bytes 65568 | tf_op jit(solution)/shard_map/ppermute | solution.py:84
  26.0 1.4 %collective-permute-start.8 = (bf16[128,256]{1,0:T(8,128)(2,1)S(1)}, bf16[128,256]{1,0:T(8,128)(2,1)S(1)}, u32[]{:S(2)}, u32[]{:S(2)}) collective-permute-start(bf16[128,256]{1,0:T(8,128)(2,1)S(1)} %get-tuple-element.27), channel_id=1, source_target_pairs={{2,6},{4,0},{6,10},{8,4},{10,14},{12,8},{3,7},{5,1},{7,11},{9,5},{... | collective-permute-start | bytes 196616 | tf_op jit(solution)/shard_map/ppermute | solution.py:147
  27.5 1.3 %collective-permute-start.6 = (bf16[256,256]{1,0:T(8,128)(2,1)S(1)}, bf16[256,256]{1,0:T(8,128)(2,1)S(1)}, u32[]{:S(2)}, u32[]{:S(2)}) collective-permute-start(bf16[256,256]{1,0:T(8,128)(2,1)S(1)} %get-tuple-element.33), channel_id=1, source_target_pairs={{2,0},{4,2},{6,4},{8,6},{10,8},{12,10},{14,12},{3,1},{5,3},{7,5},{... | collective-permute-start | bytes 393224 | tf_op jit(solution)/shard_map/ppermute | solution.py:13
  28.8 4.8 %collective-permute-start.5 = (bf16[256,256]{1,0:T(8,128)(2,1)S(1)}, bf16[256,256]{1,0:T(8,128)(2,1)S(1)}, u32[]{:S(2)}, u32[]{:S(2)}) collective-permute-start(bf16[256,256]{1,0:T(8,128)(2,1)S(1)} %get-tuple-element.32), channel_id=1, source_target_pairs={{0,2},{2,4},{4,6},{6,8},{8,10},{10,12},{12,14},{1,3},{3,5},{5,7},{... | collective-permute-start | bytes 393224 | tf_op jit(solution)/shard_map/ppermute | solution.py:13
  33.7 0.9 %collective-permute-done.6 = bf16[256,256]{1,0:T(8,128)(2,1)S(1)} collective-permute-done((bf16[256,256]{1,0:T(8,128)(2,1)S(1)}, bf16[256,256]{1,0:T(8,128)(2,1)S(1)}, u32[]{:S(2)}, u32[]{:S(2)}) %collective-permute-start.6) | collective-permute-done | bytes 131104 | tf_op jit(solution)/shard_map/ppermute | solution.py:13
  34.7 2.5 %collective-permute-done.5 = bf16[256,256]{1,0:T(8,128)(2,1)S(1)} collective-permute-done((bf16[256,256]{1,0:T(8,128)(2,1)S(1)}, bf16[256,256]{1,0:T(8,128)(2,1)S(1)}, u32[]{:S(2)}, u32[]{:S(2)}) %collective-permute-start.5) | collective-permute-done | bytes 131104 | tf_op jit(solution)/shard_map/ppermute | solution.py:13
  38.1 5.5 %collective-permute-start.11 = (bf16[128,256]{1,0:T(8,128)(2,1)S(1)}, bf16[128,256]{1,0:T(8,128)(2,1)S(1)}, u32[]{:S(2)}, u32[]{:S(2)}) collective-permute-start(bf16[128,256]{1,0:T(8,128)(2,1)S(1)} %get-tuple-element.16), channel_id=1, source_target_pairs={{0,12},{4,0},{8,4},{12,8},{1,13},{5,1},{9,5},{13,9},{2,14},{6,2},{... | collective-permute-start | bytes 196616 | tf_op jit(solution)/shard_map/ppermute | solution.py:84
  43.7 1.9 %collective-permute-start.9 = (bf16[128,256]{1,0:T(8,128)(2,1)S(1)}, bf16[128,256]{1,0:T(8,128)(2,1)S(1)}, u32[]{:S(2)}, u32[]{:S(2)}) collective-permute-start(bf16[128,256]{1,0:T(8,128)(2,1)S(1)} %get-tuple-element.15), channel_id=1, source_target_pairs={{0,4},{4,8},{8,12},{12,0},{1,5},{5,9},{9,13},{13,1},{2,6},{6,10},{... | collective-permute-start | bytes 196616 | tf_op jit(solution)/shard_map/ppermute | solution.py:84
  45.9 3.0 %collective-permute-done.10 = bf16[128,256]{1,0:T(8,128)(2,1)S(1)} collective-permute-done((bf16[128,256]{1,0:T(8,128)(2,1)S(1)}, bf16[128,256]{1,0:T(8,128)(2,1)S(1)}, u32[]{:S(2)}, u32[]{:S(2)}) %collective-permute-start.10) | collective-permute-done | bytes 65568 | tf_op jit(solution)/shard_map/ppermute | solution.py:84
  48.8 0.9 %collective-permute-done.9 = bf16[128,256]{1,0:T(8,128)(2,1)S(1)} collective-permute-done((bf16[128,256]{1,0:T(8,128)(2,1)S(1)}, bf16[128,256]{1,0:T(8,128)(2,1)S(1)}, u32[]{:S(2)}, u32[]{:S(2)}) %collective-permute-start.9) | collective-permute-done | bytes 65568 | tf_op jit(solution)/shard_map/ppermute | solution.py:84
  49.7 1.1 %fusion.1 = bf16[1,1024,256]{2,1,0:T(8,128)(2,1)} fusion(f32[1024,256]{1,0:T(8,128)S(1)} %convolution_add_fusion, bf16[1024,128]{1,0:T(8,128)(2,1)S(1)} %bitcast_select_fusion, bf16[128,256]{1,0:T(8,128)(2,1)S(1)} %collective-permute-done.11, bf16[128,256]{1,0:T(8,128)(2,1)S(1)} %collective-permute-done.10, bf16[128,256]{1,0:T(8,128)(2,1)S(1)} %collective-permute-done.9, ...), kind=kOutput, calls=%fused_computation.5 | convolution fusion | flops 67895296 | bytes 2097156 | tf_op jit(solution)/shard_map/dot_general | solution.py:130
  (58 shorter events, 3.6 us)
Async XLA Ops:
  0.0 1.1 %copy-start = (bf16[1,1024,256]{2,1,0:T(8,128)(2,1)S(1)}, bf16[1,1024,256]{2,1,0:T(8,128)(2,1)}, u32[]{:S(2)}) copy-start(bf16[1,1024,256]{2,1,0:T(8,128)(2,1)} %param.7) | copy-start | bytes 1572868
  0.0 14.4 %collective-permute-start = (bf16[4,64,256]{2,1,0:T(8,128)(2,1)}, bf16[4,64,256]{2,1,0:T(8,128)(2,1)}, u32[]{:S(2)}, u32[]{:S(2)}) collective-permute-start(bf16[4,64,256]{2,1,0:T(8,128)(2,1)} %bitcast.79), channel_id=1, source_target_pairs={{0,1},{1,0},{2,3},{3,2},{4,5},{5,4},{6,7},{7,6},{8,9},{9,8},{10,11... | collective-permute-start | bytes 393224 | tf_op jit(solution)/shard_map/ppermute | solution.py:17
  1.1 2.4 %copy-start.4 = (bf16[1,1024,128]{2,1,0:T(8,128)(2,1)S(1)}, bf16[1,1024,128]{2,1,0:T(8,128)(2,1)}, u32[]{:S(2)}) copy-start(bf16[1,1024,128]{2,1,0:T(8,128)(2,1)} %param.11) | copy-start | bytes 786436
  3.5 1.0 %copy-start.2 = (f32[1024,256]{1,0:T(8,128)}, f32[1024,256]{1,0:T(8,128)S(1)}, u32[]{:S(2)}) copy-start(f32[1024,256]{1,0:T(8,128)S(1)} %fusion.7) | copy-start | bytes 3145732
  3.5 4.5 %copy-start.1 = (bf16[1,1024,1024]{2,1,0:T(8,128)(2,1)S(1)}, bf16[1,1024,1024]{2,1,0:T(8,128)(2,1)}, u32[]{:S(2)}) copy-start(bf16[1,1024,1024]{2,1,0:T(8,128)(2,1)} %param.8) | copy-start | bytes 6291460
  3.5 4.6 %copy-start.7 = (s32[1,2,128]{2,1,0:T(2,128)S(1)}, s32[1,2,128]{2,1,0:T(2,128)}, u32[]{:S(2)}) copy-start(s32[1,2,128]{2,1,0:T(2,128)} %param.10) | copy-start | bytes 3076
  4.8 8.3 %collective-permute-start.1 = (bf16[128,256]{1,0:T(8,128)(2,1)S(1)}, bf16[128,256]{1,0:T(8,128)(2,1)}, u32[]{:S(2)}, u32[]{:S(2)}) collective-permute-start(bf16[128,256]{1,0:T(8,128)(2,1)S(1)} %convolution_convert_fusion.2), channel_id=1, source_target_pairs={{0,2},{2,0},{1,3},{3,1},{4,6},{6,4},{5,7},{7,5},{8,10},{10,8},{9,1... | collective-permute-start | bytes 196616 | tf_op jit(solution)/shard_map/ppermute | solution.py:17
  8.2 2.8 %copy-start.6 = (f32[1,2,128]{2,1,0:T(2,128)S(1)}, f32[1,2,128]{2,1,0:T(2,128)}, u32[]{:S(2)}) copy-start(f32[1,2,128]{2,1,0:T(2,128)} %param.9) | copy-start | bytes 3076
  10.1 4.2 %copy-start.5 = (bf16[4,1,64,1,256]{4,2,3,1,0:T(8,128)(2,1)S(1)}, bf16[4,1,64,1,256]{4,2,3,1,0:T(8,128)(2,1)}, u32[]{:S(2)}) copy-start(bf16[4,1,64,1,256]{4,2,3,1,0:T(8,128)(2,1)} %param.13) | copy-start | bytes 393220
  14.0 6.5 %collective-permute-start.7 = (bf16[128,388]{1,0:T(8,128)(2,1)S(1)}, bf16[128,388]{1,0:T(8,128)(2,1)S(1)}, u32[]{:S(2)}, u32[]{:S(2)}) collective-permute-start(bf16[128,388]{1,0:T(8,128)(2,1)S(1)} %pad_maximum_fusion.8), channel_id=1, source_target_pairs={{0,2},{2,0},{1,3},{3,1},{4,6},{6,4},{5,7},{7,5},{8,10},{10,8},{9,1... | collective-permute-start | bytes 297992 | tf_op jit(solution)/shard_map/ppermute | solution.py:17
  15.6 6.4 %collective-permute-start.4 = (bf16[128,256]{1,0:T(8,128)(2,1)S(1)}, bf16[128,256]{1,0:T(8,128)(2,1)S(1)}, u32[]{:S(2)}, u32[]{:S(2)}) collective-permute-start(bf16[128,256]{1,0:T(8,128)(2,1)S(1)} %get-tuple-element.19), channel_id=1, source_target_pairs={{0,12},{4,0},{8,4},{12,8},{1,13},{5,1},{9,5},{13,9},{2,14},{6,2},{... | collective-permute-start | bytes 196616 | tf_op jit(solution)/shard_map/ppermute | solution.py:84
  19.4 6.3 %collective-permute-start.3 = (bf16[128,256]{1,0:T(8,128)(2,1)S(1)}, bf16[128,256]{1,0:T(8,128)(2,1)S(1)}, u32[]{:S(2)}, u32[]{:S(2)}) collective-permute-start(bf16[128,256]{1,0:T(8,128)(2,1)S(1)} %get-tuple-element.20), channel_id=1, source_target_pairs={{0,8},{4,12},{8,0},{12,4},{1,9},{5,13},{9,1},{13,5},{2,10},{6,14},... | collective-permute-start | bytes 196616 | tf_op jit(solution)/shard_map/ppermute | solution.py:84
  19.4 6.3 %collective-permute-start.2 = (bf16[128,256]{1,0:T(8,128)(2,1)S(1)}, bf16[128,256]{1,0:T(8,128)(2,1)S(1)}, u32[]{:S(2)}, u32[]{:S(2)}) collective-permute-start(bf16[128,256]{1,0:T(8,128)(2,1)S(1)} %get-tuple-element.18), channel_id=1, source_target_pairs={{0,4},{4,8},{8,12},{12,0},{1,5},{5,9},{9,13},{13,1},{2,6},{6,10},{... | collective-permute-start | bytes 196616 | tf_op jit(solution)/shard_map/ppermute | solution.py:84
  26.0 19.6 %copy-start.3 = (f32[1024,256]{1,0:T(8,128)S(1)}, f32[1024,256]{1,0:T(8,128)}, u32[]{:S(2)}) copy-start(f32[1024,256]{1,0:T(8,128)} %copy-done.2) | copy-start | bytes 3145732
  26.0 7.5 %collective-permute-start.8 = (bf16[128,256]{1,0:T(8,128)(2,1)S(1)}, bf16[128,256]{1,0:T(8,128)(2,1)S(1)}, u32[]{:S(2)}, u32[]{:S(2)}) collective-permute-start(bf16[128,256]{1,0:T(8,128)(2,1)S(1)} %get-tuple-element.27), channel_id=1, source_target_pairs={{2,6},{4,0},{6,10},{8,4},{10,14},{12,8},{3,7},{5,1},{7,11},{9,5},{... | collective-permute-start | bytes 196616 | tf_op jit(solution)/shard_map/ppermute | solution.py:147
  27.5 7.1 %collective-permute-start.6 = (bf16[256,256]{1,0:T(8,128)(2,1)S(1)}, bf16[256,256]{1,0:T(8,128)(2,1)S(1)}, u32[]{:S(2)}, u32[]{:S(2)}) collective-permute-start(bf16[256,256]{1,0:T(8,128)(2,1)S(1)} %get-tuple-element.33), channel_id=1, source_target_pairs={{2,0},{4,2},{6,4},{8,6},{10,8},{12,10},{14,12},{3,1},{5,3},{7,5},{... | collective-permute-start | bytes 393224 | tf_op jit(solution)/shard_map/ppermute | solution.py:13
  28.8 8.3 %collective-permute-start.5 = (bf16[256,256]{1,0:T(8,128)(2,1)S(1)}, bf16[256,256]{1,0:T(8,128)(2,1)S(1)}, u32[]{:S(2)}, u32[]{:S(2)}) collective-permute-start(bf16[256,256]{1,0:T(8,128)(2,1)S(1)} %get-tuple-element.32), channel_id=1, source_target_pairs={{0,2},{2,4},{4,6},{6,8},{8,10},{10,12},{12,14},{1,3},{3,5},{5,7},{... | collective-permute-start | bytes 393224 | tf_op jit(solution)/shard_map/ppermute | solution.py:13
  38.1 7.7 %collective-permute-start.11 = (bf16[128,256]{1,0:T(8,128)(2,1)S(1)}, bf16[128,256]{1,0:T(8,128)(2,1)S(1)}, u32[]{:S(2)}, u32[]{:S(2)}) collective-permute-start(bf16[128,256]{1,0:T(8,128)(2,1)S(1)} %get-tuple-element.16), channel_id=1, source_target_pairs={{0,12},{4,0},{8,4},{12,8},{1,13},{5,1},{9,5},{13,9},{2,14},{6,2},{... | collective-permute-start | bytes 196616 | tf_op jit(solution)/shard_map/ppermute | solution.py:84
  43.7 5.2 %collective-permute-start.10 = (bf16[128,256]{1,0:T(8,128)(2,1)S(1)}, bf16[128,256]{1,0:T(8,128)(2,1)S(1)}, u32[]{:S(2)}, u32[]{:S(2)}) collective-permute-start(bf16[128,256]{1,0:T(8,128)(2,1)S(1)} %get-tuple-element.17), channel_id=1, source_target_pairs={{0,8},{4,12},{8,0},{12,4},{1,9},{5,13},{9,1},{13,5},{2,10},{6,14},... | collective-permute-start | bytes 196616 | tf_op jit(solution)/shard_map/ppermute | solution.py:84
  43.7 6.1 %collective-permute-start.9 = (bf16[128,256]{1,0:T(8,128)(2,1)S(1)}, bf16[128,256]{1,0:T(8,128)(2,1)S(1)}, u32[]{:S(2)}, u32[]{:S(2)}) collective-permute-start(bf16[128,256]{1,0:T(8,128)(2,1)S(1)} %get-tuple-element.15), channel_id=1, source_target_pairs={{0,4},{4,8},{8,12},{12,0},{1,5},{5,9},{9,13},{13,1},{2,6},{6,10},{... | collective-permute-start | bytes 196616 | tf_op jit(solution)/shard_map/ppermute | solution.py:84

commit v12 on v9

--- a/solution.py
+++ b/solution.py
@@ -44,11 +44,8 @@
     sub_count = lax.axis_size("sub")
     sub_index = lax.axis_index("sub")
     slot_ids = jnp.arange(slot_count, dtype=jnp.int32)
-    masked_basis = jnp.where(
-        slot_ids[None, :] < deflation_counts[0],
-        deflation_basis[0],
-        jnp.zeros((), deflation_basis.dtype),
-    )
+    basis = deflation_basis[0]
+    live = (slot_ids < deflation_counts[0])[:, None]
     half_block = coarse_inverse[:, 0, :, 0, :]
     columns = gathered(half_block, "rep", 1)
     lower_gain = coupling[0, 0][:, None]
@@ -56,16 +53,17 @@
 
     lower_at = trace_rows[0, 0]
     upper_at = trace_rows[0, 1]
-    lower_basis = masked_basis[lower_at]
-    upper_basis = masked_basis[upper_at]
+    lower_basis = basis[lower_at]
+    upper_basis = basis[upper_at]
     face_inverse = jnp.concatenate(
         [inverse[:, :face_rows], inverse[:, iface_rows - face_rows :]], axis=1
     )
 
     def coarse_input(defect):
-        return lax.dot_general(
-            masked_basis, defect, (((0,), (0,)), ((), ())), preferred_element_type=jnp.float32
-        ).astype(jnp.bfloat16)
+        projected = lax.dot_general(
+            basis, defect, (((0,), (0,)), ((), ())), preferred_element_type=jnp.float32
+        )
+        return jnp.where(live, projected, 0.0).astype(jnp.bfloat16)
 
     def coarse_of(inputs):
         partial = jnp.einsum(
@@ -85,8 +83,12 @@
     tile_index = lax.axis_index("tile")
     gains = coupling[0]
     if pairwise:
-        sends = jnp.dot(masked_basis.T, face_inverse, preferred_element_type=jnp.float32)
-        keeps = jnp.dot(masked_basis.T, masked_basis, preferred_element_type=jnp.float32)
+        sends = jnp.where(
+            live, jnp.dot(basis.T, face_inverse, preferred_element_type=jnp.float32), 0.0
+        )
+        keeps = jnp.where(
+            live & live.T, jnp.dot(basis.T, basis, preferred_element_type=jnp.float32), 0.0
+        )
         mine = jnp.concatenate([sends, keeps], axis=1).astype(jnp.bfloat16)
         gains_high = gains.T.astype(jnp.bfloat16)
         gains_low = (gains.T - gains_high.astype(jnp.float32)).astype(jnp.bfloat16)
@@ -135,7 +137,8 @@
     earlier = None
     for cycle_index in range(ROUNDS):
         coarse = coarse_of(inputs)
-        correction = jnp.dot(masked_basis, coarse, preferred_element_type=jnp.float32)
+        coarse = jnp.where(live, coarse, jnp.zeros((), coarse.dtype))
+        correction = jnp.dot(basis, coarse, preferred_element_type=jnp.float32)
         iterate = local_solve + correction
         if cycle_index == ROUNDS - 1:
             break

time: 47.4 us -> 46.4 us (0.979)
  other arithmetic: 2.15 us -> 0.91 us
    select_n x1, other arithmetic: 0.98 us -> 0.05 us  [local(): coarse = jnp.where(live, coarse, jnp.zeros((), coarse.dtype))]
where the time goes in v12:
time: 46.4 us; the launch traced here: 46.1 us
  starting transfers between devices  19.5 us (42%)
  waiting for transfers between devices  14.2 us (31%)
  matrix products  6.24 us (13%)
  local copies, waits for them, and re-layouts  4.27 us (9%)
  between operations  1.03 us (2%)
  other arithmetic  0.91 us (2%)
    ppermute x6, starting transfers between devices, coarse_of(): lax.ppermute(piece, 'sub', [(i, (i + k) % sub_count) for i in range(sub_c...  10 us
    ppermute x6, waiting for transfers between devices, coarse_of(): lax.ppermute(piece, 'sub', [(i, (i + k) % sub_count) for i in range(sub_c...  8.86 us
    ppermute x3, starting transfers between devices, swapped(): return lax.ppermute(shard, axis, [(0, 1), (1, 0)])  7.55 us
    ppermute x3, waiting for transfers between devices, swapped(): return lax.ppermute(shard, axis, [(0, 1), (1, 0)])  3.79 us
    dot_general x1, matrix products, local(): base_solve = jnp.dot(inverse, source, preferred_element_type=jnp.float32)  2.35 us
    ppermute x1, waiting for transfers between devices, local(): crossing = lax.ppermute(toward_diagonal, DUCT, crossing_pairs)  1.53 us
    ppermute x1, starting transfers between devices, local(): crossing = lax.ppermute(toward_diagonal, DUCT, crossing_pairs)  1.29 us
    dot_general x1, matrix products, local(): correction = jnp.dot(basis, coarse, preferred_element_type=jnp.float32)  1.1 us
  transfers between devices with their start and end apart: 11, of which 7 were waited for; matrix products, arithmetic and copies ran while one was open for 11% of the time, Pallas kernels for 0%

profile of v12, /device:TPU:0, one launch (start us, length us, event | category | flops | bytes accessed | tf_op | source)
XLA Modules:
  0.0 46.1 jit_solution(13665647701531600269)
XLA Ops:
  0.7 0.7 %fusion.40 = (bf16[128,2]{0,1:T(2,128)(2,1)S(1)}, bf16[128,2]{0,1:T(2,128)(2,1)S(1)}) fusion(f32[1,2,128]{2,1,0:T(2,128)} %param.9), kind=kLoop, calls=%fused_computation.88 | loop fusion | flops 1024 | bytes 2048 | tf_op jit(solution)/shard_map/convert_element_type | solution.py:94
  1.4 2.4 %fusion.11 = f32[1024,256]{1,0:T(8,128)S(1)} fusion(bf16[1,1024,256]{2,1,0:T(8,128)(2,1)S(1)} %copy-done, bf16[1,1024,1024]{2,1,0:T(8,128)(2,1)} %param.8), kind=kOutput, calls=%fused_computation.27 | convolution fusion | flops 536870912 | bytes 3670016 | tf_op jit(solution)/shard_map/dot_general | solution.py:118
  4.2 3.0 %collective-permute-start.1 = (bf16[128,260]{0,1:T(8,128)(2,1)S(1)}, bf16[128,260]{0,1:T(8,128)(2,1)S(1)}, u32[]{:S(2)}, u32[]{:S(2)}) collective-permute-start(bf16[128,260]{0,1:T(8,128)(2,1)S(1)} %pad_maximum_fusion.10), channel_id=1, source_target_pairs={{0,2},{2,0},{1,3},{3,1},{4,6},{6,4},{5,7},{7,5},{8,10},{10,8},{9,1... | collective-permute-start | bytes 199688 | tf_op jit(solution)/shard_map/ppermute | solution.py:17
  7.5 1.1 %fusion.55 = (bf16[1024,128]{1,0:T(8,128)(2,1)S(1)}, bf16[1024,128]{1,0:T(8,128)(2,1)S(1)}) fusion(bf16[1024,1024]{1,0:T(8,128)(2,1)} %bitcast.97), kind=kLoop, calls=%fused_computation.109 | loop fusion | bytes 1048576 | tf_op jit(solution)/shard_map/slice | solution.py:59
  8.6 0.4 fusion.4
  9.0 0.8 %gather_fusion = f32[128,256]{1,0:T(8,128)S(1)} fusion(f32[1024,256]{1,0:T(8,128)S(1)} %fusion.11, s32[1024]{0:T(1024)S(1)} %get-tuple-element.35), kind=kCustom, calls=%fused_computation | custom fusion | bytes 262656 | tf_op jit(solution)/shard_map/gather | solution.py:146
  9.7 0.7 %gather_fusion.1 = bf16[128,128]{1,0:T(8,128)(2,1)S(1)} fusion(bf16[1024,128]{1,0:T(8,128)(2,1)S(1)} %bitcast.93, s32[1024]{0:T(1024)S(1)} %get-tuple-element.35), kind=kCustom, calls=%fused_computation.1 | custom fusion | bytes 66048 | tf_op jit(solution)/shard_map/gather | solution.py:56
  10.4 0.8 %gather_fusion.2 = f32[128,256]{1,0:T(8,128)S(1)} fusion(f32[1024,256]{1,0:T(8,128)S(1)} %fusion.11, s32[1024]{0:T(1024)S(1)} %get-tuple-element.34), kind=kCustom, calls=%fused_computation.2 | custom fusion | bytes 262656 | tf_op jit(solution)/shard_map/gather | solution.py:149
  11.2 0.7 %gather_fusion.3 = bf16[128,128]{1,0:T(8,128)(2,1)S(1)} fusion(bf16[1024,128]{1,0:T(8,128)(2,1)S(1)} %bitcast.94, s32[1024]{0:T(1024)S(1)} %get-tuple-element.34), kind=kCustom, calls=%fused_computation.3 | custom fusion | bytes 66048 | tf_op jit(solution)/shard_map/gather | solution.py:57
  12.5 1.6 %collective-permute-start.2 = (bf16[128,256]{0,1:T(8,128)(2,1)S(1)}, bf16[128,256]{0,1:T(8,128)(2,1)S(1)}, u32[]{:S(2)}, u32[]{:S(2)}) collective-permute-start(bf16[128,256]{0,1:T(8,128)(2,1)S(1)} %get-tuple-element.14), channel_id=1, source_target_pairs={{0,4},{4,8},{8,12},{12,0},{1,5},{5,9},{9,13},{13,1},{2,6},{6,10},{... | collective-permute-start | bytes 196616 | tf_op jit(solution)/shard_map/ppermute | solution.py:77
  14.2 2.6 %collective-permute-start.3 = (bf16[128,256]{0,1:T(8,128)(2,1)S(1)}, bf16[128,256]{0,1:T(8,128)(2,1)S(1)}, u32[]{:S(2)}, u32[]{:S(2)}) collective-permute-start(bf16[128,256]{0,1:T(8,128)(2,1)S(1)} %get-tuple-element.16), channel_id=1, source_target_pairs={{0,8},{4,12},{8,0},{12,4},{1,9},{5,13},{9,1},{13,5},{2,10},{6,14},... | collective-permute-start | bytes 196616 | tf_op jit(solution)/shard_map/ppermute | solution.py:77
  16.7 1.4 %collective-permute-start.4 = (bf16[128,256]{0,1:T(8,128)(2,1)S(1)}, bf16[128,256]{0,1:T(8,128)(2,1)S(1)}, u32[]{:S(2)}, u32[]{:S(2)}) collective-permute-start(bf16[128,256]{0,1:T(8,128)(2,1)S(1)} %get-tuple-element.15), channel_id=1, source_target_pairs={{0,12},{4,0},{8,4},{12,8},{1,13},{5,1},{9,5},{13,9},{2,14},{6,2},{... | collective-permute-start | bytes 196616 | tf_op jit(solution)/shard_map/ppermute | solution.py:77
  18.1 1.0 %collective-permute-done.2 = bf16[128,256]{0,1:T(8,128)(2,1)S(1)} collective-permute-done((bf16[128,256]{0,1:T(8,128)(2,1)S(1)}, bf16[128,256]{0,1:T(8,128)(2,1)S(1)}, u32[]{:S(2)}, u32[]{:S(2)}) %collective-permute-start.2) | collective-permute-done | bytes 65568 | tf_op jit(solution)/shard_map/ppermute | solution.py:77
  19.1 2.8 %collective-permute-done.3 = bf16[128,256]{0,1:T(8,128)(2,1)S(1)} collective-permute-done((bf16[128,256]{0,1:T(8,128)(2,1)S(1)}, bf16[128,256]{0,1:T(8,128)(2,1)S(1)}, u32[]{:S(2)}, u32[]{:S(2)}) %collective-permute-start.3) | collective-permute-done | bytes 65568 | tf_op jit(solution)/shard_map/ppermute | solution.py:77
  22.5 0.7 %collective-permute-start.5 = (bf16[128,256]{0,1:T(8,128)(2,1)S(1)}, bf16[128,256]{0,1:T(8,128)(2,1)S(1)}, u32[]{:S(2)}, u32[]{:S(2)}) collective-permute-start(bf16[128,256]{0,1:T(8,128)(2,1)S(1)} %get-tuple-element.24), channel_id=1, source_target_pairs={{2,4},{4,2},{6,8},{8,6},{10,12},{12,10},{3,5},{5,3},{7,9},{9,7},{1... | collective-permute-start | bytes 196616 | tf_op jit(solution)/shard_map/ppermute | solution.py:157
  23.2 1.3 %collective-permute-start.7 = (bf16[128,256]{0,1:T(8,128)(2,1)S(1)}, bf16[128,256]{0,1:T(8,128)(2,1)S(1)}, u32[]{:S(2)}, u32[]{:S(2)}) collective-permute-start(bf16[128,256]{0,1:T(8,128)(2,1)S(1)} %get-tuple-element.24), channel_id=1, source_target_pairs={{2,6},{4,0},{6,10},{8,4},{10,14},{12,8},{3,7},{5,1},{7,11},{9,5},{... | collective-permute-start | bytes 196616 | tf_op jit(solution)/shard_map/ppermute | solution.py:158
  24.5 4.5 %collective-permute-start.6 = (bf16[128,896]{0,1:T(8,128)(2,1)S(1)}, bf16[128,896]{0,1:T(8,128)(2,1)S(1)}, u32[]{:S(2)}, u32[]{:S(2)}) collective-permute-start(bf16[128,896]{0,1:T(8,128)(2,1)S(1)} %pad_maximum_fusion.4), channel_id=1, source_target_pairs={{0,2},{2,0},{1,3},{3,1},{4,6},{6,4},{5,7},{7,5},{8,10},{10,8},{9,1... | collective-permute-start | bytes 688136 | tf_op jit(solution)/shard_map/ppermute | solution.py:17
  29.0 1.5 %collective-permute-done.7 = bf16[128,256]{0,1:T(8,128)(2,1)S(1)} collective-permute-done((bf16[128,256]{0,1:T(8,128)(2,1)S(1)}, bf16[128,256]{0,1:T(8,128)(2,1)S(1)}, u32[]{:S(2)}, u32[]{:S(2)}) %collective-permute-start.7) | collective-permute-done | bytes 65568 | tf_op jit(solution)/shard_map/ppermute | solution.py:158
  30.6 3.8 %collective-permute-done.6 = bf16[128,896]{0,1:T(8,128)(2,1)S(1)} collective-permute-done((bf16[128,896]{0,1:T(8,128)(2,1)S(1)}, bf16[128,896]{0,1:T(8,128)(2,1)S(1)}, u32[]{:S(2)}, u32[]{:S(2)}) %collective-permute-start.6) | collective-permute-done | bytes 229408 | tf_op jit(solution)/shard_map/ppermute | solution.py:17
  35.4 3.6 %collective-permute-start.10 = (bf16[128,256]{0,1:T(8,128)(2,1)S(1)}, bf16[128,256]{0,1:T(8,128)(2,1)S(1)}, u32[]{:S(2)}, u32[]{:S(2)}) collective-permute-start(bf16[128,256]{0,1:T(8,128)(2,1)S(1)} %get-tuple-element.12), channel_id=1, source_target_pairs={{0,12},{4,0},{8,4},{12,8},{1,13},{5,1},{9,5},{13,9},{2,14},{6,2},{... | collective-permute-start | bytes 196616 | tf_op jit(solution)/shard_map/ppermute | solution.py:77
  39.0 0.9 %collective-permute-start.9 = (bf16[128,256]{0,1:T(8,128)(2,1)S(1)}, bf16[128,256]{0,1:T(8,128)(2,1)S(1)}, u32[]{:S(2)}, u32[]{:S(2)}) collective-permute-start(bf16[128,256]{0,1:T(8,128)(2,1)S(1)} %get-tuple-element.13), channel_id=1, source_target_pairs={{0,8},{4,12},{8,0},{12,4},{1,9},{5,13},{9,1},{13,5},{2,10},{6,14},... | collective-permute-start | bytes 196616 | tf_op jit(solution)/shard_map/ppermute | solution.py:77
  40.2 0.7 %collective-permute-done.10 = bf16[128,256]{0,1:T(8,128)(2,1)S(1)} collective-permute-done((bf16[128,256]{0,1:T(8,128)(2,1)S(1)}, bf16[128,256]{0,1:T(8,128)(2,1)S(1)}, u32[]{:S(2)}, u32[]{:S(2)}) %collective-permute-start.10) | collective-permute-done | bytes 65568 | tf_op jit(solution)/shard_map/ppermute | solution.py:77
  40.9 4.2 %collective-permute-done.8 = bf16[128,256]{0,1:T(8,128)(2,1)S(1)} collective-permute-done((bf16[128,256]{0,1:T(8,128)(2,1)S(1)}, bf16[128,256]{0,1:T(8,128)(2,1)S(1)}, u32[]{:S(2)}, u32[]{:S(2)}) %collective-permute-start.8) | collective-permute-done | bytes 65568 | tf_op jit(solution)/shard_map/ppermute | solution.py:77
  45.0 1.1 %fusion.2 = bf16[1,1024,256]{2,1,0:T(8,128)(2,1)} fusion(f32[1024,256]{1,0:T(8,128)S(1)} %convolution_add_fusion, bf16[128,256]{0,1:T(8,128)(2,1)S(1)} %collective-permute-done.10, bf16[128,256]{0,1:T(8,128)(2,1)S(1)} %collective-permute-done.9, bf16[128,256]{0,1:T(8,128)(2,1)S(1)} %collective-permute-done.8, ...), kind=kOutput, calls=%fused_computation.8 | convolution fusion | flops 67928064 | bytes 2097668 | tf_op jit(solution)/shard_map/dot_general | solution.py:141
  (46 shorter events, 3.2 us)
Async XLA Ops:
  0.0 1.4 %copy-start = (bf16[1,1024,256]{2,1,0:T(8,128)(2,1)S(1)}, bf16[1,1024,256]{2,1,0:T(8,128)(2,1)}, u32[]{:S(2)}) copy-start(bf16[1,1024,256]{2,1,0:T(8,128)(2,1)} %param.7) | copy-start | bytes 1572868
  1.4 2.4 %copy-start.1 = (bf16[1,1024,128]{2,1,0:T(8,128)(2,1)S(1)}, bf16[1,1024,128]{2,1,0:T(8,128)(2,1)}, u32[]{:S(2)}) copy-start(bf16[1,1024,128]{2,1,0:T(8,128)(2,1)} %param.11) | copy-start | bytes 786436
  1.4 5.8 %copy-start.2 = (bf16[4,1,64,1,256]{4,2,3,1,0:T(8,128)(2,1)S(1)}, bf16[4,1,64,1,256]{4,2,3,1,0:T(8,128)(2,1)}, u32[]{:S(2)}) copy-start(bf16[4,1,64,1,256]{4,2,3,1,0:T(8,128)(2,1)} %param.13) | copy-start | bytes 393220
  1.4 6.1 %copy-start.3 = (f32[1,2,128]{2,1,0:T(2,128)S(1)}, f32[1,2,128]{2,1,0:T(2,128)}, u32[]{:S(2)}) copy-start(f32[1,2,128]{2,1,0:T(2,128)} %param.9) | copy-start | bytes 3076
  1.4 6.1 %copy-start.4 = (s32[1,2,128]{2,1,0:T(2,128)S(1)}, s32[1,2,128]{2,1,0:T(2,128)}, u32[]{:S(2)}) copy-start(s32[1,2,128]{2,1,0:T(2,128)} %param.10) | copy-start | bytes 3076
  4.2 8.0 %collective-permute-start.1 = (bf16[128,260]{0,1:T(8,128)(2,1)S(1)}, bf16[128,260]{0,1:T(8,128)(2,1)S(1)}, u32[]{:S(2)}, u32[]{:S(2)}) collective-permute-start(bf16[128,260]{0,1:T(8,128)(2,1)S(1)} %pad_maximum_fusion.10), channel_id=1, source_target_pairs={{0,2},{2,0},{1,3},{3,1},{4,6},{6,4},{5,7},{7,5},{8,10},{10,8},{9,1... | collective-permute-start | bytes 199688 | tf_op jit(solution)/shard_map/ppermute | solution.py:17
  7.2 5.0 %collective-permute-start = (bf16[4,64,256]{2,1,0:T(8,128)(2,1)S(1)}, bf16[4,64,256]{2,1,0:T(8,128)(2,1)S(1)}, u32[]{:S(2)}, u32[]{:S(2)}) collective-permute-start(bf16[4,64,256]{2,1,0:T(8,128)(2,1)S(1)} %bitcast.96), channel_id=1, source_target_pairs={{0,1},{1,0},{2,3},{3,2},{4,5},{5,4},{6,7},{7,6},{8,9},{9,8},{10,11... | collective-permute-start | bytes 393224 | tf_op jit(solution)/shard_map/ppermute | solution.py:17
  12.5 6.6 %collective-permute-start.2 = (bf16[128,256]{0,1:T(8,128)(2,1)S(1)}, bf16[128,256]{0,1:T(8,128)(2,1)S(1)}, u32[]{:S(2)}, u32[]{:S(2)}) collective-permute-start(bf16[128,256]{0,1:T(8,128)(2,1)S(1)} %get-tuple-element.14), channel_id=1, source_target_pairs={{0,4},{4,8},{8,12},{12,0},{1,5},{5,9},{9,13},{13,1},{2,6},{6,10},{... | collective-permute-start | bytes 196616 | tf_op jit(solution)/shard_map/ppermute | solution.py:77
  14.2 7.7 %collective-permute-start.3 = (bf16[128,256]{0,1:T(8,128)(2,1)S(1)}, bf16[128,256]{0,1:T(8,128)(2,1)S(1)}, u32[]{:S(2)}, u32[]{:S(2)}) collective-permute-start(bf16[128,256]{0,1:T(8,128)(2,1)S(1)} %get-tuple-element.16), channel_id=1, source_target_pairs={{0,8},{4,12},{8,0},{12,4},{1,9},{5,13},{9,1},{13,5},{2,10},{6,14},... | collective-permute-start | bytes 196616 | tf_op jit(solution)/shard_map/ppermute | solution.py:77
  16.7 5.4 %collective-permute-start.4 = (bf16[128,256]{0,1:T(8,128)(2,1)S(1)}, bf16[128,256]{0,1:T(8,128)(2,1)S(1)}, u32[]{:S(2)}, u32[]{:S(2)}) collective-permute-start(bf16[128,256]{0,1:T(8,128)(2,1)S(1)} %get-tuple-element.15), channel_id=1, source_target_pairs={{0,12},{4,0},{8,4},{12,8},{1,13},{5,1},{9,5},{13,9},{2,14},{6,2},{... | collective-permute-start | bytes 196616 | tf_op jit(solution)/shard_map/ppermute | solution.py:77
  22.5 8.1 %collective-permute-start.5 = (bf16[128,256]{0,1:T(8,128)(2,1)S(1)}, bf16[128,256]{0,1:T(8,128)(2,1)S(1)}, u32[]{:S(2)}, u32[]{:S(2)}) collective-permute-start(bf16[128,256]{0,1:T(8,128)(2,1)S(1)} %get-tuple-element.24), channel_id=1, source_target_pairs={{2,4},{4,2},{6,8},{8,6},{10,12},{12,10},{3,5},{5,3},{7,9},{9,7},{1... | collective-permute-start | bytes 196616 | tf_op jit(solution)/shard_map/ppermute | solution.py:157
  23.2 7.4 %collective-permute-start.7 = (bf16[128,256]{0,1:T(8,128)(2,1)S(1)}, bf16[128,256]{0,1:T(8,128)(2,1)S(1)}, u32[]{:S(2)}, u32[]{:S(2)}) collective-permute-start(bf16[128,256]{0,1:T(8,128)(2,1)S(1)} %get-tuple-element.24), channel_id=1, source_target_pairs={{2,6},{4,0},{6,10},{8,4},{10,14},{12,8},{3,7},{5,1},{7,11},{9,5},{... | collective-permute-start | bytes 196616 | tf_op jit(solution)/shard_map/ppermute | solution.py:158
  24.5 9.9 %collective-permute-start.6 = (bf16[128,896]{0,1:T(8,128)(2,1)S(1)}, bf16[128,896]{0,1:T(8,128)(2,1)S(1)}, u32[]{:S(2)}, u32[]{:S(2)}) collective-permute-start(bf16[128,896]{0,1:T(8,128)(2,1)S(1)} %pad_maximum_fusion.4), channel_id=1, source_target_pairs={{0,2},{2,0},{1,3},{3,1},{4,6},{6,4},{5,7},{7,5},{8,10},{10,8},{9,1... | collective-permute-start | bytes 688136 | tf_op jit(solution)/shard_map/ppermute | solution.py:17
  35.4 5.5 %collective-permute-start.10 = (bf16[128,256]{0,1:T(8,128)(2,1)S(1)}, bf16[128,256]{0,1:T(8,128)(2,1)S(1)}, u32[]{:S(2)}, u32[]{:S(2)}) collective-permute-start(bf16[128,256]{0,1:T(8,128)(2,1)S(1)} %get-tuple-element.12), channel_id=1, source_target_pairs={{0,12},{4,0},{8,4},{12,8},{1,13},{5,1},{9,5},{13,9},{2,14},{6,2},{... | collective-permute-start | bytes 196616 | tf_op jit(solution)/shard_map/ppermute | solution.py:77
  39.0 6.1 %collective-permute-start.8 = (bf16[128,256]{0,1:T(8,128)(2,1)S(1)}, bf16[128,256]{0,1:T(8,128)(2,1)S(1)}, u32[]{:S(2)}, u32[]{:S(2)}) collective-permute-start(bf16[128,256]{0,1:T(8,128)(2,1)S(1)} %get-tuple-element.11), channel_id=1, source_target_pairs={{0,4},{4,8},{8,12},{12,0},{1,5},{5,9},{9,13},{13,1},{2,6},{6,10},{... | collective-permute-start | bytes 196616 | tf_op jit(solution)/shard_map/ppermute | solution.py:77
  39.0 6.1 %collective-permute-start.9 = (bf16[128,256]{0,1:T(8,128)(2,1)S(1)}, bf16[128,256]{0,1:T(8,128)(2,1)S(1)}, u32[]{:S(2)}, u32[]{:S(2)}) collective-permute-start(bf16[128,256]{0,1:T(8,128)(2,1)S(1)} %get-tuple-element.13), channel_id=1, source_target_pairs={{0,8},{4,12},{8,0},{12,4},{1,9},{5,13},{9,1},{13,5},{2,10},{6,14},... | collective-permute-start | bytes 196616 | tf_op jit(solution)/shard_map/ppermute | solution.py:77

commit v13 on v12

--- a/solution.py
+++ b/solution.py
@@ -53,8 +53,6 @@
 
     lower_at = trace_rows[0, 0]
     upper_at = trace_rows[0, 1]
-    lower_basis = basis[lower_at]
-    upper_basis = basis[upper_at]
     face_inverse = jnp.concatenate(
         [inverse[:, :face_rows], inverse[:, iface_rows - face_rows :]], axis=1
     )
@@ -65,10 +63,11 @@
         )
         return jnp.where(live, projected, 0.0).astype(jnp.bfloat16)
 
-    def coarse_of(inputs):
+    def coarse_of(inputs, riders):
         partial = jnp.einsum(
             "jsc,cm->jsm", columns, inputs, preferred_element_type=jnp.float32
         ).astype(jnp.bfloat16)
+        partial, riders = lax.optimization_barrier((partial, riders))
         total = lax.dynamic_index_in_dim(partial, sub_index, 0, keepdims=False).astype(
             jnp.float32
         )
@@ -77,19 +76,12 @@
             total = total + lax.ppermute(
                 piece, "sub", [(i, (i + k) % sub_count) for i in range(sub_count)]
             ).astype(jnp.float32)
-        return total.astype(jnp.bfloat16)
+        return total.astype(jnp.bfloat16), riders
 
     pairwise = lax.axis_size("tile") == 2 and ROUNDS == 2
     tile_index = lax.axis_index("tile")
     gains = coupling[0]
     if pairwise:
-        sends = jnp.where(
-            live, jnp.dot(basis.T, face_inverse, preferred_element_type=jnp.float32), 0.0
-        )
-        keeps = jnp.where(
-            live & live.T, jnp.dot(basis.T, basis, preferred_element_type=jnp.float32), 0.0
-        )
-        mine = jnp.concatenate([sends, keeps], axis=1).astype(jnp.bfloat16)
         gains_high = gains.T.astype(jnp.bfloat16)
         gains_low = (gains.T - gains_high.astype(jnp.float32)).astype(jnp.bfloat16)
         gains_pair = jnp.concatenate([gains_high, gains_low], axis=1)
@@ -136,17 +128,33 @@
         inputs = gathered(projected, "tile", 0)
     earlier = None
     for cycle_index in range(ROUNDS):
-        coarse = coarse_of(inputs)
+        coarse, (solve_now, basis_now, faces_inverse_now) = coarse_of(
+            inputs, (local_solve, basis, face_inverse)
+        )
+        lower_basis = basis_now[lower_at]
+        upper_basis = basis_now[upper_at]
+        if pairwise and cycle_index == 0:
+            sends = jnp.where(
+                live,
+                jnp.dot(basis_now.T, faces_inverse_now, preferred_element_type=jnp.float32),
+                0.0,
+            )
+            keeps = jnp.where(
+                live & live.T,
+                jnp.dot(basis_now.T, basis_now, preferred_element_type=jnp.float32),
+                0.0,
+            )
+            mine = jnp.concatenate([sends, keeps], axis=1).astype(jnp.bfloat16)
         coarse = jnp.where(live, coarse, jnp.zeros((), coarse.dtype))
         correction = jnp.dot(basis, coarse, preferred_element_type=jnp.float32)
         iterate = local_solve + correction
         if cycle_index == ROUNDS - 1:
             break
         lower_trace = (
-            local_solve[lower_at] + jnp.dot(lower_basis, coarse, preferred_element_type=jnp.float32)
+            solve_now[lower_at] + jnp.dot(lower_basis, coarse, preferred_element_type=jnp.float32)
         ).astype(jnp.bfloat16)
         upper_trace = (
-            local_solve[upper_at] + jnp.dot(upper_basis, coarse, preferred_element_type=jnp.float32)
+            solve_now[upper_at] + jnp.dot(upper_basis, coarse, preferred_element_type=jnp.float32)
         ).astype(jnp.bfloat16)
         rows = lower_trace.shape[0]
         if pairwise:

time: 46.4 us -> 44.9 us (0.968)
  waiting for transfers between devices: 14.2 us -> 9.15 us
  starting transfers between devices: 19.5 us -> 21.4 us
  other arithmetic: 0.91 us -> 1.87 us
  local copies, waits for them, and re-layouts: 4.27 us -> 4.92 us
    ppermute x6, waiting for transfers between devices: 8.86 us -> 4.17 us  [coarse_of(): lax.ppermute(piece, 'sub', [(i, (i + k) % sub_count) for i in range(sub_c...]
    ppermute x6, starting transfers between devices: 10 us -> 12.2 us  [coarse_of(): lax.ppermute(piece, 'sub', [(i, (i + k) % sub_count) for i in range(sub_c...]
    ppermute x3, waiting for transfers between devices: 3.79 us -> 2.24 us  [swapped(): return lax.ppermute(shard, axis, [(0, 1), (1, 0)])]
    ppermute x1, waiting for transfers between devices: 1.53 us -> 2.73 us  [local(): crossing = lax.ppermute(toward_diagonal, DUCT, crossing_pairs)]
    select_n x1, other arithmetic: 0.05 us -> 0.95 us  [local(): coarse = jnp.where(live, coarse, jnp.zeros((), coarse.dtype))]
    squeeze x2, local copies, waits for them, and re-layouts: 0.05 us -> 0.7 us  [coarse_of(): lax.dynamic_index_in_dim(partial, (sub_index + k) % sub_count, 0, keepdim...]
  transfers between devices with their start and end apart: 11 -> 11, of which waited for: 7 -> 5; matrix products, arithmetic and copies ran while one was open for 11% -> 11% of each run, Pallas kernels for 0% -> 0%
where the time goes in v13:
time: 44.9 us; the launch traced here: 44.7 us
  starting transfers between devices  21.4 us (48%)
  waiting for transfers between devices  9.15 us (20%)
  matrix products  6.25 us (14%)
  local copies, waits for them, and re-layouts  4.92 us (11%)
  other arithmetic  1.87 us (4%)
  between operations  1.04 us (2%)
    ppermute x6, starting transfers between devices, coarse_of(): lax.ppermute(piece, 'sub', [(i, (i + k) % sub_count) for i in range(sub_c...  12.2 us
    ppermute x3, starting transfers between devices, swapped(): return lax.ppermute(shard, axis, [(0, 1), (1, 0)])  7.28 us
    ppermute x6, waiting for transfers between devices, coarse_of(): lax.ppermute(piece, 'sub', [(i, (i + k) % sub_count) for i in range(sub_c...  4.17 us
    ppermute x1, waiting for transfers between devices, local(): crossing = lax.ppermute(toward_diagonal, DUCT, crossing_pairs)  2.73 us
    dot_general x1, matrix products, local(): base_solve = jnp.dot(inverse, source, preferred_element_type=jnp.float32)  2.35 us
    ppermute x3, waiting for transfers between devices, swapped(): return lax.ppermute(shard, axis, [(0, 1), (1, 0)])  2.24 us
    ppermute x1, starting transfers between devices, local(): crossing = lax.ppermute(toward_diagonal, DUCT, crossing_pairs)  1.29 us
    dot_general x1, matrix products, local(): correction = jnp.dot(basis, coarse, preferred_element_type=jnp.float32)  1.1 us
  transfers between devices with their start and end apart: 11, of which 5 were waited for; matrix products, arithmetic and copies ran while one was open for 11% of the time, Pallas kernels for 0%

profile of v13, /device:TPU:0, one launch (start us, length us, event | category | flops | bytes accessed | tf_op | source)
XLA Modules:
  0.0 44.7 jit_solution(16268661766178968740)
XLA Ops:
  0.7 0.7 %fusion.40 = (bf16[128,2]{0,1:T(2,128)(2,1)S(1)}, bf16[128,2]{0,1:T(2,128)(2,1)S(1)}) fusion(f32[1,2,128]{2,1,0:T(2,128)} %param.9), kind=kLoop, calls=%fused_computation.88 | loop fusion | flops 1024 | bytes 2048 | tf_op jit(solution)/shard_map/convert_element_type | solution.py:86
  1.4 2.4 %fusion.11 = f32[1024,256]{1,0:T(8,128)S(1)} fusion(bf16[1,1024,256]{2,1,0:T(8,128)(2,1)S(1)} %copy-done, bf16[1,1024,1024]{2,1,0:T(8,128)(2,1)} %param.8), kind=kOutput, calls=%fused_computation.27 | convolution fusion | flops 536870912 | bytes 3670016 | tf_op jit(solution)/shard_map/dot_general | solution.py:110
  4.2 3.0 %collective-permute-start.1 = (bf16[128,260]{0,1:T(8,128)(2,1)S(1)}, bf16[128,260]{0,1:T(8,128)(2,1)S(1)}, u32[]{:S(2)}, u32[]{:S(2)}) collective-permute-start(bf16[128,260]{0,1:T(8,128)(2,1)S(1)} %pad_maximum_fusion.8), channel_id=1, source_target_pairs={{0,2},{2,0},{1,3},{3,1},{4,6},{6,4},{5,7},{7,5},{8,10},{10,8},{9,1... | collective-permute-start | bytes 199688 | tf_op jit(solution)/shard_map/ppermute | solution.py:17
  7.2 1.1 %fusion.52 = (bf16[1024,128]{1,0:T(8,128)(2,1)S(1)}, bf16[1024,128]{1,0:T(8,128)(2,1)S(1)}) fusion(bf16[1024,1024]{1,0:T(8,128)(2,1)} %bitcast.97), kind=kLoop, calls=%fused_computation.106 | loop fusion | bytes 1048576 | tf_op jit(solution)/shard_map/slice | solution.py:57
  8.4 1.0 %collective-permute-done.1 = bf16[128,260]{0,1:T(8,128)(2,1)S(1)} collective-permute-done((bf16[128,260]{0,1:T(8,128)(2,1)S(1)}, bf16[128,260]{0,1:T(8,128)(2,1)S(1)}, u32[]{:S(2)}, u32[]{:S(2)}) %collective-permute-start.1) | collective-permute-done | bytes 66592 | tf_op jit(solution)/shard_map/ppermute | solution.py:17
  9.8 0.7 %dynamic-slice_bitcast_fusion.5 = (bf16[128,256]{0,1:T(8,128)(2,1)}, bf16[128,256]{0,1:T(8,128)(2,1)}, bf16[128,256]{0,1:T(8,128)(2,1)}) fusion(bf16[4,128,256]{1,2,0:T(8,128)(2,1)S(1)} %convolution_convert_fusion.1, s32[]{:T(128)S(6)} %select_n.145, s32[]{:T(128)S(6)} %select_n.149, s32[]{:T(128)S(6)} %select_n.147), kind=kLoop, calls=%fused_computation.70 | loop fusion | bytes 393228 | tf_op jit(solution)/shard_map/jit(dynamic_index_in_dim)/squeeze | solution.py:75
  10.5 2.1 %collective-permute-start.2 = (bf16[128,256]{0,1:T(8,128)(2,1)}, bf16[128,256]{0,1:T(8,128)(2,1)}, u32[]{:S(2)}, u32[]{:S(2)}) collective-permute-start(bf16[128,256]{0,1:T(8,128)(2,1)} %get-tuple-element.24), channel_id=1, source_target_pairs={{0,4},{4,8},{8,12},{12,0},{1,5},{5,9},{9,13},{13,1},{2,6},{6,10},{... | collective-permute-start | bytes 196616 | tf_op jit(solution)/shard_map/ppermute | solution.py:76
  12.6 2.6 %collective-permute-start.3 = (bf16[128,256]{0,1:T(8,128)(2,1)}, bf16[128,256]{0,1:T(8,128)(2,1)}, u32[]{:S(2)}, u32[]{:S(2)}) collective-permute-start(bf16[128,256]{0,1:T(8,128)(2,1)} %get-tuple-element.26), channel_id=1, source_target_pairs={{0,8},{4,12},{8,0},{12,4},{1,9},{5,13},{9,1},{13,5},{2,10},{6,14},... | collective-permute-start | bytes 196616 | tf_op jit(solution)/shard_map/ppermute | solution.py:76
  15.2 1.3 %collective-permute-start.4 = (bf16[128,256]{0,1:T(8,128)(2,1)}, bf16[128,256]{0,1:T(8,128)(2,1)}, u32[]{:S(2)}, u32[]{:S(2)}) collective-permute-start(bf16[128,256]{0,1:T(8,128)(2,1)} %get-tuple-element.25), channel_id=1, source_target_pairs={{0,12},{4,0},{8,4},{12,8},{1,13},{5,1},{9,5},{13,9},{2,14},{6,2},{... | collective-permute-start | bytes 196616 | tf_op jit(solution)/shard_map/ppermute | solution.py:76
  16.5 0.3 fusion.4
  17.2 0.7 %gather_fusion.1 = bf16[128,128]{1,0:T(8,128)(2,1)S(1)} fusion(bf16[1024,128]{1,0:T(8,128)(2,1)S(1)} %bitcast.94, s32[1024]{0:T(1024)S(1)} %get-tuple-element.45), kind=kCustom, calls=%fused_computation.1 | custom fusion | bytes 66048 | tf_op jit(solution)/shard_map/gather | solution.py:134
  17.9 0.8 %gather_fusion = f32[128,256]{1,0:T(8,128)S(1)} fusion(f32[1024,256]{1,0:T(8,128)S(1)} %fusion.11, s32[1024]{0:T(1024)S(1)} %get-tuple-element.45), kind=kCustom, calls=%fused_computation | custom fusion | bytes 262656 | tf_op jit(solution)/shard_map/gather | solution.py:154
  18.6 0.7 %gather_fusion.3 = bf16[128,128]{1,0:T(8,128)(2,1)S(1)} fusion(bf16[1024,128]{1,0:T(8,128)(2,1)S(1)} %bitcast.95, s32[1024]{0:T(1024)S(1)} %get-tuple-element.44), kind=kCustom, calls=%fused_computation.3 | custom fusion | bytes 66048 | tf_op jit(solution)/shard_map/gather | solution.py:135
  19.4 0.8 %gather_fusion.2 = f32[128,256]{1,0:T(8,128)S(1)} fusion(f32[1024,256]{1,0:T(8,128)S(1)} %fusion.11, s32[1024]{0:T(1024)S(1)} %get-tuple-element.44), kind=kCustom, calls=%fused_computation.2 | custom fusion | bytes 262656 | tf_op jit(solution)/shard_map/gather | solution.py:157
  20.3 1.0 %fusion.28 = bf16[128,256]{0,1:T(8,128)(2,1)S(1)} fusion(bf16[128,256]{0,1:T(8,128)(2,1)} %collective-permute-done.4, bf16[128,256]{0,1:T(8,128)(2,1)} %collective-permute-done.3, bf16[128,256]{0,1:T(8,128)(2,1)} %collective-permute-done.2, bf16[4,128,256]{1,2,0:T(8,128)(2,1)S(1)} %convolution_convert_fusion.1, s32[]{:T(128)S(6)} %select_n.143, ...), kind=kLoop, calls=%fused_computation.58 | loop fusion | flops 294912 | bytes 327812 | tf_op jit(solution)/shard_map/jit(_where)/select_n | solution.py:148
  21.6 0.7 %collective-permute-start.5 = (bf16[128,256]{0,1:T(8,128)(2,1)S(1)}, bf16[128,256]{0,1:T(8,128)(2,1)S(1)}, u32[]{:S(2)}, u32[]{:S(2)}) collective-permute-start(bf16[128,256]{0,1:T(8,128)(2,1)S(1)} %get-tuple-element.34), channel_id=1, source_target_pairs={{2,4},{4,2},{6,8},{8,6},{10,12},{12,10},{3,5},{5,3},{7,9},{9,7},{1... | collective-permute-start | bytes 196616 | tf_op jit(solution)/shard_map/ppermute | solution.py:165
  22.3 1.3 %collective-permute-start.7 = (bf16[128,256]{0,1:T(8,128)(2,1)S(1)}, bf16[128,256]{0,1:T(8,128)(2,1)S(1)}, u32[]{:S(2)}, u32[]{:S(2)}) collective-permute-start(bf16[128,256]{0,1:T(8,128)(2,1)S(1)} %get-tuple-element.34), channel_id=1, source_target_pairs={{2,6},{4,0},{6,10},{8,4},{10,14},{12,8},{3,7},{5,1},{7,11},{9,5},{... | collective-permute-start | bytes 196616 | tf_op jit(solution)/shard_map/ppermute | solution.py:166
  23.6 4.3 %collective-permute-start.6 = (bf16[128,896]{0,1:T(8,128)(2,1)S(1)}, bf16[128,896]{0,1:T(8,128)(2,1)S(1)}, u32[]{:S(2)}, u32[]{:S(2)}) collective-permute-start(bf16[128,896]{0,1:T(8,128)(2,1)S(1)} %pad_maximum_fusion.2), channel_id=1, source_target_pairs={{0,2},{2,0},{1,3},{3,1},{4,6},{6,4},{5,7},{7,5},{8,10},{10,8},{9,1... | collective-permute-start | bytes 688136 | tf_op jit(solution)/shard_map/ppermute | solution.py:17
  27.9 2.7 %collective-permute-done.7 = bf16[128,256]{0,1:T(8,128)(2,1)S(1)} collective-permute-done((bf16[128,256]{0,1:T(8,128)(2,1)S(1)}, bf16[128,256]{0,1:T(8,128)(2,1)S(1)}, u32[]{:S(2)}, u32[]{:S(2)}) %collective-permute-start.7) | collective-permute-done | bytes 65568 | tf_op jit(solution)/shard_map/ppermute | solution.py:166
  30.7 1.2 %collective-permute-done.6 = bf16[128,896]{0,1:T(8,128)(2,1)S(1)} collective-permute-done((bf16[128,896]{0,1:T(8,128)(2,1)S(1)}, bf16[128,896]{0,1:T(8,128)(2,1)S(1)}, u32[]{:S(2)}, u32[]{:S(2)}) %collective-permute-start.6) | collective-permute-done | bytes 229408 | tf_op jit(solution)/shard_map/ppermute | solution.py:17
  33.2 4.3 %collective-permute-start.10 = (bf16[128,256]{0,1:T(8,128)(2,1)S(1)}, bf16[128,256]{0,1:T(8,128)(2,1)S(1)}, u32[]{:S(2)}, u32[]{:S(2)}) collective-permute-start(bf16[128,256]{0,1:T(8,128)(2,1)S(1)} %get-tuple-element.22), channel_id=1, source_target_pairs={{0,12},{4,0},{8,4},{12,8},{1,13},{5,1},{9,5},{13,9},{2,14},{6,2},{... | collective-permute-start | bytes 196616 | tf_op jit(solution)/shard_map/ppermute | solution.py:76
  37.5 1.9 %collective-permute-start.9 = (bf16[128,256]{0,1:T(8,128)(2,1)S(1)}, bf16[128,256]{0,1:T(8,128)(2,1)S(1)}, u32[]{:S(2)}, u32[]{:S(2)}) collective-permute-start(bf16[128,256]{0,1:T(8,128)(2,1)S(1)} %get-tuple-element.23), channel_id=1, source_target_pairs={{0,8},{4,12},{8,0},{12,4},{1,9},{5,13},{9,1},{13,5},{2,10},{6,14},... | collective-permute-start | bytes 196616 | tf_op jit(solution)/shard_map/ppermute | solution.py:76
  39.6 3.9 %collective-permute-done.8 = bf16[128,256]{0,1:T(8,128)(2,1)S(1)} collective-permute-done((bf16[128,256]{0,1:T(8,128)(2,1)S(1)}, bf16[128,256]{0,1:T(8,128)(2,1)S(1)}, u32[]{:S(2)}, u32[]{:S(2)}) %collective-permute-start.8) | collective-permute-done | bytes 65568 | tf_op jit(solution)/shard_map/ppermute | solution.py:76
  43.6 1.1 %fusion.2 = bf16[1,1024,256]{2,1,0:T(8,128)(2,1)} fusion(f32[1024,256]{1,0:T(8,128)S(1)} %convolution_add_fusion, bf16[128,256]{0,1:T(8,128)(2,1)S(1)} %collective-permute-done.10, bf16[128,256]{0,1:T(8,128)(2,1)S(1)} %collective-permute-done.9, bf16[128,256]{0,1:T(8,128)(2,1)S(1)} %collective-permute-done.8, ...), kind=kOutput, calls=%fused_computation.8 | convolution fusion | flops 67928064 | bytes 2097668 | tf_op jit(solution)/shard_map/dot_general | solution.py:149
  (47 shorter events, 3.2 us)
Async XLA Ops:
  0.0 1.4 %copy-start = (bf16[1,1024,256]{2,1,0:T(8,128)(2,1)S(1)}, bf16[1,1024,256]{2,1,0:T(8,128)(2,1)}, u32[]{:S(2)}) copy-start(bf16[1,1024,256]{2,1,0:T(8,128)(2,1)} %param.7) | copy-start | bytes 1572868
  1.4 2.4 %copy-start.1 = (bf16[1,1024,128]{2,1,0:T(8,128)(2,1)S(1)}, bf16[1,1024,128]{2,1,0:T(8,128)(2,1)}, u32[]{:S(2)}) copy-start(bf16[1,1024,128]{2,1,0:T(8,128)(2,1)} %param.11) | copy-start | bytes 786436
  1.4 5.8 %copy-start.2 = (bf16[4,1,64,1,256]{4,2,3,1,0:T(8,128)(2,1)S(1)}, bf16[4,1,64,1,256]{4,2,3,1,0:T(8,128)(2,1)}, u32[]{:S(2)}) copy-start(bf16[4,1,64,1,256]{4,2,3,1,0:T(8,128)(2,1)} %param.13) | copy-start | bytes 393220
  1.4 5.8 %copy-start.3 = (f32[1,2,128]{2,1,0:T(2,128)S(1)}, f32[1,2,128]{2,1,0:T(2,128)}, u32[]{:S(2)}) copy-start(f32[1,2,128]{2,1,0:T(2,128)} %param.9) | copy-start | bytes 3076
  3.8 4.5 %copy-start.4 = (s32[1,2,128]{2,1,0:T(2,128)S(1)}, s32[1,2,128]{2,1,0:T(2,128)}, u32[]{:S(2)}) copy-start(s32[1,2,128]{2,1,0:T(2,128)} %param.10) | copy-start | bytes 3076
  4.2 5.3 %collective-permute-start.1 = (bf16[128,260]{0,1:T(8,128)(2,1)S(1)}, bf16[128,260]{0,1:T(8,128)(2,1)S(1)}, u32[]{:S(2)}, u32[]{:S(2)}) collective-permute-start(bf16[128,260]{0,1:T(8,128)(2,1)S(1)} %pad_maximum_fusion.8), channel_id=1, source_target_pairs={{0,2},{2,0},{1,3},{3,1},{4,6},{6,4},{5,7},{7,5},{8,10},{10,8},{9,1... | collective-permute-start | bytes 199688 | tf_op jit(solution)/shard_map/ppermute | solution.py:17
  7.2 2.3 %collective-permute-start = (bf16[4,64,256]{2,1,0:T(8,128)(2,1)S(1)}, bf16[4,64,256]{2,1,0:T(8,128)(2,1)S(1)}, u32[]{:S(2)}, u32[]{:S(2)}) collective-permute-start(bf16[4,64,256]{2,1,0:T(8,128)(2,1)S(1)} %bitcast.96), channel_id=1, source_target_pairs={{0,1},{1,0},{2,3},{3,2},{4,5},{5,4},{6,7},{7,6},{8,9},{9,8},{10,11... | collective-permute-start | bytes 393224 | tf_op jit(solution)/shard_map/ppermute | solution.py:17
  10.5 9.8 %collective-permute-start.2 = (bf16[128,256]{0,1:T(8,128)(2,1)}, bf16[128,256]{0,1:T(8,128)(2,1)}, u32[]{:S(2)}, u32[]{:S(2)}) collective-permute-start(bf16[128,256]{0,1:T(8,128)(2,1)} %get-tuple-element.24), channel_id=1, source_target_pairs={{0,4},{4,8},{8,12},{12,0},{1,5},{5,9},{9,13},{13,1},{2,6},{6,10},{... | collective-permute-start | bytes 196616 | tf_op jit(solution)/shard_map/ppermute | solution.py:76
  12.6 7.7 %collective-permute-start.3 = (bf16[128,256]{0,1:T(8,128)(2,1)}, bf16[128,256]{0,1:T(8,128)(2,1)}, u32[]{:S(2)}, u32[]{:S(2)}) collective-permute-start(bf16[128,256]{0,1:T(8,128)(2,1)} %get-tuple-element.26), channel_id=1, source_target_pairs={{0,8},{4,12},{8,0},{12,4},{1,9},{5,13},{9,1},{13,5},{2,10},{6,14},... | collective-permute-start | bytes 196616 | tf_op jit(solution)/shard_map/ppermute | solution.py:76
  15.2 5.1 %collective-permute-start.4 = (bf16[128,256]{0,1:T(8,128)(2,1)}, bf16[128,256]{0,1:T(8,128)(2,1)}, u32[]{:S(2)}, u32[]{:S(2)}) collective-permute-start(bf16[128,256]{0,1:T(8,128)(2,1)} %get-tuple-element.25), channel_id=1, source_target_pairs={{0,12},{4,0},{8,4},{12,8},{1,13},{5,1},{9,5},{13,9},{2,14},{6,2},{... | collective-permute-start | bytes 196616 | tf_op jit(solution)/shard_map/ppermute | solution.py:76
  21.6 9.1 %collective-permute-start.5 = (bf16[128,256]{0,1:T(8,128)(2,1)S(1)}, bf16[128,256]{0,1:T(8,128)(2,1)S(1)}, u32[]{:S(2)}, u32[]{:S(2)}) collective-permute-start(bf16[128,256]{0,1:T(8,128)(2,1)S(1)} %get-tuple-element.34), channel_id=1, source_target_pairs={{2,4},{4,2},{6,8},{8,6},{10,12},{12,10},{3,5},{5,3},{7,9},{9,7},{1... | collective-permute-start | bytes 196616 | tf_op jit(solution)/shard_map/ppermute | solution.py:165
  22.3 8.3 %collective-permute-start.7 = (bf16[128,256]{0,1:T(8,128)(2,1)S(1)}, bf16[128,256]{0,1:T(8,128)(2,1)S(1)}, u32[]{:S(2)}, u32[]{:S(2)}) collective-permute-start(bf16[128,256]{0,1:T(8,128)(2,1)S(1)} %get-tuple-element.34), channel_id=1, source_target_pairs={{2,6},{4,0},{6,10},{8,4},{10,14},{12,8},{3,7},{5,1},{7,11},{9,5},{... | collective-permute-start | bytes 196616 | tf_op jit(solution)/shard_map/ppermute | solution.py:166
  23.6 8.3 %collective-permute-start.6 = (bf16[128,896]{0,1:T(8,128)(2,1)S(1)}, bf16[128,896]{0,1:T(8,128)(2,1)S(1)}, u32[]{:S(2)}, u32[]{:S(2)}) collective-permute-start(bf16[128,896]{0,1:T(8,128)(2,1)S(1)} %pad_maximum_fusion.2), channel_id=1, source_target_pairs={{0,2},{2,0},{1,3},{3,1},{4,6},{6,4},{5,7},{7,5},{8,10},{10,8},{9,1... | collective-permute-start | bytes 688136 | tf_op jit(solution)/shard_map/ppermute | solution.py:17
  33.2 6.4 %collective-permute-start.10 = (bf16[128,256]{0,1:T(8,128)(2,1)S(1)}, bf16[128,256]{0,1:T(8,128)(2,1)S(1)}, u32[]{:S(2)}, u32[]{:S(2)}) collective-permute-start(bf16[128,256]{0,1:T(8,128)(2,1)S(1)} %get-tuple-element.22), channel_id=1, source_target_pairs={{0,12},{4,0},{8,4},{12,8},{1,13},{5,1},{9,5},{13,9},{2,14},{6,2},{... | collective-permute-start | bytes 196616 | tf_op jit(solution)/shard_map/ppermute | solution.py:76
  37.5 6.1 %collective-permute-start.8 = (bf16[128,256]{0,1:T(8,128)(2,1)S(1)}, bf16[128,256]{0,1:T(8,128)(2,1)S(1)}, u32[]{:S(2)}, u32[]{:S(2)}) collective-permute-start(bf16[128,256]{0,1:T(8,128)(2,1)S(1)} %get-tuple-element.21), channel_id=1, source_target_pairs={{0,4},{4,8},{8,12},{12,0},{1,5},{5,9},{9,13},{13,1},{2,6},{6,10},{... | collective-permute-start | bytes 196616 | tf_op jit(solution)/shard_map/ppermute | solution.py:76
  37.5 6.1 %collective-permute-start.9 = (bf16[128,256]{0,1:T(8,128)(2,1)S(1)}, bf16[128,256]{0,1:T(8,128)(2,1)S(1)}, u32[]{:S(2)}, u32[]{:S(2)}) collective-permute-start(bf16[128,256]{0,1:T(8,128)(2,1)S(1)} %get-tuple-element.23), channel_id=1, source_target_pairs={{0,8},{4,12},{8,0},{12,4},{1,9},{5,13},{9,1},{13,5},{2,10},{6,14},... | collective-permute-start | bytes 196616 | tf_op jit(solution)/shard_map/ppermute | solution.py:76

commit v14 on v13

--- a/solution.py
+++ b/solution.py
@@ -112,7 +112,7 @@
     projected = coarse_input(local_solve.astype(jnp.bfloat16))
     if pairwise:
         width = projected.shape[1]
-        got = swapped(jnp.concatenate([projected, gains_pair], axis=1), "tile")
+        got = swapped(projected, "tile")
         first = tile_index == 0
         inputs = jnp.concatenate(
             [
@@ -121,9 +121,6 @@
             ],
             axis=0,
         )
-        tail = got[:, width:].astype(jnp.float32)
-        pair = gains.shape[0]
-        partner_gains = (tail[:, :pair] + tail[:, pair:]).T
     else:
         inputs = gathered(projected, "tile", 0)
     earlier = None
@@ -161,7 +158,9 @@
             toward_partner = jnp.where(first, upper_trace, lower_trace)
             toward_diagonal = jnp.where(first, lower_trace, upper_trace)
             width = toward_partner.shape[1]
-            got = swapped(jnp.concatenate([toward_partner, coarse, mine], axis=1), "tile")
+            got = swapped(
+                jnp.concatenate([toward_partner, coarse, mine, gains_pair], axis=1), "tile"
+            )
             from_diagonal = lax.ppermute(toward_diagonal, DUCT, diagonal_pairs)
             crossing = lax.ppermute(toward_diagonal, DUCT, crossing_pairs)
             from_partner = got[:, :width]
@@ -171,7 +170,10 @@
             partner_lower = jnp.where(first, upper_trace, crossing).astype(jnp.float32)
             partner_upper = jnp.where(first, crossing, lower_trace).astype(jnp.float32)
             partner_coarse = got[:, width : 2 * width]
-            theirs = got[:, 2 * width :]
+            theirs = got[:, 2 * width : 2 * width + mine.shape[1]]
+            tail = got[:, 2 * width + mine.shape[1] :].astype(jnp.float32)
+            pair = gains.shape[0]
+            partner_gains = (tail[:, :pair] + tail[:, pair:]).T
             partner_faces = face_rows_of(partner_gains, partner_lower, partner_upper)
             own = projection_of(mine, faces, coarse)
             other = projection_of(theirs, partner_faces, partner_coarse)

time: 44.9 us -> 42.5 us (0.947)
  starting transfers between devices: 21.4 us -> 17.1 us
  waiting for transfers between devices: 9.15 us -> 10.5 us
  local copies, waits for them, and re-layouts: 4.92 us -> 5.61 us
  other arithmetic: 1.87 us -> 1.4 us
    ppermute x3, starting transfers between devices: 7.28 us -> 4.51 us  [swapped(): return lax.ppermute(shard, axis, [(0, 1), (1, 0)])]
    ppermute x3, waiting for transfers between devices: 2.24 us -> 3.89 us  [swapped(): return lax.ppermute(shard, axis, [(0, 1), (1, 0)])]
    ppermute x6, starting transfers between devices: 12.2 us -> 10.6 us  [coarse_of(): lax.ppermute(piece, 'sub', [(i, (i + k) % sub_count) for i in range(sub_c...]
    convert_element_type x1, other arithmetic: 0.69 us -> 0.01 us  [local(): gains_low = (gains.T - gains_high.astype(jnp.float32)).astype(jnp.bfloat16)]
    dot_general x1, matrix products: 0.17 us -> 0.79 us  [local(): jnp.dot(upper_basis, coarse, preferred_element_type=jnp.float32)]
    ppermute x1, waiting for transfers between devices: 2.73 us -> 2.19 us  [local(): crossing = lax.ppermute(toward_diagonal, DUCT, crossing_pairs)]
  transfers between devices with their start and end apart: 11 -> 11, of which waited for: 5 -> 6; matrix products, arithmetic and copies ran while one was open for 11% -> 14% of each run, Pallas kernels for 0% -> 0%
where the time goes in v14:
time: 42.5 us; the launch traced here: 42.2 us
  starting transfers between devices  17.1 us (40%)
  waiting for transfers between devices  10.5 us (25%)
  matrix products  6.62 us (16%)
  local copies, waits for them, and re-layouts  5.61 us (13%)
  other arithmetic  1.4 us (3%)
  between operations  1.02 us (2%)
    ppermute x6, starting transfers between devices, coarse_of(): lax.ppermute(piece, 'sub', [(i, (i + k) % sub_count) for i in range(sub_c...  10.6 us
    ppermute x3, starting transfers between devices, swapped(): return lax.ppermute(shard, axis, [(0, 1), (1, 0)])  4.51 us
    ppermute x6, waiting for transfers between devices, coarse_of(): lax.ppermute(piece, 'sub', [(i, (i + k) % sub_count) for i in range(sub_c...  4.4 us
    ppermute x3, waiting for transfers between devices, swapped(): return lax.ppermute(shard, axis, [(0, 1), (1, 0)])  3.89 us
    dot_general x1, matrix products, local(): base_solve = jnp.dot(inverse, source, preferred_element_type=jnp.float32)  2.35 us
    ppermute x1, waiting for transfers between devices, local(): crossing = lax.ppermute(toward_diagonal, DUCT, crossing_pairs)  2.19 us
    ppermute x1, starting transfers between devices, local(): crossing = lax.ppermute(toward_diagonal, DUCT, crossing_pairs)  1.29 us
    dot_general x1, matrix products, local(): correction = jnp.dot(basis, coarse, preferred_element_type=jnp.float32)  1.15 us
  transfers between devices with their start and end apart: 11, of which 6 were waited for; matrix products, arithmetic and copies ran while one was open for 14% of the time, Pallas kernels for 0%

profile of v14, /device:TPU:0, one launch (start us, length us, event | category | flops | bytes accessed | tf_op | source)
XLA Modules:
  0.0 42.2 jit_solution(5638851922460340270)
XLA Ops:
  1.1 2.4 %fusion.11 = f32[1024,256]{1,0:T(8,128)S(1)} fusion(bf16[1,1024,256]{2,1,0:T(8,128)(2,1)S(1)} %copy-done, bf16[1,1024,1024]{2,1,0:T(8,128)(2,1)} %param.8), kind=kOutput, calls=%fused_computation.27 | convolution fusion | flops 536870912 | bytes 3670016 | tf_op jit(solution)/shard_map/dot_general | solution.py:110
  3.7 3.0 %collective-permute-start.1 = (bf16[128,256]{1,0:T(8,128)(2,1)S(1)}, bf16[128,256]{1,0:T(8,128)(2,1)S(1)}, u32[]{:S(2)}, u32[]{:S(2)}) collective-permute-start(bf16[128,256]{1,0:T(8,128)(2,1)S(1)} %fusion.9), channel_id=1, source_target_pairs={{0,2},{2,0},{1,3},{3,1},{4,6},{6,4},{5,7},{7,5},{8,10},{10,8},{9,1... | collective-permute-start | bytes 196616 | tf_op jit(solution)/shard_map/ppermute | solution.py:17
  6.8 1.1 %fusion.53 = (bf16[1024,128]{1,0:T(8,128)(2,1)S(1)}, bf16[1024,128]{1,0:T(8,128)(2,1)S(1)}) fusion(bf16[1024,1024]{1,0:T(8,128)(2,1)} %bitcast.93), kind=kLoop, calls=%fused_computation.105 | loop fusion | bytes 1048576 | tf_op jit(solution)/shard_map/slice | solution.py:57
  8.2 0.8 %collective-permute-done.1 = bf16[128,256]{1,0:T(8,128)(2,1)S(1)} collective-permute-done((bf16[128,256]{1,0:T(8,128)(2,1)S(1)}, bf16[128,256]{1,0:T(8,128)(2,1)S(1)}, u32[]{:S(2)}, u32[]{:S(2)}) %collective-permute-start.1) | collective-permute-done | bytes 65568 | tf_op jit(solution)/shard_map/ppermute | solution.py:17
  9.3 0.7 %dynamic-slice_bitcast_fusion.5 = (bf16[128,256]{1,0:T(8,128)(2,1)}, bf16[128,256]{1,0:T(8,128)(2,1)}, bf16[128,256]{1,0:T(8,128)(2,1)}) fusion(bf16[4,128,256]{2,1,0:T(8,128)(2,1)S(1)} %convolution_convert_fusion.1, s32[]{:T(128)S(6)} %select_n.145, s32[]{:T(128)S(6)} %select_n.149, s32[]{:T(128)S(6)} %select_n.147), kind=kLoop, calls=%fused_computation.72 | loop fusion | bytes 393228 | tf_op jit(solution)/shard_map/jit(dynamic_index_in_dim)/squeeze | solution.py:75
  10.0 2.1 %collective-permute-start.2 = (bf16[128,256]{1,0:T(8,128)(2,1)}, bf16[128,256]{1,0:T(8,128)(2,1)}, u32[]{:S(2)}, u32[]{:S(2)}) collective-permute-start(bf16[128,256]{1,0:T(8,128)(2,1)} %get-tuple-element.26), channel_id=1, source_target_pairs={{0,4},{4,8},{8,12},{12,0},{1,5},{5,9},{9,13},{13,1},{2,6},{6,10},{... | collective-permute-start | bytes 196616 | tf_op jit(solution)/shard_map/ppermute | solution.py:76
  12.1 2.6 %collective-permute-start.3 = (bf16[128,256]{1,0:T(8,128)(2,1)}, bf16[128,256]{1,0:T(8,128)(2,1)}, u32[]{:S(2)}, u32[]{:S(2)}) collective-permute-start(bf16[128,256]{1,0:T(8,128)(2,1)} %get-tuple-element.28), channel_id=1, source_target_pairs={{0,8},{4,12},{8,0},{12,4},{1,9},{5,13},{9,1},{13,5},{2,10},{6,14},... | collective-permute-start | bytes 196616 | tf_op jit(solution)/shard_map/ppermute | solution.py:76
  14.7 1.3 %collective-permute-start.4 = (bf16[128,256]{1,0:T(8,128)(2,1)}, bf16[128,256]{1,0:T(8,128)(2,1)}, u32[]{:S(2)}, u32[]{:S(2)}) collective-permute-start(bf16[128,256]{1,0:T(8,128)(2,1)} %get-tuple-element.27), channel_id=1, source_target_pairs={{0,12},{4,0},{8,4},{12,8},{1,13},{5,1},{9,5},{13,9},{2,14},{6,2},{... | collective-permute-start | bytes 196616 | tf_op jit(solution)/shard_map/ppermute | solution.py:76
  16.6 0.7 %gather_fusion.1 = bf16[128,128]{1,0:T(8,128)(2,1)S(1)} fusion(bf16[1024,128]{1,0:T(8,128)(2,1)S(1)} %bitcast.90, s32[1024]{0:T(1024)S(1)} %get-tuple-element.45), kind=kCustom, calls=%fused_computation.1 | custom fusion | bytes 66048 | tf_op jit(solution)/shard_map/gather | solution.py:131
  17.3 0.8 %gather_fusion = f32[128,256]{1,0:T(8,128)S(1)} fusion(f32[1024,256]{1,0:T(8,128)S(1)} %fusion.11, s32[1024]{0:T(1024)S(1)} %get-tuple-element.45), kind=kCustom, calls=%fused_computation | custom fusion | bytes 262656 | tf_op jit(solution)/shard_map/gather | solution.py:151
  18.0 0.7 %gather_fusion.3 = bf16[128,128]{1,0:T(8,128)(2,1)S(1)} fusion(bf16[1024,128]{1,0:T(8,128)(2,1)S(1)} %bitcast.91, s32[1024]{0:T(1024)S(1)} %get-tuple-element.44), kind=kCustom, calls=%fused_computation.3 | custom fusion | bytes 66048 | tf_op jit(solution)/shard_map/gather | solution.py:132
  18.8 0.8 %gather_fusion.2 = f32[128,256]{1,0:T(8,128)S(1)} fusion(f32[1024,256]{1,0:T(8,128)S(1)} %fusion.11, s32[1024]{0:T(1024)S(1)} %get-tuple-element.44), kind=kCustom, calls=%fused_computation.2 | custom fusion | bytes 262656 | tf_op jit(solution)/shard_map/gather | solution.py:154
  19.6 1.0 %fusion.28 = bf16[128,256]{1,0:T(8,128)(2,1)S(1)} fusion(bf16[128,256]{1,0:T(8,128)(2,1)} %collective-permute-done.4, bf16[128,256]{1,0:T(8,128)(2,1)} %collective-permute-done.3, bf16[128,256]{1,0:T(8,128)(2,1)} %collective-permute-done.2, bf16[4,128,256]{2,1,0:T(8,128)(2,1)S(1)} %convolution_convert_fusion.1, s32[]{:T(128)S(6)} %select_n.143, ...), kind=kLoop, calls=%fused_computation.56 | loop fusion | flops 294912 | bytes 327812 | tf_op jit(solution)/shard_map/jit(_where)/select_n | solution.py:145
  20.7 0.8 %broadcast_select_fusion.4 = (bf16[128,256]{1,0:T(8,128)(2,1)S(1)}, bf16[128,256]{1,0:T(8,128)(2,1)}, bf16[128,256]{1,0:T(8,128)(2,1)S(1)}) fusion(bf16[128,256]{1,0:T(8,128)(2,1)S(1)} %fusion.5, pred[]{:T(512)S(6)} %eq.13, f32[128,256]{1,0:T(8,128)S(1)} %gather_fusion.2, bf16[128,128]{1,0:T(8,128)(2,1)S(1)} %gather_fusion.3, bf16[128,256]{1,0:T(8,128)(2,1)S(1)} %fusion.28), kind=kOutput, calls=%fused_computation.76 | convolution fusion | flops 8519680 | bytes 491521 | tf_op jit(solution)/shard_map/dot_general | solution.py:154
  21.6 1.5 %collective-permute-start.6 = (bf16[128,900]{1,0:T(8,128)(2,1)S(1)}, bf16[128,900]{1,0:T(8,128)(2,1)S(1)}, u32[]{:S(2)}, u32[]{:S(2)}) collective-permute-start(bf16[128,900]{1,0:T(8,128)(2,1)S(1)} %concatenate.29), channel_id=1, source_target_pairs={{0,2},{2,0},{1,3},{3,1},{4,6},{6,4},{5,7},{7,5},{8,10},{10,8},{9,1... | collective-permute-start | bytes 691208 | tf_op jit(solution)/shard_map/ppermute | solution.py:17
  23.1 0.7 %collective-permute-start.5 = (bf16[128,256]{1,0:T(8,128)(2,1)}, bf16[128,256]{1,0:T(8,128)(2,1)S(1)}, u32[]{:S(2)}, u32[]{:S(2)}) collective-permute-start(bf16[128,256]{1,0:T(8,128)(2,1)} %get-tuple-element.34), channel_id=1, source_target_pairs={{2,4},{4,2},{6,8},{8,6},{10,12},{12,10},{3,5},{5,3},{7,9},{9,7},{1... | collective-permute-start | bytes 196616 | tf_op jit(solution)/shard_map/ppermute | solution.py:164
  23.8 1.3 %collective-permute-start.7 = (bf16[128,256]{1,0:T(8,128)(2,1)}, bf16[128,256]{1,0:T(8,128)(2,1)S(1)}, u32[]{:S(2)}, u32[]{:S(2)}) collective-permute-start(bf16[128,256]{1,0:T(8,128)(2,1)} %get-tuple-element.34), channel_id=1, source_target_pairs={{2,6},{4,0},{6,10},{8,4},{10,14},{12,8},{3,7},{5,1},{7,11},{9,5},{... | collective-permute-start | bytes 196616 | tf_op jit(solution)/shard_map/ppermute | solution.py:165
  25.1 3.1 %collective-permute-done.6 = bf16[128,900]{1,0:T(8,128)(2,1)S(1)} collective-permute-done((bf16[128,900]{1,0:T(8,128)(2,1)S(1)}, bf16[128,900]{1,0:T(8,128)(2,1)S(1)}, u32[]{:S(2)}, u32[]{:S(2)}) %collective-permute-start.6) | collective-permute-done | bytes 230432 | tf_op jit(solution)/shard_map/ppermute | solution.py:17
  29.3 2.2 %collective-permute-done.7 = bf16[128,256]{1,0:T(8,128)(2,1)S(1)} collective-permute-done((bf16[128,256]{1,0:T(8,128)(2,1)}, bf16[128,256]{1,0:T(8,128)(2,1)S(1)}, u32[]{:S(2)}, u32[]{:S(2)}) %collective-permute-start.7) | collective-permute-done | bytes 65568 | tf_op jit(solution)/shard_map/ppermute | solution.py:165
  32.2 2.9 %collective-permute-start.10 = (bf16[128,256]{1,0:T(8,128)(2,1)S(1)}, bf16[128,256]{1,0:T(8,128)(2,1)S(1)}, u32[]{:S(2)}, u32[]{:S(2)}) collective-permute-start(bf16[128,256]{1,0:T(8,128)(2,1)S(1)} %get-tuple-element.24), channel_id=1, source_target_pairs={{0,12},{4,0},{8,4},{12,8},{1,13},{5,1},{9,5},{13,9},{2,14},{6,2},{... | collective-permute-start | bytes 196616 | tf_op jit(solution)/shard_map/ppermute | solution.py:76
  35.0 1.7 %collective-permute-start.9 = (bf16[128,256]{1,0:T(8,128)(2,1)S(1)}, bf16[128,256]{1,0:T(8,128)(2,1)S(1)}, u32[]{:S(2)}, u32[]{:S(2)}) collective-permute-start(bf16[128,256]{1,0:T(8,128)(2,1)S(1)} %get-tuple-element.25), channel_id=1, source_target_pairs={{0,8},{4,12},{8,0},{12,4},{1,9},{5,13},{9,1},{13,5},{2,10},{6,14},... | collective-permute-start | bytes 196616 | tf_op jit(solution)/shard_map/ppermute | solution.py:76
  36.8 0.4 collective-permute-done.10
  37.1 4.0 %collective-permute-done.8 = bf16[128,256]{1,0:T(8,128)(2,1)S(1)} collective-permute-done((bf16[128,256]{1,0:T(8,128)(2,1)S(1)}, bf16[128,256]{1,0:T(8,128)(2,1)S(1)}, u32[]{:S(2)}, u32[]{:S(2)}) %collective-permute-start.8) | collective-permute-done | bytes 65568 | tf_op jit(solution)/shard_map/ppermute | solution.py:76
  41.1 1.2 %fusion.2 = bf16[1,1024,256]{2,1,0:T(8,128)(2,1)} fusion(f32[1024,256]{1,0:T(8,128)S(1)} %convolution_add_fusion, bf16[128,256]{1,0:T(8,128)(2,1)S(1)} %collective-permute-done.10, bf16[128,256]{1,0:T(8,128)(2,1)S(1)} %collective-permute-done.9, bf16[128,256]{1,0:T(8,128)(2,1)S(1)} %collective-permute-done.8, ...), kind=kOutput, calls=%fused_computation.8 | convolution fusion | flops 67928064 | bytes 2097668 | tf_op jit(solution)/shard_map/dot_general | solution.py:146
  (46 shorter events, 3.7 us)
Async XLA Ops:
  0.0 1.1 %copy-start = (bf16[1,1024,256]{2,1,0:T(8,128)(2,1)S(1)}, bf16[1,1024,256]{2,1,0:T(8,128)(2,1)}, u32[]{:S(2)}) copy-start(bf16[1,1024,256]{2,1,0:T(8,128)(2,1)} %param.7) | copy-start | bytes 1572868
  1.1 2.4 %copy-start.1 = (bf16[1,1024,128]{2,1,0:T(8,128)(2,1)S(1)}, bf16[1,1024,128]{2,1,0:T(8,128)(2,1)}, u32[]{:S(2)}) copy-start(bf16[1,1024,128]{2,1,0:T(8,128)(2,1)} %param.11) | copy-start | bytes 786436
  1.1 5.7 %copy-start.2 = (bf16[4,1,64,1,256]{4,2,3,1,0:T(8,128)(2,1)S(1)}, bf16[4,1,64,1,256]{4,2,3,1,0:T(8,128)(2,1)}, u32[]{:S(2)}) copy-start(bf16[4,1,64,1,256]{4,2,3,1,0:T(8,128)(2,1)} %param.13) | copy-start | bytes 393220
  3.4 4.4 %copy-start.4 = (s32[1,2,128]{2,1,0:T(2,128)S(1)}, s32[1,2,128]{2,1,0:T(2,128)}, u32[]{:S(2)}) copy-start(s32[1,2,128]{2,1,0:T(2,128)} %param.10) | copy-start | bytes 3076
  3.4 4.4 %copy-start.3 = (f32[1,2,128]{2,1,0:T(2,128)S(1)}, f32[1,2,128]{2,1,0:T(2,128)}, u32[]{:S(2)}) copy-start(f32[1,2,128]{2,1,0:T(2,128)} %param.9) | copy-start | bytes 3076
  3.7 5.2 %collective-permute-start.1 = (bf16[128,256]{1,0:T(8,128)(2,1)S(1)}, bf16[128,256]{1,0:T(8,128)(2,1)S(1)}, u32[]{:S(2)}, u32[]{:S(2)}) collective-permute-start(bf16[128,256]{1,0:T(8,128)(2,1)S(1)} %fusion.9), channel_id=1, source_target_pairs={{0,2},{2,0},{1,3},{3,1},{4,6},{6,4},{5,7},{7,5},{8,10},{10,8},{9,1... | collective-permute-start | bytes 196616 | tf_op jit(solution)/shard_map/ppermute | solution.py:17
  6.8 2.3 %collective-permute-start = (bf16[4,64,256]{2,1,0:T(8,128)(2,1)S(1)}, bf16[4,64,256]{2,1,0:T(8,128)(2,1)S(1)}, u32[]{:S(2)}, u32[]{:S(2)}) collective-permute-start(bf16[4,64,256]{2,1,0:T(8,128)(2,1)S(1)} %bitcast.92), channel_id=1, source_target_pairs={{0,1},{1,0},{2,3},{3,2},{4,5},{5,4},{6,7},{7,6},{8,9},{9,8},{10,11... | collective-permute-start | bytes 393224 | tf_op jit(solution)/shard_map/ppermute | solution.py:17
  10.0 9.5 %collective-permute-start.2 = (bf16[128,256]{1,0:T(8,128)(2,1)}, bf16[128,256]{1,0:T(8,128)(2,1)}, u32[]{:S(2)}, u32[]{:S(2)}) collective-permute-start(bf16[128,256]{1,0:T(8,128)(2,1)} %get-tuple-element.26), channel_id=1, source_target_pairs={{0,4},{4,8},{8,12},{12,0},{1,5},{5,9},{9,13},{13,1},{2,6},{6,10},{... | collective-permute-start | bytes 196616 | tf_op jit(solution)/shard_map/ppermute | solution.py:76
  12.1 7.5 %collective-permute-start.3 = (bf16[128,256]{1,0:T(8,128)(2,1)}, bf16[128,256]{1,0:T(8,128)(2,1)}, u32[]{:S(2)}, u32[]{:S(2)}) collective-permute-start(bf16[128,256]{1,0:T(8,128)(2,1)} %get-tuple-element.28), channel_id=1, source_target_pairs={{0,8},{4,12},{8,0},{12,4},{1,9},{5,13},{9,1},{13,5},{2,10},{6,14},... | collective-permute-start | bytes 196616 | tf_op jit(solution)/shard_map/ppermute | solution.py:76
  14.7 4.9 %collective-permute-start.4 = (bf16[128,256]{1,0:T(8,128)(2,1)}, bf16[128,256]{1,0:T(8,128)(2,1)}, u32[]{:S(2)}, u32[]{:S(2)}) collective-permute-start(bf16[128,256]{1,0:T(8,128)(2,1)} %get-tuple-element.27), channel_id=1, source_target_pairs={{0,12},{4,0},{8,4},{12,8},{1,13},{5,1},{9,5},{13,9},{2,14},{6,2},{... | collective-permute-start | bytes 196616 | tf_op jit(solution)/shard_map/ppermute | solution.py:76
  21.6 6.6 %collective-permute-start.6 = (bf16[128,900]{1,0:T(8,128)(2,1)S(1)}, bf16[128,900]{1,0:T(8,128)(2,1)S(1)}, u32[]{:S(2)}, u32[]{:S(2)}) collective-permute-start(bf16[128,900]{1,0:T(8,128)(2,1)S(1)} %concatenate.29), channel_id=1, source_target_pairs={{0,2},{2,0},{1,3},{3,1},{4,6},{6,4},{5,7},{7,5},{8,10},{10,8},{9,1... | collective-permute-start | bytes 691208 | tf_op jit(solution)/shard_map/ppermute | solution.py:17
  23.1 2.0 %collective-permute-start.5 = (bf16[128,256]{1,0:T(8,128)(2,1)}, bf16[128,256]{1,0:T(8,128)(2,1)S(1)}, u32[]{:S(2)}, u32[]{:S(2)}) collective-permute-start(bf16[128,256]{1,0:T(8,128)(2,1)} %get-tuple-element.34), channel_id=1, source_target_pairs={{2,4},{4,2},{6,8},{8,6},{10,12},{12,10},{3,5},{5,3},{7,9},{9,7},{1... | collective-permute-start | bytes 196616 | tf_op jit(solution)/shard_map/ppermute | solution.py:164
  23.8 7.6 %collective-permute-start.7 = (bf16[128,256]{1,0:T(8,128)(2,1)}, bf16[128,256]{1,0:T(8,128)(2,1)S(1)}, u32[]{:S(2)}, u32[]{:S(2)}) collective-permute-start(bf16[128,256]{1,0:T(8,128)(2,1)} %get-tuple-element.34), channel_id=1, source_target_pairs={{2,6},{4,0},{6,10},{8,4},{10,14},{12,8},{3,7},{5,1},{7,11},{9,5},{... | collective-permute-start | bytes 196616 | tf_op jit(solution)/shard_map/ppermute | solution.py:165
  32.2 5.0 %collective-permute-start.10 = (bf16[128,256]{1,0:T(8,128)(2,1)S(1)}, bf16[128,256]{1,0:T(8,128)(2,1)S(1)}, u32[]{:S(2)}, u32[]{:S(2)}) collective-permute-start(bf16[128,256]{1,0:T(8,128)(2,1)S(1)} %get-tuple-element.24), channel_id=1, source_target_pairs={{0,12},{4,0},{8,4},{12,8},{1,13},{5,1},{9,5},{13,9},{2,14},{6,2},{... | collective-permute-start | bytes 196616 | tf_op jit(solution)/shard_map/ppermute | solution.py:76
  35.0 6.1 %collective-permute-start.8 = (bf16[128,256]{1,0:T(8,128)(2,1)S(1)}, bf16[128,256]{1,0:T(8,128)(2,1)S(1)}, u32[]{:S(2)}, u32[]{:S(2)}) collective-permute-start(bf16[128,256]{1,0:T(8,128)(2,1)S(1)} %get-tuple-element.23), channel_id=1, source_target_pairs={{0,4},{4,8},{8,12},{12,0},{1,5},{5,9},{9,13},{13,1},{2,6},{6,10},{... | collective-permute-start | bytes 196616 | tf_op jit(solution)/shard_map/ppermute | solution.py:76
  35.0 6.1 %collective-permute-start.9 = (bf16[128,256]{1,0:T(8,128)(2,1)S(1)}, bf16[128,256]{1,0:T(8,128)(2,1)S(1)}, u32[]{:S(2)}, u32[]{:S(2)}) collective-permute-start(bf16[128,256]{1,0:T(8,128)(2,1)S(1)} %get-tuple-element.25), channel_id=1, source_target_pairs={{0,8},{4,12},{8,0},{12,4},{1,9},{5,13},{9,1},{13,5},{2,10},{6,14},... | collective-permute-start | bytes 196616 | tf_op jit(solution)/shard_map/ppermute | solution.py:76

commit v15 on v14

--- a/solution.py
+++ b/solution.py
@@ -128,8 +128,9 @@
         coarse, (solve_now, basis_now, faces_inverse_now) = coarse_of(
             inputs, (local_solve, basis, face_inverse)
         )
-        lower_basis = basis_now[lower_at]
-        upper_basis = basis_now[upper_at]
+        trace_at = jnp.concatenate([lower_at, upper_at])
+        trace_basis = jnp.take(basis_now, trace_at, axis=0)
+        trace_solve = jnp.take(solve_now, trace_at, axis=0)
         if pairwise and cycle_index == 0:
             sends = jnp.where(
                 live,
@@ -147,13 +148,12 @@
         iterate = local_solve + correction
         if cycle_index == ROUNDS - 1:
             break
-        lower_trace = (
-            solve_now[lower_at] + jnp.dot(lower_basis, coarse, preferred_element_type=jnp.float32)
-        ).astype(jnp.bfloat16)
-        upper_trace = (
-            solve_now[upper_at] + jnp.dot(upper_basis, coarse, preferred_element_type=jnp.float32)
-        ).astype(jnp.bfloat16)
-        rows = lower_trace.shape[0]
+        traces = (
+            trace_solve + jnp.dot(trace_basis, coarse, preferred_element_type=jnp.float32)
+        ).astype(jnp.bfloat16)
+        rows = lower_at.shape[0]
+        lower_trace = traces[:rows]
+        upper_trace = traces[rows:]
         if pairwise:
             toward_partner = jnp.where(first, upper_trace, lower_trace)
             toward_diagonal = jnp.where(first, lower_trace, upper_trace)

time: 42.5 us -> 43.3 us (1.019)
  matrix products: 6.62 us -> 5.89 us
  waiting for transfers between devices: 10.5 us -> 11.2 us
  starting transfers between devices: 17.1 us -> 17.6 us
    ppermute x6, waiting for transfers between devices: 4.4 us -> 5.91 us  [coarse_of(): lax.ppermute(piece, 'sub', [(i, (i + k) % sub_count) for i in range(sub_c...]
    ppermute x1, waiting for transfers between devices: 2.19 us -> 0.75 us  [local(): crossing = lax.ppermute(toward_diagonal, DUCT, crossing_pairs)]
    gather x4 -> x2, local copies, waits for them, and re-layouts: 2.93 us -> 1.82 us  [the longest x1 0.97 us: local(): trace_solve = jnp.take(solve_now, trace_at, axis=0)]
    concatenate x1, local copies, waits for them, and re-layouts: 0.1 us -> 0.86 us  [local(): jnp.concatenate([toward_partner, coarse, mine, gains_pair], axis=1)]
    dot_general x2 -> x1, matrix products: 0.93 us -> 0.23 us  [local(): jnp.dot(trace_basis, coarse, preferred_element_type=jnp.float32)]
    ppermute x3, waiting for transfers between devices: 3.89 us -> 4.56 us  [swapped(): return lax.ppermute(shard, axis, [(0, 1), (1, 0)])]
    convert_element_type x1, local copies, waits for them, and re-layouts: 0.13 us -> 0.72 us  [local(): gains_low = (gains.T - gains_high.astype(jnp.float32)).astype(jnp.bfloat16)]
    ppermute x6, starting transfers between devices: 10.6 us -> 11.2 us  [coarse_of(): lax.ppermute(piece, 'sub', [(i, (i + k) % sub_count) for i in range(sub_c...]
  transfers between devices with their start and end apart: 11 -> 11, of which waited for: 6 -> 7; matrix products, arithmetic and copies ran while one was open for 14% -> 12% of each run, Pallas kernels for 0% -> 0%
where the time goes in v15:
time: 43.3 us; the launch traced here: 43 us
  starting transfers between devices  17.6 us (41%)
  waiting for transfers between devices  11.2 us (26%)
  matrix products  5.89 us (14%)
  local copies, waits for them, and re-layouts  5.85 us (14%)
  other arithmetic  1.43 us (3%)
  between operations  1.02 us (2%)
    ppermute x6, starting transfers between devices, coarse_of(): lax.ppermute(piece, 'sub', [(i, (i + k) % sub_count) for i in range(sub_c...  11.2 us
    ppermute x6, waiting for transfers between devices, coarse_of(): lax.ppermute(piece, 'sub', [(i, (i + k) % sub_count) for i in range(sub_c...  5.91 us
    ppermute x3, waiting for transfers between devices, swapped(): return lax.ppermute(shard, axis, [(0, 1), (1, 0)])  4.56 us
    ppermute x3, starting transfers between devices, swapped(): return lax.ppermute(shard, axis, [(0, 1), (1, 0)])  4.48 us
    dot_general x1, matrix products, local(): base_solve = jnp.dot(inverse, source, preferred_element_type=jnp.float32)  2.35 us
    ppermute x1, starting transfers between devices, local(): crossing = lax.ppermute(toward_diagonal, DUCT, crossing_pairs)  1.29 us
    dot_general x1, matrix products, local(): correction = jnp.dot(basis, coarse, preferred_element_type=jnp.float32)  1.14 us
    slice x1, local copies, waits for them, and re-layouts, local(): inverse[:, :face_rows]  1.07 us
  transfers between devices with their start and end apart: 11, of which 7 were waited for; matrix products, arithmetic and copies ran while one was open for 12% of the time, Pallas kernels for 0%

profile of v15, /device:TPU:0, one launch (start us, length us, event | category | flops | bytes accessed | tf_op | source)
XLA Modules:
  0.0 43.0 jit_solution(2245847131511194064)
XLA Ops:
  0.7 0.3 copy-done
  1.1 2.4 %fusion.10 = f32[1024,256]{1,0:T(8,128)S(1)} fusion(bf16[1,1024,256]{2,1,0:T(8,128)(2,1)S(1)} %copy-done, bf16[1,1024,1024]{2,1,0:T(8,128)(2,1)} %param.8), kind=kOutput, calls=%fused_computation.23 | convolution fusion | flops 536870912 | bytes 3670016 | tf_op jit(solution)/shard_map/dot_general | solution.py:110
  3.7 3.0 %collective-permute-start.1 = (bf16[128,256]{1,0:T(8,128)(2,1)S(1)}, bf16[128,256]{1,0:T(8,128)(2,1)S(1)}, u32[]{:S(2)}, u32[]{:S(2)}) collective-permute-start(bf16[128,256]{1,0:T(8,128)(2,1)S(1)} %fusion.8), channel_id=1, source_target_pairs={{0,2},{2,0},{1,3},{3,1},{4,6},{6,4},{5,7},{7,5},{8,10},{10,8},{9,1... | collective-permute-start | bytes 196616 | tf_op jit(solution)/shard_map/ppermute | solution.py:17
  6.8 1.1 %fusion.54 = (bf16[1024,128]{1,0:T(8,128)(2,1)S(1)}, bf16[1024,128]{1,0:T(8,128)(2,1)S(1)}) fusion(bf16[1024,1024]{1,0:T(8,128)(2,1)} %bitcast.90), kind=kLoop, calls=%fused_computation.107 | loop fusion | bytes 1048576 | tf_op jit(solution)/shard_map/slice | solution.py:57
  8.0 0.7 %copy.19 = bf16[128,2]{1,0:T(8,128)(2,1)} copy(bf16[128,2]{0,1:T(2,128)(2,1)S(1)} %get-tuple-element.17) | data formatting | bytes 1024 | tf_op jit(solution)/shard_map/convert_element_type | solution.py:86
  9.3 0.7 %dynamic-slice_bitcast_fusion.5 = (bf16[128,256]{1,0:T(8,128)(2,1)}, bf16[128,256]{1,0:T(8,128)(2,1)}, bf16[128,256]{1,0:T(8,128)(2,1)}) fusion(bf16[4,128,256]{2,1,0:T(8,128)(2,1)S(1)} %convolution_convert_fusion.1, s32[]{:T(128)S(6)} %select_n.152, s32[]{:T(128)S(6)} %select_n.156, s32[]{:T(128)S(6)} %select_n.154), kind=kLoop, calls=%fused_computation.68 | loop fusion | bytes 393228 | tf_op jit(solution)/shard_map/jit(dynamic_index_in_dim)/squeeze | solution.py:75
  10.0 2.1 %collective-permute-start.2 = (bf16[128,256]{1,0:T(8,128)(2,1)}, bf16[128,256]{1,0:T(8,128)(2,1)}, u32[]{:S(2)}, u32[]{:S(2)}) collective-permute-start(bf16[128,256]{1,0:T(8,128)(2,1)} %get-tuple-element.26), channel_id=1, source_target_pairs={{0,4},{4,8},{8,12},{12,0},{1,5},{5,9},{9,13},{13,1},{2,6},{6,10},{... | collective-permute-start | bytes 196616 | tf_op jit(solution)/shard_map/ppermute | solution.py:76
  12.1 2.6 %collective-permute-start.3 = (bf16[128,256]{1,0:T(8,128)(2,1)}, bf16[128,256]{1,0:T(8,128)(2,1)}, u32[]{:S(2)}, u32[]{:S(2)}) collective-permute-start(bf16[128,256]{1,0:T(8,128)(2,1)} %get-tuple-element.28), channel_id=1, source_target_pairs={{0,8},{4,12},{8,0},{12,4},{1,9},{5,13},{9,1},{13,5},{2,10},{6,14},... | collective-permute-start | bytes 196616 | tf_op jit(solution)/shard_map/ppermute | solution.py:76
  14.7 1.3 %collective-permute-start.4 = (bf16[128,256]{1,0:T(8,128)(2,1)}, bf16[128,256]{1,0:T(8,128)(2,1)}, u32[]{:S(2)}, u32[]{:S(2)}) collective-permute-start(bf16[128,256]{1,0:T(8,128)(2,1)} %get-tuple-element.27), channel_id=1, source_target_pairs={{0,12},{4,0},{8,4},{12,8},{1,13},{5,1},{9,5},{13,9},{2,14},{6,2},{... | collective-permute-start | bytes 196616 | tf_op jit(solution)/shard_map/ppermute | solution.py:76
  16.6 0.9 %gather_fusion.1 = bf16[256,128]{1,0:T(8,128)(2,1)S(1)} fusion(bf16[1024,128]{1,0:T(8,128)(2,1)S(1)} %bitcast.88, s32[1024]{0:T(1024)S(1)} %pad_clamp_fusion), kind=kCustom, calls=%fused_computation.1 | custom fusion | bytes 132096 | tf_op jit(solution)/shard_map/jit(_take)/gather | solution.py:132
  17.4 1.0 %gather_fusion = f32[256,256]{1,0:T(8,128)S(1)} fusion(f32[1024,256]{1,0:T(8,128)S(1)} %fusion.10, s32[1024]{0:T(1024)S(1)} %pad_clamp_fusion), kind=kCustom, calls=%fused_computation | custom fusion | bytes 525312 | tf_op jit(solution)/shard_map/jit(_take)/gather | solution.py:133
  18.4 1.1 %collective-permute-done.3 = bf16[128,256]{1,0:T(8,128)(2,1)} collective-permute-done((bf16[128,256]{1,0:T(8,128)(2,1)}, bf16[128,256]{1,0:T(8,128)(2,1)}, u32[]{:S(2)}, u32[]{:S(2)}) %collective-permute-start.3) | collective-permute-done | bytes 65568 | tf_op jit(solution)/shard_map/ppermute | solution.py:76
  19.7 1.0 %fusion.27 = bf16[128,256]{1,0:T(8,128)(2,1)S(1)} fusion(bf16[128,256]{1,0:T(8,128)(2,1)} %collective-permute-done.4, bf16[128,256]{1,0:T(8,128)(2,1)} %collective-permute-done.3, bf16[128,256]{1,0:T(8,128)(2,1)} %collective-permute-done.2, bf16[4,128,256]{2,1,0:T(8,128)(2,1)S(1)} %convolution_convert_fusion.1, s32[]{:T(128)S(6)} %select_n.150, ...), kind=kLoop, calls=%fused_computation.52 | loop fusion | flops 294912 | bytes 327812 | tf_op jit(solution)/shard_map/jit(_where)/select_n | solution.py:146
  20.9 0.9 %concatenate.69 = bf16[128,900]{1,0:T(8,128)(2,1)S(1)} concatenate(bf16[128,256]{1,0:T(8,128)(2,1)S(1)} %get-tuple-element.35, bf16[128,256]{1,0:T(8,128)(2,1)S(1)} %fusion.27, bf16[128,256]{1,0:T(8,128)(2,1)S(1)} %fusion.5, bf16[128,128]{1,0:T(8,128)(2,1)S(1)} %fusion.9, bf16[128,2]{1,0:T(8,128)(2,1)S(1)} %copy.18, bf16[128,2]{1,0:T(8,128)(2,1)} %copy.19), dimensions={1} | concatenate | bytes 460800 | tf_op jit(solution)/shard_map/concatenate | solution.py:162
  21.8 1.5 %collective-permute-start.6 = (bf16[128,900]{1,0:T(8,128)(2,1)S(1)}, bf16[128,900]{1,0:T(8,128)(2,1)S(1)}, u32[]{:S(2)}, u32[]{:S(2)}) collective-permute-start(bf16[128,900]{1,0:T(8,128)(2,1)S(1)} %concatenate.69), channel_id=1, source_target_pairs={{0,2},{2,0},{1,3},{3,1},{4,6},{6,4},{5,7},{7,5},{8,10},{10,8},{9,1... | collective-permute-start | bytes 691208 | tf_op jit(solution)/shard_map/ppermute | solution.py:17
  23.3 0.7 %collective-permute-start.5 = (bf16[128,256]{1,0:T(8,128)(2,1)S(1)}, bf16[128,256]{1,0:T(8,128)(2,1)S(1)}, u32[]{:S(2)}, u32[]{:S(2)}) collective-permute-start(bf16[128,256]{1,0:T(8,128)(2,1)S(1)} %get-tuple-element.36), channel_id=1, source_target_pairs={{2,4},{4,2},{6,8},{8,6},{10,12},{12,10},{3,5},{5,3},{7,9},{9,7},{1... | collective-permute-start | bytes 196616 | tf_op jit(solution)/shard_map/ppermute | solution.py:164
  23.9 1.3 %collective-permute-start.7 = (bf16[128,256]{1,0:T(8,128)(2,1)S(1)}, bf16[128,256]{1,0:T(8,128)(2,1)S(1)}, u32[]{:S(2)}, u32[]{:S(2)}) collective-permute-start(bf16[128,256]{1,0:T(8,128)(2,1)S(1)} %get-tuple-element.36), channel_id=1, source_target_pairs={{2,6},{4,0},{6,10},{8,4},{10,14},{12,8},{3,7},{5,1},{7,11},{9,5},{... | collective-permute-start | bytes 196616 | tf_op jit(solution)/shard_map/ppermute | solution.py:165
  25.3 4.4 %collective-permute-done.6 = bf16[128,900]{1,0:T(8,128)(2,1)S(1)} collective-permute-done((bf16[128,900]{1,0:T(8,128)(2,1)S(1)}, bf16[128,900]{1,0:T(8,128)(2,1)S(1)}, u32[]{:S(2)}, u32[]{:S(2)}) %collective-permute-start.6) | collective-permute-done | bytes 230432 | tf_op jit(solution)/shard_map/ppermute | solution.py:17
  30.7 0.8 %collective-permute-done.7 = bf16[128,256]{1,0:T(8,128)(2,1)S(1)} collective-permute-done((bf16[128,256]{1,0:T(8,128)(2,1)S(1)}, bf16[128,256]{1,0:T(8,128)(2,1)S(1)}, u32[]{:S(2)}, u32[]{:S(2)}) %collective-permute-start.7) | collective-permute-done | bytes 65568 | tf_op jit(solution)/shard_map/ppermute | solution.py:165
  32.1 2.8 %collective-permute-start.10 = (bf16[128,256]{1,0:T(8,128)(2,1)S(1)}, bf16[128,256]{1,0:T(8,128)(2,1)S(1)}, u32[]{:S(2)}, u32[]{:S(2)}) collective-permute-start(bf16[128,256]{1,0:T(8,128)(2,1)S(1)} %get-tuple-element.24), channel_id=1, source_target_pairs={{0,12},{4,0},{8,4},{12,8},{1,13},{5,1},{9,5},{13,9},{2,14},{6,2},{... | collective-permute-start | bytes 196616 | tf_op jit(solution)/shard_map/ppermute | solution.py:76
  34.9 2.3 %collective-permute-start.9 = (bf16[128,256]{1,0:T(8,128)(2,1)S(1)}, bf16[128,256]{1,0:T(8,128)(2,1)S(1)}, u32[]{:S(2)}, u32[]{:S(2)}) collective-permute-start(bf16[128,256]{1,0:T(8,128)(2,1)S(1)} %get-tuple-element.25), channel_id=1, source_target_pairs={{0,8},{4,12},{8,0},{12,4},{1,9},{5,13},{9,1},{13,5},{2,10},{6,14},... | collective-permute-start | bytes 196616 | tf_op jit(solution)/shard_map/ppermute | solution.py:76
  37.2 3.8 %collective-permute-done.8 = bf16[128,256]{1,0:T(8,128)(2,1)S(1)} collective-permute-done((bf16[128,256]{1,0:T(8,128)(2,1)S(1)}, bf16[128,256]{1,0:T(8,128)(2,1)S(1)}, u32[]{:S(2)}, u32[]{:S(2)}) %collective-permute-start.8) | collective-permute-done | bytes 65568 | tf_op jit(solution)/shard_map/ppermute | solution.py:76
  41.1 0.8 %collective-permute-done.9 = bf16[128,256]{1,0:T(8,128)(2,1)S(1)} collective-permute-done((bf16[128,256]{1,0:T(8,128)(2,1)S(1)}, bf16[128,256]{1,0:T(8,128)(2,1)S(1)}, u32[]{:S(2)}, u32[]{:S(2)}) %collective-permute-start.9) | collective-permute-done | bytes 65568 | tf_op jit(solution)/shard_map/ppermute | solution.py:76
  41.9 1.1 %fusion.2 = bf16[1,1024,256]{2,1,0:T(8,128)(2,1)} fusion(f32[1024,256]{1,0:T(8,128)S(1)} %convolution_add_fusion, bf16[128,256]{1,0:T(8,128)(2,1)S(1)} %collective-permute-done.10, bf16[128,256]{1,0:T(8,128)(2,1)S(1)} %collective-permute-done.9, bf16[128,256]{1,0:T(8,128)(2,1)S(1)} %collective-permute-done.8, ...), kind=kOutput, calls=%fused_computation.6 | convolution fusion | flops 67928064 | bytes 2097668 | tf_op jit(solution)/shard_map/dot_general | solution.py:147
  (46 shorter events, 3.6 us)
Async XLA Ops:
  0.0 1.1 %copy-start = (bf16[1,1024,256]{2,1,0:T(8,128)(2,1)S(1)}, bf16[1,1024,256]{2,1,0:T(8,128)(2,1)}, u32[]{:S(2)}) copy-start(bf16[1,1024,256]{2,1,0:T(8,128)(2,1)} %param.7) | copy-start | bytes 1572868
  1.1 2.4 %copy-start.1 = (bf16[1,1024,128]{2,1,0:T(8,128)(2,1)S(1)}, bf16[1,1024,128]{2,1,0:T(8,128)(2,1)}, u32[]{:S(2)}) copy-start(bf16[1,1024,128]{2,1,0:T(8,128)(2,1)} %param.11) | copy-start | bytes 786436
  1.1 5.7 %copy-start.2 = (bf16[4,1,64,1,256]{4,2,3,1,0:T(8,128)(2,1)S(1)}, bf16[4,1,64,1,256]{4,2,3,1,0:T(8,128)(2,1)}, u32[]{:S(2)}) copy-start(bf16[4,1,64,1,256]{4,2,3,1,0:T(8,128)(2,1)} %param.13) | copy-start | bytes 393220
  3.4 4.4 %copy-start.4 = (s32[1,2,128]{2,1,0:T(2,128)S(1)}, s32[1,2,128]{2,1,0:T(2,128)}, u32[]{:S(2)}) copy-start(s32[1,2,128]{2,1,0:T(2,128)} %param.10) | copy-start | bytes 3076
  3.4 4.4 %copy-start.3 = (f32[1,2,128]{2,1,0:T(2,128)S(1)}, f32[1,2,128]{2,1,0:T(2,128)}, u32[]{:S(2)}) copy-start(f32[1,2,128]{2,1,0:T(2,128)} %param.9) | copy-start | bytes 3076
  3.7 5.2 %collective-permute-start.1 = (bf16[128,256]{1,0:T(8,128)(2,1)S(1)}, bf16[128,256]{1,0:T(8,128)(2,1)S(1)}, u32[]{:S(2)}, u32[]{:S(2)}) collective-permute-start(bf16[128,256]{1,0:T(8,128)(2,1)S(1)} %fusion.8), channel_id=1, source_target_pairs={{0,2},{2,0},{1,3},{3,1},{4,6},{6,4},{5,7},{7,5},{8,10},{10,8},{9,1... | collective-permute-start | bytes 196616 | tf_op jit(solution)/shard_map/ppermute | solution.py:17
  6.8 2.3 %collective-permute-start = (bf16[4,64,256]{2,1,0:T(8,128)(2,1)S(1)}, bf16[4,64,256]{2,1,0:T(8,128)(2,1)S(1)}, u32[]{:S(2)}, u32[]{:S(2)}) collective-permute-start(bf16[4,64,256]{2,1,0:T(8,128)(2,1)S(1)} %bitcast.89), channel_id=1, source_target_pairs={{0,1},{1,0},{2,3},{3,2},{4,5},{5,4},{6,7},{7,6},{8,9},{9,8},{10,11... | collective-permute-start | bytes 393224 | tf_op jit(solution)/shard_map/ppermute | solution.py:17
  10.0 8.4 %collective-permute-start.2 = (bf16[128,256]{1,0:T(8,128)(2,1)}, bf16[128,256]{1,0:T(8,128)(2,1)}, u32[]{:S(2)}, u32[]{:S(2)}) collective-permute-start(bf16[128,256]{1,0:T(8,128)(2,1)} %get-tuple-element.26), channel_id=1, source_target_pairs={{0,4},{4,8},{8,12},{12,0},{1,5},{5,9},{9,13},{13,1},{2,6},{6,10},{... | collective-permute-start | bytes 196616 | tf_op jit(solution)/shard_map/ppermute | solution.py:76
  12.1 7.4 %collective-permute-start.3 = (bf16[128,256]{1,0:T(8,128)(2,1)}, bf16[128,256]{1,0:T(8,128)(2,1)}, u32[]{:S(2)}, u32[]{:S(2)}) collective-permute-start(bf16[128,256]{1,0:T(8,128)(2,1)} %get-tuple-element.28), channel_id=1, source_target_pairs={{0,8},{4,12},{8,0},{12,4},{1,9},{5,13},{9,1},{13,5},{2,10},{6,14},... | collective-permute-start | bytes 196616 | tf_op jit(solution)/shard_map/ppermute | solution.py:76
  14.7 5.0 %collective-permute-start.4 = (bf16[128,256]{1,0:T(8,128)(2,1)}, bf16[128,256]{1,0:T(8,128)(2,1)}, u32[]{:S(2)}, u32[]{:S(2)}) collective-permute-start(bf16[128,256]{1,0:T(8,128)(2,1)} %get-tuple-element.27), channel_id=1, source_target_pairs={{0,12},{4,0},{8,4},{12,8},{1,13},{5,1},{9,5},{13,9},{2,14},{6,2},{... | collective-permute-start | bytes 196616 | tf_op jit(solution)/shard_map/ppermute | solution.py:76
  21.8 7.9 %collective-permute-start.6 = (bf16[128,900]{1,0:T(8,128)(2,1)S(1)}, bf16[128,900]{1,0:T(8,128)(2,1)S(1)}, u32[]{:S(2)}, u32[]{:S(2)}) collective-permute-start(bf16[128,900]{1,0:T(8,128)(2,1)S(1)} %concatenate.69), channel_id=1, source_target_pairs={{0,2},{2,0},{1,3},{3,1},{4,6},{6,4},{5,7},{7,5},{8,10},{10,8},{9,1... | collective-permute-start | bytes 691208 | tf_op jit(solution)/shard_map/ppermute | solution.py:17
  23.3 2.0 %collective-permute-start.5 = (bf16[128,256]{1,0:T(8,128)(2,1)S(1)}, bf16[128,256]{1,0:T(8,128)(2,1)S(1)}, u32[]{:S(2)}, u32[]{:S(2)}) collective-permute-start(bf16[128,256]{1,0:T(8,128)(2,1)S(1)} %get-tuple-element.36), channel_id=1, source_target_pairs={{2,4},{4,2},{6,8},{8,6},{10,12},{12,10},{3,5},{5,3},{7,9},{9,7},{1... | collective-permute-start | bytes 196616 | tf_op jit(solution)/shard_map/ppermute | solution.py:164
  23.9 7.5 %collective-permute-start.7 = (bf16[128,256]{1,0:T(8,128)(2,1)S(1)}, bf16[128,256]{1,0:T(8,128)(2,1)S(1)}, u32[]{:S(2)}, u32[]{:S(2)}) collective-permute-start(bf16[128,256]{1,0:T(8,128)(2,1)S(1)} %get-tuple-element.36), channel_id=1, source_target_pairs={{2,6},{4,0},{6,10},{8,4},{10,14},{12,8},{3,7},{5,1},{7,11},{9,5},{... | collective-permute-start | bytes 196616 | tf_op jit(solution)/shard_map/ppermute | solution.py:165
  32.1 5.1 %collective-permute-start.10 = (bf16[128,256]{1,0:T(8,128)(2,1)S(1)}, bf16[128,256]{1,0:T(8,128)(2,1)S(1)}, u32[]{:S(2)}, u32[]{:S(2)}) collective-permute-start(bf16[128,256]{1,0:T(8,128)(2,1)S(1)} %get-tuple-element.24), channel_id=1, source_target_pairs={{0,12},{4,0},{8,4},{12,8},{1,13},{5,1},{9,5},{13,9},{2,14},{6,2},{... | collective-permute-start | bytes 196616 | tf_op jit(solution)/shard_map/ppermute | solution.py:76
  34.9 6.2 %collective-permute-start.8 = (bf16[128,256]{1,0:T(8,128)(2,1)S(1)}, bf16[128,256]{1,0:T(8,128)(2,1)S(1)}, u32[]{:S(2)}, u32[]{:S(2)}) collective-permute-start(bf16[128,256]{1,0:T(8,128)(2,1)S(1)} %get-tuple-element.23), channel_id=1, source_target_pairs={{0,4},{4,8},{8,12},{12,0},{1,5},{5,9},{9,13},{13,1},{2,6},{6,10},{... | collective-permute-start | bytes 196616 | tf_op jit(solution)/shard_map/ppermute | solution.py:76
  34.9 7.0 %collective-permute-start.9 = (bf16[128,256]{1,0:T(8,128)(2,1)S(1)}, bf16[128,256]{1,0:T(8,128)(2,1)S(1)}, u32[]{:S(2)}, u32[]{:S(2)}) collective-permute-start(bf16[128,256]{1,0:T(8,128)(2,1)S(1)} %get-tuple-element.25), channel_id=1, source_target_pairs={{0,8},{4,12},{8,0},{12,4},{1,9},{5,13},{9,1},{13,5},{2,10},{6,14},... | collective-permute-start | bytes 196616 | tf_op jit(solution)/shard_map/ppermute | solution.py:76

commit v16 on v14

--- a/solution.py
+++ b/solution.py
@@ -142,6 +142,11 @@
                 0.0,
             )
             mine = jnp.concatenate([sends, keeps], axis=1).astype(jnp.bfloat16)
+            got_once = swapped(jnp.concatenate([mine, gains_pair], axis=1), "tile")
+            theirs = got_once[:, : mine.shape[1]]
+            tail = got_once[:, mine.shape[1] :].astype(jnp.float32)
+            pair = gains.shape[0]
+            partner_gains = (tail[:, :pair] + tail[:, pair:]).T
         coarse = jnp.where(live, coarse, jnp.zeros((), coarse.dtype))
         correction = jnp.dot(basis, coarse, preferred_element_type=jnp.float32)
         iterate = local_solve + correction
@@ -158,9 +163,7 @@
             toward_partner = jnp.where(first, upper_trace, lower_trace)
             toward_diagonal = jnp.where(first, lower_trace, upper_trace)
             width = toward_partner.shape[1]
-            got = swapped(
-                jnp.concatenate([toward_partner, coarse, mine, gains_pair], axis=1), "tile"
-            )
+            got = swapped(jnp.concatenate([toward_partner, coarse], axis=1), "tile")
             from_diagonal = lax.ppermute(toward_diagonal, DUCT, diagonal_pairs)
             crossing = lax.ppermute(toward_diagonal, DUCT, crossing_pairs)
             from_partner = got[:, :width]
@@ -170,10 +173,6 @@
             partner_lower = jnp.where(first, upper_trace, crossing).astype(jnp.float32)
             partner_upper = jnp.where(first, crossing, lower_trace).astype(jnp.float32)
             partner_coarse = got[:, width : 2 * width]
-            theirs = got[:, 2 * width : 2 * width + mine.shape[1]]
-            tail = got[:, 2 * width + mine.shape[1] :].astype(jnp.float32)
-            pair = gains.shape[0]
-            partner_gains = (tail[:, :pair] + tail[:, pair:]).T
             partner_faces = face_rows_of(partner_gains, partner_lower, partner_upper)
             own = projection_of(mine, faces, coarse)
             other = projection_of(theirs, partner_faces, partner_coarse)

time: 42.5 us -> 47.4 us (1.12)
  starting transfers between devices: 17.1 us -> 20.7 us
  local copies, waits for them, and re-layouts: 5.61 us -> 7.86 us
  matrix products: 6.62 us -> 5.96 us
    ppermute x3 -> x4, starting transfers between devices: 4.51 us -> 10.2 us  [swapped(): return lax.ppermute(shard, axis, [(0, 1), (1, 0)])]
    ppermute x6, waiting for transfers between devices: 4.4 us -> 7.63 us  [coarse_of(): lax.ppermute(piece, 'sub', [(i, (i + k) % sub_count) for i in range(sub_c...]
    ppermute x6, starting transfers between devices: 10.6 us -> 8.53 us  [coarse_of(): lax.ppermute(piece, 'sub', [(i, (i + k) % sub_count) for i in range(sub_c...]
    ppermute x1, waiting for transfers between devices: 2.19 us -> 0.17 us  [local(): crossing = lax.ppermute(toward_diagonal, DUCT, crossing_pairs)]
    ppermute x3 -> x4, waiting for transfers between devices: 3.89 us -> 2.39 us  [swapped(): return lax.ppermute(shard, axis, [(0, 1), (1, 0)])]
    select_n x1, other arithmetic: 0.99 us -> 0.09 us  [local(): coarse = jnp.where(live, coarse, jnp.zeros((), coarse.dtype))]
    concatenate x0 -> x2, other arithmetic: none -> 0.87 us  [the longest x1 0.86 us: local(): got_once = swapped(jnp.concatenate([mine, gains_pair], axis=1), 'tile')]
    squeeze x2, local copies, waits for them, and re-layouts: 0.71 us -> 0.05 us  [coarse_of(): lax.dynamic_index_in_dim(partial, (sub_index + k) % sub_count, 0, keepdim...]
  transfers between devices with their start and end apart: 11 -> 12, of which waited for: 6 -> 6; matrix products, arithmetic and copies ran while one was open for 14% -> 16% of each run, Pallas kernels for 0% -> 0%
where the time goes in v16:
time: 47.4 us; the launch traced here: 47.1 us
  starting transfers between devices  20.7 us (44%)
  waiting for transfers between devices  10.2 us (22%)
  local copies, waits for them, and re-layouts  7.86 us (17%)
  matrix products  5.96 us (13%)
  other arithmetic  1.37 us (3%)
  between operations  1.03 us (2%)
    ppermute x4, starting transfers between devices, swapped(): return lax.ppermute(shard, axis, [(0, 1), (1, 0)])  10.2 us
    ppermute x6, starting transfers between devices, coarse_of(): lax.ppermute(piece, 'sub', [(i, (i + k) % sub_count) for i in range(sub_c...  8.53 us
    ppermute x6, waiting for transfers between devices, coarse_of(): lax.ppermute(piece, 'sub', [(i, (i + k) % sub_count) for i in range(sub_c...  7.63 us
    ppermute x4, waiting for transfers between devices, swapped(): return lax.ppermute(shard, axis, [(0, 1), (1, 0)])  2.39 us
    dot_general x1, matrix products, local(): base_solve = jnp.dot(inverse, source, preferred_element_type=jnp.float32)  2.34 us
    gather x1, local copies, waits for them, and re-layouts, local(): upper_basis = basis_now[upper_at]  1.31 us
    gather x1, local copies, waits for them, and re-layouts, local(): lower_basis = basis_now[lower_at]  1.3 us
    ppermute x1, starting transfers between devices, local(): crossing = lax.ppermute(toward_diagonal, DUCT, crossing_pairs)  1.29 us
  transfers between devices with their start and end apart: 12, of which 6 were waited for; matrix products, arithmetic and copies ran while one was open for 16% of the time, Pallas kernels for 0%

profile of v16, /device:TPU:0, one launch (start us, length us, event | category | flops | bytes accessed | tf_op | source)
XLA Modules:
  0.0 47.1 jit_solution(4702113664062203983)
XLA Ops:
  1.2 2.3 %fusion.11 = f32[1024,256]{1,0:T(8,128)S(1)} fusion(bf16[1,1024,256]{2,1,0:T(8,128)(2,1)S(1)} %copy-done, bf16[1,1024,1024]{2,1,0:T(8,128)(2,1)} %param.8), kind=kOutput, calls=%fused_computation.27 | convolution fusion | flops 536870912 | bytes 3670016 | tf_op jit(solution)/shard_map/dot_general | solution.py:110
  3.8 2.9 %collective-permute-start.1 = (bf16[128,256]{1,0:T(8,128)(2,1)S(1)}, bf16[128,256]{1,0:T(8,128)(2,1)S(1)}, u32[]{:S(2)}, u32[]{:S(2)}) collective-permute-start(bf16[128,256]{1,0:T(8,128)(2,1)S(1)} %fusion.9), channel_id=1, source_target_pairs={{0,2},{2,0},{1,3},{3,1},{4,6},{6,4},{5,7},{7,5},{8,10},{10,8},{9,1... | collective-permute-start | bytes 196616 | tf_op jit(solution)/shard_map/ppermute | solution.py:17
  7.3 1.1 %fusion.53 = (bf16[1024,128]{1,0:T(8,128)(2,1)S(1)}, bf16[1024,128]{1,0:T(8,128)(2,1)S(1)}) fusion(bf16[1024,1024]{1,0:T(8,128)(2,1)} %bitcast.93), kind=kLoop, calls=%fused_computation.107 | loop fusion | bytes 1048576 | tf_op jit(solution)/shard_map/slice | solution.py:57
  8.4 0.7 %copy.16 = bf16[128,2]{1,0:T(8,128)(2,1)} copy(bf16[128,2]{0,1:T(2,128)(2,1)S(1)} %get-tuple-element.17) | data formatting | bytes 1024 | tf_op jit(solution)/shard_map/convert_element_type | solution.py:86
  9.1 0.7 %copy.15 = bf16[128,2]{1,0:T(8,128)(2,1)} copy(bf16[128,2]{0,1:T(2,128)(2,1)S(1)} %get-tuple-element.18) | data formatting | bytes 1024 | tf_op jit(solution)/shard_map/convert_element_type | solution.py:85
  10.7 0.8 %gather_fusion = f32[128,256]{1,0:T(8,128)S(1)} fusion(f32[1024,256]{1,0:T(8,128)S(1)} %fusion.11, s32[1024]{0:T(1024)S(1)} %get-tuple-element.45), kind=kCustom, calls=%fused_computation | custom fusion | bytes 262656 | tf_op jit(solution)/shard_map/gather | solution.py:156
  11.4 1.3 %gather_fusion.1 = bf16[128,128]{1,0:T(8,128)(2,1)} fusion(bf16[1024,128]{1,0:T(8,128)(2,1)S(1)} %bitcast.88, s32[1024]{0:T(1024)S(1)} %get-tuple-element.45), kind=kCustom, calls=%fused_computation.1 | custom fusion | bytes 66048 | tf_op jit(solution)/shard_map/gather | solution.py:131
  12.7 0.8 %gather_fusion.2 = f32[128,256]{1,0:T(8,128)S(1)} fusion(f32[1024,256]{1,0:T(8,128)S(1)} %fusion.11, s32[1024]{0:T(1024)S(1)} %get-tuple-element.44), kind=kCustom, calls=%fused_computation.2 | custom fusion | bytes 262656 | tf_op jit(solution)/shard_map/gather | solution.py:159
  13.5 1.3 %gather_fusion.3 = bf16[128,128]{1,0:T(8,128)(2,1)} fusion(bf16[1024,128]{1,0:T(8,128)(2,1)S(1)} %bitcast.89, s32[1024]{0:T(1024)S(1)} %get-tuple-element.44), kind=kCustom, calls=%fused_computation.3 | custom fusion | bytes 66048 | tf_op jit(solution)/shard_map/gather | solution.py:132
  15.1 3.7 %collective-permute-start.4 = (bf16[128,256]{1,0:T(8,128)(2,1)S(1)}, bf16[128,256]{1,0:T(8,128)(2,1)S(1)}, u32[]{:S(2)}, u32[]{:S(2)}) collective-permute-start(bf16[128,256]{1,0:T(8,128)(2,1)S(1)} %get-tuple-element.25), channel_id=1, source_target_pairs={{0,12},{4,0},{8,4},{12,8},{1,13},{5,1},{9,5},{13,9},{2,14},{6,2},{... | collective-permute-start | bytes 196616 | tf_op jit(solution)/shard_map/ppermute | solution.py:76
  18.8 1.0 %collective-permute-start.2 = (bf16[128,256]{1,0:T(8,128)(2,1)S(1)}, bf16[128,256]{1,0:T(8,128)(2,1)S(1)}, u32[]{:S(2)}, u32[]{:S(2)}) collective-permute-start(bf16[128,256]{1,0:T(8,128)(2,1)S(1)} %get-tuple-element.24), channel_id=1, source_target_pairs={{0,4},{4,8},{8,12},{12,0},{1,5},{5,9},{9,13},{13,1},{2,6},{6,10},{... | collective-permute-start | bytes 196616 | tf_op jit(solution)/shard_map/ppermute | solution.py:76
  20.1 0.9 %pad_maximum_fusion.6 = bf16[128,388]{1,0:T(8,128)(2,1)S(1)} fusion(bf16[128,2]{1,0:T(8,128)(2,1)} %copy.16, bf16[128,2]{1,0:T(8,128)(2,1)} %copy.15, bf16[128,128]{1,0:T(8,128)(2,1)S(1)} %fusion.10, bf16[128,256]{1,0:T(8,128)(2,1)S(1)} %fusion.4), kind=kLoop, calls=%fused_computation.36 | loop fusion | flops 397312 | bytes 198656 | tf_op jit(solution)/shard_map/concatenate | solution.py:145
  20.9 1.1 %collective-permute-start.7 = (bf16[128,388]{1,0:T(8,128)(2,1)S(1)}, bf16[128,388]{1,0:T(8,128)(2,1)S(1)}, u32[]{:S(2)}, u32[]{:S(2)}) collective-permute-start(bf16[128,388]{1,0:T(8,128)(2,1)S(1)} %pad_maximum_fusion.6), channel_id=1, source_target_pairs={{0,2},{2,0},{1,3},{3,1},{4,6},{6,4},{5,7},{7,5},{8,10},{10,8},{9,1... | collective-permute-start | bytes 297992 | tf_op jit(solution)/shard_map/ppermute | solution.py:17
  22.1 3.2 %collective-permute-done.3 = bf16[128,256]{1,0:T(8,128)(2,1)S(1)} collective-permute-done((bf16[128,256]{1,0:T(8,128)(2,1)S(1)}, bf16[128,256]{1,0:T(8,128)(2,1)S(1)}, u32[]{:S(2)}, u32[]{:S(2)}) %collective-permute-start.3) | collective-permute-done | bytes 65568 | tf_op jit(solution)/shard_map/ppermute | solution.py:76
  26.4 1.3 %collective-permute-start.8 = (bf16[128,256]{1,0:T(8,128)(2,1)S(1)}, bf16[128,256]{1,0:T(8,128)(2,1)S(1)}, u32[]{:S(2)}, u32[]{:S(2)}) collective-permute-start(bf16[128,256]{1,0:T(8,128)(2,1)S(1)} %get-tuple-element.34), channel_id=1, source_target_pairs={{2,6},{4,0},{6,10},{8,4},{10,14},{12,8},{3,7},{5,1},{7,11},{9,5},{... | collective-permute-start | bytes 196616 | tf_op jit(solution)/shard_map/ppermute | solution.py:168
  27.7 5.7 %collective-permute-start.6 = (bf16[128,512]{1,0:T(8,128)(2,1)S(1)}, bf16[128,512]{1,0:T(8,128)(2,1)S(1)}, u32[]{:S(2)}, u32[]{:S(2)}) collective-permute-start(bf16[128,512]{1,0:T(8,128)(2,1)S(1)} %pad_maximum_fusion.4), channel_id=1, source_target_pairs={{0,2},{2,0},{1,3},{3,1},{4,6},{6,4},{5,7},{7,5},{8,10},{10,8},{9,1... | collective-permute-start | bytes 393224 | tf_op jit(solution)/shard_map/ppermute | solution.py:17
  34.0 2.4 %collective-permute-done.6 = bf16[128,512]{1,0:T(8,128)(2,1)S(1)} collective-permute-done((bf16[128,512]{1,0:T(8,128)(2,1)S(1)}, bf16[128,512]{1,0:T(8,128)(2,1)S(1)}, u32[]{:S(2)}, u32[]{:S(2)}) %collective-permute-start.6) | collective-permute-done | bytes 131104 | tf_op jit(solution)/shard_map/ppermute | solution.py:17
  37.7 1.5 %collective-permute-start.11 = (bf16[128,256]{1,0:T(8,128)(2,1)S(1)}, bf16[128,256]{1,0:T(8,128)(2,1)S(1)}, u32[]{:S(2)}, u32[]{:S(2)}) collective-permute-start(bf16[128,256]{1,0:T(8,128)(2,1)S(1)} %get-tuple-element.22), channel_id=1, source_target_pairs={{0,12},{4,0},{8,4},{12,8},{1,13},{5,1},{9,5},{13,9},{2,14},{6,2},{... | collective-permute-start | bytes 196616 | tf_op jit(solution)/shard_map/ppermute | solution.py:76
  39.2 0.7 %collective-permute-start.10 = (bf16[128,256]{1,0:T(8,128)(2,1)S(1)}, bf16[128,256]{1,0:T(8,128)(2,1)S(1)}, u32[]{:S(2)}, u32[]{:S(2)}) collective-permute-start(bf16[128,256]{1,0:T(8,128)(2,1)S(1)} %get-tuple-element.23), channel_id=1, source_target_pairs={{0,8},{4,12},{8,0},{12,4},{1,9},{5,13},{9,1},{13,5},{2,10},{6,14},... | collective-permute-start | bytes 196616 | tf_op jit(solution)/shard_map/ppermute | solution.py:76
  39.9 1.6 %collective-permute-start.9 = (bf16[128,256]{1,0:T(8,128)(2,1)S(1)}, bf16[128,256]{1,0:T(8,128)(2,1)S(1)}, u32[]{:S(2)}, u32[]{:S(2)}) collective-permute-start(bf16[128,256]{1,0:T(8,128)(2,1)S(1)} %get-tuple-element.21), channel_id=1, source_target_pairs={{0,4},{4,8},{8,12},{12,0},{1,5},{5,9},{9,13},{13,1},{2,6},{6,10},{... | collective-permute-start | bytes 196616 | tf_op jit(solution)/shard_map/ppermute | solution.py:76
  41.5 1.7 %collective-permute-done.11 = bf16[128,256]{1,0:T(8,128)(2,1)S(1)} collective-permute-done((bf16[128,256]{1,0:T(8,128)(2,1)S(1)}, bf16[128,256]{1,0:T(8,128)(2,1)S(1)}, u32[]{:S(2)}, u32[]{:S(2)}) %collective-permute-start.11) | collective-permute-done | bytes 65568 | tf_op jit(solution)/shard_map/ppermute | solution.py:76
  43.3 1.8 %collective-permute-done.10 = bf16[128,256]{1,0:T(8,128)(2,1)S(1)} collective-permute-done((bf16[128,256]{1,0:T(8,128)(2,1)S(1)}, bf16[128,256]{1,0:T(8,128)(2,1)S(1)}, u32[]{:S(2)}, u32[]{:S(2)}) %collective-permute-start.10) | collective-permute-done | bytes 65568 | tf_op jit(solution)/shard_map/ppermute | solution.py:76
  45.1 0.9 %collective-permute-done.9 = bf16[128,256]{1,0:T(8,128)(2,1)S(1)} collective-permute-done((bf16[128,256]{1,0:T(8,128)(2,1)S(1)}, bf16[128,256]{1,0:T(8,128)(2,1)S(1)}, u32[]{:S(2)}, u32[]{:S(2)}) %collective-permute-start.9) | collective-permute-done | bytes 65568 | tf_op jit(solution)/shard_map/ppermute | solution.py:76
  46.0 1.1 %fusion.2 = bf16[1,1024,256]{2,1,0:T(8,128)(2,1)} fusion(f32[1024,256]{1,0:T(8,128)S(1)} %convolution_add_fusion, bf16[128,256]{1,0:T(8,128)(2,1)S(1)} %collective-permute-done.11, bf16[128,256]{1,0:T(8,128)(2,1)S(1)} %collective-permute-done.10, bf16[128,256]{1,0:T(8,128)(2,1)S(1)} %collective-permute-done.9, ...), kind=kOutput, calls=%fused_computation.8 | convolution fusion | flops 67928064 | bytes 2097668 | tf_op jit(solution)/shard_map/dot_general | solution.py:151
  (59 shorter events, 5.5 us)
Async XLA Ops:
  0.0 1.1 %copy-start = (bf16[1,1024,256]{2,1,0:T(8,128)(2,1)S(1)}, bf16[1,1024,256]{2,1,0:T(8,128)(2,1)}, u32[]{:S(2)}) copy-start(bf16[1,1024,256]{2,1,0:T(8,128)(2,1)} %param.7) | copy-start | bytes 1572868
  0.0 10.0 %collective-permute-start = (bf16[4,64,256]{2,1,0:T(8,128)(2,1)}, bf16[4,64,256]{2,1,0:T(8,128)(2,1)S(1)}, u32[]{:S(2)}, u32[]{:S(2)}) collective-permute-start(bf16[4,64,256]{2,1,0:T(8,128)(2,1)} %bitcast.92), channel_id=1, source_target_pairs={{0,1},{1,0},{2,3},{3,2},{4,5},{5,4},{6,7},{7,6},{8,9},{9,8},{10,11... | collective-permute-start | bytes 393224 | tf_op jit(solution)/shard_map/ppermute | solution.py:17
  1.1 2.4 %copy-start.1 = (bf16[1,1024,128]{2,1,0:T(8,128)(2,1)S(1)}, bf16[1,1024,128]{2,1,0:T(8,128)(2,1)}, u32[]{:S(2)}) copy-start(bf16[1,1024,128]{2,1,0:T(8,128)(2,1)} %param.11) | copy-start | bytes 786436
  1.1 5.6 %copy-start.7 = (f32[1,2,128]{2,1,0:T(2,128)S(1)}, f32[1,2,128]{2,1,0:T(2,128)}, u32[]{:S(2)}) copy-start(f32[1,2,128]{2,1,0:T(2,128)} %param.9) | copy-start | bytes 3076
  3.5 4.8 %copy-start.9 = (s32[1,2,128]{2,1,0:T(2,128)S(1)}, s32[1,2,128]{2,1,0:T(2,128)}, u32[]{:S(2)}) copy-start(s32[1,2,128]{2,1,0:T(2,128)} %param.10) | copy-start | bytes 3076
  3.5 6.4 %copy-start.2 = (bf16[4,1,64,1,256]{4,2,3,1,0:T(8,128)(2,1)S(1)}, bf16[4,1,64,1,256]{4,2,3,1,0:T(8,128)(2,1)}, u32[]{:S(2)}) copy-start(bf16[4,1,64,1,256]{4,2,3,1,0:T(8,128)(2,1)} %param.13) | copy-start | bytes 393220
  3.8 6.1 %collective-permute-start.1 = (bf16[128,256]{1,0:T(8,128)(2,1)S(1)}, bf16[128,256]{1,0:T(8,128)(2,1)S(1)}, u32[]{:S(2)}, u32[]{:S(2)}) collective-permute-start(bf16[128,256]{1,0:T(8,128)(2,1)S(1)} %fusion.9), channel_id=1, source_target_pairs={{0,2},{2,0},{1,3},{3,1},{4,6},{6,4},{5,7},{7,5},{8,10},{10,8},{9,1... | collective-permute-start | bytes 196616 | tf_op jit(solution)/shard_map/ppermute | solution.py:17
  10.0 0.7 %copy-start.3 = (bf16[4,64,256]{2,1,0:T(8,128)(2,1)}, bf16[4,64,256]{2,1,0:T(8,128)(2,1)S(1)}, u32[]{:S(2)}) copy-start(bf16[4,64,256]{2,1,0:T(8,128)(2,1)S(1)} %get-tuple-element.28) | copy-start | bytes 393220
  14.8 10.6 %copy-start.6 = (bf16[128,128]{1,0:T(8,128)(2,1)S(1)}, bf16[128,128]{1,0:T(8,128)(2,1)}, u32[]{:S(2)}) copy-start(bf16[128,128]{1,0:T(8,128)(2,1)} %gather_fusion.1) | copy-start | bytes 98308
  14.8 10.7 %copy-start.5 = (bf16[128,128]{1,0:T(8,128)(2,1)S(1)}, bf16[128,128]{1,0:T(8,128)(2,1)}, u32[]{:S(2)}) copy-start(bf16[128,128]{1,0:T(8,128)(2,1)} %gather_fusion.3) | copy-start | bytes 98308
  14.8 21.6 %copy-start.8 = (f32[128]{0:T(128)S(1)}, f32[128]{0:T(128)}, u32[]{:S(2)}) copy-start(f32[128]{0:T(128)} %get-tuple-element.40) | copy-start | bytes 1540
  15.1 7.0 %collective-permute-start.4 = (bf16[128,256]{1,0:T(8,128)(2,1)S(1)}, bf16[128,256]{1,0:T(8,128)(2,1)S(1)}, u32[]{:S(2)}, u32[]{:S(2)}) collective-permute-start(bf16[128,256]{1,0:T(8,128)(2,1)S(1)} %get-tuple-element.25), channel_id=1, source_target_pairs={{0,12},{4,0},{8,4},{12,8},{1,13},{5,1},{9,5},{13,9},{2,14},{6,2},{... | collective-permute-start | bytes 196616 | tf_op jit(solution)/shard_map/ppermute | solution.py:76
  18.8 6.5 %collective-permute-start.3 = (bf16[128,256]{1,0:T(8,128)(2,1)S(1)}, bf16[128,256]{1,0:T(8,128)(2,1)S(1)}, u32[]{:S(2)}, u32[]{:S(2)}) collective-permute-start(bf16[128,256]{1,0:T(8,128)(2,1)S(1)} %get-tuple-element.26), channel_id=1, source_target_pairs={{0,8},{4,12},{8,0},{12,4},{1,9},{5,13},{9,1},{13,5},{2,10},{6,14},... | collective-permute-start | bytes 196616 | tf_op jit(solution)/shard_map/ppermute | solution.py:76
  18.8 6.5 %collective-permute-start.2 = (bf16[128,256]{1,0:T(8,128)(2,1)S(1)}, bf16[128,256]{1,0:T(8,128)(2,1)S(1)}, u32[]{:S(2)}, u32[]{:S(2)}) collective-permute-start(bf16[128,256]{1,0:T(8,128)(2,1)S(1)} %get-tuple-element.24), channel_id=1, source_target_pairs={{0,4},{4,8},{8,12},{12,0},{1,5},{5,9},{9,13},{13,1},{2,6},{6,10},{... | collective-permute-start | bytes 196616 | tf_op jit(solution)/shard_map/ppermute | solution.py:76
  20.9 12.5 %collective-permute-start.7 = (bf16[128,388]{1,0:T(8,128)(2,1)S(1)}, bf16[128,388]{1,0:T(8,128)(2,1)S(1)}, u32[]{:S(2)}, u32[]{:S(2)}) collective-permute-start(bf16[128,388]{1,0:T(8,128)(2,1)S(1)} %pad_maximum_fusion.6), channel_id=1, source_target_pairs={{0,2},{2,0},{1,3},{3,1},{4,6},{6,4},{5,7},{7,5},{8,10},{10,8},{9,1... | collective-permute-start | bytes 297992 | tf_op jit(solution)/shard_map/ppermute | solution.py:17
  25.7 8.3 %collective-permute-start.5 = (bf16[128,256]{1,0:T(8,128)(2,1)S(1)}, bf16[128,256]{1,0:T(8,128)(2,1)S(1)}, u32[]{:S(2)}, u32[]{:S(2)}) collective-permute-start(bf16[128,256]{1,0:T(8,128)(2,1)S(1)} %get-tuple-element.34), channel_id=1, source_target_pairs={{2,4},{4,2},{6,8},{8,6},{10,12},{12,10},{3,5},{5,3},{7,9},{9,7},{1... | collective-permute-start | bytes 196616 | tf_op jit(solution)/shard_map/ppermute | solution.py:167
  26.4 7.5 %collective-permute-start.8 = (bf16[128,256]{1,0:T(8,128)(2,1)S(1)}, bf16[128,256]{1,0:T(8,128)(2,1)S(1)}, u32[]{:S(2)}, u32[]{:S(2)}) collective-permute-start(bf16[128,256]{1,0:T(8,128)(2,1)S(1)} %get-tuple-element.34), channel_id=1, source_target_pairs={{2,6},{4,0},{6,10},{8,4},{10,14},{12,8},{3,7},{5,1},{7,11},{9,5},{... | collective-permute-start | bytes 196616 | tf_op jit(solution)/shard_map/ppermute | solution.py:168
  27.7 8.7 %collective-permute-start.6 = (bf16[128,512]{1,0:T(8,128)(2,1)S(1)}, bf16[128,512]{1,0:T(8,128)(2,1)S(1)}, u32[]{:S(2)}, u32[]{:S(2)}) collective-permute-start(bf16[128,512]{1,0:T(8,128)(2,1)S(1)} %pad_maximum_fusion.4), channel_id=1, source_target_pairs={{0,2},{2,0},{1,3},{3,1},{4,6},{6,4},{5,7},{7,5},{8,10},{10,8},{9,1... | collective-permute-start | bytes 393224 | tf_op jit(solution)/shard_map/ppermute | solution.py:17
  36.5 1.0 %copy-start.4 = (bf16[4,64,256]{2,1,0:T(8,128)(2,1)S(1)}, bf16[4,64,256]{2,1,0:T(8,128)(2,1)}, u32[]{:S(2)}) copy-start(bf16[4,64,256]{2,1,0:T(8,128)(2,1)} %copy-done.3) | copy-start | bytes 393220
  37.7 5.6 %collective-permute-start.11 = (bf16[128,256]{1,0:T(8,128)(2,1)S(1)}, bf16[128,256]{1,0:T(8,128)(2,1)S(1)}, u32[]{:S(2)}, u32[]{:S(2)}) collective-permute-start(bf16[128,256]{1,0:T(8,128)(2,1)S(1)} %get-tuple-element.22), channel_id=1, source_target_pairs={{0,12},{4,0},{8,4},{12,8},{1,13},{5,1},{9,5},{13,9},{2,14},{6,2},{... | collective-permute-start | bytes 196616 | tf_op jit(solution)/shard_map/ppermute | solution.py:76
  39.2 5.9 %collective-permute-start.10 = (bf16[128,256]{1,0:T(8,128)(2,1)S(1)}, bf16[128,256]{1,0:T(8,128)(2,1)S(1)}, u32[]{:S(2)}, u32[]{:S(2)}) collective-permute-start(bf16[128,256]{1,0:T(8,128)(2,1)S(1)} %get-tuple-element.23), channel_id=1, source_target_pairs={{0,8},{4,12},{8,0},{12,4},{1,9},{5,13},{9,1},{13,5},{2,10},{6,14},... | collective-permute-start | bytes 196616 | tf_op jit(solution)/shard_map/ppermute | solution.py:76
  39.9 6.1 %collective-permute-start.9 = (bf16[128,256]{1,0:T(8,128)(2,1)S(1)}, bf16[128,256]{1,0:T(8,128)(2,1)S(1)}, u32[]{:S(2)}, u32[]{:S(2)}) collective-permute-start(bf16[128,256]{1,0:T(8,128)(2,1)S(1)} %get-tuple-element.21), channel_id=1, source_target_pairs={{0,4},{4,8},{8,12},{12,0},{1,5},{5,9},{9,13},{13,1},{2,6},{6,10},{... | collective-permute-start | bytes 196616 | tf_op jit(solution)/shard_map/ppermute | solution.py:76

commit v17 on v14

--- a/solution.py
+++ b/solution.py
@@ -68,14 +68,8 @@
             "jsc,cm->jsm", columns, inputs, preferred_element_type=jnp.float32
         ).astype(jnp.bfloat16)
         partial, riders = lax.optimization_barrier((partial, riders))
-        total = lax.dynamic_index_in_dim(partial, sub_index, 0, keepdims=False).astype(
-            jnp.float32
-        )
-        for k in range(1, sub_count):
-            piece = lax.dynamic_index_in_dim(partial, (sub_index + k) % sub_count, 0, keepdims=False)
-            total = total + lax.ppermute(
-                piece, "sub", [(i, (i + k) % sub_count) for i in range(sub_count)]
-            ).astype(jnp.float32)
+        arrived = lax.all_to_all(partial, "sub", split_axis=0, concat_axis=0, tiled=True)
+        total = jnp.sum(arrived.astype(jnp.float32), axis=0)
         return total.astype(jnp.bfloat16), riders
 
     pairwise = lax.axis_size("tile") == 2 and ROUNDS == 2

time: 42.5 us -> 54.9 us (1.29)
  blocking collectives: 0 us -> 13.4 us
  starting transfers between devices: 17.1 us -> 10.6 us
  local copies, waits for them, and re-layouts: 5.61 us -> 8.09 us
  waiting for transfers between devices: 10.5 us -> 12.6 us
  matrix products: 6.62 us -> 8.09 us
  other arithmetic: 1.4 us -> 0.58 us
    all_to_all x0 -> x1, blocking collectives: none -> 13.4 us  [coarse_of(): lax.all_to_all(partial, 'sub', split_axis=0, concat_axis=0, tiled=True)]
    ppermute x6 -> x0, starting transfers between devices: 10.6 us -> none  [coarse_of(): lax.ppermute(piece, 'sub', [(i, (i + k) % sub_count) for i in range(sub_c...]
    all_to_all x0 -> x1, waiting for transfers between devices: none -> 8.84 us  [coarse_of(): lax.all_to_all(partial, 'sub', split_axis=0, concat_axis=0, tiled=True)]
    all_to_all x0 -> x1, starting transfers between devices: none -> 5.02 us  [coarse_of(): lax.all_to_all(partial, 'sub', split_axis=0, concat_axis=0, tiled=True)]
    ppermute x6 -> x0, waiting for transfers between devices: 4.4 us -> none  [coarse_of(): lax.ppermute(piece, 'sub', [(i, (i + k) % sub_count) for i in range(sub_c...]
    ppermute x1, waiting for transfers between devices: 2.19 us -> 0.05 us  [local(): crossing = lax.ppermute(toward_diagonal, DUCT, crossing_pairs)]
    select_n x1, other arithmetic: 0.99 us -> 0.09 us  [local(): coarse = jnp.where(live, coarse, jnp.zeros((), coarse.dtype))]
    ppermute x3, starting transfers between devices: 4.51 us -> 3.62 us  [swapped(): return lax.ppermute(shard, axis, [(0, 1), (1, 0)])]
  transfers between devices with their start and end apart: 11 -> 6, of which waited for: 6 -> 2; matrix products, arithmetic and copies ran while one was open for 14% -> 8% of each run, Pallas kernels for 0% -> 0%
where the time goes in v17:
time: 54.9 us; the launch traced here: 54.4 us
  blocking collectives  13.4 us (24%)
  waiting for transfers between devices  12.6 us (23%)
  starting transfers between devices  10.6 us (19%)
  local copies, waits for them, and re-layouts  8.09 us (15%)
  matrix products  8.09 us (15%)
  between operations  1.04 us (2%)
  other arithmetic  0.58 us (1%)
    all_to_all x1, blocking collectives, coarse_of(): lax.all_to_all(partial, 'sub', split_axis=0, concat_axis=0, tiled=True)  13.4 us
    all_to_all x1, waiting for transfers between devices, coarse_of(): lax.all_to_all(partial, 'sub', split_axis=0, concat_axis=0, tiled=True)  8.84 us
    all_to_all x1, starting transfers between devices, coarse_of(): lax.all_to_all(partial, 'sub', split_axis=0, concat_axis=0, tiled=True)  5.02 us
    ppermute x3, waiting for transfers between devices, swapped(): return lax.ppermute(shard, axis, [(0, 1), (1, 0)])  3.72 us
    ppermute x3, starting transfers between devices, swapped(): return lax.ppermute(shard, axis, [(0, 1), (1, 0)])  3.62 us
    dot_general x1, matrix products, local(): base_solve = jnp.dot(inverse, source, preferred_element_type=jnp.float32)  2.35 us
    gather x1, local copies, waits for them, and re-layouts, local(): lower_basis = basis_now[lower_at]  1.3 us
    ppermute x1, starting transfers between devices, local(): crossing = lax.ppermute(toward_diagonal, DUCT, crossing_pairs)  1.28 us
  transfers between devices with their start and end apart: 6, of which 2 were waited for; matrix products, arithmetic and copies ran while one was open for 8% of the time, Pallas kernels for 0%

profile of v17, /device:TPU:0, one launch (start us, length us, event | category | flops | bytes accessed | tf_op | source)
XLA Modules:
  0.0 54.4 jit_solution(6375619556401154060)
XLA Ops:
  0.7 0.3 copy-done
  1.1 2.4 %fusion.11 = f32[1024,256]{1,0:T(8,128)S(1)} fusion(bf16[1,1024,256]{2,1,0:T(8,128)(2,1)S(1)} %copy-done, bf16[1,1024,1024]{2,1,0:T(8,128)(2,1)} %param.8), kind=kOutput, calls=%fused_computation.27 | convolution fusion | flops 536870912 | bytes 3670016 | tf_op jit(solution)/shard_map/dot_general | solution.py:104
  3.7 3.0 %collective-permute-start.1 = (bf16[128,256]{1,0:T(8,128)(2,1)S(1)}, bf16[128,256]{1,0:T(8,128)(2,1)S(1)}, u32[]{:S(2)}, u32[]{:S(2)}) collective-permute-start(bf16[128,256]{1,0:T(8,128)(2,1)S(1)} %fusion.9), channel_id=1, source_target_pairs={{0,2},{2,0},{1,3},{3,1},{4,6},{6,4},{5,7},{7,5},{8,10},{10,8},{9,1... | collective-permute-start | bytes 196616 | tf_op jit(solution)/shard_map/ppermute | solution.py:17
  6.8 1.1 %fusion.41 = (bf16[1024,128]{1,0:T(8,128)(2,1)S(1)}, bf16[1024,128]{1,0:T(8,128)(2,1)S(1)}) fusion(bf16[1024,1024]{1,0:T(8,128)(2,1)} %bitcast.72), kind=kLoop, calls=%fused_computation.87 | loop fusion | bytes 1048576 | tf_op jit(solution)/shard_map/slice | solution.py:57
  7.9 0.7 %copy.18 = bf16[128,2]{1,0:T(8,128)(2,1)} copy(bf16[128,2]{0,1:T(2,128)(2,1)S(1)} %get-tuple-element.18) | data formatting | bytes 1024 | tf_op jit(solution)/shard_map/convert_element_type | solution.py:79
  8.6 0.7 %copy.19 = bf16[128,2]{1,0:T(8,128)(2,1)} copy(bf16[128,2]{0,1:T(2,128)(2,1)S(1)} %get-tuple-element.17) | data formatting | bytes 1024 | tf_op jit(solution)/shard_map/convert_element_type | solution.py:80
  9.5 0.6 %copy-done.4 = bf16[4,64,256]{2,1,0:T(8,128)(2,1)} copy-done((bf16[4,64,256]{2,1,0:T(8,128)(2,1)}, bf16[4,64,256]{2,1,0:T(8,128)(2,1)S(1)}, u32[]{:S(2)}) %copy-start.4) | copy-done | bytes 131096
  10.1 0.9 %convolution_convert_fusion.1 = bf16[4,128,256]{2,1,0:T(8,128)(2,1)} fusion(bf16[4,64,256]{2,1,0:T(8,128)(2,1)S(1)} %get-tuple-element.24, bf16[4,64,256]{2,1,0:T(8,128)(2,1)S(1)} %get-tuple-element.23, bf16[128,256]{1,0:T(8,128)(2,1)S(1)} %get-tuple-element.30, bf16[128,256]{1,0:T(8,128)(2,1)S(1)} %get-tuple-element.29), kind=kOutput, calls=%fused_computation.10 | convolution fusion | flops 68026368 | bytes 655360 | tf_op jit(solution)/shard_map/jsc,cm->jsm/dot_general | solution.py:67
  11.1 1.3 %gather_fusion.1 = bf16[128,128]{1,0:T(8,128)(2,1)} fusion(bf16[1024,128]{1,0:T(8,128)(2,1)S(1)} %bitcast.67, s32[1024]{0:T(1024)S(1)} %get-tuple-element.39), kind=kCustom, calls=%fused_computation.1 | custom fusion | bytes 66048 | tf_op jit(solution)/shard_map/gather | solution.py:125
  12.4 0.8 %gather_fusion = f32[128,256]{1,0:T(8,128)S(1)} fusion(f32[1024,256]{1,0:T(8,128)S(1)} %fusion.11, s32[1024]{0:T(1024)S(1)} %get-tuple-element.39), kind=kCustom, calls=%fused_computation | custom fusion | bytes 262656 | tf_op jit(solution)/shard_map/gather | solution.py:145
  13.1 0.7 %gather_fusion.3 = bf16[128,128]{1,0:T(8,128)(2,1)S(1)} fusion(bf16[1024,128]{1,0:T(8,128)(2,1)S(1)} %bitcast.68, s32[1024]{0:T(1024)S(1)} %get-tuple-element.38), kind=kCustom, calls=%fused_computation.3 | custom fusion | bytes 66048 | tf_op jit(solution)/shard_map/gather | solution.py:126
  13.8 0.8 %gather_fusion.2 = f32[128,256]{1,0:T(8,128)S(1)} fusion(f32[1024,256]{1,0:T(8,128)S(1)} %fusion.11, s32[1024]{0:T(1024)S(1)} %get-tuple-element.38), kind=kCustom, calls=%fused_computation.2 | custom fusion | bytes 262656 | tf_op jit(solution)/shard_map/gather | solution.py:148
  14.6 5.0 %all-to-all-start = ((bf16[4,128,256]{2,1,0:T(8,128)(2,1)}), bf16[4,128,256]{2,1,0:T(8,128)(2,1)S(1)}, u32[]{:S(2)}, u32[]{:S(2)}) async-start(bf16[4,128,256]{2,1,0:T(8,128)(2,1)} %convolution_convert_fusion.1), calls=%async_computation | async-start | bytes 524288 | tf_op jit(solution)/shard_map/all_to_all | solution.py:71
  20.2 8.8 %all-to-all-done = bf16[4,128,256]{2,1,0:T(8,128)(2,1)S(1)} async-done(((bf16[4,128,256]{2,1,0:T(8,128)(2,1)}), bf16[4,128,256]{2,1,0:T(8,128)(2,1)S(1)}, u32[]{:S(2)}, u32[]{:S(2)}) %all-to-all-start) | async-done | bytes 262176 | tf_op jit(solution)/shard_map/all_to_all | solution.py:71
  29.1 0.9 %fusion.5 = bf16[128,256]{1,0:T(8,128)(2,1)S(1)} fusion(f32[128,256]{1,0:T(8,128)S(1)} %gather_fusion, bf16[128,128]{1,0:T(8,128)(2,1)} %gather_fusion.1, bf16[128,256]{1,0:T(8,128)(2,1)S(1)} %broadcast_select_fusion.2), kind=kOutput, calls=%fused_computation.19 | convolution fusion | flops 8454144 | bytes 294912 | tf_op jit(solution)/shard_map/dot_general | solution.py:145
  30.0 0.8 %broadcast_select_fusion.5 = (bf16[128,256]{1,0:T(8,128)(2,1)S(1)}, bf16[128,256]{1,0:T(8,128)(2,1)}, bf16[128,256]{1,0:T(8,128)(2,1)}) fusion(bf16[128,256]{1,0:T(8,128)(2,1)S(1)} %fusion.5, pred[]{:T(512)S(6)} %eq.6, f32[128,256]{1,0:T(8,128)S(1)} %gather_fusion.2, bf16[128,128]{1,0:T(8,128)(2,1)S(1)} %gather_fusion.3, ...), kind=kOutput, calls=%fused_computation.59 | convolution fusion | flops 8519680 | bytes 491521 | tf_op jit(solution)/shard_map/dot_general | solution.py:148
  30.9 0.9 %concatenate.29 = bf16[128,900]{1,0:T(8,128)(2,1)S(1)} concatenate(bf16[128,256]{1,0:T(8,128)(2,1)S(1)} %get-tuple-element.27, bf16[128,256]{1,0:T(8,128)(2,1)S(1)} %broadcast_select_fusion.2, bf16[128,256]{1,0:T(8,128)(2,1)S(1)} %fusion.4, bf16[128,128]{1,0:T(8,128)(2,1)S(1)} %fusion.10, bf16[128,2]{1,0:T(8,128)(2,1)} %copy.18, bf16[128,2]{1,0:T(8,128)(2,1)} %copy.19), dimensions={1} | concatenate | bytes 460800 | tf_op jit(solution)/shard_map/concatenate | solution.py:156
  31.7 0.6 %collective-permute-start.3 = (bf16[128,900]{1,0:T(8,128)(2,1)S(1)}, bf16[128,900]{1,0:T(8,128)(2,1)S(1)}, u32[]{:S(2)}, u32[]{:S(2)}) collective-permute-start(bf16[128,900]{1,0:T(8,128)(2,1)S(1)} %concatenate.29), channel_id=1, source_target_pairs={{0,2},{2,0},{1,3},{3,1},{4,6},{6,4},{5,7},{7,5},{8,10},{10,8},{9,1... | collective-permute-start | bytes 691208 | tf_op jit(solution)/shard_map/ppermute | solution.py:17
  32.4 1.3 %collective-permute-start.4 = (bf16[128,256]{1,0:T(8,128)(2,1)}, bf16[128,256]{1,0:T(8,128)(2,1)S(1)}, u32[]{:S(2)}, u32[]{:S(2)}) collective-permute-start(bf16[128,256]{1,0:T(8,128)(2,1)} %get-tuple-element.28), channel_id=1, source_target_pairs={{2,6},{4,0},{6,10},{8,4},{10,14},{12,8},{3,7},{5,1},{7,11},{9,5},{... | collective-permute-start | bytes 196616 | tf_op jit(solution)/shard_map/ppermute | solution.py:159
  33.6 0.7 %collective-permute-start.2 = (bf16[128,256]{1,0:T(8,128)(2,1)}, bf16[128,256]{1,0:T(8,128)(2,1)S(1)}, u32[]{:S(2)}, u32[]{:S(2)}) collective-permute-start(bf16[128,256]{1,0:T(8,128)(2,1)} %get-tuple-element.28), channel_id=1, source_target_pairs={{2,4},{4,2},{6,8},{8,6},{10,12},{12,10},{3,5},{5,3},{7,9},{9,7},{1... | collective-permute-start | bytes 196616 | tf_op jit(solution)/shard_map/ppermute | solution.py:158
  34.5 3.7 %collective-permute-done.3 = bf16[128,900]{1,0:T(8,128)(2,1)S(1)} collective-permute-done((bf16[128,900]{1,0:T(8,128)(2,1)S(1)}, bf16[128,900]{1,0:T(8,128)(2,1)S(1)}, u32[]{:S(2)}, u32[]{:S(2)}) %collective-permute-start.3) | collective-permute-done | bytes 230432 | tf_op jit(solution)/shard_map/ppermute | solution.py:17
  38.4 0.3 convolution_add_fusion
  39.8 13.4 %all_to_all.10 = bf16[4,128,256]{2,1,0:T(8,128)(2,1)S(1)} all-to-all(bf16[4,128,256]{2,1,0:T(8,128)(2,1)S(1)} %convolution_convert_fusion), channel_id=1, replica_groups=mesh['group'=2,'sub'=4,'tile'=2,'rep'=2] {'sub'}, dimensions={0} | all-to-all | bytes 524288 | tf_op jit(solution)/shard_map/all_to_all | solution.py:71
  53.3 1.1 %fusion.2 = bf16[1,1024,256]{2,1,0:T(8,128)(2,1)} fusion(f32[1024,256]{1,0:T(8,128)S(1)} %convolution_add_fusion, bf16[128,256]{1,0:T(8,128)(2,1)S(1)} %reduce_sum.25, pred[128]{0:T(512)(128)(4,1)S(1)} %iota_compare_fusion, bf16[1,1024,128]{2,1,0:T(8,128)(2,1)S(1)} %copy-done.1), kind=kOutput, calls=%fused_computation.8 | convolution fusion | flops 67665920 | bytes 1900672 | tf_op jit(solution)/shard_map/dot_general | solution.py:140
  (47 shorter events, 2.5 us)
Async XLA Ops:
  0.0 1.1 %copy-start = (bf16[1,1024,256]{2,1,0:T(8,128)(2,1)S(1)}, bf16[1,1024,256]{2,1,0:T(8,128)(2,1)}, u32[]{:S(2)}) copy-start(bf16[1,1024,256]{2,1,0:T(8,128)(2,1)} %param.7) | copy-start | bytes 1572868
  1.1 2.4 %copy-start.1 = (bf16[1,1024,128]{2,1,0:T(8,128)(2,1)S(1)}, bf16[1,1024,128]{2,1,0:T(8,128)(2,1)}, u32[]{:S(2)}) copy-start(bf16[1,1024,128]{2,1,0:T(8,128)(2,1)} %param.11) | copy-start | bytes 786436
  1.1 5.7 %copy-start.3 = (bf16[4,1,64,1,256]{4,2,3,1,0:T(8,128)(2,1)S(1)}, bf16[4,1,64,1,256]{4,2,3,1,0:T(8,128)(2,1)}, u32[]{:S(2)}) copy-start(bf16[4,1,64,1,256]{4,2,3,1,0:T(8,128)(2,1)} %param.13) | copy-start | bytes 393220
  3.4 4.4 %copy-start.9 = (s32[1,2,128]{2,1,0:T(2,128)S(1)}, s32[1,2,128]{2,1,0:T(2,128)}, u32[]{:S(2)}) copy-start(s32[1,2,128]{2,1,0:T(2,128)} %param.10) | copy-start | bytes 3076
  3.4 4.4 %copy-start.8 = (f32[1,2,128]{2,1,0:T(2,128)S(1)}, f32[1,2,128]{2,1,0:T(2,128)}, u32[]{:S(2)}) copy-start(f32[1,2,128]{2,1,0:T(2,128)} %param.9) | copy-start | bytes 3076
  3.7 5.7 %collective-permute-start.1 = (bf16[128,256]{1,0:T(8,128)(2,1)S(1)}, bf16[128,256]{1,0:T(8,128)(2,1)S(1)}, u32[]{:S(2)}, u32[]{:S(2)}) collective-permute-start(bf16[128,256]{1,0:T(8,128)(2,1)S(1)} %fusion.9), channel_id=1, source_target_pairs={{0,2},{2,0},{1,3},{3,1},{4,6},{6,4},{5,7},{7,5},{8,10},{10,8},{9,1... | collective-permute-start | bytes 196616 | tf_op jit(solution)/shard_map/ppermute | solution.py:17
  6.8 2.7 %collective-permute-start = (bf16[4,64,256]{2,1,0:T(8,128)(2,1)S(1)}, bf16[4,64,256]{2,1,0:T(8,128)(2,1)S(1)}, u32[]{:S(2)}, u32[]{:S(2)}) collective-permute-start(bf16[4,64,256]{2,1,0:T(8,128)(2,1)S(1)} %bitcast.71), channel_id=1, source_target_pairs={{0,1},{1,0},{2,3},{3,2},{4,5},{5,4},{6,7},{7,6},{8,9},{9,8},{10,11... | collective-permute-start | bytes 393224 | tf_op jit(solution)/shard_map/ppermute | solution.py:17
  9.5 0.6 %copy-start.4 = (bf16[4,64,256]{2,1,0:T(8,128)(2,1)}, bf16[4,64,256]{2,1,0:T(8,128)(2,1)S(1)}, u32[]{:S(2)}) copy-start(bf16[4,64,256]{2,1,0:T(8,128)(2,1)S(1)} %get-tuple-element.23) | copy-start | bytes 393220
  9.5 1.6 %copy-start.6 = (bf16[4,64,256]{2,1,0:T(8,128)(2,1)}, bf16[4,64,256]{2,1,0:T(8,128)(2,1)S(1)}, u32[]{:S(2)}) copy-start(bf16[4,64,256]{2,1,0:T(8,128)(2,1)S(1)} %get-tuple-element.24) | copy-start | bytes 393220
  14.6 14.4 %all-to-all-start = ((bf16[4,128,256]{2,1,0:T(8,128)(2,1)}), bf16[4,128,256]{2,1,0:T(8,128)(2,1)S(1)}, u32[]{:S(2)}, u32[]{:S(2)}) async-start(bf16[4,128,256]{2,1,0:T(8,128)(2,1)} %convolution_convert_fusion.1), calls=%async_computation | async-start | bytes 524288 | tf_op jit(solution)/shard_map/all_to_all | solution.py:71
  31.7 7.4 %copy-start.2 = (bf16[128,256]{1,0:T(8,128)(2,1)S(1)}, bf16[128,256]{1,0:T(8,128)(2,1)}, u32[]{:S(2)}) copy-start(bf16[128,256]{1,0:T(8,128)(2,1)} %get-tuple-element.37) | copy-start | bytes 196612
  31.7 6.4 %collective-permute-start.3 = (bf16[128,900]{1,0:T(8,128)(2,1)S(1)}, bf16[128,900]{1,0:T(8,128)(2,1)S(1)}, u32[]{:S(2)}, u32[]{:S(2)}) collective-permute-start(bf16[128,900]{1,0:T(8,128)(2,1)S(1)} %concatenate.29), channel_id=1, source_target_pairs={{0,2},{2,0},{1,3},{3,1},{4,6},{6,4},{5,7},{7,5},{8,10},{10,8},{9,1... | collective-permute-start | bytes 691208 | tf_op jit(solution)/shard_map/ppermute | solution.py:17
  32.4 6.8 %collective-permute-start.4 = (bf16[128,256]{1,0:T(8,128)(2,1)}, bf16[128,256]{1,0:T(8,128)(2,1)S(1)}, u32[]{:S(2)}, u32[]{:S(2)}) collective-permute-start(bf16[128,256]{1,0:T(8,128)(2,1)} %get-tuple-element.28), channel_id=1, source_target_pairs={{2,6},{4,0},{6,10},{8,4},{10,14},{12,8},{3,7},{5,1},{7,11},{9,5},{... | collective-permute-start | bytes 196616 | tf_op jit(solution)/shard_map/ppermute | solution.py:159
  33.6 4.6 %collective-permute-start.2 = (bf16[128,256]{1,0:T(8,128)(2,1)}, bf16[128,256]{1,0:T(8,128)(2,1)S(1)}, u32[]{:S(2)}, u32[]{:S(2)}) collective-permute-start(bf16[128,256]{1,0:T(8,128)(2,1)} %get-tuple-element.28), channel_id=1, source_target_pairs={{2,4},{4,2},{6,8},{8,6},{10,12},{12,10},{3,5},{5,3},{7,9},{9,7},{1... | collective-permute-start | bytes 196616 | tf_op jit(solution)/shard_map/ppermute | solution.py:158
  38.4 1.2 %copy-start.5 = (bf16[4,64,256]{2,1,0:T(8,128)(2,1)S(1)}, bf16[4,64,256]{2,1,0:T(8,128)(2,1)}, u32[]{:S(2)}) copy-start(bf16[4,64,256]{2,1,0:T(8,128)(2,1)} %copy-done.4) | copy-start | bytes 393220
  38.4 1.2 %copy-start.7 = (bf16[4,64,256]{2,1,0:T(8,128)(2,1)S(1)}, bf16[4,64,256]{2,1,0:T(8,128)(2,1)}, u32[]{:S(2)}) copy-start(bf16[4,64,256]{2,1,0:T(8,128)(2,1)} %copy-done.6) | copy-start | bytes 393220

commit v18 on v14

--- a/solution.py
+++ b/solution.py
@@ -97,10 +97,14 @@
                 crossing_pairs.append((i, target))
 
     def projection_of(mix, faces, coarse):
-        return (
-            jnp.dot(mix[:, : faces.shape[0]], faces, preferred_element_type=jnp.float32)
-            - jnp.dot(mix[:, faces.shape[0] :], coarse, preferred_element_type=jnp.float32)
-        ).astype(jnp.bfloat16)
+        half = mix.shape[1] // 2
+        total = 0.0
+        for part in (mix[:, :half], mix[:, half:]):
+            total = total + (
+                jnp.dot(part[:, : faces.shape[0]], faces, preferred_element_type=jnp.float32)
+                - jnp.dot(part[:, faces.shape[0] :], coarse, preferred_element_type=jnp.float32)
+            )
+        return total.astype(jnp.bfloat16)
 
     def face_rows_of(gain, lower, upper):
         return jnp.concatenate(
@@ -141,7 +145,10 @@
                 jnp.dot(basis_now.T, basis_now, preferred_element_type=jnp.float32),
                 0.0,
             )
-            mine = jnp.concatenate([sends, keeps], axis=1).astype(jnp.bfloat16)
+            exact = jnp.concatenate([sends, keeps], axis=1)
+            high = exact.astype(jnp.bfloat16)
+            low = (exact - high.astype(jnp.float32)).astype(jnp.bfloat16)
+            mine = jnp.concatenate([high, low], axis=1)
         coarse = jnp.where(live, coarse, jnp.zeros((), coarse.dtype))
         correction = jnp.dot(basis, coarse, preferred_element_type=jnp.float32)
         iterate = local_solve + correction

time: 42.5 us -> 48.9 us (1.15)
  waiting for transfers between devices: 10.5 us -> 17.2 us
  local copies, waits for them, and re-layouts: 5.61 us -> 7.09 us
  starting transfers between devices: 17.1 us -> 16.2 us
  other arithmetic: 1.4 us -> 0.53 us
    ppermute x6, waiting for transfers between devices: 4.4 us -> 10.7 us  [coarse_of(): lax.ppermute(piece, 'sub', [(i, (i + k) % sub_count) for i in range(sub_c...]
    ppermute x3, waiting for transfers between devices: 3.89 us -> 6.53 us  [swapped(): return lax.ppermute(shard, axis, [(0, 1), (1, 0)])]
    ppermute x1, waiting for transfers between devices: 2.19 us -> 0.01 us  [local(): crossing = lax.ppermute(toward_diagonal, DUCT, crossing_pairs)]
    ppermute x6, starting transfers between devices: 10.6 us -> 9.37 us  [coarse_of(): lax.ppermute(piece, 'sub', [(i, (i + k) % sub_count) for i in range(sub_c...]
    select_n x1, other arithmetic: 0.99 us -> 0.09 us  [local(): coarse = jnp.where(live, coarse, jnp.zeros((), coarse.dtype))]
    concatenate x1, local copies, waits for them, and re-layouts: 0.1 us -> 0.9 us  [local(): jnp.concatenate([toward_partner, coarse, mine, gains_pair], axis=1)]
    squeeze x2, local copies, waits for them, and re-layouts: 0.71 us -> 0.05 us  [coarse_of(): lax.dynamic_index_in_dim(partial, (sub_index + k) % sub_count, 0, keepdim...]
    dot_general x1, matrix products: 0.79 us -> 0.15 us  [local(): jnp.dot(upper_basis, coarse, preferred_element_type=jnp.float32)]
where the time goes in v18:
time: 48.9 us; the launch traced here: 48.7 us
  waiting for transfers between devices  17.2 us (35%)
  starting transfers between devices  16.2 us (33%)
  local copies, waits for them, and re-layouts  7.09 us (14%)
  matrix products  6.59 us (13%)
  between operations  1.07 us (2%)
  other arithmetic  0.53 us (1%)
    ppermute x6, waiting for transfers between devices, coarse_of(): lax.ppermute(piece, 'sub', [(i, (i + k) % sub_count) for i in range(sub_c...  10.7 us
    ppermute x6, starting transfers between devices, coarse_of(): lax.ppermute(piece, 'sub', [(i, (i + k) % sub_count) for i in range(sub_c...  9.37 us
    ppermute x3, waiting for transfers between devices, swapped(): return lax.ppermute(shard, axis, [(0, 1), (1, 0)])  6.53 us
    ppermute x3, starting transfers between devices, swapped(): return lax.ppermute(shard, axis, [(0, 1), (1, 0)])  4.85 us
    dot_general x1, matrix products, local(): base_solve = jnp.dot(inverse, source, preferred_element_type=jnp.float32)  2.34 us
    ppermute x1, starting transfers between devices, local(): crossing = lax.ppermute(toward_diagonal, DUCT, crossing_pairs)  1.29 us
    dot_general x1, matrix products, local(): correction = jnp.dot(basis, coarse, preferred_element_type=jnp.float32)  1.15 us
    slice x1, local copies, waits for them, and re-layouts, local(): inverse[:, :face_rows]  1.07 us
  transfers between devices with their start and end apart: 11, of which 6 were waited for; matrix products, arithmetic and copies ran while one was open for 14% of the time, Pallas kernels for 0%

profile of v18, /device:TPU:0, one launch (start us, length us, event | category | flops | bytes accessed | tf_op | source)
XLA Modules:
  0.0 48.7 jit_solution(2846511428811606039)
XLA Ops:
  1.2 2.3 %fusion.11 = f32[1024,256]{1,0:T(8,128)S(1)} fusion(bf16[1,1024,256]{2,1,0:T(8,128)(2,1)S(1)} %copy-done, bf16[1,1024,1024]{2,1,0:T(8,128)(2,1)} %param.8), kind=kOutput, calls=%fused_computation.29 | convolution fusion | flops 536870912 | bytes 3670016 | tf_op jit(solution)/shard_map/dot_general | solution.py:114
  3.8 2.9 %collective-permute-start.1 = (bf16[128,256]{1,0:T(8,128)(2,1)S(1)}, bf16[128,256]{1,0:T(8,128)(2,1)S(1)}, u32[]{:S(2)}, u32[]{:S(2)}) collective-permute-start(bf16[128,256]{1,0:T(8,128)(2,1)S(1)} %fusion.10), channel_id=1, source_target_pairs={{0,2},{2,0},{1,3},{3,1},{4,6},{6,4},{5,7},{7,5},{8,10},{10,8},{9,1... | collective-permute-start | bytes 196616 | tf_op jit(solution)/shard_map/ppermute | solution.py:17
  6.8 0.7 %copy.16 = bf16[128,2]{1,0:T(8,128)(2,1)} copy(bf16[128,2]{0,1:T(2,128)(2,1)S(1)} %get-tuple-element.17) | data formatting | bytes 1024 | tf_op jit(solution)/shard_map/convert_element_type | solution.py:86
  7.5 0.7 %copy.15 = bf16[128,2]{1,0:T(8,128)(2,1)} copy(bf16[128,2]{0,1:T(2,128)(2,1)S(1)} %get-tuple-element.18) | data formatting | bytes 1024 | tf_op jit(solution)/shard_map/convert_element_type | solution.py:85
  8.2 1.1 %fusion.62 = (bf16[1024,128]{1,0:T(8,128)(2,1)S(1)}, bf16[1024,128]{1,0:T(8,128)(2,1)S(1)}) fusion(bf16[1024,1024]{1,0:T(8,128)(2,1)} %bitcast.92), kind=kLoop, calls=%fused_computation.119 | loop fusion | bytes 1048576 | tf_op jit(solution)/shard_map/slice | solution.py:57
  10.5 0.7 %gather_fusion.3 = bf16[128,128]{1,0:T(8,128)(2,1)S(1)} fusion(bf16[1024,128]{1,0:T(8,128)(2,1)S(1)} %bitcast.88, s32[1024]{0:T(1024)S(1)} %get-tuple-element.44), kind=kCustom, calls=%fused_computation.3 | custom fusion | bytes 66048 | tf_op jit(solution)/shard_map/gather | solution.py:136
  11.2 0.7 %gather_fusion.1 = bf16[128,128]{1,0:T(8,128)(2,1)S(1)} fusion(bf16[1024,128]{1,0:T(8,128)(2,1)S(1)} %bitcast.89, s32[1024]{0:T(1024)S(1)} %get-tuple-element.45), kind=kCustom, calls=%fused_computation.1 | custom fusion | bytes 66048 | tf_op jit(solution)/shard_map/gather | solution.py:135
  11.9 0.8 %gather_fusion = f32[128,256]{1,0:T(8,128)S(1)} fusion(f32[1024,256]{1,0:T(8,128)S(1)} %fusion.11, s32[1024]{0:T(1024)S(1)} %get-tuple-element.45), kind=kCustom, calls=%fused_computation | custom fusion | bytes 262656 | tf_op jit(solution)/shard_map/gather | solution.py:158
  12.6 0.8 %gather_fusion.2 = f32[128,256]{1,0:T(8,128)S(1)} fusion(f32[1024,256]{1,0:T(8,128)S(1)} %fusion.11, s32[1024]{0:T(1024)S(1)} %get-tuple-element.44), kind=kCustom, calls=%fused_computation.2 | custom fusion | bytes 262656 | tf_op jit(solution)/shard_map/gather | solution.py:161
  13.7 1.7 %collective-permute-start.2 = (bf16[128,256]{1,0:T(8,128)(2,1)S(1)}, bf16[128,256]{1,0:T(8,128)(2,1)S(1)}, u32[]{:S(2)}, u32[]{:S(2)}) collective-permute-start(bf16[128,256]{1,0:T(8,128)(2,1)S(1)} %get-tuple-element.26), channel_id=1, source_target_pairs={{0,4},{4,8},{8,12},{12,0},{1,5},{5,9},{9,13},{13,1},{2,6},{6,10},{... | collective-permute-start | bytes 196616 | tf_op jit(solution)/shard_map/ppermute | solution.py:76
  15.4 2.2 %collective-permute-start.4 = (bf16[128,256]{1,0:T(8,128)(2,1)S(1)}, bf16[128,256]{1,0:T(8,128)(2,1)S(1)}, u32[]{:S(2)}, u32[]{:S(2)}) collective-permute-start(bf16[128,256]{1,0:T(8,128)(2,1)S(1)} %get-tuple-element.27), channel_id=1, source_target_pairs={{0,12},{4,0},{8,4},{12,8},{1,13},{5,1},{9,5},{13,9},{2,14},{6,2},{... | collective-permute-start | bytes 196616 | tf_op jit(solution)/shard_map/ppermute | solution.py:76
  17.6 0.9 %collective-permute-start.3 = (bf16[128,256]{1,0:T(8,128)(2,1)S(1)}, bf16[128,256]{1,0:T(8,128)(2,1)S(1)}, u32[]{:S(2)}, u32[]{:S(2)}) collective-permute-start(bf16[128,256]{1,0:T(8,128)(2,1)S(1)} %get-tuple-element.28), channel_id=1, source_target_pairs={{0,8},{4,12},{8,0},{12,4},{1,9},{5,13},{9,1},{13,5},{2,10},{6,14},... | collective-permute-start | bytes 196616 | tf_op jit(solution)/shard_map/ppermute | solution.py:76
  18.5 1.7 %collective-permute-done.2 = bf16[128,256]{1,0:T(8,128)(2,1)S(1)} collective-permute-done((bf16[128,256]{1,0:T(8,128)(2,1)S(1)}, bf16[128,256]{1,0:T(8,128)(2,1)S(1)}, u32[]{:S(2)}, u32[]{:S(2)}) %collective-permute-start.2) | collective-permute-done | bytes 65568 | tf_op jit(solution)/shard_map/ppermute | solution.py:76
  20.4 3.3 %collective-permute-done.3 = bf16[128,256]{1,0:T(8,128)(2,1)S(1)} collective-permute-done((bf16[128,256]{1,0:T(8,128)(2,1)S(1)}, bf16[128,256]{1,0:T(8,128)(2,1)S(1)}, u32[]{:S(2)}, u32[]{:S(2)}) %collective-permute-start.3) | collective-permute-done | bytes 65568 | tf_op jit(solution)/shard_map/ppermute | solution.py:76
  24.1 0.9 %concatenate.30 = bf16[128,1284]{1,0:T(8,128)(2,1)S(1)} concatenate(bf16[128,256]{1,0:T(8,128)(2,1)S(1)} %get-tuple-element.33, bf16[128,256]{1,0:T(8,128)(2,1)S(1)} %fusion.25, bf16[128,384]{1,0:T(8,128)(2,1)S(1)} %fusion.14, bf16[128,384]{1,0:T(8,128)(2,1)S(1)} %subtract_convert_fusion, bf16[128,2]{1,0:T(8,128)(2,1)} %copy.15, bf16[128,2]{1,0:T(8,128)(2,1)} %copy.16), dimensions={1} | concatenate | bytes 657408 | tf_op jit(solution)/shard_map/concatenate | solution.py:169
  25.0 1.5 %collective-permute-start.6 = (bf16[128,1284]{1,0:T(8,128)(2,1)S(1)}, bf16[128,1284]{1,0:T(8,128)(2,1)S(1)}, u32[]{:S(2)}, u32[]{:S(2)}) collective-permute-start(bf16[128,1284]{1,0:T(8,128)(2,1)S(1)} %concatenate.30), channel_id=1, source_target_pairs={{0,2},{2,0},{1,3},{3,1},{4,6},{6,4},{5,7},{7,5},{8,10},{10,8},{9,1... | collective-permute-start | bytes 986120 | tf_op jit(solution)/shard_map/ppermute | solution.py:17
  26.5 0.7 %collective-permute-start.5 = (bf16[128,256]{1,0:T(8,128)(2,1)S(1)}, bf16[128,256]{1,0:T(8,128)(2,1)S(1)}, u32[]{:S(2)}, u32[]{:S(2)}) collective-permute-start(bf16[128,256]{1,0:T(8,128)(2,1)S(1)} %get-tuple-element.34), channel_id=1, source_target_pairs={{2,4},{4,2},{6,8},{8,6},{10,12},{12,10},{3,5},{5,3},{7,9},{9,7},{1... | collective-permute-start | bytes 196616 | tf_op jit(solution)/shard_map/ppermute | solution.py:171
  27.2 1.3 %collective-permute-start.7 = (bf16[128,256]{1,0:T(8,128)(2,1)S(1)}, bf16[128,256]{1,0:T(8,128)(2,1)S(1)}, u32[]{:S(2)}, u32[]{:S(2)}) collective-permute-start(bf16[128,256]{1,0:T(8,128)(2,1)S(1)} %get-tuple-element.34), channel_id=1, source_target_pairs={{2,6},{4,0},{6,10},{8,4},{10,14},{12,8},{3,7},{5,1},{7,11},{9,5},{... | collective-permute-start | bytes 196616 | tf_op jit(solution)/shard_map/ppermute | solution.py:172
  28.5 6.5 %collective-permute-done.6 = bf16[128,1284]{1,0:T(8,128)(2,1)S(1)} collective-permute-done((bf16[128,1284]{1,0:T(8,128)(2,1)S(1)}, bf16[128,1284]{1,0:T(8,128)(2,1)S(1)}, u32[]{:S(2)}, u32[]{:S(2)}) %collective-permute-start.6) | collective-permute-done | bytes 328736 | tf_op jit(solution)/shard_map/ppermute | solution.py:17
  37.4 1.2 %collective-permute-start.8 = (bf16[128,256]{1,0:T(8,128)(2,1)S(1)}, bf16[128,256]{1,0:T(8,128)(2,1)S(1)}, u32[]{:S(2)}, u32[]{:S(2)}) collective-permute-start(bf16[128,256]{1,0:T(8,128)(2,1)S(1)} %get-tuple-element.23), channel_id=1, source_target_pairs={{0,4},{4,8},{8,12},{12,0},{1,5},{5,9},{9,13},{13,1},{2,6},{6,10},{... | collective-permute-start | bytes 196616 | tf_op jit(solution)/shard_map/ppermute | solution.py:76
  38.6 2.9 %collective-permute-start.10 = (bf16[128,256]{1,0:T(8,128)(2,1)S(1)}, bf16[128,256]{1,0:T(8,128)(2,1)S(1)}, u32[]{:S(2)}, u32[]{:S(2)}) collective-permute-start(bf16[128,256]{1,0:T(8,128)(2,1)S(1)} %get-tuple-element.24), channel_id=1, source_target_pairs={{0,12},{4,0},{8,4},{12,8},{1,13},{5,1},{9,5},{13,9},{2,14},{6,2},{... | collective-permute-start | bytes 196616 | tf_op jit(solution)/shard_map/ppermute | solution.py:76
  42.0 2.5 %collective-permute-done.8 = bf16[128,256]{1,0:T(8,128)(2,1)S(1)} collective-permute-done((bf16[128,256]{1,0:T(8,128)(2,1)S(1)}, bf16[128,256]{1,0:T(8,128)(2,1)S(1)}, u32[]{:S(2)}, u32[]{:S(2)}) %collective-permute-start.8) | collective-permute-done | bytes 65568 | tf_op jit(solution)/shard_map/ppermute | solution.py:76
  44.5 3.0 %collective-permute-done.9 = bf16[128,256]{1,0:T(8,128)(2,1)S(1)} collective-permute-done((bf16[128,256]{1,0:T(8,128)(2,1)S(1)}, bf16[128,256]{1,0:T(8,128)(2,1)S(1)}, u32[]{:S(2)}, u32[]{:S(2)}) %collective-permute-start.9) | collective-permute-done | bytes 65568 | tf_op jit(solution)/shard_map/ppermute | solution.py:76
  47.5 1.1 %fusion.2 = bf16[1,1024,256]{2,1,0:T(8,128)(2,1)} fusion(f32[1024,256]{1,0:T(8,128)S(1)} %convolution_add_fusion, bf16[128,256]{1,0:T(8,128)(2,1)S(1)} %collective-permute-done.10, bf16[128,256]{1,0:T(8,128)(2,1)S(1)} %collective-permute-done.9, bf16[128,256]{1,0:T(8,128)(2,1)S(1)} %collective-permute-done.8, ...), kind=kOutput, calls=%fused_computation.8 | convolution fusion | flops 67928064 | bytes 2097668 | tf_op jit(solution)/shard_map/dot_general | solution.py:153
  (60 shorter events, 5.5 us)
Async XLA Ops:
  0.0 1.1 %copy-start = (bf16[1,1024,256]{2,1,0:T(8,128)(2,1)S(1)}, bf16[1,1024,256]{2,1,0:T(8,128)(2,1)}, u32[]{:S(2)}) copy-start(bf16[1,1024,256]{2,1,0:T(8,128)(2,1)} %param.7) | copy-start | bytes 1572868
  0.0 9.4 %collective-permute-start = (bf16[4,64,256]{2,1,0:T(8,128)(2,1)}, bf16[4,64,256]{2,1,0:T(8,128)(2,1)S(1)}, u32[]{:S(2)}, u32[]{:S(2)}) collective-permute-start(bf16[4,64,256]{2,1,0:T(8,128)(2,1)} %bitcast.91), channel_id=1, source_target_pairs={{0,1},{1,0},{2,3},{3,2},{4,5},{5,4},{6,7},{7,6},{8,9},{9,8},{10,11... | collective-permute-start | bytes 393224 | tf_op jit(solution)/shard_map/ppermute | solution.py:17
  1.1 2.4 %copy-start.1 = (bf16[1,1024,128]{2,1,0:T(8,128)(2,1)S(1)}, bf16[1,1024,128]{2,1,0:T(8,128)(2,1)}, u32[]{:S(2)}) copy-start(bf16[1,1024,128]{2,1,0:T(8,128)(2,1)} %param.11) | copy-start | bytes 786436
  1.1 5.6 %copy-start.8 = (s32[1,2,128]{2,1,0:T(2,128)S(1)}, s32[1,2,128]{2,1,0:T(2,128)}, u32[]{:S(2)}) copy-start(s32[1,2,128]{2,1,0:T(2,128)} %param.10) | copy-start | bytes 3076
  1.2 5.6 %copy-start.7 = (f32[1,2,128]{2,1,0:T(2,128)S(1)}, f32[1,2,128]{2,1,0:T(2,128)}, u32[]{:S(2)}) copy-start(f32[1,2,128]{2,1,0:T(2,128)} %param.9) | copy-start | bytes 3076
  3.5 5.9 %copy-start.2 = (bf16[4,1,64,1,256]{4,2,3,1,0:T(8,128)(2,1)S(1)}, bf16[4,1,64,1,256]{4,2,3,1,0:T(8,128)(2,1)}, u32[]{:S(2)}) copy-start(bf16[4,1,64,1,256]{4,2,3,1,0:T(8,128)(2,1)} %param.13) | copy-start | bytes 393220
  3.8 5.6 %collective-permute-start.1 = (bf16[128,256]{1,0:T(8,128)(2,1)S(1)}, bf16[128,256]{1,0:T(8,128)(2,1)S(1)}, u32[]{:S(2)}, u32[]{:S(2)}) collective-permute-start(bf16[128,256]{1,0:T(8,128)(2,1)S(1)} %fusion.10), channel_id=1, source_target_pairs={{0,2},{2,0},{1,3},{3,1},{4,6},{6,4},{5,7},{7,5},{8,10},{10,8},{9,1... | collective-permute-start | bytes 196616 | tf_op jit(solution)/shard_map/ppermute | solution.py:17
  9.5 0.7 %copy-start.3 = (bf16[4,64,256]{2,1,0:T(8,128)(2,1)}, bf16[4,64,256]{2,1,0:T(8,128)(2,1)S(1)}, u32[]{:S(2)}) copy-start(bf16[4,64,256]{2,1,0:T(8,128)(2,1)S(1)} %get-tuple-element.29) | copy-start | bytes 393220
  9.5 0.7 %copy-start.5 = (bf16[4,64,256]{2,1,0:T(8,128)(2,1)}, bf16[4,64,256]{2,1,0:T(8,128)(2,1)S(1)}, u32[]{:S(2)}) copy-start(bf16[4,64,256]{2,1,0:T(8,128)(2,1)S(1)} %get-tuple-element.30) | copy-start | bytes 393220
  13.7 6.5 %collective-permute-start.2 = (bf16[128,256]{1,0:T(8,128)(2,1)S(1)}, bf16[128,256]{1,0:T(8,128)(2,1)S(1)}, u32[]{:S(2)}, u32[]{:S(2)}) collective-permute-start(bf16[128,256]{1,0:T(8,128)(2,1)S(1)} %get-tuple-element.26), channel_id=1, source_target_pairs={{0,4},{4,8},{8,12},{12,0},{1,5},{5,9},{9,13},{13,1},{2,6},{6,10},{... | collective-permute-start | bytes 196616 | tf_op jit(solution)/shard_map/ppermute | solution.py:76
  15.4 5.0 %collective-permute-start.4 = (bf16[128,256]{1,0:T(8,128)(2,1)S(1)}, bf16[128,256]{1,0:T(8,128)(2,1)S(1)}, u32[]{:S(2)}, u32[]{:S(2)}) collective-permute-start(bf16[128,256]{1,0:T(8,128)(2,1)S(1)} %get-tuple-element.27), channel_id=1, source_target_pairs={{0,12},{4,0},{8,4},{12,8},{1,13},{5,1},{9,5},{13,9},{2,14},{6,2},{... | collective-permute-start | bytes 196616 | tf_op jit(solution)/shard_map/ppermute | solution.py:76
  17.6 6.1 %collective-permute-start.3 = (bf16[128,256]{1,0:T(8,128)(2,1)S(1)}, bf16[128,256]{1,0:T(8,128)(2,1)S(1)}, u32[]{:S(2)}, u32[]{:S(2)}) collective-permute-start(bf16[128,256]{1,0:T(8,128)(2,1)S(1)} %get-tuple-element.28), channel_id=1, source_target_pairs={{0,8},{4,12},{8,0},{12,4},{1,9},{5,13},{9,1},{13,5},{2,10},{6,14},... | collective-permute-start | bytes 196616 | tf_op jit(solution)/shard_map/ppermute | solution.py:76
  25.0 10.0 %collective-permute-start.6 = (bf16[128,1284]{1,0:T(8,128)(2,1)S(1)}, bf16[128,1284]{1,0:T(8,128)(2,1)S(1)}, u32[]{:S(2)}, u32[]{:S(2)}) collective-permute-start(bf16[128,1284]{1,0:T(8,128)(2,1)S(1)} %concatenate.30), channel_id=1, source_target_pairs={{0,2},{2,0},{1,3},{3,1},{4,6},{6,4},{5,7},{7,5},{8,10},{10,8},{9,1... | collective-permute-start | bytes 986120 | tf_op jit(solution)/shard_map/ppermute | solution.py:17
  26.5 2.0 %collective-permute-start.5 = (bf16[128,256]{1,0:T(8,128)(2,1)S(1)}, bf16[128,256]{1,0:T(8,128)(2,1)S(1)}, u32[]{:S(2)}, u32[]{:S(2)}) collective-permute-start(bf16[128,256]{1,0:T(8,128)(2,1)S(1)} %get-tuple-element.34), channel_id=1, source_target_pairs={{2,4},{4,2},{6,8},{8,6},{10,12},{12,10},{3,5},{5,3},{7,9},{9,7},{1... | collective-permute-start | bytes 196616 | tf_op jit(solution)/shard_map/ppermute | solution.py:171
  27.2 9.3 %collective-permute-start.7 = (bf16[128,256]{1,0:T(8,128)(2,1)S(1)}, bf16[128,256]{1,0:T(8,128)(2,1)S(1)}, u32[]{:S(2)}, u32[]{:S(2)}) collective-permute-start(bf16[128,256]{1,0:T(8,128)(2,1)S(1)} %get-tuple-element.34), channel_id=1, source_target_pairs={{2,6},{4,0},{6,10},{8,4},{10,14},{12,8},{3,7},{5,1},{7,11},{9,5},{... | collective-permute-start | bytes 196616 | tf_op jit(solution)/shard_map/ppermute | solution.py:172
  35.4 1.7 %copy-start.4 = (bf16[4,64,256]{2,1,0:T(8,128)(2,1)S(1)}, bf16[4,64,256]{2,1,0:T(8,128)(2,1)}, u32[]{:S(2)}) copy-start(bf16[4,64,256]{2,1,0:T(8,128)(2,1)} %copy-done.3) | copy-start | bytes 393220
  35.4 1.7 %copy-start.6 = (bf16[4,64,256]{2,1,0:T(8,128)(2,1)S(1)}, bf16[4,64,256]{2,1,0:T(8,128)(2,1)}, u32[]{:S(2)}) copy-start(bf16[4,64,256]{2,1,0:T(8,128)(2,1)} %copy-done.5) | copy-start | bytes 393220
  37.4 7.1 %collective-permute-start.8 = (bf16[128,256]{1,0:T(8,128)(2,1)S(1)}, bf16[128,256]{1,0:T(8,128)(2,1)S(1)}, u32[]{:S(2)}, u32[]{:S(2)}) collective-permute-start(bf16[128,256]{1,0:T(8,128)(2,1)S(1)} %get-tuple-element.23), channel_id=1, source_target_pairs={{0,4},{4,8},{8,12},{12,0},{1,5},{5,9},{9,13},{13,1},{2,6},{6,10},{... | collective-permute-start | bytes 196616 | tf_op jit(solution)/shard_map/ppermute | solution.py:76
  38.6 5.9 %collective-permute-start.10 = (bf16[128,256]{1,0:T(8,128)(2,1)S(1)}, bf16[128,256]{1,0:T(8,128)(2,1)S(1)}, u32[]{:S(2)}, u32[]{:S(2)}) collective-permute-start(bf16[128,256]{1,0:T(8,128)(2,1)S(1)} %get-tuple-element.24), channel_id=1, source_target_pairs={{0,12},{4,0},{8,4},{12,8},{1,13},{5,1},{9,5},{13,9},{2,14},{6,2},{... | collective-permute-start | bytes 196616 | tf_op jit(solution)/shard_map/ppermute | solution.py:76
  41.5 6.0 %collective-permute-start.9 = (bf16[128,256]{1,0:T(8,128)(2,1)S(1)}, bf16[128,256]{1,0:T(8,128)(2,1)S(1)}, u32[]{:S(2)}, u32[]{:S(2)}) collective-permute-start(bf16[128,256]{1,0:T(8,128)(2,1)S(1)} %get-tuple-element.25), channel_id=1, source_target_pairs={{0,8},{4,12},{8,0},{12,4},{1,9},{5,13},{9,1},{13,5},{2,10},{6,14},... | collective-permute-start | bytes 196616 | tf_op jit(solution)/shard_map/ppermute | solution.py:76

commit v19 on v14

--- a/solution.py
+++ b/solution.py
@@ -96,10 +96,9 @@
             if 0 <= target < peers:
                 crossing_pairs.append((i, target))
 
-    def projection_of(mix, faces, coarse):
+    def projection_of(mix, faces, kept):
         return (
-            jnp.dot(mix[:, : faces.shape[0]], faces, preferred_element_type=jnp.float32)
-            - jnp.dot(mix[:, faces.shape[0] :], coarse, preferred_element_type=jnp.float32)
+            jnp.dot(mix, faces, preferred_element_type=jnp.float32) - kept.astype(jnp.float32)
         ).astype(jnp.bfloat16)
 
     def face_rows_of(gain, lower, upper):
@@ -141,7 +140,8 @@
                 jnp.dot(basis_now.T, basis_now, preferred_element_type=jnp.float32),
                 0.0,
             )
-            mine = jnp.concatenate([sends, keeps], axis=1).astype(jnp.bfloat16)
+            mine = sends.astype(jnp.bfloat16)
+            kept_mix = keeps.astype(jnp.bfloat16)
         coarse = jnp.where(live, coarse, jnp.zeros((), coarse.dtype))
         correction = jnp.dot(basis, coarse, preferred_element_type=jnp.float32)
         iterate = local_solve + correction
@@ -158,8 +158,11 @@
             toward_partner = jnp.where(first, upper_trace, lower_trace)
             toward_diagonal = jnp.where(first, lower_trace, upper_trace)
             width = toward_partner.shape[1]
+            kept = jnp.dot(kept_mix, coarse, preferred_element_type=jnp.float32).astype(
+                jnp.bfloat16
+            )
             got = swapped(
-                jnp.concatenate([toward_partner, coarse, mine, gains_pair], axis=1), "tile"
+                jnp.concatenate([toward_partner, kept, mine, gains_pair], axis=1), "tile"
             )
             from_diagonal = lax.ppermute(toward_diagonal, DUCT, diagonal_pairs)
             crossing = lax.ppermute(toward_diagonal, DUCT, crossing_pairs)
@@ -169,14 +172,14 @@
             faces = face_rows_of(gains, from_lower, from_upper)
             partner_lower = jnp.where(first, upper_trace, crossing).astype(jnp.float32)
             partner_upper = jnp.where(first, crossing, lower_trace).astype(jnp.float32)
-            partner_coarse = got[:, width : 2 * width]
+            partner_kept = got[:, width : 2 * width]
             theirs = got[:, 2 * width : 2 * width + mine.shape[1]]
             tail = got[:, 2 * width + mine.shape[1] :].astype(jnp.float32)
             pair = gains.shape[0]
             partner_gains = (tail[:, :pair] + tail[:, pair:]).T
             partner_faces = face_rows_of(partner_gains, partner_lower, partner_upper)
-            own = projection_of(mine, faces, coarse)
-            other = projection_of(theirs, partner_faces, partner_coarse)
+            own = projection_of(mine, faces, kept)
+            other = projection_of(theirs, partner_faces, partner_kept)
             inputs = jnp.concatenate(
                 [jnp.where(first, own, other), jnp.where(first, other, own)], axis=0
             )

time: 42.5 us -> 43 us (1.012)
  starting transfers between devices: 17.1 us -> 20 us
  waiting for transfers between devices: 10.5 us -> 8.91 us
  matrix products: 6.62 us -> 5.81 us
    ppermute x6, starting transfers between devices: 10.6 us -> 13.6 us  [coarse_of(): lax.ppermute(piece, 'sub', [(i, (i + k) % sub_count) for i in range(sub_c...]
    ppermute x1, waiting for transfers between devices: 2.19 us -> 0.85 us  [local(): crossing = lax.ppermute(toward_diagonal, DUCT, crossing_pairs)]
    dot_general x1, matrix products: 0.79 us -> 0.15 us  [local(): jnp.dot(upper_basis, coarse, preferred_element_type=jnp.float32)]
    dot_general x5 -> x3, matrix products: 0.88 us -> 0.73 us  [the longest x1 0.39 us: local(): jnp.dot(kept_mix, coarse, preferred_element_type=jnp.float32)]
  transfers between devices with their start and end apart: 11 -> 11, of which waited for: 6 -> 7; matrix products, arithmetic and copies ran while one was open for 14% -> 12% of each run, Pallas kernels for 0% -> 0%
where the time goes in v19:
time: 43 us; the launch traced here: 42.7 us
  starting transfers between devices  20 us (47%)
  waiting for transfers between devices  8.91 us (21%)
  matrix products  5.81 us (14%)
  local copies, waits for them, and re-layouts  5.62 us (13%)
  other arithmetic  1.4 us (3%)
  between operations  0.99 us (2%)
    ppermute x6, starting transfers between devices, coarse_of(): lax.ppermute(piece, 'sub', [(i, (i + k) % sub_count) for i in range(sub_c...  13.6 us
    ppermute x6, waiting for transfers between devices, coarse_of(): lax.ppermute(piece, 'sub', [(i, (i + k) % sub_count) for i in range(sub_c...  4.58 us
    ppermute x3, starting transfers between devices, swapped(): return lax.ppermute(shard, axis, [(0, 1), (1, 0)])  4.41 us
    ppermute x3, waiting for transfers between devices, swapped(): return lax.ppermute(shard, axis, [(0, 1), (1, 0)])  3.48 us
    dot_general x1, matrix products, local(): base_solve = jnp.dot(inverse, source, preferred_element_type=jnp.float32)  2.35 us
    ppermute x1, starting transfers between devices, local(): crossing = lax.ppermute(toward_diagonal, DUCT, crossing_pairs)  1.28 us
    dot_general x1, matrix products, local(): correction = jnp.dot(basis, coarse, preferred_element_type=jnp.float32)  1.14 us
    slice x1, local copies, waits for them, and re-layouts, local(): inverse[:, :face_rows]  1.07 us
  transfers between devices with their start and end apart: 11, of which 7 were waited for; matrix products, arithmetic and copies ran while one was open for 12% of the time, Pallas kernels for 0%

profile of v19, /device:TPU:0, one launch (start us, length us, event | category | flops | bytes accessed | tf_op | source)
XLA Modules:
  0.0 42.7 jit_solution(1567659805012616486)
XLA Ops:
  0.7 0.3 copy-done
  1.1 2.4 %fusion.11 = f32[1024,256]{1,0:T(8,128)S(1)} fusion(bf16[1,1024,256]{2,1,0:T(8,128)(2,1)S(1)} %copy-done, bf16[1,1024,1024]{2,1,0:T(8,128)(2,1)} %param.8), kind=kOutput, calls=%fused_computation.28 | convolution fusion | flops 536870912 | bytes 3670016 | tf_op jit(solution)/shard_map/dot_general | solution.py:109
  3.7 3.0 %collective-permute-start.1 = (bf16[128,256]{1,0:T(8,128)(2,1)S(1)}, bf16[128,256]{1,0:T(8,128)(2,1)S(1)}, u32[]{:S(2)}, u32[]{:S(2)}) collective-permute-start(bf16[128,256]{1,0:T(8,128)(2,1)S(1)} %fusion.9), channel_id=1, source_target_pairs={{0,2},{2,0},{1,3},{3,1},{4,6},{6,4},{5,7},{7,5},{8,10},{10,8},{9,1... | collective-permute-start | bytes 196616 | tf_op jit(solution)/shard_map/ppermute | solution.py:17
  6.8 1.1 %fusion.54 = (bf16[1024,128]{1,0:T(8,128)(2,1)S(1)}, bf16[1024,128]{1,0:T(8,128)(2,1)S(1)}) fusion(bf16[1024,1024]{1,0:T(8,128)(2,1)} %bitcast.92), kind=kLoop, calls=%fused_computation.107 | loop fusion | bytes 1048576 | tf_op jit(solution)/shard_map/slice | solution.py:57
  8.2 0.8 %collective-permute-done.1 = bf16[128,256]{1,0:T(8,128)(2,1)S(1)} collective-permute-done((bf16[128,256]{1,0:T(8,128)(2,1)S(1)}, bf16[128,256]{1,0:T(8,128)(2,1)S(1)}, u32[]{:S(2)}, u32[]{:S(2)}) %collective-permute-start.1) | collective-permute-done | bytes 65568 | tf_op jit(solution)/shard_map/ppermute | solution.py:17
  9.3 0.7 %dynamic-slice_bitcast_fusion.5 = (bf16[128,256]{1,0:T(8,128)(2,1)}, bf16[128,256]{1,0:T(8,128)(2,1)}, bf16[128,256]{1,0:T(8,128)(2,1)}) fusion(bf16[4,128,256]{2,1,0:T(8,128)(2,1)S(1)} %convolution_convert_fusion.1, s32[]{:T(128)S(6)} %select_n.145, s32[]{:T(128)S(6)} %select_n.149, s32[]{:T(128)S(6)} %select_n.147), kind=kLoop, calls=%fused_computation.70 | loop fusion | bytes 393228 | tf_op jit(solution)/shard_map/jit(dynamic_index_in_dim)/squeeze | solution.py:75
  10.0 2.1 %collective-permute-start.2 = (bf16[128,256]{1,0:T(8,128)(2,1)}, bf16[128,256]{1,0:T(8,128)(2,1)}, u32[]{:S(2)}, u32[]{:S(2)}) collective-permute-start(bf16[128,256]{1,0:T(8,128)(2,1)} %get-tuple-element.26), channel_id=1, source_target_pairs={{0,4},{4,8},{8,12},{12,0},{1,5},{5,9},{9,13},{13,1},{2,6},{6,10},{... | collective-permute-start | bytes 196616 | tf_op jit(solution)/shard_map/ppermute | solution.py:76
  12.1 2.6 %collective-permute-start.3 = (bf16[128,256]{1,0:T(8,128)(2,1)}, bf16[128,256]{1,0:T(8,128)(2,1)}, u32[]{:S(2)}, u32[]{:S(2)}) collective-permute-start(bf16[128,256]{1,0:T(8,128)(2,1)} %get-tuple-element.28), channel_id=1, source_target_pairs={{0,8},{4,12},{8,0},{12,4},{1,9},{5,13},{9,1},{13,5},{2,10},{6,14},... | collective-permute-start | bytes 196616 | tf_op jit(solution)/shard_map/ppermute | solution.py:76
  14.7 1.3 %collective-permute-start.4 = (bf16[128,256]{1,0:T(8,128)(2,1)}, bf16[128,256]{1,0:T(8,128)(2,1)}, u32[]{:S(2)}, u32[]{:S(2)}) collective-permute-start(bf16[128,256]{1,0:T(8,128)(2,1)} %get-tuple-element.27), channel_id=1, source_target_pairs={{0,12},{4,0},{8,4},{12,8},{1,13},{5,1},{9,5},{13,9},{2,14},{6,2},{... | collective-permute-start | bytes 196616 | tf_op jit(solution)/shard_map/ppermute | solution.py:76
  16.3 0.7 %gather_fusion.1 = bf16[128,128]{1,0:T(8,128)(2,1)S(1)} fusion(bf16[1024,128]{1,0:T(8,128)(2,1)S(1)} %bitcast.88, s32[1024]{0:T(1024)S(1)} %get-tuple-element.45), kind=kCustom, calls=%fused_computation.1 | custom fusion | bytes 66048 | tf_op jit(solution)/shard_map/gather | solution.py:130
  17.0 0.8 %gather_fusion = f32[128,256]{1,0:T(8,128)S(1)} fusion(f32[1024,256]{1,0:T(8,128)S(1)} %fusion.11, s32[1024]{0:T(1024)S(1)} %get-tuple-element.45), kind=kCustom, calls=%fused_computation | custom fusion | bytes 262656 | tf_op jit(solution)/shard_map/gather | solution.py:151
  17.8 0.7 %gather_fusion.3 = bf16[128,128]{1,0:T(8,128)(2,1)S(1)} fusion(bf16[1024,128]{1,0:T(8,128)(2,1)S(1)} %bitcast.89, s32[1024]{0:T(1024)S(1)} %get-tuple-element.44), kind=kCustom, calls=%fused_computation.3 | custom fusion | bytes 66048 | tf_op jit(solution)/shard_map/gather | solution.py:131
  18.5 0.8 %gather_fusion.2 = f32[128,256]{1,0:T(8,128)S(1)} fusion(f32[1024,256]{1,0:T(8,128)S(1)} %fusion.11, s32[1024]{0:T(1024)S(1)} %get-tuple-element.44), kind=kCustom, calls=%fused_computation.2 | custom fusion | bytes 262656 | tf_op jit(solution)/shard_map/gather | solution.py:154
  19.6 1.0 %fusion.27 = bf16[128,256]{1,0:T(8,128)(2,1)S(1)} fusion(bf16[128,256]{1,0:T(8,128)(2,1)} %collective-permute-done.4, bf16[128,256]{1,0:T(8,128)(2,1)} %collective-permute-done.3, bf16[128,256]{1,0:T(8,128)(2,1)} %collective-permute-done.2, bf16[4,128,256]{2,1,0:T(8,128)(2,1)S(1)} %convolution_convert_fusion.1, s32[]{:T(128)S(6)} %select_n.143, ...), kind=kLoop, calls=%fused_computation.56 | loop fusion | flops 294912 | bytes 327812 | tf_op jit(solution)/shard_map/jit(_where)/select_n | solution.py:145
  20.6 0.4 convolution_convert_fusion.2
  21.4 1.4 %collective-permute-start.6 = (bf16[128,772]{1,0:T(8,128)(2,1)S(1)}, bf16[128,772]{1,0:T(8,128)(2,1)S(1)}, u32[]{:S(2)}, u32[]{:S(2)}) collective-permute-start(bf16[128,772]{1,0:T(8,128)(2,1)S(1)} %concatenate.26), channel_id=1, source_target_pairs={{0,2},{2,0},{1,3},{3,1},{4,6},{6,4},{5,7},{7,5},{8,10},{10,8},{9,1... | collective-permute-start | bytes 592904 | tf_op jit(solution)/shard_map/ppermute | solution.py:17
  22.8 1.3 %collective-permute-start.7 = (bf16[128,256]{1,0:T(8,128)(2,1)S(1)}, bf16[128,256]{1,0:T(8,128)(2,1)S(1)}, u32[]{:S(2)}, u32[]{:S(2)}) collective-permute-start(bf16[128,256]{1,0:T(8,128)(2,1)S(1)} %get-tuple-element.34), channel_id=1, source_target_pairs={{2,6},{4,0},{6,10},{8,4},{10,14},{12,8},{3,7},{5,1},{7,11},{9,5},{... | collective-permute-start | bytes 196616 | tf_op jit(solution)/shard_map/ppermute | solution.py:168
  24.1 0.7 %collective-permute-start.5 = (bf16[128,256]{1,0:T(8,128)(2,1)S(1)}, bf16[128,256]{1,0:T(8,128)(2,1)S(1)}, u32[]{:S(2)}, u32[]{:S(2)}) collective-permute-start(bf16[128,256]{1,0:T(8,128)(2,1)S(1)} %get-tuple-element.34), channel_id=1, source_target_pairs={{2,4},{4,2},{6,8},{8,6},{10,12},{12,10},{3,5},{5,3},{7,9},{9,7},{1... | collective-permute-start | bytes 196616 | tf_op jit(solution)/shard_map/ppermute | solution.py:167
  24.8 2.7 %collective-permute-done.6 = bf16[128,772]{1,0:T(8,128)(2,1)S(1)} collective-permute-done((bf16[128,772]{1,0:T(8,128)(2,1)S(1)}, bf16[128,772]{1,0:T(8,128)(2,1)S(1)}, u32[]{:S(2)}, u32[]{:S(2)}) %collective-permute-start.6) | collective-permute-done | bytes 197664 | tf_op jit(solution)/shard_map/ppermute | solution.py:17
  28.2 0.9 %collective-permute-done.7 = bf16[128,256]{1,0:T(8,128)(2,1)S(1)} collective-permute-done((bf16[128,256]{1,0:T(8,128)(2,1)S(1)}, bf16[128,256]{1,0:T(8,128)(2,1)S(1)}, u32[]{:S(2)}, u32[]{:S(2)}) %collective-permute-start.7) | collective-permute-done | bytes 65568 | tf_op jit(solution)/shard_map/ppermute | solution.py:168
  29.8 5.7 %collective-permute-start.10 = (bf16[128,256]{1,0:T(8,128)(2,1)S(1)}, bf16[128,256]{1,0:T(8,128)(2,1)S(1)}, u32[]{:S(2)}, u32[]{:S(2)}) collective-permute-start(bf16[128,256]{1,0:T(8,128)(2,1)S(1)} %get-tuple-element.24), channel_id=1, source_target_pairs={{0,12},{4,0},{8,4},{12,8},{1,13},{5,1},{9,5},{13,9},{2,14},{6,2},{... | collective-permute-start | bytes 196616 | tf_op jit(solution)/shard_map/ppermute | solution.py:76
  35.5 1.8 %collective-permute-start.9 = (bf16[128,256]{1,0:T(8,128)(2,1)S(1)}, bf16[128,256]{1,0:T(8,128)(2,1)S(1)}, u32[]{:S(2)}, u32[]{:S(2)}) collective-permute-start(bf16[128,256]{1,0:T(8,128)(2,1)S(1)} %get-tuple-element.25), channel_id=1, source_target_pairs={{0,8},{4,12},{8,0},{12,4},{1,9},{5,13},{9,1},{13,5},{2,10},{6,14},... | collective-permute-start | bytes 196616 | tf_op jit(solution)/shard_map/ppermute | solution.py:76
  37.4 4.1 %collective-permute-done.8 = bf16[128,256]{1,0:T(8,128)(2,1)S(1)} collective-permute-done((bf16[128,256]{1,0:T(8,128)(2,1)S(1)}, bf16[128,256]{1,0:T(8,128)(2,1)S(1)}, u32[]{:S(2)}, u32[]{:S(2)}) %collective-permute-start.8) | collective-permute-done | bytes 65568 | tf_op jit(solution)/shard_map/ppermute | solution.py:76
  41.6 1.1 %fusion.2 = bf16[1,1024,256]{2,1,0:T(8,128)(2,1)} fusion(f32[1024,256]{1,0:T(8,128)S(1)} %convolution_add_fusion, bf16[128,256]{1,0:T(8,128)(2,1)S(1)} %collective-permute-done.10, bf16[128,256]{1,0:T(8,128)(2,1)S(1)} %collective-permute-done.9, bf16[128,256]{1,0:T(8,128)(2,1)S(1)} %collective-permute-done.8, ...), kind=kOutput, calls=%fused_computation.8 | convolution fusion | flops 67928064 | bytes 2097668 | tf_op jit(solution)/shard_map/dot_general | solution.py:146
  (44 shorter events, 3.4 us)
Async XLA Ops:
  0.0 1.1 %copy-start = (bf16[1,1024,256]{2,1,0:T(8,128)(2,1)S(1)}, bf16[1,1024,256]{2,1,0:T(8,128)(2,1)}, u32[]{:S(2)}) copy-start(bf16[1,1024,256]{2,1,0:T(8,128)(2,1)} %param.7) | copy-start | bytes 1572868
  1.1 2.4 %copy-start.1 = (bf16[1,1024,128]{2,1,0:T(8,128)(2,1)S(1)}, bf16[1,1024,128]{2,1,0:T(8,128)(2,1)}, u32[]{:S(2)}) copy-start(bf16[1,1024,128]{2,1,0:T(8,128)(2,1)} %param.11) | copy-start | bytes 786436
  1.1 5.7 %copy-start.2 = (bf16[4,1,64,1,256]{4,2,3,1,0:T(8,128)(2,1)S(1)}, bf16[4,1,64,1,256]{4,2,3,1,0:T(8,128)(2,1)}, u32[]{:S(2)}) copy-start(bf16[4,1,64,1,256]{4,2,3,1,0:T(8,128)(2,1)} %param.13) | copy-start | bytes 393220
  3.4 4.4 %copy-start.4 = (s32[1,2,128]{2,1,0:T(2,128)S(1)}, s32[1,2,128]{2,1,0:T(2,128)}, u32[]{:S(2)}) copy-start(s32[1,2,128]{2,1,0:T(2,128)} %param.10) | copy-start | bytes 3076
  3.4 4.4 %copy-start.3 = (f32[1,2,128]{2,1,0:T(2,128)S(1)}, f32[1,2,128]{2,1,0:T(2,128)}, u32[]{:S(2)}) copy-start(f32[1,2,128]{2,1,0:T(2,128)} %param.9) | copy-start | bytes 3076
  3.7 5.2 %collective-permute-start.1 = (bf16[128,256]{1,0:T(8,128)(2,1)S(1)}, bf16[128,256]{1,0:T(8,128)(2,1)S(1)}, u32[]{:S(2)}, u32[]{:S(2)}) collective-permute-start(bf16[128,256]{1,0:T(8,128)(2,1)S(1)} %fusion.9), channel_id=1, source_target_pairs={{0,2},{2,0},{1,3},{3,1},{4,6},{6,4},{5,7},{7,5},{8,10},{10,8},{9,1... | collective-permute-start | bytes 196616 | tf_op jit(solution)/shard_map/ppermute | solution.py:17
  6.8 2.3 %collective-permute-start = (bf16[4,64,256]{2,1,0:T(8,128)(2,1)S(1)}, bf16[4,64,256]{2,1,0:T(8,128)(2,1)S(1)}, u32[]{:S(2)}, u32[]{:S(2)}) collective-permute-start(bf16[4,64,256]{2,1,0:T(8,128)(2,1)S(1)} %bitcast.91), channel_id=1, source_target_pairs={{0,1},{1,0},{2,3},{3,2},{4,5},{5,4},{6,7},{7,6},{8,9},{9,8},{10,11... | collective-permute-start | bytes 393224 | tf_op jit(solution)/shard_map/ppermute | solution.py:17
  10.0 9.3 %collective-permute-start.2 = (bf16[128,256]{1,0:T(8,128)(2,1)}, bf16[128,256]{1,0:T(8,128)(2,1)}, u32[]{:S(2)}, u32[]{:S(2)}) collective-permute-start(bf16[128,256]{1,0:T(8,128)(2,1)} %get-tuple-element.26), channel_id=1, source_target_pairs={{0,4},{4,8},{8,12},{12,0},{1,5},{5,9},{9,13},{13,1},{2,6},{6,10},{... | collective-permute-start | bytes 196616 | tf_op jit(solution)/shard_map/ppermute | solution.py:76
  12.1 7.4 %collective-permute-start.3 = (bf16[128,256]{1,0:T(8,128)(2,1)}, bf16[128,256]{1,0:T(8,128)(2,1)}, u32[]{:S(2)}, u32[]{:S(2)}) collective-permute-start(bf16[128,256]{1,0:T(8,128)(2,1)} %get-tuple-element.28), channel_id=1, source_target_pairs={{0,8},{4,12},{8,0},{12,4},{1,9},{5,13},{9,1},{13,5},{2,10},{6,14},... | collective-permute-start | bytes 196616 | tf_op jit(solution)/shard_map/ppermute | solution.py:76
  14.7 4.9 %collective-permute-start.4 = (bf16[128,256]{1,0:T(8,128)(2,1)}, bf16[128,256]{1,0:T(8,128)(2,1)}, u32[]{:S(2)}, u32[]{:S(2)}) collective-permute-start(bf16[128,256]{1,0:T(8,128)(2,1)} %get-tuple-element.27), channel_id=1, source_target_pairs={{0,12},{4,0},{8,4},{12,8},{1,13},{5,1},{9,5},{13,9},{2,14},{6,2},{... | collective-permute-start | bytes 196616 | tf_op jit(solution)/shard_map/ppermute | solution.py:76
  21.4 6.1 %collective-permute-start.6 = (bf16[128,772]{1,0:T(8,128)(2,1)S(1)}, bf16[128,772]{1,0:T(8,128)(2,1)S(1)}, u32[]{:S(2)}, u32[]{:S(2)}) collective-permute-start(bf16[128,772]{1,0:T(8,128)(2,1)S(1)} %concatenate.26), channel_id=1, source_target_pairs={{0,2},{2,0},{1,3},{3,1},{4,6},{6,4},{5,7},{7,5},{8,10},{10,8},{9,1... | collective-permute-start | bytes 592904 | tf_op jit(solution)/shard_map/ppermute | solution.py:17
  22.8 6.2 %collective-permute-start.7 = (bf16[128,256]{1,0:T(8,128)(2,1)S(1)}, bf16[128,256]{1,0:T(8,128)(2,1)S(1)}, u32[]{:S(2)}, u32[]{:S(2)}) collective-permute-start(bf16[128,256]{1,0:T(8,128)(2,1)S(1)} %get-tuple-element.34), channel_id=1, source_target_pairs={{2,6},{4,0},{6,10},{8,4},{10,14},{12,8},{3,7},{5,1},{7,11},{9,5},{... | collective-permute-start | bytes 196616 | tf_op jit(solution)/shard_map/ppermute | solution.py:168
  24.1 3.5 %collective-permute-start.5 = (bf16[128,256]{1,0:T(8,128)(2,1)S(1)}, bf16[128,256]{1,0:T(8,128)(2,1)S(1)}, u32[]{:S(2)}, u32[]{:S(2)}) collective-permute-start(bf16[128,256]{1,0:T(8,128)(2,1)S(1)} %get-tuple-element.34), channel_id=1, source_target_pairs={{2,4},{4,2},{6,8},{8,6},{10,12},{12,10},{3,5},{5,3},{7,9},{9,7},{1... | collective-permute-start | bytes 196616 | tf_op jit(solution)/shard_map/ppermute | solution.py:167
  29.8 7.7 %collective-permute-start.10 = (bf16[128,256]{1,0:T(8,128)(2,1)S(1)}, bf16[128,256]{1,0:T(8,128)(2,1)S(1)}, u32[]{:S(2)}, u32[]{:S(2)}) collective-permute-start(bf16[128,256]{1,0:T(8,128)(2,1)S(1)} %get-tuple-element.24), channel_id=1, source_target_pairs={{0,12},{4,0},{8,4},{12,8},{1,13},{5,1},{9,5},{13,9},{2,14},{6,2},{... | collective-permute-start | bytes 196616 | tf_op jit(solution)/shard_map/ppermute | solution.py:76
  35.5 6.1 %collective-permute-start.8 = (bf16[128,256]{1,0:T(8,128)(2,1)S(1)}, bf16[128,256]{1,0:T(8,128)(2,1)S(1)}, u32[]{:S(2)}, u32[]{:S(2)}) collective-permute-start(bf16[128,256]{1,0:T(8,128)(2,1)S(1)} %get-tuple-element.23), channel_id=1, source_target_pairs={{0,4},{4,8},{8,12},{12,0},{1,5},{5,9},{9,13},{13,1},{2,6},{6,10},{... | collective-permute-start | bytes 196616 | tf_op jit(solution)/shard_map/ppermute | solution.py:76
  35.5 6.1 %collective-permute-start.9 = (bf16[128,256]{1,0:T(8,128)(2,1)S(1)}, bf16[128,256]{1,0:T(8,128)(2,1)S(1)}, u32[]{:S(2)}, u32[]{:S(2)}) collective-permute-start(bf16[128,256]{1,0:T(8,128)(2,1)S(1)} %get-tuple-element.25), channel_id=1, source_target_pairs={{0,8},{4,12},{8,0},{12,4},{1,9},{5,13},{9,1},{13,5},{2,10},{6,14},... | collective-permute-start | bytes 196616 | tf_op jit(solution)/shard_map/ppermute | solution.py:76

commit v20 on v14

--- a/solution.py
+++ b/solution.py
@@ -128,8 +128,13 @@
         coarse, (solve_now, basis_now, faces_inverse_now) = coarse_of(
             inputs, (local_solve, basis, face_inverse)
         )
-        lower_basis = basis_now[lower_at]
-        upper_basis = basis_now[upper_at]
+        if pairwise:
+            near_at = jnp.where(first, upper_at, lower_at)
+            far_at = jnp.where(first, lower_at, upper_at)
+        else:
+            near_at, far_at = upper_at, lower_at
+        near_basis = basis_now[near_at]
+        far_basis = basis_now[far_at]
         if pairwise and cycle_index == 0:
             sends = jnp.where(
                 live,
@@ -147,16 +152,16 @@
         iterate = local_solve + correction
         if cycle_index == ROUNDS - 1:
             break
-        lower_trace = (
-            solve_now[lower_at] + jnp.dot(lower_basis, coarse, preferred_element_type=jnp.float32)
-        ).astype(jnp.bfloat16)
-        upper_trace = (
-            solve_now[upper_at] + jnp.dot(upper_basis, coarse, preferred_element_type=jnp.float32)
-        ).astype(jnp.bfloat16)
-        rows = lower_trace.shape[0]
+        near_trace = (
+            solve_now[near_at] + jnp.dot(near_basis, coarse, preferred_element_type=jnp.float32)
+        ).astype(jnp.bfloat16)
+        far_trace = (
+            solve_now[far_at] + jnp.dot(far_basis, coarse, preferred_element_type=jnp.float32)
+        ).astype(jnp.bfloat16)
+        upper_trace, lower_trace = near_trace, far_trace
         if pairwise:
-            toward_partner = jnp.where(first, upper_trace, lower_trace)
-            toward_diagonal = jnp.where(first, lower_trace, upper_trace)
+            toward_partner = near_trace
+            toward_diagonal = far_trace
             width = toward_partner.shape[1]
             got = swapped(
                 jnp.concatenate([toward_partner, coarse, mine, gains_pair], axis=1), "tile"
@@ -167,8 +172,8 @@
             from_lower = jnp.where(first, from_diagonal, from_partner).astype(jnp.float32)
             from_upper = jnp.where(first, from_partner, from_diagonal).astype(jnp.float32)
             faces = face_rows_of(gains, from_lower, from_upper)
-            partner_lower = jnp.where(first, upper_trace, crossing).astype(jnp.float32)
-            partner_upper = jnp.where(first, crossing, lower_trace).astype(jnp.float32)
+            partner_lower = jnp.where(first, toward_partner, crossing).astype(jnp.float32)
+            partner_upper = jnp.where(first, crossing, toward_partner).astype(jnp.float32)
             partner_coarse = got[:, width : 2 * width]
             theirs = got[:, 2 * width : 2 * width + mine.shape[1]]
             tail = got[:, 2 * width + mine.shape[1] :].astype(jnp.float32)

time: 42.5 us -> 43.2 us (1.016)
  waiting for transfers between devices: 10.5 us -> 13.3 us
  starting transfers between devices: 17.1 us -> 16 us
  matrix products: 6.62 us -> 5.96 us
    ppermute x6, waiting for transfers between devices: 4.4 us -> 7.31 us  [coarse_of(): lax.ppermute(piece, 'sub', [(i, (i + k) % sub_count) for i in range(sub_c...]
    ppermute x6, starting transfers between devices: 10.6 us -> 9.14 us  [coarse_of(): lax.ppermute(piece, 'sub', [(i, (i + k) % sub_count) for i in range(sub_c...]
    dot_general x2, matrix products: 0.93 us -> 0.3 us  [the longest x1 0.15 us: local(): jnp.dot(near_basis, coarse, preferred_element_type=jnp.float32)]
  transfers between devices with their start and end apart: 11 -> 11, of which waited for: 6 -> 8; matrix products, arithmetic and copies ran while one was open for 14% -> 20% of each run, Pallas kernels for 0% -> 0%
where the time goes in v20:
time: 43.2 us; the launch traced here: 42.9 us
  starting transfers between devices  16 us (37%)
  waiting for transfers between devices  13.3 us (31%)
  matrix products  5.96 us (14%)
  local copies, waits for them, and re-layouts  5.29 us (12%)
  other arithmetic  1.4 us (3%)
  between operations  0.98 us (2%)
    ppermute x6, starting transfers between devices, coarse_of(): lax.ppermute(piece, 'sub', [(i, (i + k) % sub_count) for i in range(sub_c...  9.14 us
    ppermute x6, waiting for transfers between devices, coarse_of(): lax.ppermute(piece, 'sub', [(i, (i + k) % sub_count) for i in range(sub_c...  7.31 us
    ppermute x3, starting transfers between devices, swapped(): return lax.ppermute(shard, axis, [(0, 1), (1, 0)])  4.93 us
    ppermute x3, waiting for transfers between devices, swapped(): return lax.ppermute(shard, axis, [(0, 1), (1, 0)])  3.65 us
    dot_general x1, matrix products, local(): base_solve = jnp.dot(inverse, source, preferred_element_type=jnp.float32)  2.34 us
    ppermute x1, waiting for transfers between devices, local(): crossing = lax.ppermute(toward_diagonal, DUCT, crossing_pairs)  2.32 us
    ppermute x1, starting transfers between devices, local(): crossing = lax.ppermute(toward_diagonal, DUCT, crossing_pairs)  1.29 us
    dot_general x1, matrix products, local(): correction = jnp.dot(basis, coarse, preferred_element_type=jnp.float32)  1.14 us
  transfers between devices with their start and end apart: 11, of which 8 were waited for; matrix products, arithmetic and copies ran while one was open for 20% of the time, Pallas kernels for 0%

profile of v20, /device:TPU:0, one launch (start us, length us, event | category | flops | bytes accessed | tf_op | source)
XLA Modules:
  0.0 42.9 jit_solution(10497123134328905381)
XLA Ops:
  1.1 2.3 %fusion.11 = f32[1024,256]{1,0:T(8,128)S(1)} fusion(bf16[1,1024,256]{2,1,0:T(8,128)(2,1)S(1)} %copy-done, bf16[1,1024,1024]{2,1,0:T(8,128)(2,1)} %param.8), kind=kOutput, calls=%fused_computation.27 | convolution fusion | flops 536870912 | bytes 3670016 | tf_op jit(solution)/shard_map/dot_general | solution.py:110
  3.8 2.9 %collective-permute-start.1 = (bf16[128,256]{1,0:T(8,128)(2,1)S(1)}, bf16[128,256]{1,0:T(8,128)(2,1)S(1)}, u32[]{:S(2)}, u32[]{:S(2)}) collective-permute-start(bf16[128,256]{1,0:T(8,128)(2,1)S(1)} %fusion.9), channel_id=1, source_target_pairs={{0,2},{2,0},{1,3},{3,1},{4,6},{6,4},{5,7},{7,5},{8,10},{10,8},{9,1... | collective-permute-start | bytes 196616 | tf_op jit(solution)/shard_map/ppermute | solution.py:17
  6.8 1.1 %fusion.55 = (bf16[1024,128]{1,0:T(8,128)(2,1)S(1)}, bf16[1024,128]{1,0:T(8,128)(2,1)S(1)}) fusion(bf16[1024,1024]{1,0:T(8,128)(2,1)} %bitcast.101), kind=kLoop, calls=%fused_computation.107 | loop fusion | bytes 1048576 | tf_op jit(solution)/shard_map/slice | solution.py:57
  8.2 0.9 %collective-permute-done.1 = bf16[128,256]{1,0:T(8,128)(2,1)S(1)} collective-permute-done((bf16[128,256]{1,0:T(8,128)(2,1)S(1)}, bf16[128,256]{1,0:T(8,128)(2,1)S(1)}, u32[]{:S(2)}, u32[]{:S(2)}) %collective-permute-start.1) | collective-permute-done | bytes 65568 | tf_op jit(solution)/shard_map/ppermute | solution.py:17
  9.5 0.7 %dynamic-slice_bitcast_fusion.5 = (bf16[128,256]{1,0:T(8,128)(2,1)}, bf16[128,256]{1,0:T(8,128)(2,1)}, bf16[128,256]{1,0:T(8,128)(2,1)}) fusion(bf16[4,128,256]{2,1,0:T(8,128)(2,1)S(1)} %convolution_convert_fusion.1, s32[]{:T(128)S(6)} %select_n.172, s32[]{:T(128)S(6)} %select_n.176, s32[]{:T(128)S(6)} %select_n.174), kind=kLoop, calls=%fused_computation.72 | loop fusion | bytes 393228 | tf_op jit(solution)/shard_map/jit(dynamic_index_in_dim)/squeeze | solution.py:75
  10.1 4.0 %collective-permute-start.4 = (bf16[128,256]{1,0:T(8,128)(2,1)}, bf16[128,256]{1,0:T(8,128)(2,1)}, u32[]{:S(2)}, u32[]{:S(2)}) collective-permute-start(bf16[128,256]{1,0:T(8,128)(2,1)} %get-tuple-element.27), channel_id=1, source_target_pairs={{0,12},{4,0},{8,4},{12,8},{1,13},{5,1},{9,5},{13,9},{2,14},{6,2},{... | collective-permute-start | bytes 196616 | tf_op jit(solution)/shard_map/ppermute | solution.py:76
  14.1 1.0 %collective-permute-start.2 = (bf16[128,256]{1,0:T(8,128)(2,1)}, bf16[128,256]{1,0:T(8,128)(2,1)}, u32[]{:S(2)}, u32[]{:S(2)}) collective-permute-start(bf16[128,256]{1,0:T(8,128)(2,1)} %get-tuple-element.26), channel_id=1, source_target_pairs={{0,4},{4,8},{8,12},{12,0},{1,5},{5,9},{9,13},{13,1},{2,6},{6,10},{... | collective-permute-start | bytes 196616 | tf_op jit(solution)/shard_map/ppermute | solution.py:76
  15.7 0.7 %gather_fusion.1 = bf16[128,128]{1,0:T(8,128)(2,1)S(1)} fusion(bf16[1024,128]{1,0:T(8,128)(2,1)S(1)} %bitcast.98, s32[1024]{0:T(1024)S(1)} %get-tuple-element.42), kind=kCustom, calls=%fused_computation.1 | custom fusion | bytes 66048 | tf_op jit(solution)/shard_map/gather | solution.py:137
  16.4 0.8 %gather_fusion = f32[128,256]{1,0:T(8,128)S(1)} fusion(f32[1024,256]{1,0:T(8,128)S(1)} %fusion.11, s32[1024]{0:T(1024)S(1)} %get-tuple-element.42), kind=kCustom, calls=%fused_computation | custom fusion | bytes 262656 | tf_op jit(solution)/shard_map/gather | solution.py:159
  17.1 0.8 %gather_fusion.2 = f32[128,256]{1,0:T(8,128)S(1)} fusion(f32[1024,256]{1,0:T(8,128)S(1)} %fusion.11, s32[1024]{0:T(1024)S(1)} %get-tuple-element.41), kind=kCustom, calls=%fused_computation.2 | custom fusion | bytes 262656 | tf_op jit(solution)/shard_map/gather | solution.py:156
  17.9 0.7 %gather_fusion.3 = bf16[128,128]{1,0:T(8,128)(2,1)S(1)} fusion(bf16[1024,128]{1,0:T(8,128)(2,1)S(1)} %bitcast.99, s32[1024]{0:T(1024)S(1)} %get-tuple-element.41), kind=kCustom, calls=%fused_computation.3 | custom fusion | bytes 66048 | tf_op jit(solution)/shard_map/gather | solution.py:136
  18.6 1.0 %collective-permute-done.3 = bf16[128,256]{1,0:T(8,128)(2,1)} collective-permute-done((bf16[128,256]{1,0:T(8,128)(2,1)}, bf16[128,256]{1,0:T(8,128)(2,1)}, u32[]{:S(2)}, u32[]{:S(2)}) %collective-permute-start.3) | collective-permute-done | bytes 65568 | tf_op jit(solution)/shard_map/ppermute | solution.py:76
  19.6 0.9 %collective-permute-done.2 = bf16[128,256]{1,0:T(8,128)(2,1)} collective-permute-done((bf16[128,256]{1,0:T(8,128)(2,1)}, bf16[128,256]{1,0:T(8,128)(2,1)}, u32[]{:S(2)}, u32[]{:S(2)}) %collective-permute-start.2) | collective-permute-done | bytes 65568 | tf_op jit(solution)/shard_map/ppermute | solution.py:76
  20.5 1.0 %fusion.28 = bf16[128,256]{1,0:T(8,128)(2,1)S(1)} fusion(bf16[128,256]{1,0:T(8,128)(2,1)} %collective-permute-done.4, bf16[128,256]{1,0:T(8,128)(2,1)} %collective-permute-done.3, bf16[128,256]{1,0:T(8,128)(2,1)} %collective-permute-done.2, bf16[4,128,256]{2,1,0:T(8,128)(2,1)S(1)} %convolution_convert_fusion.1, s32[]{:T(128)S(6)} %select_n.170, ...), kind=kLoop, calls=%fused_computation.56 | loop fusion | flops 294912 | bytes 327812 | tf_op jit(solution)/shard_map/jit(_where)/select_n | solution.py:150
  21.7 1.5 %collective-permute-start.6 = (bf16[128,900]{1,0:T(8,128)(2,1)S(1)}, bf16[128,900]{1,0:T(8,128)(2,1)S(1)}, u32[]{:S(2)}, u32[]{:S(2)}) collective-permute-start(bf16[128,900]{1,0:T(8,128)(2,1)S(1)} %concatenate.29), channel_id=1, source_target_pairs={{0,2},{2,0},{1,3},{3,1},{4,6},{6,4},{5,7},{7,5},{8,10},{10,8},{9,1... | collective-permute-start | bytes 691208 | tf_op jit(solution)/shard_map/ppermute | solution.py:17
  23.4 0.7 %collective-permute-start.5 = (bf16[128,256]{1,0:T(8,128)(2,1)S(1)}, bf16[128,256]{1,0:T(8,128)(2,1)S(1)}, u32[]{:S(2)}, u32[]{:S(2)}) collective-permute-start(bf16[128,256]{1,0:T(8,128)(2,1)S(1)} %fusion.5), channel_id=1, source_target_pairs={{2,4},{4,2},{6,8},{8,6},{10,12},{12,10},{3,5},{5,3},{7,9},{9,7},{1... | collective-permute-start | bytes 196616 | tf_op jit(solution)/shard_map/ppermute | solution.py:169
  24.1 1.3 %collective-permute-start.7 = (bf16[128,256]{1,0:T(8,128)(2,1)S(1)}, bf16[128,256]{1,0:T(8,128)(2,1)S(1)}, u32[]{:S(2)}, u32[]{:S(2)}) collective-permute-start(bf16[128,256]{1,0:T(8,128)(2,1)S(1)} %fusion.5), channel_id=1, source_target_pairs={{2,6},{4,0},{6,10},{8,4},{10,14},{12,8},{3,7},{5,1},{7,11},{9,5},{... | collective-permute-start | bytes 196616 | tf_op jit(solution)/shard_map/ppermute | solution.py:170
  25.4 2.7 %collective-permute-done.6 = bf16[128,900]{1,0:T(8,128)(2,1)S(1)} collective-permute-done((bf16[128,900]{1,0:T(8,128)(2,1)S(1)}, bf16[128,900]{1,0:T(8,128)(2,1)S(1)}, u32[]{:S(2)}, u32[]{:S(2)}) %collective-permute-start.6) | collective-permute-done | bytes 230432 | tf_op jit(solution)/shard_map/ppermute | solution.py:17
  29.2 2.3 %collective-permute-done.7 = bf16[128,256]{1,0:T(8,128)(2,1)S(1)} collective-permute-done((bf16[128,256]{1,0:T(8,128)(2,1)S(1)}, bf16[128,256]{1,0:T(8,128)(2,1)S(1)}, u32[]{:S(2)}, u32[]{:S(2)}) %collective-permute-start.7) | collective-permute-done | bytes 65568 | tf_op jit(solution)/shard_map/ppermute | solution.py:170
  32.2 1.7 %collective-permute-start.10 = (bf16[128,256]{1,0:T(8,128)(2,1)S(1)}, bf16[128,256]{1,0:T(8,128)(2,1)S(1)}, u32[]{:S(2)}, u32[]{:S(2)}) collective-permute-start(bf16[128,256]{1,0:T(8,128)(2,1)S(1)} %get-tuple-element.24), channel_id=1, source_target_pairs={{0,12},{4,0},{8,4},{12,8},{1,13},{5,1},{9,5},{13,9},{2,14},{6,2},{... | collective-permute-start | bytes 196616 | tf_op jit(solution)/shard_map/ppermute | solution.py:76
  33.9 1.9 %collective-permute-start.9 = (bf16[128,256]{1,0:T(8,128)(2,1)S(1)}, bf16[128,256]{1,0:T(8,128)(2,1)S(1)}, u32[]{:S(2)}, u32[]{:S(2)}) collective-permute-start(bf16[128,256]{1,0:T(8,128)(2,1)S(1)} %get-tuple-element.25), channel_id=1, source_target_pairs={{0,8},{4,12},{8,0},{12,4},{1,9},{5,13},{9,1},{13,5},{2,10},{6,14},... | collective-permute-start | bytes 196616 | tf_op jit(solution)/shard_map/ppermute | solution.py:76
  36.5 3.1 %collective-permute-done.9 = bf16[128,256]{1,0:T(8,128)(2,1)S(1)} collective-permute-done((bf16[128,256]{1,0:T(8,128)(2,1)S(1)}, bf16[128,256]{1,0:T(8,128)(2,1)S(1)}, u32[]{:S(2)}, u32[]{:S(2)}) %collective-permute-start.9) | collective-permute-done | bytes 65568 | tf_op jit(solution)/shard_map/ppermute | solution.py:76
  39.7 2.1 %collective-permute-done.8 = bf16[128,256]{1,0:T(8,128)(2,1)S(1)} collective-permute-done((bf16[128,256]{1,0:T(8,128)(2,1)S(1)}, bf16[128,256]{1,0:T(8,128)(2,1)S(1)}, u32[]{:S(2)}, u32[]{:S(2)}) %collective-permute-start.8) | collective-permute-done | bytes 65568 | tf_op jit(solution)/shard_map/ppermute | solution.py:76
  41.8 1.1 %fusion.2 = bf16[1,1024,256]{2,1,0:T(8,128)(2,1)} fusion(f32[1024,256]{1,0:T(8,128)S(1)} %convolution_add_fusion, bf16[128,256]{1,0:T(8,128)(2,1)S(1)} %collective-permute-done.10, bf16[128,256]{1,0:T(8,128)(2,1)S(1)} %collective-permute-done.9, bf16[128,256]{1,0:T(8,128)(2,1)S(1)} %collective-permute-done.8, ...), kind=kOutput, calls=%fused_computation.8 | convolution fusion | flops 67928064 | bytes 2097668 | tf_op jit(solution)/shard_map/dot_general | solution.py:151
  (46 shorter events, 4.8 us)
Async XLA Ops:
  0.0 1.1 %copy-start = (bf16[1,1024,256]{2,1,0:T(8,128)(2,1)S(1)}, bf16[1,1024,256]{2,1,0:T(8,128)(2,1)}, u32[]{:S(2)}) copy-start(bf16[1,1024,256]{2,1,0:T(8,128)(2,1)} %param.7) | copy-start | bytes 1572868
  0.0 9.2 %collective-permute-start = (bf16[4,64,256]{2,1,0:T(8,128)(2,1)}, bf16[4,64,256]{2,1,0:T(8,128)(2,1)S(1)}, u32[]{:S(2)}, u32[]{:S(2)}) collective-permute-start(bf16[4,64,256]{2,1,0:T(8,128)(2,1)} %bitcast.100), channel_id=1, source_target_pairs={{0,1},{1,0},{2,3},{3,2},{4,5},{5,4},{6,7},{7,6},{8,9},{9,8},{10,11... | collective-permute-start | bytes 393224 | tf_op jit(solution)/shard_map/ppermute | solution.py:17
  1.1 2.4 %copy-start.1 = (bf16[1,1024,128]{2,1,0:T(8,128)(2,1)S(1)}, bf16[1,1024,128]{2,1,0:T(8,128)(2,1)}, u32[]{:S(2)}) copy-start(bf16[1,1024,128]{2,1,0:T(8,128)(2,1)} %param.11) | copy-start | bytes 786436
  3.5 4.3 %copy-start.3 = (f32[1,2,128]{2,1,0:T(2,128)S(1)}, f32[1,2,128]{2,1,0:T(2,128)}, u32[]{:S(2)}) copy-start(f32[1,2,128]{2,1,0:T(2,128)} %param.9) | copy-start | bytes 3076
  3.5 4.7 %copy-start.4 = (s32[1,2,128]{2,1,0:T(2,128)S(1)}, s32[1,2,128]{2,1,0:T(2,128)}, u32[]{:S(2)}) copy-start(s32[1,2,128]{2,1,0:T(2,128)} %param.10) | copy-start | bytes 3076
  3.5 5.7 %copy-start.2 = (bf16[4,1,64,1,256]{4,2,3,1,0:T(8,128)(2,1)S(1)}, bf16[4,1,64,1,256]{4,2,3,1,0:T(8,128)(2,1)}, u32[]{:S(2)}) copy-start(bf16[4,1,64,1,256]{4,2,3,1,0:T(8,128)(2,1)} %param.13) | copy-start | bytes 393220
  3.8 5.3 %collective-permute-start.1 = (bf16[128,256]{1,0:T(8,128)(2,1)S(1)}, bf16[128,256]{1,0:T(8,128)(2,1)S(1)}, u32[]{:S(2)}, u32[]{:S(2)}) collective-permute-start(bf16[128,256]{1,0:T(8,128)(2,1)S(1)} %fusion.9), channel_id=1, source_target_pairs={{0,2},{2,0},{1,3},{3,1},{4,6},{6,4},{5,7},{7,5},{8,10},{10,8},{9,1... | collective-permute-start | bytes 196616 | tf_op jit(solution)/shard_map/ppermute | solution.py:17
  10.1 8.5 %collective-permute-start.4 = (bf16[128,256]{1,0:T(8,128)(2,1)}, bf16[128,256]{1,0:T(8,128)(2,1)}, u32[]{:S(2)}, u32[]{:S(2)}) collective-permute-start(bf16[128,256]{1,0:T(8,128)(2,1)} %get-tuple-element.27), channel_id=1, source_target_pairs={{0,12},{4,0},{8,4},{12,8},{1,13},{5,1},{9,5},{13,9},{2,14},{6,2},{... | collective-permute-start | bytes 196616 | tf_op jit(solution)/shard_map/ppermute | solution.py:76
  14.1 5.5 %collective-permute-start.3 = (bf16[128,256]{1,0:T(8,128)(2,1)}, bf16[128,256]{1,0:T(8,128)(2,1)}, u32[]{:S(2)}, u32[]{:S(2)}) collective-permute-start(bf16[128,256]{1,0:T(8,128)(2,1)} %get-tuple-element.28), channel_id=1, source_target_pairs={{0,8},{4,12},{8,0},{12,4},{1,9},{5,13},{9,1},{13,5},{2,10},{6,14},... | collective-permute-start | bytes 196616 | tf_op jit(solution)/shard_map/ppermute | solution.py:76
  14.1 6.4 %collective-permute-start.2 = (bf16[128,256]{1,0:T(8,128)(2,1)}, bf16[128,256]{1,0:T(8,128)(2,1)}, u32[]{:S(2)}, u32[]{:S(2)}) collective-permute-start(bf16[128,256]{1,0:T(8,128)(2,1)} %get-tuple-element.26), channel_id=1, source_target_pairs={{0,4},{4,8},{8,12},{12,0},{1,5},{5,9},{9,13},{13,1},{2,6},{6,10},{... | collective-permute-start | bytes 196616 | tf_op jit(solution)/shard_map/ppermute | solution.py:76
  21.7 6.4 %collective-permute-start.6 = (bf16[128,900]{1,0:T(8,128)(2,1)S(1)}, bf16[128,900]{1,0:T(8,128)(2,1)S(1)}, u32[]{:S(2)}, u32[]{:S(2)}) collective-permute-start(bf16[128,900]{1,0:T(8,128)(2,1)S(1)} %concatenate.29), channel_id=1, source_target_pairs={{0,2},{2,0},{1,3},{3,1},{4,6},{6,4},{5,7},{7,5},{8,10},{10,8},{9,1... | collective-permute-start | bytes 691208 | tf_op jit(solution)/shard_map/ppermute | solution.py:17
  23.4 2.0 %collective-permute-start.5 = (bf16[128,256]{1,0:T(8,128)(2,1)S(1)}, bf16[128,256]{1,0:T(8,128)(2,1)S(1)}, u32[]{:S(2)}, u32[]{:S(2)}) collective-permute-start(bf16[128,256]{1,0:T(8,128)(2,1)S(1)} %fusion.5), channel_id=1, source_target_pairs={{2,4},{4,2},{6,8},{8,6},{10,12},{12,10},{3,5},{5,3},{7,9},{9,7},{1... | collective-permute-start | bytes 196616 | tf_op jit(solution)/shard_map/ppermute | solution.py:169
  24.1 7.4 %collective-permute-start.7 = (bf16[128,256]{1,0:T(8,128)(2,1)S(1)}, bf16[128,256]{1,0:T(8,128)(2,1)S(1)}, u32[]{:S(2)}, u32[]{:S(2)}) collective-permute-start(bf16[128,256]{1,0:T(8,128)(2,1)S(1)} %fusion.5), channel_id=1, source_target_pairs={{2,6},{4,0},{6,10},{8,4},{10,14},{12,8},{3,7},{5,1},{7,11},{9,5},{... | collective-permute-start | bytes 196616 | tf_op jit(solution)/shard_map/ppermute | solution.py:170
  32.2 4.3 %collective-permute-start.10 = (bf16[128,256]{1,0:T(8,128)(2,1)S(1)}, bf16[128,256]{1,0:T(8,128)(2,1)S(1)}, u32[]{:S(2)}, u32[]{:S(2)}) collective-permute-start(bf16[128,256]{1,0:T(8,128)(2,1)S(1)} %get-tuple-element.24), channel_id=1, source_target_pairs={{0,12},{4,0},{8,4},{12,8},{1,13},{5,1},{9,5},{13,9},{2,14},{6,2},{... | collective-permute-start | bytes 196616 | tf_op jit(solution)/shard_map/ppermute | solution.py:76
  33.9 5.8 %collective-permute-start.9 = (bf16[128,256]{1,0:T(8,128)(2,1)S(1)}, bf16[128,256]{1,0:T(8,128)(2,1)S(1)}, u32[]{:S(2)}, u32[]{:S(2)}) collective-permute-start(bf16[128,256]{1,0:T(8,128)(2,1)S(1)} %get-tuple-element.25), channel_id=1, source_target_pairs={{0,8},{4,12},{8,0},{12,4},{1,9},{5,13},{9,1},{13,5},{2,10},{6,14},... | collective-permute-start | bytes 196616 | tf_op jit(solution)/shard_map/ppermute | solution.py:76
  35.7 6.1 %collective-permute-start.8 = (bf16[128,256]{1,0:T(8,128)(2,1)S(1)}, bf16[128,256]{1,0:T(8,128)(2,1)S(1)}, u32[]{:S(2)}, u32[]{:S(2)}) collective-permute-start(bf16[128,256]{1,0:T(8,128)(2,1)S(1)} %get-tuple-element.23), channel_id=1, source_target_pairs={{0,4},{4,8},{8,12},{12,0},{1,5},{5,9},{9,13},{13,1},{2,6},{6,10},{... | collective-permute-start | bytes 196616 | tf_op jit(solution)/shard_map/ppermute | solution.py:76

commit v21 on v14

--- a/solution.py
+++ b/solution.py
@@ -71,11 +71,16 @@
         total = lax.dynamic_index_in_dim(partial, sub_index, 0, keepdims=False).astype(
             jnp.float32
         )
+        paired = sub_count & (sub_count - 1) == 0
         for k in range(1, sub_count):
-            piece = lax.dynamic_index_in_dim(partial, (sub_index + k) % sub_count, 0, keepdims=False)
-            total = total + lax.ppermute(
-                piece, "sub", [(i, (i + k) % sub_count) for i in range(sub_count)]
-            ).astype(jnp.float32)
+            if paired:
+                target = sub_index ^ k
+                pairs = [(i, i ^ k) for i in range(sub_count)]
+            else:
+                target = (sub_index + k) % sub_count
+                pairs = [(i, (i + k) % sub_count) for i in range(sub_count)]
+            piece = lax.dynamic_index_in_dim(partial, target, 0, keepdims=False)
+            total = total + lax.ppermute(piece, "sub", pairs).astype(jnp.float32)
         return total.astype(jnp.bfloat16), riders
 
     pairwise = lax.axis_size("tile") == 2 and ROUNDS == 2

time: 42.5 us -> 43.5 us (1.024)
  waiting for transfers between devices: 10.5 us -> 12.7 us
  starting transfers between devices: 17.1 us -> 15.9 us
    ppermute x6, waiting for transfers between devices: 4.4 us -> 6.66 us  [coarse_of(): total = total + lax.ppermute(piece, 'sub', pairs).astype(jnp.float32)]
    ppermute x6, starting transfers between devices: 10.6 us -> 9.43 us  [coarse_of(): total = total + lax.ppermute(piece, 'sub', pairs).astype(jnp.float32)]
  transfers between devices with their start and end apart: 11 -> 11, of which waited for: 6 -> 8; matrix products, arithmetic and copies ran while one was open for 14% -> 14% of each run, Pallas kernels for 0% -> 0%
where the time goes in v21:
time: 43.5 us; the launch traced here: 43.3 us
  starting transfers between devices  15.9 us (37%)
  waiting for transfers between devices  12.7 us (29%)
  matrix products  6.62 us (15%)
  local copies, waits for them, and re-layouts  5.61 us (13%)
  other arithmetic  1.4 us (3%)
  between operations  1.01 us (2%)
    ppermute x6, starting transfers between devices, coarse_of(): total = total + lax.ppermute(piece, 'sub', pairs).astype(jnp.float32)  9.43 us
    ppermute x6, waiting for transfers between devices, coarse_of(): total = total + lax.ppermute(piece, 'sub', pairs).astype(jnp.float32)  6.66 us
    ppermute x3, starting transfers between devices, swapped(): return lax.ppermute(shard, axis, [(0, 1), (1, 0)])  4.55 us
    ppermute x3, waiting for transfers between devices, swapped(): return lax.ppermute(shard, axis, [(0, 1), (1, 0)])  3.66 us
    ppermute x1, waiting for transfers between devices, local(): crossing = lax.ppermute(toward_diagonal, DUCT, crossing_pairs)  2.38 us
    dot_general x1, matrix products, local(): base_solve = jnp.dot(inverse, source, preferred_element_type=jnp.float32)  2.35 us
    ppermute x1, starting transfers between devices, local(): crossing = lax.ppermute(toward_diagonal, DUCT, crossing_pairs)  1.29 us
    dot_general x1, matrix products, local(): correction = jnp.dot(basis, coarse, preferred_element_type=jnp.float32)  1.15 us
  transfers between devices with their start and end apart: 11, of which 8 were waited for; matrix products, arithmetic and copies ran while one was open for 14% of the time, Pallas kernels for 0%

profile of v21, /device:TPU:0, one launch (start us, length us, event | category | flops | bytes accessed | tf_op | source)
XLA Modules:
  0.0 43.3 jit_solution(12645790956321851689)
XLA Ops:
  1.1 2.4 %fusion.11 = f32[1024,256]{1,0:T(8,128)S(1)} fusion(bf16[1,1024,256]{2,1,0:T(8,128)(2,1)S(1)} %copy-done, bf16[1,1024,1024]{2,1,0:T(8,128)(2,1)} %param.8), kind=kOutput, calls=%fused_computation.27 | convolution fusion | flops 536870912 | bytes 3670016 | tf_op jit(solution)/shard_map/dot_general | solution.py:115
  3.7 3.0 %collective-permute-start.1 = (bf16[128,256]{1,0:T(8,128)(2,1)S(1)}, bf16[128,256]{1,0:T(8,128)(2,1)S(1)}, u32[]{:S(2)}, u32[]{:S(2)}) collective-permute-start(bf16[128,256]{1,0:T(8,128)(2,1)S(1)} %fusion.9), channel_id=1, source_target_pairs={{0,2},{2,0},{1,3},{3,1},{4,6},{6,4},{5,7},{7,5},{8,10},{10,8},{9,1... | collective-permute-start | bytes 196616 | tf_op jit(solution)/shard_map/ppermute | solution.py:17
  6.8 1.1 %fusion.53 = (bf16[1024,128]{1,0:T(8,128)(2,1)S(1)}, bf16[1024,128]{1,0:T(8,128)(2,1)S(1)}) fusion(bf16[1024,1024]{1,0:T(8,128)(2,1)} %bitcast.93), kind=kLoop, calls=%fused_computation.105 | loop fusion | bytes 1048576 | tf_op jit(solution)/shard_map/slice | solution.py:57
  8.2 0.7 %collective-permute-done.1 = bf16[128,256]{1,0:T(8,128)(2,1)S(1)} collective-permute-done((bf16[128,256]{1,0:T(8,128)(2,1)S(1)}, bf16[128,256]{1,0:T(8,128)(2,1)S(1)}, u32[]{:S(2)}, u32[]{:S(2)}) %collective-permute-start.1) | collective-permute-done | bytes 65568 | tf_op jit(solution)/shard_map/ppermute | solution.py:17
  10.0 2.1 %collective-permute-start.2 = (bf16[128,256]{1,0:T(8,128)(2,1)}, bf16[128,256]{1,0:T(8,128)(2,1)}, u32[]{:S(2)}, u32[]{:S(2)}) collective-permute-start(bf16[128,256]{1,0:T(8,128)(2,1)} %get-tuple-element.26), channel_id=1, source_target_pairs={{0,4},{4,0},{8,12},{12,8},{1,5},{5,1},{9,13},{13,9},{2,6},{6,2},{1... | collective-permute-start | bytes 196616 | tf_op jit(solution)/shard_map/ppermute | solution.py:83
  12.1 2.6 %collective-permute-start.3 = (bf16[128,256]{1,0:T(8,128)(2,1)}, bf16[128,256]{1,0:T(8,128)(2,1)}, u32[]{:S(2)}, u32[]{:S(2)}) collective-permute-start(bf16[128,256]{1,0:T(8,128)(2,1)} %get-tuple-element.28), channel_id=1, source_target_pairs={{0,8},{4,12},{8,0},{12,4},{1,9},{5,13},{9,1},{13,5},{2,10},{6,14},... | collective-permute-start | bytes 196616 | tf_op jit(solution)/shard_map/ppermute | solution.py:83
  15.2 0.7 %gather_fusion.1 = bf16[128,128]{1,0:T(8,128)(2,1)S(1)} fusion(bf16[1024,128]{1,0:T(8,128)(2,1)S(1)} %bitcast.90, s32[1024]{0:T(1024)S(1)} %get-tuple-element.45), kind=kCustom, calls=%fused_computation.1 | custom fusion | bytes 66048 | tf_op jit(solution)/shard_map/gather | solution.py:136
  15.9 0.8 %gather_fusion = f32[128,256]{1,0:T(8,128)S(1)} fusion(f32[1024,256]{1,0:T(8,128)S(1)} %fusion.11, s32[1024]{0:T(1024)S(1)} %get-tuple-element.45), kind=kCustom, calls=%fused_computation | custom fusion | bytes 262656 | tf_op jit(solution)/shard_map/gather | solution.py:156
  16.7 0.7 %gather_fusion.3 = bf16[128,128]{1,0:T(8,128)(2,1)S(1)} fusion(bf16[1024,128]{1,0:T(8,128)(2,1)S(1)} %bitcast.91, s32[1024]{0:T(1024)S(1)} %get-tuple-element.44), kind=kCustom, calls=%fused_computation.3 | custom fusion | bytes 66048 | tf_op jit(solution)/shard_map/gather | solution.py:137
  17.4 0.8 %gather_fusion.2 = f32[128,256]{1,0:T(8,128)S(1)} fusion(f32[1024,256]{1,0:T(8,128)S(1)} %fusion.11, s32[1024]{0:T(1024)S(1)} %get-tuple-element.44), kind=kCustom, calls=%fused_computation.2 | custom fusion | bytes 262656 | tf_op jit(solution)/shard_map/gather | solution.py:159
  18.2 0.9 %collective-permute-done.3 = bf16[128,256]{1,0:T(8,128)(2,1)} collective-permute-done((bf16[128,256]{1,0:T(8,128)(2,1)}, bf16[128,256]{1,0:T(8,128)(2,1)}, u32[]{:S(2)}, u32[]{:S(2)}) %collective-permute-start.3) | collective-permute-done | bytes 65568 | tf_op jit(solution)/shard_map/ppermute | solution.py:83
  19.1 2.0 %collective-permute-done.4 = bf16[128,256]{1,0:T(8,128)(2,1)} collective-permute-done((bf16[128,256]{1,0:T(8,128)(2,1)}, bf16[128,256]{1,0:T(8,128)(2,1)}, u32[]{:S(2)}, u32[]{:S(2)}) %collective-permute-start.4) | collective-permute-done | bytes 65568 | tf_op jit(solution)/shard_map/ppermute | solution.py:83
  21.1 1.0 %fusion.28 = bf16[128,256]{1,0:T(8,128)(2,1)S(1)} fusion(bf16[128,256]{1,0:T(8,128)(2,1)} %collective-permute-done.4, bf16[128,256]{1,0:T(8,128)(2,1)} %collective-permute-done.3, bf16[128,256]{1,0:T(8,128)(2,1)} %collective-permute-done.2, bf16[4,128,256]{2,1,0:T(8,128)(2,1)S(1)} %convolution_convert_fusion.1, s32[]{:T(128)S(6)} %select_n.122, ...), kind=kLoop, calls=%fused_computation.56 | loop fusion | flops 294912 | bytes 327812 | tf_op jit(solution)/shard_map/jit(_where)/select_n | solution.py:150
  22.2 0.8 %broadcast_select_fusion.4 = (bf16[128,256]{1,0:T(8,128)(2,1)S(1)}, bf16[128,256]{1,0:T(8,128)(2,1)}, bf16[128,256]{1,0:T(8,128)(2,1)S(1)}) fusion(bf16[128,256]{1,0:T(8,128)(2,1)S(1)} %fusion.5, pred[]{:T(512)S(6)} %eq.6, f32[128,256]{1,0:T(8,128)S(1)} %gather_fusion.2, bf16[128,128]{1,0:T(8,128)(2,1)S(1)} %gather_fusion.3, bf16[128,256]{1,0:T(8,128)(2,1)S(1)} %fusion.28), kind=kOutput, calls=%fused_computation.76 | convolution fusion | flops 8519680 | bytes 491521 | tf_op jit(solution)/shard_map/dot_general | solution.py:159
  23.1 1.5 %collective-permute-start.6 = (bf16[128,900]{1,0:T(8,128)(2,1)S(1)}, bf16[128,900]{1,0:T(8,128)(2,1)S(1)}, u32[]{:S(2)}, u32[]{:S(2)}) collective-permute-start(bf16[128,900]{1,0:T(8,128)(2,1)S(1)} %concatenate.29), channel_id=1, source_target_pairs={{0,2},{2,0},{1,3},{3,1},{4,6},{6,4},{5,7},{7,5},{8,10},{10,8},{9,1... | collective-permute-start | bytes 691208 | tf_op jit(solution)/shard_map/ppermute | solution.py:17
  25.3 1.3 %collective-permute-start.7 = (bf16[128,256]{1,0:T(8,128)(2,1)}, bf16[128,256]{1,0:T(8,128)(2,1)S(1)}, u32[]{:S(2)}, u32[]{:S(2)}) collective-permute-start(bf16[128,256]{1,0:T(8,128)(2,1)} %get-tuple-element.34), channel_id=1, source_target_pairs={{2,6},{4,0},{6,10},{8,4},{10,14},{12,8},{3,7},{5,1},{7,11},{9,5},{... | collective-permute-start | bytes 196616 | tf_op jit(solution)/shard_map/ppermute | solution.py:170
  26.6 2.9 %collective-permute-done.6 = bf16[128,900]{1,0:T(8,128)(2,1)S(1)} collective-permute-done((bf16[128,900]{1,0:T(8,128)(2,1)S(1)}, bf16[128,900]{1,0:T(8,128)(2,1)S(1)}, u32[]{:S(2)}, u32[]{:S(2)}) %collective-permute-start.6) | collective-permute-done | bytes 230432 | tf_op jit(solution)/shard_map/ppermute | solution.py:17
  30.5 2.4 %collective-permute-done.7 = bf16[128,256]{1,0:T(8,128)(2,1)S(1)} collective-permute-done((bf16[128,256]{1,0:T(8,128)(2,1)}, bf16[128,256]{1,0:T(8,128)(2,1)S(1)}, u32[]{:S(2)}, u32[]{:S(2)}) %collective-permute-start.7) | collective-permute-done | bytes 65568 | tf_op jit(solution)/shard_map/ppermute | solution.py:170
  33.6 1.0 %collective-permute-start.10 = (bf16[128,256]{1,0:T(8,128)(2,1)S(1)}, bf16[128,256]{1,0:T(8,128)(2,1)S(1)}, u32[]{:S(2)}, u32[]{:S(2)}) collective-permute-start(bf16[128,256]{1,0:T(8,128)(2,1)S(1)} %get-tuple-element.24), channel_id=1, source_target_pairs={{0,12},{4,8},{8,4},{12,0},{1,13},{5,9},{9,5},{13,1},{2,14},{6,10},... | collective-permute-start | bytes 196616 | tf_op jit(solution)/shard_map/ppermute | solution.py:83
  34.7 2.3 %collective-permute-start.8 = (bf16[128,256]{1,0:T(8,128)(2,1)S(1)}, bf16[128,256]{1,0:T(8,128)(2,1)S(1)}, u32[]{:S(2)}, u32[]{:S(2)}) collective-permute-start(bf16[128,256]{1,0:T(8,128)(2,1)S(1)} %get-tuple-element.23), channel_id=1, source_target_pairs={{0,4},{4,0},{8,12},{12,8},{1,5},{5,1},{9,13},{13,9},{2,6},{6,2},{1... | collective-permute-start | bytes 196616 | tf_op jit(solution)/shard_map/ppermute | solution.py:83
  37.0 1.4 %collective-permute-start.9 = (bf16[128,256]{1,0:T(8,128)(2,1)S(1)}, bf16[128,256]{1,0:T(8,128)(2,1)S(1)}, u32[]{:S(2)}, u32[]{:S(2)}) collective-permute-start(bf16[128,256]{1,0:T(8,128)(2,1)S(1)} %get-tuple-element.25), channel_id=1, source_target_pairs={{0,8},{4,12},{8,0},{12,4},{1,9},{5,13},{9,1},{13,5},{2,10},{6,14},... | collective-permute-start | bytes 196616 | tf_op jit(solution)/shard_map/ppermute | solution.py:83
  38.3 1.5 %collective-permute-done.10 = bf16[128,256]{1,0:T(8,128)(2,1)S(1)} collective-permute-done((bf16[128,256]{1,0:T(8,128)(2,1)S(1)}, bf16[128,256]{1,0:T(8,128)(2,1)S(1)}, u32[]{:S(2)}, u32[]{:S(2)}) %collective-permute-start.10) | collective-permute-done | bytes 65568 | tf_op jit(solution)/shard_map/ppermute | solution.py:83
  39.9 2.2 %collective-permute-done.9 = bf16[128,256]{1,0:T(8,128)(2,1)S(1)} collective-permute-done((bf16[128,256]{1,0:T(8,128)(2,1)S(1)}, bf16[128,256]{1,0:T(8,128)(2,1)S(1)}, u32[]{:S(2)}, u32[]{:S(2)}) %collective-permute-start.9) | collective-permute-done | bytes 65568 | tf_op jit(solution)/shard_map/ppermute | solution.py:83
  42.1 1.1 %fusion.2 = bf16[1,1024,256]{2,1,0:T(8,128)(2,1)} fusion(f32[1024,256]{1,0:T(8,128)S(1)} %convolution_add_fusion, bf16[128,256]{1,0:T(8,128)(2,1)S(1)} %collective-permute-done.10, bf16[128,256]{1,0:T(8,128)(2,1)S(1)} %collective-permute-done.9, bf16[128,256]{1,0:T(8,128)(2,1)S(1)} %collective-permute-done.8, ...), kind=kOutput, calls=%fused_computation.8 | convolution fusion | flops 67928064 | bytes 2097668 | tf_op jit(solution)/shard_map/dot_general | solution.py:151
  (46 shorter events, 5.1 us)
Async XLA Ops:
  0.0 1.1 %copy-start = (bf16[1,1024,256]{2,1,0:T(8,128)(2,1)S(1)}, bf16[1,1024,256]{2,1,0:T(8,128)(2,1)}, u32[]{:S(2)}) copy-start(bf16[1,1024,256]{2,1,0:T(8,128)(2,1)} %param.7) | copy-start | bytes 1572868
  1.1 2.4 %copy-start.1 = (bf16[1,1024,128]{2,1,0:T(8,128)(2,1)S(1)}, bf16[1,1024,128]{2,1,0:T(8,128)(2,1)}, u32[]{:S(2)}) copy-start(bf16[1,1024,128]{2,1,0:T(8,128)(2,1)} %param.11) | copy-start | bytes 786436
  1.1 5.7 %copy-start.2 = (bf16[4,1,64,1,256]{4,2,3,1,0:T(8,128)(2,1)S(1)}, bf16[4,1,64,1,256]{4,2,3,1,0:T(8,128)(2,1)}, u32[]{:S(2)}) copy-start(bf16[4,1,64,1,256]{4,2,3,1,0:T(8,128)(2,1)} %param.13) | copy-start | bytes 393220
  3.4 4.4 %copy-start.4 = (s32[1,2,128]{2,1,0:T(2,128)S(1)}, s32[1,2,128]{2,1,0:T(2,128)}, u32[]{:S(2)}) copy-start(s32[1,2,128]{2,1,0:T(2,128)} %param.10) | copy-start | bytes 3076
  3.4 4.4 %copy-start.3 = (f32[1,2,128]{2,1,0:T(2,128)S(1)}, f32[1,2,128]{2,1,0:T(2,128)}, u32[]{:S(2)}) copy-start(f32[1,2,128]{2,1,0:T(2,128)} %param.9) | copy-start | bytes 3076
  3.7 5.2 %collective-permute-start.1 = (bf16[128,256]{1,0:T(8,128)(2,1)S(1)}, bf16[128,256]{1,0:T(8,128)(2,1)S(1)}, u32[]{:S(2)}, u32[]{:S(2)}) collective-permute-start(bf16[128,256]{1,0:T(8,128)(2,1)S(1)} %fusion.9), channel_id=1, source_target_pairs={{0,2},{2,0},{1,3},{3,1},{4,6},{6,4},{5,7},{7,5},{8,10},{10,8},{9,1... | collective-permute-start | bytes 196616 | tf_op jit(solution)/shard_map/ppermute | solution.py:17
  6.8 2.3 %collective-permute-start = (bf16[4,64,256]{2,1,0:T(8,128)(2,1)S(1)}, bf16[4,64,256]{2,1,0:T(8,128)(2,1)S(1)}, u32[]{:S(2)}, u32[]{:S(2)}) collective-permute-start(bf16[4,64,256]{2,1,0:T(8,128)(2,1)S(1)} %bitcast.92), channel_id=1, source_target_pairs={{0,1},{1,0},{2,3},{3,2},{4,5},{5,4},{6,7},{7,6},{8,9},{9,8},{10,11... | collective-permute-start | bytes 393224 | tf_op jit(solution)/shard_map/ppermute | solution.py:17
  10.0 8.2 %collective-permute-start.2 = (bf16[128,256]{1,0:T(8,128)(2,1)}, bf16[128,256]{1,0:T(8,128)(2,1)}, u32[]{:S(2)}, u32[]{:S(2)}) collective-permute-start(bf16[128,256]{1,0:T(8,128)(2,1)} %get-tuple-element.26), channel_id=1, source_target_pairs={{0,4},{4,0},{8,12},{12,8},{1,5},{5,1},{9,13},{13,9},{2,6},{6,2},{1... | collective-permute-start | bytes 196616 | tf_op jit(solution)/shard_map/ppermute | solution.py:83
  12.1 7.0 %collective-permute-start.3 = (bf16[128,256]{1,0:T(8,128)(2,1)}, bf16[128,256]{1,0:T(8,128)(2,1)}, u32[]{:S(2)}, u32[]{:S(2)}) collective-permute-start(bf16[128,256]{1,0:T(8,128)(2,1)} %get-tuple-element.28), channel_id=1, source_target_pairs={{0,8},{4,12},{8,0},{12,4},{1,9},{5,13},{9,1},{13,5},{2,10},{6,14},... | collective-permute-start | bytes 196616 | tf_op jit(solution)/shard_map/ppermute | solution.py:83
  14.7 6.4 %collective-permute-start.4 = (bf16[128,256]{1,0:T(8,128)(2,1)}, bf16[128,256]{1,0:T(8,128)(2,1)}, u32[]{:S(2)}, u32[]{:S(2)}) collective-permute-start(bf16[128,256]{1,0:T(8,128)(2,1)} %get-tuple-element.27), channel_id=1, source_target_pairs={{0,12},{4,8},{8,4},{12,0},{1,13},{5,9},{9,5},{13,1},{2,14},{6,10},... | collective-permute-start | bytes 196616 | tf_op jit(solution)/shard_map/ppermute | solution.py:83
  23.1 6.4 %collective-permute-start.6 = (bf16[128,900]{1,0:T(8,128)(2,1)S(1)}, bf16[128,900]{1,0:T(8,128)(2,1)S(1)}, u32[]{:S(2)}, u32[]{:S(2)}) collective-permute-start(bf16[128,900]{1,0:T(8,128)(2,1)S(1)} %concatenate.29), channel_id=1, source_target_pairs={{0,2},{2,0},{1,3},{3,1},{4,6},{6,4},{5,7},{7,5},{8,10},{10,8},{9,1... | collective-permute-start | bytes 691208 | tf_op jit(solution)/shard_map/ppermute | solution.py:17
  24.6 2.0 %collective-permute-start.5 = (bf16[128,256]{1,0:T(8,128)(2,1)}, bf16[128,256]{1,0:T(8,128)(2,1)S(1)}, u32[]{:S(2)}, u32[]{:S(2)}) collective-permute-start(bf16[128,256]{1,0:T(8,128)(2,1)} %get-tuple-element.34), channel_id=1, source_target_pairs={{2,4},{4,2},{6,8},{8,6},{10,12},{12,10},{3,5},{5,3},{7,9},{9,7},{1... | collective-permute-start | bytes 196616 | tf_op jit(solution)/shard_map/ppermute | solution.py:169
  25.3 7.6 %collective-permute-start.7 = (bf16[128,256]{1,0:T(8,128)(2,1)}, bf16[128,256]{1,0:T(8,128)(2,1)S(1)}, u32[]{:S(2)}, u32[]{:S(2)}) collective-permute-start(bf16[128,256]{1,0:T(8,128)(2,1)} %get-tuple-element.34), channel_id=1, source_target_pairs={{2,6},{4,0},{6,10},{8,4},{10,14},{12,8},{3,7},{5,1},{7,11},{9,5},{... | collective-permute-start | bytes 196616 | tf_op jit(solution)/shard_map/ppermute | solution.py:170
  33.6 6.2 %collective-permute-start.10 = (bf16[128,256]{1,0:T(8,128)(2,1)S(1)}, bf16[128,256]{1,0:T(8,128)(2,1)S(1)}, u32[]{:S(2)}, u32[]{:S(2)}) collective-permute-start(bf16[128,256]{1,0:T(8,128)(2,1)S(1)} %get-tuple-element.24), channel_id=1, source_target_pairs={{0,12},{4,8},{8,4},{12,0},{1,13},{5,9},{9,5},{13,1},{2,14},{6,10},... | collective-permute-start | bytes 196616 | tf_op jit(solution)/shard_map/ppermute | solution.py:83
  34.7 5.3 %collective-permute-start.8 = (bf16[128,256]{1,0:T(8,128)(2,1)S(1)}, bf16[128,256]{1,0:T(8,128)(2,1)S(1)}, u32[]{:S(2)}, u32[]{:S(2)}) collective-permute-start(bf16[128,256]{1,0:T(8,128)(2,1)S(1)} %get-tuple-element.23), channel_id=1, source_target_pairs={{0,4},{4,0},{8,12},{12,8},{1,5},{5,1},{9,13},{13,9},{2,6},{6,2},{1... | collective-permute-start | bytes 196616 | tf_op jit(solution)/shard_map/ppermute | solution.py:83
  37.0 5.2 %collective-permute-start.9 = (bf16[128,256]{1,0:T(8,128)(2,1)S(1)}, bf16[128,256]{1,0:T(8,128)(2,1)S(1)}, u32[]{:S(2)}, u32[]{:S(2)}) collective-permute-start(bf16[128,256]{1,0:T(8,128)(2,1)S(1)} %get-tuple-element.25), channel_id=1, source_target_pairs={{0,8},{4,12},{8,0},{12,4},{1,9},{5,13},{9,1},{13,5},{2,10},{6,14},... | collective-permute-start | bytes 196616 | tf_op jit(solution)/shard_map/ppermute | solution.py:83

commit v22 on v14

--- a/solution.py
+++ b/solution.py
@@ -144,7 +144,7 @@
             mine = jnp.concatenate([sends, keeps], axis=1).astype(jnp.bfloat16)
         coarse = jnp.where(live, coarse, jnp.zeros((), coarse.dtype))
         correction = jnp.dot(basis, coarse, preferred_element_type=jnp.float32)
-        iterate = local_solve + correction
+        iterate = solve_now + correction
         if cycle_index == ROUNDS - 1:
             break
         lower_trace = (

time: 42.5 us -> 42.5 us (level)
    dot_general x1, matrix products: 0.14 us -> 0.79 us  [local(): jnp.dot(lower_basis, coarse, preferred_element_type=jnp.float32)]
    dot_general x1, matrix products: 0.79 us -> 0.14 us  [local(): jnp.dot(upper_basis, coarse, preferred_element_type=jnp.float32)]
where the time goes in v22:
time: 42.5 us; the launch traced here: 42.2 us
  starting transfers between devices  17.1 us (40%)
  waiting for transfers between devices  10.5 us (25%)
  matrix products  6.63 us (16%)
  local copies, waits for them, and re-layouts  5.61 us (13%)
  other arithmetic  1.41 us (3%)
  between operations  1.02 us (2%)
    ppermute x6, starting transfers between devices, coarse_of(): lax.ppermute(piece, 'sub', [(i, (i + k) % sub_count) for i in range(sub_c...  10.6 us
    ppermute x3, starting transfers between devices, swapped(): return lax.ppermute(shard, axis, [(0, 1), (1, 0)])  4.51 us
    ppermute x6, waiting for transfers between devices, coarse_of(): lax.ppermute(piece, 'sub', [(i, (i + k) % sub_count) for i in range(sub_c...  4.39 us
    ppermute x3, waiting for transfers between devices, swapped(): return lax.ppermute(shard, axis, [(0, 1), (1, 0)])  3.89 us
    dot_general x1, matrix products, local(): base_solve = jnp.dot(inverse, source, preferred_element_type=jnp.float32)  2.35 us
    ppermute x1, waiting for transfers between devices, local(): crossing = lax.ppermute(toward_diagonal, DUCT, crossing_pairs)  2.19 us
    ppermute x1, starting transfers between devices, local(): crossing = lax.ppermute(toward_diagonal, DUCT, crossing_pairs)  1.29 us
    dot_general x1, matrix products, local(): correction = jnp.dot(basis, coarse, preferred_element_type=jnp.float32)  1.15 us
  transfers between devices with their start and end apart: 11, of which 6 were waited for; matrix products, arithmetic and copies ran while one was open for 14% of the time, Pallas kernels for 0%

profile of v22, /device:TPU:0, one launch (start us, length us, event | category | flops | bytes accessed | tf_op | source)
XLA Modules:
  0.0 42.2 jit_solution(10334142990081759436)
XLA Ops:
  1.1 2.4 %fusion.11 = f32[1024,256]{1,0:T(8,128)S(1)} fusion(bf16[1,1024,256]{2,1,0:T(8,128)(2,1)S(1)} %copy-done, bf16[1,1024,1024]{2,1,0:T(8,128)(2,1)} %param.8), kind=kOutput, calls=%fused_computation.27 | convolution fusion | flops 536870912 | bytes 3670016 | tf_op jit(solution)/shard_map/dot_general | solution.py:110
  3.7 3.0 %collective-permute-start.1 = (bf16[128,256]{1,0:T(8,128)(2,1)S(1)}, bf16[128,256]{1,0:T(8,128)(2,1)S(1)}, u32[]{:S(2)}, u32[]{:S(2)}) collective-permute-start(bf16[128,256]{1,0:T(8,128)(2,1)S(1)} %fusion.9), channel_id=1, source_target_pairs={{0,2},{2,0},{1,3},{3,1},{4,6},{6,4},{5,7},{7,5},{8,10},{10,8},{9,1... | collective-permute-start | bytes 196616 | tf_op jit(solution)/shard_map/ppermute | solution.py:17
  6.8 1.1 %fusion.53 = (bf16[1024,128]{1,0:T(8,128)(2,1)S(1)}, bf16[1024,128]{1,0:T(8,128)(2,1)S(1)}) fusion(bf16[1024,1024]{1,0:T(8,128)(2,1)} %bitcast.93), kind=kLoop, calls=%fused_computation.105 | loop fusion | bytes 1048576 | tf_op jit(solution)/shard_map/slice | solution.py:57
  8.2 0.8 %collective-permute-done.1 = bf16[128,256]{1,0:T(8,128)(2,1)S(1)} collective-permute-done((bf16[128,256]{1,0:T(8,128)(2,1)S(1)}, bf16[128,256]{1,0:T(8,128)(2,1)S(1)}, u32[]{:S(2)}, u32[]{:S(2)}) %collective-permute-start.1) | collective-permute-done | bytes 65568 | tf_op jit(solution)/shard_map/ppermute | solution.py:17
  9.3 0.7 %dynamic-slice_bitcast_fusion.5 = (bf16[128,256]{1,0:T(8,128)(2,1)}, bf16[128,256]{1,0:T(8,128)(2,1)}, bf16[128,256]{1,0:T(8,128)(2,1)}) fusion(bf16[4,128,256]{2,1,0:T(8,128)(2,1)S(1)} %convolution_convert_fusion.1, s32[]{:T(128)S(6)} %select_n.146, s32[]{:T(128)S(6)} %select_n.150, s32[]{:T(128)S(6)} %select_n.148), kind=kLoop, calls=%fused_computation.72 | loop fusion | bytes 393228 | tf_op jit(solution)/shard_map/jit(dynamic_index_in_dim)/squeeze | solution.py:75
  10.0 2.1 %collective-permute-start.2 = (bf16[128,256]{1,0:T(8,128)(2,1)}, bf16[128,256]{1,0:T(8,128)(2,1)}, u32[]{:S(2)}, u32[]{:S(2)}) collective-permute-start(bf16[128,256]{1,0:T(8,128)(2,1)} %get-tuple-element.28), channel_id=1, source_target_pairs={{0,4},{4,8},{8,12},{12,0},{1,5},{5,9},{9,13},{13,1},{2,6},{6,10},{... | collective-permute-start | bytes 196616 | tf_op jit(solution)/shard_map/ppermute | solution.py:76
  12.1 2.6 %collective-permute-start.3 = (bf16[128,256]{1,0:T(8,128)(2,1)}, bf16[128,256]{1,0:T(8,128)(2,1)}, u32[]{:S(2)}, u32[]{:S(2)}) collective-permute-start(bf16[128,256]{1,0:T(8,128)(2,1)} %get-tuple-element.30), channel_id=1, source_target_pairs={{0,8},{4,12},{8,0},{12,4},{1,9},{5,13},{9,1},{13,5},{2,10},{6,14},... | collective-permute-start | bytes 196616 | tf_op jit(solution)/shard_map/ppermute | solution.py:76
  14.7 1.3 %collective-permute-start.4 = (bf16[128,256]{1,0:T(8,128)(2,1)}, bf16[128,256]{1,0:T(8,128)(2,1)}, u32[]{:S(2)}, u32[]{:S(2)}) collective-permute-start(bf16[128,256]{1,0:T(8,128)(2,1)} %get-tuple-element.29), channel_id=1, source_target_pairs={{0,12},{4,0},{8,4},{12,8},{1,13},{5,1},{9,5},{13,9},{2,14},{6,2},{... | collective-permute-start | bytes 196616 | tf_op jit(solution)/shard_map/ppermute | solution.py:76
  16.6 0.7 %gather_fusion.3 = bf16[128,128]{1,0:T(8,128)(2,1)S(1)} fusion(bf16[1024,128]{1,0:T(8,128)(2,1)S(1)} %bitcast.90, s32[1024]{0:T(1024)S(1)} %get-tuple-element.46), kind=kCustom, calls=%fused_computation.3 | custom fusion | bytes 66048 | tf_op jit(solution)/shard_map/gather | solution.py:132
  17.3 0.8 %gather_fusion.2 = f32[128,256]{1,0:T(8,128)S(1)} fusion(f32[1024,256]{1,0:T(8,128)S(1)} %fusion.11, s32[1024]{0:T(1024)S(1)} %get-tuple-element.46), kind=kCustom, calls=%fused_computation.2 | custom fusion | bytes 262656 | tf_op jit(solution)/shard_map/gather | solution.py:154
  18.0 0.7 %gather_fusion.1 = bf16[128,128]{1,0:T(8,128)(2,1)S(1)} fusion(bf16[1024,128]{1,0:T(8,128)(2,1)S(1)} %bitcast.91, s32[1024]{0:T(1024)S(1)} %get-tuple-element.47), kind=kCustom, calls=%fused_computation.1 | custom fusion | bytes 66048 | tf_op jit(solution)/shard_map/gather | solution.py:131
  18.8 0.8 %gather_fusion = f32[128,256]{1,0:T(8,128)S(1)} fusion(f32[1024,256]{1,0:T(8,128)S(1)} %fusion.11, s32[1024]{0:T(1024)S(1)} %get-tuple-element.47), kind=kCustom, calls=%fused_computation | custom fusion | bytes 262656 | tf_op jit(solution)/shard_map/gather | solution.py:151
  19.6 1.0 %fusion.28 = bf16[128,256]{1,0:T(8,128)(2,1)S(1)} fusion(bf16[128,256]{1,0:T(8,128)(2,1)} %collective-permute-done.4, bf16[128,256]{1,0:T(8,128)(2,1)} %collective-permute-done.3, bf16[128,256]{1,0:T(8,128)(2,1)} %collective-permute-done.2, bf16[4,128,256]{2,1,0:T(8,128)(2,1)S(1)} %convolution_convert_fusion.1, s32[]{:T(128)S(6)} %select_n.144, ...), kind=kLoop, calls=%fused_computation.56 | loop fusion | flops 294912 | bytes 327812 | tf_op jit(solution)/shard_map/jit(_where)/select_n | solution.py:145
  20.7 0.8 %broadcast_select_fusion.5 = (bf16[128,256]{1,0:T(8,128)(2,1)}, bf16[128,256]{1,0:T(8,128)(2,1)S(1)}, bf16[128,256]{1,0:T(8,128)(2,1)S(1)}) fusion(bf16[128,256]{1,0:T(8,128)(2,1)S(1)} %fusion.6, pred[]{:T(512)S(6)} %eq.14, f32[128,256]{1,0:T(8,128)S(1)} %gather_fusion, bf16[128,128]{1,0:T(8,128)(2,1)S(1)} %gather_fusion.1, bf16[128,256]{1,0:T(8,128)(2,1)S(1)} %fusion.28), kind=kOutput, calls=%fused_computation.77 | convolution fusion | flops 8519680 | bytes 491521 | tf_op jit(solution)/shard_map/dot_general | solution.py:151
  21.6 1.5 %collective-permute-start.6 = (bf16[128,900]{1,0:T(8,128)(2,1)S(1)}, bf16[128,900]{1,0:T(8,128)(2,1)S(1)}, u32[]{:S(2)}, u32[]{:S(2)}) collective-permute-start(bf16[128,900]{1,0:T(8,128)(2,1)S(1)} %concatenate.29), channel_id=1, source_target_pairs={{0,2},{2,0},{1,3},{3,1},{4,6},{6,4},{5,7},{7,5},{8,10},{10,8},{9,1... | collective-permute-start | bytes 691208 | tf_op jit(solution)/shard_map/ppermute | solution.py:17
  23.1 0.7 %collective-permute-start.5 = (bf16[128,256]{1,0:T(8,128)(2,1)}, bf16[128,256]{1,0:T(8,128)(2,1)S(1)}, u32[]{:S(2)}, u32[]{:S(2)}) collective-permute-start(bf16[128,256]{1,0:T(8,128)(2,1)} %get-tuple-element.35), channel_id=1, source_target_pairs={{2,4},{4,2},{6,8},{8,6},{10,12},{12,10},{3,5},{5,3},{7,9},{9,7},{1... | collective-permute-start | bytes 196616 | tf_op jit(solution)/shard_map/ppermute | solution.py:164
  23.8 1.3 %collective-permute-start.7 = (bf16[128,256]{1,0:T(8,128)(2,1)}, bf16[128,256]{1,0:T(8,128)(2,1)S(1)}, u32[]{:S(2)}, u32[]{:S(2)}) collective-permute-start(bf16[128,256]{1,0:T(8,128)(2,1)} %get-tuple-element.35), channel_id=1, source_target_pairs={{2,6},{4,0},{6,10},{8,4},{10,14},{12,8},{3,7},{5,1},{7,11},{9,5},{... | collective-permute-start | bytes 196616 | tf_op jit(solution)/shard_map/ppermute | solution.py:165
  25.1 3.1 %collective-permute-done.6 = bf16[128,900]{1,0:T(8,128)(2,1)S(1)} collective-permute-done((bf16[128,900]{1,0:T(8,128)(2,1)S(1)}, bf16[128,900]{1,0:T(8,128)(2,1)S(1)}, u32[]{:S(2)}, u32[]{:S(2)}) %collective-permute-start.6) | collective-permute-done | bytes 230432 | tf_op jit(solution)/shard_map/ppermute | solution.py:17
  29.3 2.2 %collective-permute-done.7 = bf16[128,256]{1,0:T(8,128)(2,1)S(1)} collective-permute-done((bf16[128,256]{1,0:T(8,128)(2,1)}, bf16[128,256]{1,0:T(8,128)(2,1)S(1)}, u32[]{:S(2)}, u32[]{:S(2)}) %collective-permute-start.7) | collective-permute-done | bytes 65568 | tf_op jit(solution)/shard_map/ppermute | solution.py:165
  32.2 2.9 %collective-permute-start.10 = (bf16[128,256]{1,0:T(8,128)(2,1)S(1)}, bf16[128,256]{1,0:T(8,128)(2,1)S(1)}, u32[]{:S(2)}, u32[]{:S(2)}) collective-permute-start(bf16[128,256]{1,0:T(8,128)(2,1)S(1)} %get-tuple-element.26), channel_id=1, source_target_pairs={{0,12},{4,0},{8,4},{12,8},{1,13},{5,1},{9,5},{13,9},{2,14},{6,2},{... | collective-permute-start | bytes 196616 | tf_op jit(solution)/shard_map/ppermute | solution.py:76
  35.0 1.7 %collective-permute-start.9 = (bf16[128,256]{1,0:T(8,128)(2,1)S(1)}, bf16[128,256]{1,0:T(8,128)(2,1)S(1)}, u32[]{:S(2)}, u32[]{:S(2)}) collective-permute-start(bf16[128,256]{1,0:T(8,128)(2,1)S(1)} %get-tuple-element.27), channel_id=1, source_target_pairs={{0,8},{4,12},{8,0},{12,4},{1,9},{5,13},{9,1},{13,5},{2,10},{6,14},... | collective-permute-start | bytes 196616 | tf_op jit(solution)/shard_map/ppermute | solution.py:76
  36.8 0.4 collective-permute-done.10
  37.1 4.0 %collective-permute-done.8 = bf16[128,256]{1,0:T(8,128)(2,1)S(1)} collective-permute-done((bf16[128,256]{1,0:T(8,128)(2,1)S(1)}, bf16[128,256]{1,0:T(8,128)(2,1)S(1)}, u32[]{:S(2)}, u32[]{:S(2)}) %collective-permute-start.8) | collective-permute-done | bytes 65568 | tf_op jit(solution)/shard_map/ppermute | solution.py:76
  41.1 1.2 %fusion.2 = bf16[1,1024,256]{2,1,0:T(8,128)(2,1)} fusion(f32[1024,256]{1,0:T(8,128)S(1)} %convolution_add_fusion, bf16[128,256]{1,0:T(8,128)(2,1)S(1)} %collective-permute-done.10, bf16[128,256]{1,0:T(8,128)(2,1)S(1)} %collective-permute-done.9, bf16[128,256]{1,0:T(8,128)(2,1)S(1)} %collective-permute-done.8, ...), kind=kOutput, calls=%fused_computation.8 | convolution fusion | flops 67928064 | bytes 2097668 | tf_op jit(solution)/shard_map/dot_general | solution.py:146
  (46 shorter events, 3.8 us)
Async XLA Ops:
  0.0 1.1 %copy-start = (bf16[1,1024,256]{2,1,0:T(8,128)(2,1)S(1)}, bf16[1,1024,256]{2,1,0:T(8,128)(2,1)}, u32[]{:S(2)}) copy-start(bf16[1,1024,256]{2,1,0:T(8,128)(2,1)} %param.7) | copy-start | bytes 1572868
  1.1 2.4 %copy-start.1 = (bf16[1,1024,128]{2,1,0:T(8,128)(2,1)S(1)}, bf16[1,1024,128]{2,1,0:T(8,128)(2,1)}, u32[]{:S(2)}) copy-start(bf16[1,1024,128]{2,1,0:T(8,128)(2,1)} %param.11) | copy-start | bytes 786436
  1.1 5.7 %copy-start.2 = (bf16[4,1,64,1,256]{4,2,3,1,0:T(8,128)(2,1)S(1)}, bf16[4,1,64,1,256]{4,2,3,1,0:T(8,128)(2,1)}, u32[]{:S(2)}) copy-start(bf16[4,1,64,1,256]{4,2,3,1,0:T(8,128)(2,1)} %param.13) | copy-start | bytes 393220
  3.4 4.4 %copy-start.4 = (s32[1,2,128]{2,1,0:T(2,128)S(1)}, s32[1,2,128]{2,1,0:T(2,128)}, u32[]{:S(2)}) copy-start(s32[1,2,128]{2,1,0:T(2,128)} %param.10) | copy-start | bytes 3076
  3.4 4.4 %copy-start.3 = (f32[1,2,128]{2,1,0:T(2,128)S(1)}, f32[1,2,128]{2,1,0:T(2,128)}, u32[]{:S(2)}) copy-start(f32[1,2,128]{2,1,0:T(2,128)} %param.9) | copy-start | bytes 3076
  3.7 5.2 %collective-permute-start.1 = (bf16[128,256]{1,0:T(8,128)(2,1)S(1)}, bf16[128,256]{1,0:T(8,128)(2,1)S(1)}, u32[]{:S(2)}, u32[]{:S(2)}) collective-permute-start(bf16[128,256]{1,0:T(8,128)(2,1)S(1)} %fusion.9), channel_id=1, source_target_pairs={{0,2},{2,0},{1,3},{3,1},{4,6},{6,4},{5,7},{7,5},{8,10},{10,8},{9,1... | collective-permute-start | bytes 196616 | tf_op jit(solution)/shard_map/ppermute | solution.py:17
  6.8 2.3 %collective-permute-start = (bf16[4,64,256]{2,1,0:T(8,128)(2,1)S(1)}, bf16[4,64,256]{2,1,0:T(8,128)(2,1)S(1)}, u32[]{:S(2)}, u32[]{:S(2)}) collective-permute-start(bf16[4,64,256]{2,1,0:T(8,128)(2,1)S(1)} %bitcast.92), channel_id=1, source_target_pairs={{0,1},{1,0},{2,3},{3,2},{4,5},{5,4},{6,7},{7,6},{8,9},{9,8},{10,11... | collective-permute-start | bytes 393224 | tf_op jit(solution)/shard_map/ppermute | solution.py:17
  10.0 9.5 %collective-permute-start.2 = (bf16[128,256]{1,0:T(8,128)(2,1)}, bf16[128,256]{1,0:T(8,128)(2,1)}, u32[]{:S(2)}, u32[]{:S(2)}) collective-permute-start(bf16[128,256]{1,0:T(8,128)(2,1)} %get-tuple-element.28), channel_id=1, source_target_pairs={{0,4},{4,8},{8,12},{12,0},{1,5},{5,9},{9,13},{13,1},{2,6},{6,10},{... | collective-permute-start | bytes 196616 | tf_op jit(solution)/shard_map/ppermute | solution.py:76
  12.1 7.5 %collective-permute-start.3 = (bf16[128,256]{1,0:T(8,128)(2,1)}, bf16[128,256]{1,0:T(8,128)(2,1)}, u32[]{:S(2)}, u32[]{:S(2)}) collective-permute-start(bf16[128,256]{1,0:T(8,128)(2,1)} %get-tuple-element.30), channel_id=1, source_target_pairs={{0,8},{4,12},{8,0},{12,4},{1,9},{5,13},{9,1},{13,5},{2,10},{6,14},... | collective-permute-start | bytes 196616 | tf_op jit(solution)/shard_map/ppermute | solution.py:76
  14.7 4.9 %collective-permute-start.4 = (bf16[128,256]{1,0:T(8,128)(2,1)}, bf16[128,256]{1,0:T(8,128)(2,1)}, u32[]{:S(2)}, u32[]{:S(2)}) collective-permute-start(bf16[128,256]{1,0:T(8,128)(2,1)} %get-tuple-element.29), channel_id=1, source_target_pairs={{0,12},{4,0},{8,4},{12,8},{1,13},{5,1},{9,5},{13,9},{2,14},{6,2},{... | collective-permute-start | bytes 196616 | tf_op jit(solution)/shard_map/ppermute | solution.py:76
  21.6 6.6 %collective-permute-start.6 = (bf16[128,900]{1,0:T(8,128)(2,1)S(1)}, bf16[128,900]{1,0:T(8,128)(2,1)S(1)}, u32[]{:S(2)}, u32[]{:S(2)}) collective-permute-start(bf16[128,900]{1,0:T(8,128)(2,1)S(1)} %concatenate.29), channel_id=1, source_target_pairs={{0,2},{2,0},{1,3},{3,1},{4,6},{6,4},{5,7},{7,5},{8,10},{10,8},{9,1... | collective-permute-start | bytes 691208 | tf_op jit(solution)/shard_map/ppermute | solution.py:17
  23.1 2.0 %collective-permute-start.5 = (bf16[128,256]{1,0:T(8,128)(2,1)}, bf16[128,256]{1,0:T(8,128)(2,1)S(1)}, u32[]{:S(2)}, u32[]{:S(2)}) collective-permute-start(bf16[128,256]{1,0:T(8,128)(2,1)} %get-tuple-element.35), channel_id=1, source_target_pairs={{2,4},{4,2},{6,8},{8,6},{10,12},{12,10},{3,5},{5,3},{7,9},{9,7},{1... | collective-permute-start | bytes 196616 | tf_op jit(solution)/shard_map/ppermute | solution.py:164
  23.8 7.6 %collective-permute-start.7 = (bf16[128,256]{1,0:T(8,128)(2,1)}, bf16[128,256]{1,0:T(8,128)(2,1)S(1)}, u32[]{:S(2)}, u32[]{:S(2)}) collective-permute-start(bf16[128,256]{1,0:T(8,128)(2,1)} %get-tuple-element.35), channel_id=1, source_target_pairs={{2,6},{4,0},{6,10},{8,4},{10,14},{12,8},{3,7},{5,1},{7,11},{9,5},{... | collective-permute-start | bytes 196616 | tf_op jit(solution)/shard_map/ppermute | solution.py:165
  32.2 5.0 %collective-permute-start.10 = (bf16[128,256]{1,0:T(8,128)(2,1)S(1)}, bf16[128,256]{1,0:T(8,128)(2,1)S(1)}, u32[]{:S(2)}, u32[]{:S(2)}) collective-permute-start(bf16[128,256]{1,0:T(8,128)(2,1)S(1)} %get-tuple-element.26), channel_id=1, source_target_pairs={{0,12},{4,0},{8,4},{12,8},{1,13},{5,1},{9,5},{13,9},{2,14},{6,2},{... | collective-permute-start | bytes 196616 | tf_op jit(solution)/shard_map/ppermute | solution.py:76
  35.0 6.1 %collective-permute-start.8 = (bf16[128,256]{1,0:T(8,128)(2,1)S(1)}, bf16[128,256]{1,0:T(8,128)(2,1)S(1)}, u32[]{:S(2)}, u32[]{:S(2)}) collective-permute-start(bf16[128,256]{1,0:T(8,128)(2,1)S(1)} %get-tuple-element.25), channel_id=1, source_target_pairs={{0,4},{4,8},{8,12},{12,0},{1,5},{5,9},{9,13},{13,1},{2,6},{6,10},{... | collective-permute-start | bytes 196616 | tf_op jit(solution)/shard_map/ppermute | solution.py:76
  35.0 6.1 %collective-permute-start.9 = (bf16[128,256]{1,0:T(8,128)(2,1)S(1)}, bf16[128,256]{1,0:T(8,128)(2,1)S(1)}, u32[]{:S(2)}, u32[]{:S(2)}) collective-permute-start(bf16[128,256]{1,0:T(8,128)(2,1)S(1)} %get-tuple-element.27), channel_id=1, source_target_pairs={{0,8},{4,12},{8,0},{12,4},{1,9},{5,13},{9,1},{13,5},{2,10},{6,14},... | collective-permute-start | bytes 196616 | tf_op jit(solution)/shard_map/ppermute | solution.py:76

commit v23 on v14

--- a/solution.py
+++ b/solution.py
@@ -110,6 +110,9 @@
     base_solve = jnp.dot(inverse, source, preferred_element_type=jnp.float32)
     local_solve = base_solve
     projected = coarse_input(local_solve.astype(jnp.bfloat16))
+    row_basis, _ = lax.optimization_barrier((basis, projected))
+    lower_basis = row_basis[lower_at]
+    upper_basis = row_basis[upper_at]
     if pairwise:
         width = projected.shape[1]
         got = swapped(projected, "tile")
@@ -128,8 +131,6 @@
         coarse, (solve_now, basis_now, faces_inverse_now) = coarse_of(
             inputs, (local_solve, basis, face_inverse)
         )
-        lower_basis = basis_now[lower_at]
-        upper_basis = basis_now[upper_at]
         if pairwise and cycle_index == 0:
             sends = jnp.where(
                 live,

time: 42.5 us -> 43.8 us (1.031)
  waiting for transfers between devices: 10.5 us -> 12.2 us
    ppermute x6, waiting for transfers between devices: 4.4 us -> 6.41 us  [coarse_of(): lax.ppermute(piece, 'sub', [(i, (i + k) % sub_count) for i in range(sub_c...]
    ppermute x1, waiting for transfers between devices: 2.19 us -> 0.75 us  [local(): crossing = lax.ppermute(toward_diagonal, DUCT, crossing_pairs)]
    ppermute x3, waiting for transfers between devices: 3.89 us -> 5.07 us  [swapped(): return lax.ppermute(shard, axis, [(0, 1), (1, 0)])]
    ppermute x3, starting transfers between devices: 4.51 us -> 4.03 us  [swapped(): return lax.ppermute(shard, axis, [(0, 1), (1, 0)])]
  transfers between devices with their start and end apart: 11 -> 11, of which waited for: 6 -> 6; matrix products, arithmetic and copies ran while one was open for 14% -> 13% of each run, Pallas kernels for 0% -> 0%
where the time goes in v23:
time: 43.8 us; the launch traced here: 43.6 us
  starting transfers between devices  16.7 us (38%)
  waiting for transfers between devices  12.2 us (28%)
  matrix products  6.61 us (15%)
  local copies, waits for them, and re-layouts  5.6 us (13%)
  other arithmetic  1.37 us (3%)
  between operations  1.02 us (2%)
    ppermute x6, starting transfers between devices, coarse_of(): lax.ppermute(piece, 'sub', [(i, (i + k) % sub_count) for i in range(sub_c...  10.8 us
    ppermute x6, waiting for transfers between devices, coarse_of(): lax.ppermute(piece, 'sub', [(i, (i + k) % sub_count) for i in range(sub_c...  6.41 us
    ppermute x3, waiting for transfers between devices, swapped(): return lax.ppermute(shard, axis, [(0, 1), (1, 0)])  5.07 us
    ppermute x3, starting transfers between devices, swapped(): return lax.ppermute(shard, axis, [(0, 1), (1, 0)])  4.03 us
    dot_general x1, matrix products, local(): base_solve = jnp.dot(inverse, source, preferred_element_type=jnp.float32)  2.35 us
    ppermute x1, starting transfers between devices, local(): crossing = lax.ppermute(toward_diagonal, DUCT, crossing_pairs)  1.29 us
    dot_general x1, matrix products, local(): correction = jnp.dot(basis, coarse, preferred_element_type=jnp.float32)  1.14 us
    slice x1, local copies, waits for them, and re-layouts, local(): inverse[:, :face_rows]  1.07 us
  transfers between devices with their start and end apart: 11, of which 6 were waited for; matrix products, arithmetic and copies ran while one was open for 13% of the time, Pallas kernels for 0%

profile of v23, /device:TPU:0, one launch (start us, length us, event | category | flops | bytes accessed | tf_op | source)
XLA Modules:
  0.0 43.6 jit_solution(6726401281382115436)
XLA Ops:
  0.7 0.3 copy-done
  1.1 2.4 %fusion.11 = f32[1024,256]{1,0:T(8,128)S(1)} fusion(bf16[1,1024,256]{2,1,0:T(8,128)(2,1)S(1)} %copy-done, bf16[1,1024,1024]{2,1,0:T(8,128)(2,1)} %param.8), kind=kOutput, calls=%fused_computation.27 | convolution fusion | flops 536870912 | bytes 3670016 | tf_op jit(solution)/shard_map/dot_general | solution.py:110
  3.7 3.0 %collective-permute-start.1 = (bf16[128,256]{1,0:T(8,128)(2,1)S(1)}, bf16[128,256]{1,0:T(8,128)(2,1)S(1)}, u32[]{:S(2)}, u32[]{:S(2)}) collective-permute-start(bf16[128,256]{1,0:T(8,128)(2,1)S(1)} %fusion.9), channel_id=1, source_target_pairs={{0,2},{2,0},{1,3},{3,1},{4,6},{6,4},{5,7},{7,5},{8,10},{10,8},{9,1... | collective-permute-start | bytes 196616 | tf_op jit(solution)/shard_map/ppermute | solution.py:17
  6.8 1.1 %fusion.53 = (bf16[1024,128]{1,0:T(8,128)(2,1)S(1)}, bf16[1024,128]{1,0:T(8,128)(2,1)S(1)}) fusion(bf16[1024,1024]{1,0:T(8,128)(2,1)} %bitcast.93), kind=kLoop, calls=%fused_computation.105 | loop fusion | bytes 1048576 | tf_op jit(solution)/shard_map/slice | solution.py:57
  7.9 0.7 %gather_fusion.1 = bf16[128,128]{1,0:T(8,128)(2,1)S(1)} fusion(bf16[1024,128]{1,0:T(8,128)(2,1)S(1)} %bitcast.88, s32[1024]{0:T(1024)S(1)} %get-tuple-element.47), kind=kCustom, calls=%fused_computation.1 | custom fusion | bytes 66048 | tf_op jit(solution)/shard_map/gather | solution.py:114
  8.6 0.7 %gather_fusion.3 = bf16[128,128]{1,0:T(8,128)(2,1)S(1)} fusion(bf16[1024,128]{1,0:T(8,128)(2,1)S(1)} %bitcast.89, s32[1024]{0:T(1024)S(1)} %get-tuple-element.46), kind=kCustom, calls=%fused_computation.3 | custom fusion | bytes 66048 | tf_op jit(solution)/shard_map/gather | solution.py:115
  10.0 0.7 %dynamic-slice_bitcast_fusion.5 = (bf16[128,256]{1,0:T(8,128)(2,1)}, bf16[128,256]{1,0:T(8,128)(2,1)S(1)}, bf16[128,256]{1,0:T(8,128)(2,1)}) fusion(bf16[4,128,256]{2,1,0:T(8,128)(2,1)S(1)} %convolution_convert_fusion.1, s32[]{:T(128)S(6)} %select_n.145, s32[]{:T(128)S(6)} %select_n.149, s32[]{:T(128)S(6)} %select_n.147), kind=kLoop, calls=%fused_computation.72 | loop fusion | bytes 393228 | tf_op jit(solution)/shard_map/jit(dynamic_index_in_dim)/squeeze | solution.py:75
  10.6 1.6 %collective-permute-start.2 = (bf16[128,256]{1,0:T(8,128)(2,1)}, bf16[128,256]{1,0:T(8,128)(2,1)S(1)}, u32[]{:S(2)}, u32[]{:S(2)}) collective-permute-start(bf16[128,256]{1,0:T(8,128)(2,1)} %get-tuple-element.28), channel_id=1, source_target_pairs={{0,4},{4,8},{8,12},{12,0},{1,5},{5,9},{9,13},{13,1},{2,6},{6,10},{... | collective-permute-start | bytes 196616 | tf_op jit(solution)/shard_map/ppermute | solution.py:76
  12.2 2.6 %collective-permute-start.3 = (bf16[128,256]{1,0:T(8,128)(2,1)}, bf16[128,256]{1,0:T(8,128)(2,1)}, u32[]{:S(2)}, u32[]{:S(2)}) collective-permute-start(bf16[128,256]{1,0:T(8,128)(2,1)} %get-tuple-element.30), channel_id=1, source_target_pairs={{0,8},{4,12},{8,0},{12,4},{1,9},{5,13},{9,1},{13,5},{2,10},{6,14},... | collective-permute-start | bytes 196616 | tf_op jit(solution)/shard_map/ppermute | solution.py:76
  14.8 1.4 %collective-permute-start.4 = (bf16[128,256]{1,0:T(8,128)(2,1)S(1)}, bf16[128,256]{1,0:T(8,128)(2,1)}, u32[]{:S(2)}, u32[]{:S(2)}) collective-permute-start(bf16[128,256]{1,0:T(8,128)(2,1)S(1)} %get-tuple-element.29), channel_id=1, source_target_pairs={{0,12},{4,0},{8,4},{12,8},{1,13},{5,1},{9,5},{13,9},{2,14},{6,2},{... | collective-permute-start | bytes 196616 | tf_op jit(solution)/shard_map/ppermute | solution.py:76
  16.7 0.8 %gather_fusion = f32[128,256]{1,0:T(8,128)S(1)} fusion(f32[1024,256]{1,0:T(8,128)S(1)} %fusion.11, s32[1024]{0:T(1024)S(1)} %get-tuple-element.47), kind=kCustom, calls=%fused_computation | custom fusion | bytes 262656 | tf_op jit(solution)/shard_map/gather | solution.py:152
  17.5 0.8 %gather_fusion.2 = f32[128,256]{1,0:T(8,128)S(1)} fusion(f32[1024,256]{1,0:T(8,128)S(1)} %fusion.11, s32[1024]{0:T(1024)S(1)} %get-tuple-element.46), kind=kCustom, calls=%fused_computation.2 | custom fusion | bytes 262656 | tf_op jit(solution)/shard_map/gather | solution.py:155
  18.2 2.0 %collective-permute-done.3 = bf16[128,256]{1,0:T(8,128)(2,1)} collective-permute-done((bf16[128,256]{1,0:T(8,128)(2,1)}, bf16[128,256]{1,0:T(8,128)(2,1)}, u32[]{:S(2)}, u32[]{:S(2)}) %collective-permute-start.3) | collective-permute-done | bytes 65568 | tf_op jit(solution)/shard_map/ppermute | solution.py:76
  20.4 1.0 %fusion.28 = bf16[128,256]{1,0:T(8,128)(2,1)S(1)} fusion(bf16[128,256]{1,0:T(8,128)(2,1)} %collective-permute-done.4, bf16[128,256]{1,0:T(8,128)(2,1)} %collective-permute-done.3, bf16[128,256]{1,0:T(8,128)(2,1)S(1)} %collective-permute-done.2, bf16[4,128,256]{2,1,0:T(8,128)(2,1)S(1)} %convolution_convert_fusion.1, s32[]{:T(128)S(6)} %select_n.143, ...), kind=kLoop, calls=%fused_computation.56 | loop fusion | flops 294912 | bytes 327812 | tf_op jit(solution)/shard_map/jit(_where)/select_n | solution.py:146
  21.5 0.8 %broadcast_select_fusion.4 = (bf16[128,256]{1,0:T(8,128)(2,1)S(1)}, bf16[128,256]{1,0:T(8,128)(2,1)}, bf16[128,256]{1,0:T(8,128)(2,1)S(1)}) fusion(bf16[128,256]{1,0:T(8,128)(2,1)S(1)} %fusion.5, pred[]{:T(512)S(6)} %eq.13, f32[128,256]{1,0:T(8,128)S(1)} %gather_fusion.2, bf16[128,128]{1,0:T(8,128)(2,1)S(1)} %gather_fusion.3, bf16[128,256]{1,0:T(8,128)(2,1)S(1)} %fusion.28), kind=kOutput, calls=%fused_computation.76 | convolution fusion | flops 8519680 | bytes 491521 | tf_op jit(solution)/shard_map/dot_general | solution.py:155
  22.4 1.0 %collective-permute-start.6 = (bf16[128,900]{1,0:T(8,128)(2,1)S(1)}, bf16[128,900]{1,0:T(8,128)(2,1)S(1)}, u32[]{:S(2)}, u32[]{:S(2)}) collective-permute-start(bf16[128,900]{1,0:T(8,128)(2,1)S(1)} %concatenate.29), channel_id=1, source_target_pairs={{0,2},{2,0},{1,3},{3,1},{4,6},{6,4},{5,7},{7,5},{8,10},{10,8},{9,1... | collective-permute-start | bytes 691208 | tf_op jit(solution)/shard_map/ppermute | solution.py:17
  23.4 0.7 %collective-permute-start.5 = (bf16[128,256]{1,0:T(8,128)(2,1)}, bf16[128,256]{1,0:T(8,128)(2,1)S(1)}, u32[]{:S(2)}, u32[]{:S(2)}) collective-permute-start(bf16[128,256]{1,0:T(8,128)(2,1)} %get-tuple-element.36), channel_id=1, source_target_pairs={{2,4},{4,2},{6,8},{8,6},{10,12},{12,10},{3,5},{5,3},{7,9},{9,7},{1... | collective-permute-start | bytes 196616 | tf_op jit(solution)/shard_map/ppermute | solution.py:165
  24.1 1.3 %collective-permute-start.7 = (bf16[128,256]{1,0:T(8,128)(2,1)}, bf16[128,256]{1,0:T(8,128)(2,1)S(1)}, u32[]{:S(2)}, u32[]{:S(2)}) collective-permute-start(bf16[128,256]{1,0:T(8,128)(2,1)} %get-tuple-element.36), channel_id=1, source_target_pairs={{2,6},{4,0},{6,10},{8,4},{10,14},{12,8},{3,7},{5,1},{7,11},{9,5},{... | collective-permute-start | bytes 196616 | tf_op jit(solution)/shard_map/ppermute | solution.py:166
  25.4 5.1 %collective-permute-done.6 = bf16[128,900]{1,0:T(8,128)(2,1)S(1)} collective-permute-done((bf16[128,900]{1,0:T(8,128)(2,1)S(1)}, bf16[128,900]{1,0:T(8,128)(2,1)S(1)}, u32[]{:S(2)}, u32[]{:S(2)}) %collective-permute-start.6) | collective-permute-done | bytes 230432 | tf_op jit(solution)/shard_map/ppermute | solution.py:17
  31.4 0.7 %collective-permute-done.7 = bf16[128,256]{1,0:T(8,128)(2,1)S(1)} collective-permute-done((bf16[128,256]{1,0:T(8,128)(2,1)}, bf16[128,256]{1,0:T(8,128)(2,1)S(1)}, u32[]{:S(2)}, u32[]{:S(2)}) %collective-permute-start.7) | collective-permute-done | bytes 65568 | tf_op jit(solution)/shard_map/ppermute | solution.py:166
  32.9 3.5 %collective-permute-start.10 = (bf16[128,256]{1,0:T(8,128)(2,1)S(1)}, bf16[128,256]{1,0:T(8,128)(2,1)S(1)}, u32[]{:S(2)}, u32[]{:S(2)}) collective-permute-start(bf16[128,256]{1,0:T(8,128)(2,1)S(1)} %get-tuple-element.26), channel_id=1, source_target_pairs={{0,12},{4,0},{8,4},{12,8},{1,13},{5,1},{9,5},{13,9},{2,14},{6,2},{... | collective-permute-start | bytes 196616 | tf_op jit(solution)/shard_map/ppermute | solution.py:76
  36.3 1.8 %collective-permute-start.9 = (bf16[128,256]{1,0:T(8,128)(2,1)S(1)}, bf16[128,256]{1,0:T(8,128)(2,1)S(1)}, u32[]{:S(2)}, u32[]{:S(2)}) collective-permute-start(bf16[128,256]{1,0:T(8,128)(2,1)S(1)} %get-tuple-element.27), channel_id=1, source_target_pairs={{0,8},{4,12},{8,0},{12,4},{1,9},{5,13},{9,1},{13,5},{2,10},{6,14},... | collective-permute-start | bytes 196616 | tf_op jit(solution)/shard_map/ppermute | solution.py:76
  38.2 4.2 %collective-permute-done.8 = bf16[128,256]{1,0:T(8,128)(2,1)S(1)} collective-permute-done((bf16[128,256]{1,0:T(8,128)(2,1)S(1)}, bf16[128,256]{1,0:T(8,128)(2,1)S(1)}, u32[]{:S(2)}, u32[]{:S(2)}) %collective-permute-start.8) | collective-permute-done | bytes 65568 | tf_op jit(solution)/shard_map/ppermute | solution.py:76
  42.4 1.1 %fusion.2 = bf16[1,1024,256]{2,1,0:T(8,128)(2,1)} fusion(f32[1024,256]{1,0:T(8,128)S(1)} %convolution_add_fusion, bf16[128,256]{1,0:T(8,128)(2,1)S(1)} %collective-permute-done.10, bf16[128,256]{1,0:T(8,128)(2,1)S(1)} %collective-permute-done.9, bf16[128,256]{1,0:T(8,128)(2,1)S(1)} %collective-permute-done.8, ...), kind=kOutput, calls=%fused_computation.8 | convolution fusion | flops 67928064 | bytes 2097668 | tf_op jit(solution)/shard_map/dot_general | solution.py:147
  (46 shorter events, 3.6 us)
Async XLA Ops:
  0.0 1.1 %copy-start = (bf16[1,1024,256]{2,1,0:T(8,128)(2,1)S(1)}, bf16[1,1024,256]{2,1,0:T(8,128)(2,1)}, u32[]{:S(2)}) copy-start(bf16[1,1024,256]{2,1,0:T(8,128)(2,1)} %param.7) | copy-start | bytes 1572868
  1.1 2.4 %copy-start.1 = (bf16[1,1024,128]{2,1,0:T(8,128)(2,1)S(1)}, bf16[1,1024,128]{2,1,0:T(8,128)(2,1)}, u32[]{:S(2)}) copy-start(bf16[1,1024,128]{2,1,0:T(8,128)(2,1)} %param.11) | copy-start | bytes 786436
  1.1 5.7 %copy-start.2 = (bf16[4,1,64,1,256]{4,2,3,1,0:T(8,128)(2,1)S(1)}, bf16[4,1,64,1,256]{4,2,3,1,0:T(8,128)(2,1)}, u32[]{:S(2)}) copy-start(bf16[4,1,64,1,256]{4,2,3,1,0:T(8,128)(2,1)} %param.13) | copy-start | bytes 393220
  3.4 4.4 %copy-start.4 = (s32[1,2,128]{2,1,0:T(2,128)S(1)}, s32[1,2,128]{2,1,0:T(2,128)}, u32[]{:S(2)}) copy-start(s32[1,2,128]{2,1,0:T(2,128)} %param.10) | copy-start | bytes 3076
  3.4 5.8 %copy-start.3 = (f32[1,2,128]{2,1,0:T(2,128)S(1)}, f32[1,2,128]{2,1,0:T(2,128)}, u32[]{:S(2)}) copy-start(f32[1,2,128]{2,1,0:T(2,128)} %param.9) | copy-start | bytes 3076
  3.7 5.9 %collective-permute-start.1 = (bf16[128,256]{1,0:T(8,128)(2,1)S(1)}, bf16[128,256]{1,0:T(8,128)(2,1)S(1)}, u32[]{:S(2)}, u32[]{:S(2)}) collective-permute-start(bf16[128,256]{1,0:T(8,128)(2,1)S(1)} %fusion.9), channel_id=1, source_target_pairs={{0,2},{2,0},{1,3},{3,1},{4,6},{6,4},{5,7},{7,5},{8,10},{10,8},{9,1... | collective-permute-start | bytes 196616 | tf_op jit(solution)/shard_map/ppermute | solution.py:17
  6.8 2.9 %collective-permute-start = (bf16[4,64,256]{2,1,0:T(8,128)(2,1)S(1)}, bf16[4,64,256]{2,1,0:T(8,128)(2,1)S(1)}, u32[]{:S(2)}, u32[]{:S(2)}) collective-permute-start(bf16[4,64,256]{2,1,0:T(8,128)(2,1)S(1)} %bitcast.92), channel_id=1, source_target_pairs={{0,1},{1,0},{2,3},{3,2},{4,5},{5,4},{6,7},{7,6},{8,9},{9,8},{10,11... | collective-permute-start | bytes 393224 | tf_op jit(solution)/shard_map/ppermute | solution.py:17
  10.6 7.6 %collective-permute-start.2 = (bf16[128,256]{1,0:T(8,128)(2,1)}, bf16[128,256]{1,0:T(8,128)(2,1)S(1)}, u32[]{:S(2)}, u32[]{:S(2)}) collective-permute-start(bf16[128,256]{1,0:T(8,128)(2,1)} %get-tuple-element.28), channel_id=1, source_target_pairs={{0,4},{4,8},{8,12},{12,0},{1,5},{5,9},{9,13},{13,1},{2,6},{6,10},{... | collective-permute-start | bytes 196616 | tf_op jit(solution)/shard_map/ppermute | solution.py:76
  12.2 8.0 %collective-permute-start.3 = (bf16[128,256]{1,0:T(8,128)(2,1)}, bf16[128,256]{1,0:T(8,128)(2,1)}, u32[]{:S(2)}, u32[]{:S(2)}) collective-permute-start(bf16[128,256]{1,0:T(8,128)(2,1)} %get-tuple-element.30), channel_id=1, source_target_pairs={{0,8},{4,12},{8,0},{12,4},{1,9},{5,13},{9,1},{13,5},{2,10},{6,14},... | collective-permute-start | bytes 196616 | tf_op jit(solution)/shard_map/ppermute | solution.py:76
  14.8 5.6 %collective-permute-start.4 = (bf16[128,256]{1,0:T(8,128)(2,1)S(1)}, bf16[128,256]{1,0:T(8,128)(2,1)}, u32[]{:S(2)}, u32[]{:S(2)}) collective-permute-start(bf16[128,256]{1,0:T(8,128)(2,1)S(1)} %get-tuple-element.29), channel_id=1, source_target_pairs={{0,12},{4,0},{8,4},{12,8},{1,13},{5,1},{9,5},{13,9},{2,14},{6,2},{... | collective-permute-start | bytes 196616 | tf_op jit(solution)/shard_map/ppermute | solution.py:76
  22.4 8.1 %collective-permute-start.6 = (bf16[128,900]{1,0:T(8,128)(2,1)S(1)}, bf16[128,900]{1,0:T(8,128)(2,1)S(1)}, u32[]{:S(2)}, u32[]{:S(2)}) collective-permute-start(bf16[128,900]{1,0:T(8,128)(2,1)S(1)} %concatenate.29), channel_id=1, source_target_pairs={{0,2},{2,0},{1,3},{3,1},{4,6},{6,4},{5,7},{7,5},{8,10},{10,8},{9,1... | collective-permute-start | bytes 691208 | tf_op jit(solution)/shard_map/ppermute | solution.py:17
  23.4 2.0 %collective-permute-start.5 = (bf16[128,256]{1,0:T(8,128)(2,1)}, bf16[128,256]{1,0:T(8,128)(2,1)S(1)}, u32[]{:S(2)}, u32[]{:S(2)}) collective-permute-start(bf16[128,256]{1,0:T(8,128)(2,1)} %get-tuple-element.36), channel_id=1, source_target_pairs={{2,4},{4,2},{6,8},{8,6},{10,12},{12,10},{3,5},{5,3},{7,9},{9,7},{1... | collective-permute-start | bytes 196616 | tf_op jit(solution)/shard_map/ppermute | solution.py:165
  24.1 8.1 %collective-permute-start.7 = (bf16[128,256]{1,0:T(8,128)(2,1)}, bf16[128,256]{1,0:T(8,128)(2,1)S(1)}, u32[]{:S(2)}, u32[]{:S(2)}) collective-permute-start(bf16[128,256]{1,0:T(8,128)(2,1)} %get-tuple-element.36), channel_id=1, source_target_pairs={{2,6},{4,0},{6,10},{8,4},{10,14},{12,8},{3,7},{5,1},{7,11},{9,5},{... | collective-permute-start | bytes 196616 | tf_op jit(solution)/shard_map/ppermute | solution.py:166
  32.9 5.4 %collective-permute-start.10 = (bf16[128,256]{1,0:T(8,128)(2,1)S(1)}, bf16[128,256]{1,0:T(8,128)(2,1)S(1)}, u32[]{:S(2)}, u32[]{:S(2)}) collective-permute-start(bf16[128,256]{1,0:T(8,128)(2,1)S(1)} %get-tuple-element.26), channel_id=1, source_target_pairs={{0,12},{4,0},{8,4},{12,8},{1,13},{5,1},{9,5},{13,9},{2,14},{6,2},{... | collective-permute-start | bytes 196616 | tf_op jit(solution)/shard_map/ppermute | solution.py:76
  36.3 6.1 %collective-permute-start.8 = (bf16[128,256]{1,0:T(8,128)(2,1)S(1)}, bf16[128,256]{1,0:T(8,128)(2,1)S(1)}, u32[]{:S(2)}, u32[]{:S(2)}) collective-permute-start(bf16[128,256]{1,0:T(8,128)(2,1)S(1)} %get-tuple-element.25), channel_id=1, source_target_pairs={{0,4},{4,8},{8,12},{12,0},{1,5},{5,9},{9,13},{13,1},{2,6},{6,10},{... | collective-permute-start | bytes 196616 | tf_op jit(solution)/shard_map/ppermute | solution.py:76
  36.3 6.1 %collective-permute-start.9 = (bf16[128,256]{1,0:T(8,128)(2,1)S(1)}, bf16[128,256]{1,0:T(8,128)(2,1)S(1)}, u32[]{:S(2)}, u32[]{:S(2)}) collective-permute-start(bf16[128,256]{1,0:T(8,128)(2,1)S(1)} %get-tuple-element.27), channel_id=1, source_target_pairs={{0,8},{4,12},{8,0},{12,4},{1,9},{5,13},{9,1},{13,5},{2,10},{6,14},... | collective-permute-start | bytes 196616 | tf_op jit(solution)/shard_map/ppermute | solution.py:76

commit v24 on v14

--- a/solution.py
+++ b/solution.py
@@ -71,7 +71,8 @@
         total = lax.dynamic_index_in_dim(partial, sub_index, 0, keepdims=False).astype(
             jnp.float32
         )
-        for k in range(1, sub_count):
+        half_way = sub_count // 2
+        for k in [half_way] + [k for k in range(1, sub_count) if k != half_way]:
             piece = lax.dynamic_index_in_dim(partial, (sub_index + k) % sub_count, 0, keepdims=False)
             total = total + lax.ppermute(
                 piece, "sub", [(i, (i + k) % sub_count) for i in range(sub_count)]

time: 42.5 us -> 44.2 us (1.040)
  waiting for transfers between devices: 10.5 us -> 12.1 us
    ppermute x6, waiting for transfers between devices: 4.4 us -> 6.03 us  [coarse_of(): lax.ppermute(piece, 'sub', [(i, (i + k) % sub_count) for i in range(sub_c...]
  transfers between devices with their start and end apart: 11 -> 11, of which waited for: 6 -> 6; matrix products, arithmetic and copies ran while one was open for 14% -> 13% of each run, Pallas kernels for 0% -> 0%
where the time goes in v24:
time: 44.2 us; the launch traced here: 43.7 us
  starting transfers between devices  17 us (38%)
  waiting for transfers between devices  12.1 us (27%)
  matrix products  6.62 us (15%)
  local copies, waits for them, and re-layouts  5.61 us (13%)
  other arithmetic  1.41 us (3%)
  between operations  1.02 us (2%)
    ppermute x6, starting transfers between devices, coarse_of(): lax.ppermute(piece, 'sub', [(i, (i + k) % sub_count) for i in range(sub_c...  10.5 us
    ppermute x6, waiting for transfers between devices, coarse_of(): lax.ppermute(piece, 'sub', [(i, (i + k) % sub_count) for i in range(sub_c...  6.03 us
    ppermute x3, starting transfers between devices, swapped(): return lax.ppermute(shard, axis, [(0, 1), (1, 0)])  4.56 us
    ppermute x3, waiting for transfers between devices, swapped(): return lax.ppermute(shard, axis, [(0, 1), (1, 0)])  3.89 us
    dot_general x1, matrix products, local(): base_solve = jnp.dot(inverse, source, preferred_element_type=jnp.float32)  2.35 us
    ppermute x1, waiting for transfers between devices, local(): crossing = lax.ppermute(toward_diagonal, DUCT, crossing_pairs)  2.14 us
    ppermute x1, starting transfers between devices, local(): crossing = lax.ppermute(toward_diagonal, DUCT, crossing_pairs)  1.29 us
    dot_general x1, matrix products, local(): correction = jnp.dot(basis, coarse, preferred_element_type=jnp.float32)  1.14 us
  transfers between devices with their start and end apart: 11, of which 6 were waited for; matrix products, arithmetic and copies ran while one was open for 13% of the time, Pallas kernels for 0%

profile of v24, /device:TPU:0, one launch (start us, length us, event | category | flops | bytes accessed | tf_op | source)
XLA Modules:
  0.0 43.7 jit_solution(13673657583923320727)
XLA Ops:
  1.1 2.4 %fusion.11 = f32[1024,256]{1,0:T(8,128)S(1)} fusion(bf16[1,1024,256]{2,1,0:T(8,128)(2,1)S(1)} %copy-done, bf16[1,1024,1024]{2,1,0:T(8,128)(2,1)} %param.8), kind=kOutput, calls=%fused_computation.27 | convolution fusion | flops 536870912 | bytes 3670016 | tf_op jit(solution)/shard_map/dot_general | solution.py:111
  3.7 3.0 %collective-permute-start.1 = (bf16[128,256]{1,0:T(8,128)(2,1)S(1)}, bf16[128,256]{1,0:T(8,128)(2,1)S(1)}, u32[]{:S(2)}, u32[]{:S(2)}) collective-permute-start(bf16[128,256]{1,0:T(8,128)(2,1)S(1)} %fusion.9), channel_id=1, source_target_pairs={{0,2},{2,0},{1,3},{3,1},{4,6},{6,4},{5,7},{7,5},{8,10},{10,8},{9,1... | collective-permute-start | bytes 196616 | tf_op jit(solution)/shard_map/ppermute | solution.py:17
  6.8 1.1 %fusion.53 = (bf16[1024,128]{1,0:T(8,128)(2,1)S(1)}, bf16[1024,128]{1,0:T(8,128)(2,1)S(1)}) fusion(bf16[1024,1024]{1,0:T(8,128)(2,1)} %bitcast.93), kind=kLoop, calls=%fused_computation.105 | loop fusion | bytes 1048576 | tf_op jit(solution)/shard_map/slice | solution.py:57
  8.2 0.8 %collective-permute-done.1 = bf16[128,256]{1,0:T(8,128)(2,1)S(1)} collective-permute-done((bf16[128,256]{1,0:T(8,128)(2,1)S(1)}, bf16[128,256]{1,0:T(8,128)(2,1)S(1)}, u32[]{:S(2)}, u32[]{:S(2)}) %collective-permute-start.1) | collective-permute-done | bytes 65568 | tf_op jit(solution)/shard_map/ppermute | solution.py:17
  9.3 0.7 %dynamic-slice_bitcast_fusion.5 = (bf16[128,256]{1,0:T(8,128)(2,1)}, bf16[128,256]{1,0:T(8,128)(2,1)}, bf16[128,256]{1,0:T(8,128)(2,1)}) fusion(bf16[4,128,256]{2,1,0:T(8,128)(2,1)S(1)} %convolution_convert_fusion.1, s32[]{:T(128)S(6)} %select_n.145, s32[]{:T(128)S(6)} %select_n.149, s32[]{:T(128)S(6)} %select_n.147), kind=kLoop, calls=%fused_computation.72 | loop fusion | bytes 393228 | tf_op jit(solution)/shard_map/jit(dynamic_index_in_dim)/squeeze | solution.py:76
  10.0 3.1 %collective-permute-start.2 = (bf16[128,256]{1,0:T(8,128)(2,1)}, bf16[128,256]{1,0:T(8,128)(2,1)}, u32[]{:S(2)}, u32[]{:S(2)}) collective-permute-start(bf16[128,256]{1,0:T(8,128)(2,1)} %get-tuple-element.26), channel_id=1, source_target_pairs={{0,8},{4,12},{8,0},{12,4},{1,9},{5,13},{9,1},{13,5},{2,10},{6,14},... | collective-permute-start | bytes 196616 | tf_op jit(solution)/shard_map/ppermute | solution.py:77
  13.1 1.6 %collective-permute-start.3 = (bf16[128,256]{1,0:T(8,128)(2,1)}, bf16[128,256]{1,0:T(8,128)(2,1)}, u32[]{:S(2)}, u32[]{:S(2)}) collective-permute-start(bf16[128,256]{1,0:T(8,128)(2,1)} %get-tuple-element.28), channel_id=1, source_target_pairs={{0,4},{4,8},{8,12},{12,0},{1,5},{5,9},{9,13},{13,1},{2,6},{6,10},{... | collective-permute-start | bytes 196616 | tf_op jit(solution)/shard_map/ppermute | solution.py:77
  14.7 2.2 %collective-permute-start.4 = (bf16[128,256]{1,0:T(8,128)(2,1)}, bf16[128,256]{1,0:T(8,128)(2,1)}, u32[]{:S(2)}, u32[]{:S(2)}) collective-permute-start(bf16[128,256]{1,0:T(8,128)(2,1)} %get-tuple-element.27), channel_id=1, source_target_pairs={{0,12},{4,0},{8,4},{12,8},{1,13},{5,1},{9,5},{13,9},{2,14},{6,2},{... | collective-permute-start | bytes 196616 | tf_op jit(solution)/shard_map/ppermute | solution.py:77
  17.5 0.7 %gather_fusion.1 = bf16[128,128]{1,0:T(8,128)(2,1)S(1)} fusion(bf16[1024,128]{1,0:T(8,128)(2,1)S(1)} %bitcast.90, s32[1024]{0:T(1024)S(1)} %get-tuple-element.45), kind=kCustom, calls=%fused_computation.1 | custom fusion | bytes 66048 | tf_op jit(solution)/shard_map/gather | solution.py:132
  18.2 0.8 %gather_fusion = f32[128,256]{1,0:T(8,128)S(1)} fusion(f32[1024,256]{1,0:T(8,128)S(1)} %fusion.11, s32[1024]{0:T(1024)S(1)} %get-tuple-element.45), kind=kCustom, calls=%fused_computation | custom fusion | bytes 262656 | tf_op jit(solution)/shard_map/gather | solution.py:152
  18.9 0.7 %gather_fusion.3 = bf16[128,128]{1,0:T(8,128)(2,1)S(1)} fusion(bf16[1024,128]{1,0:T(8,128)(2,1)S(1)} %bitcast.91, s32[1024]{0:T(1024)S(1)} %get-tuple-element.44), kind=kCustom, calls=%fused_computation.3 | custom fusion | bytes 66048 | tf_op jit(solution)/shard_map/gather | solution.py:133
  19.6 0.8 %gather_fusion.2 = f32[128,256]{1,0:T(8,128)S(1)} fusion(f32[1024,256]{1,0:T(8,128)S(1)} %fusion.11, s32[1024]{0:T(1024)S(1)} %get-tuple-element.44), kind=kCustom, calls=%fused_computation.2 | custom fusion | bytes 262656 | tf_op jit(solution)/shard_map/gather | solution.py:155
  20.4 1.0 %fusion.28 = bf16[128,256]{1,0:T(8,128)(2,1)S(1)} fusion(bf16[128,256]{1,0:T(8,128)(2,1)} %collective-permute-done.4, bf16[128,256]{1,0:T(8,128)(2,1)} %collective-permute-done.3, bf16[128,256]{1,0:T(8,128)(2,1)} %collective-permute-done.2, bf16[4,128,256]{2,1,0:T(8,128)(2,1)S(1)} %convolution_convert_fusion.1, s32[]{:T(128)S(6)} %select_n.143, ...), kind=kLoop, calls=%fused_computation.56 | loop fusion | flops 294912 | bytes 327812 | tf_op jit(solution)/shard_map/jit(_where)/select_n | solution.py:146
  21.6 0.8 %broadcast_select_fusion.4 = (bf16[128,256]{1,0:T(8,128)(2,1)S(1)}, bf16[128,256]{1,0:T(8,128)(2,1)}, bf16[128,256]{1,0:T(8,128)(2,1)S(1)}) fusion(bf16[128,256]{1,0:T(8,128)(2,1)S(1)} %fusion.5, pred[]{:T(512)S(6)} %eq.13, f32[128,256]{1,0:T(8,128)S(1)} %gather_fusion.2, bf16[128,128]{1,0:T(8,128)(2,1)S(1)} %gather_fusion.3, bf16[128,256]{1,0:T(8,128)(2,1)S(1)} %fusion.28), kind=kOutput, calls=%fused_computation.76 | convolution fusion | flops 8519680 | bytes 491521 | tf_op jit(solution)/shard_map/dot_general | solution.py:155
  22.5 1.6 %collective-permute-start.6 = (bf16[128,900]{1,0:T(8,128)(2,1)S(1)}, bf16[128,900]{1,0:T(8,128)(2,1)S(1)}, u32[]{:S(2)}, u32[]{:S(2)}) collective-permute-start(bf16[128,900]{1,0:T(8,128)(2,1)S(1)} %concatenate.29), channel_id=1, source_target_pairs={{0,2},{2,0},{1,3},{3,1},{4,6},{6,4},{5,7},{7,5},{8,10},{10,8},{9,1... | collective-permute-start | bytes 691208 | tf_op jit(solution)/shard_map/ppermute | solution.py:17
  24.0 0.7 %collective-permute-start.5 = (bf16[128,256]{1,0:T(8,128)(2,1)}, bf16[128,256]{1,0:T(8,128)(2,1)S(1)}, u32[]{:S(2)}, u32[]{:S(2)}) collective-permute-start(bf16[128,256]{1,0:T(8,128)(2,1)} %get-tuple-element.34), channel_id=1, source_target_pairs={{2,4},{4,2},{6,8},{8,6},{10,12},{12,10},{3,5},{5,3},{7,9},{9,7},{1... | collective-permute-start | bytes 196616 | tf_op jit(solution)/shard_map/ppermute | solution.py:165
  24.7 1.3 %collective-permute-start.7 = (bf16[128,256]{1,0:T(8,128)(2,1)}, bf16[128,256]{1,0:T(8,128)(2,1)S(1)}, u32[]{:S(2)}, u32[]{:S(2)}) collective-permute-start(bf16[128,256]{1,0:T(8,128)(2,1)} %get-tuple-element.34), channel_id=1, source_target_pairs={{2,6},{4,0},{6,10},{8,4},{10,14},{12,8},{3,7},{5,1},{7,11},{9,5},{... | collective-permute-start | bytes 196616 | tf_op jit(solution)/shard_map/ppermute | solution.py:166
  26.0 3.1 %collective-permute-done.6 = bf16[128,900]{1,0:T(8,128)(2,1)S(1)} collective-permute-done((bf16[128,900]{1,0:T(8,128)(2,1)S(1)}, bf16[128,900]{1,0:T(8,128)(2,1)S(1)}, u32[]{:S(2)}, u32[]{:S(2)}) %collective-permute-start.6) | collective-permute-done | bytes 230432 | tf_op jit(solution)/shard_map/ppermute | solution.py:17
  30.2 2.1 %collective-permute-done.7 = bf16[128,256]{1,0:T(8,128)(2,1)S(1)} collective-permute-done((bf16[128,256]{1,0:T(8,128)(2,1)}, bf16[128,256]{1,0:T(8,128)(2,1)S(1)}, u32[]{:S(2)}, u32[]{:S(2)}) %collective-permute-start.7) | collective-permute-done | bytes 65568 | tf_op jit(solution)/shard_map/ppermute | solution.py:166
  33.0 2.9 %collective-permute-start.10 = (bf16[128,256]{1,0:T(8,128)(2,1)S(1)}, bf16[128,256]{1,0:T(8,128)(2,1)S(1)}, u32[]{:S(2)}, u32[]{:S(2)}) collective-permute-start(bf16[128,256]{1,0:T(8,128)(2,1)S(1)} %get-tuple-element.24), channel_id=1, source_target_pairs={{0,12},{4,0},{8,4},{12,8},{1,13},{5,1},{9,5},{13,9},{2,14},{6,2},{... | collective-permute-start | bytes 196616 | tf_op jit(solution)/shard_map/ppermute | solution.py:77
  36.6 1.3 %collective-permute-done.10 = bf16[128,256]{1,0:T(8,128)(2,1)S(1)} collective-permute-done((bf16[128,256]{1,0:T(8,128)(2,1)S(1)}, bf16[128,256]{1,0:T(8,128)(2,1)S(1)}, u32[]{:S(2)}, u32[]{:S(2)}) %collective-permute-start.10) | collective-permute-done | bytes 65568 | tf_op jit(solution)/shard_map/ppermute | solution.py:77
  37.8 3.3 %collective-permute-done.8 = bf16[128,256]{1,0:T(8,128)(2,1)S(1)} collective-permute-done((bf16[128,256]{1,0:T(8,128)(2,1)S(1)}, bf16[128,256]{1,0:T(8,128)(2,1)S(1)}, u32[]{:S(2)}, u32[]{:S(2)}) %collective-permute-start.8) | collective-permute-done | bytes 65568 | tf_op jit(solution)/shard_map/ppermute | solution.py:77
  41.1 1.5 %collective-permute-done.9 = bf16[128,256]{1,0:T(8,128)(2,1)S(1)} collective-permute-done((bf16[128,256]{1,0:T(8,128)(2,1)S(1)}, bf16[128,256]{1,0:T(8,128)(2,1)S(1)}, u32[]{:S(2)}, u32[]{:S(2)}) %collective-permute-start.9) | collective-permute-done | bytes 65568 | tf_op jit(solution)/shard_map/ppermute | solution.py:77
  42.6 1.1 %fusion.2 = bf16[1,1024,256]{2,1,0:T(8,128)(2,1)} fusion(f32[1024,256]{1,0:T(8,128)S(1)} %convolution_add_fusion, bf16[128,256]{1,0:T(8,128)(2,1)S(1)} %collective-permute-done.10, bf16[128,256]{1,0:T(8,128)(2,1)S(1)} %collective-permute-done.9, bf16[128,256]{1,0:T(8,128)(2,1)S(1)} %collective-permute-done.8, ...), kind=kOutput, calls=%fused_computation.8 | convolution fusion | flops 67928064 | bytes 2097668 | tf_op jit(solution)/shard_map/dot_general | solution.py:147
  (46 shorter events, 4.3 us)
Async XLA Ops:
  0.0 1.1 %copy-start = (bf16[1,1024,256]{2,1,0:T(8,128)(2,1)S(1)}, bf16[1,1024,256]{2,1,0:T(8,128)(2,1)}, u32[]{:S(2)}) copy-start(bf16[1,1024,256]{2,1,0:T(8,128)(2,1)} %param.7) | copy-start | bytes 1572868
  1.1 2.4 %copy-start.1 = (bf16[1,1024,128]{2,1,0:T(8,128)(2,1)S(1)}, bf16[1,1024,128]{2,1,0:T(8,128)(2,1)}, u32[]{:S(2)}) copy-start(bf16[1,1024,128]{2,1,0:T(8,128)(2,1)} %param.11) | copy-start | bytes 786436
  1.1 5.7 %copy-start.2 = (bf16[4,1,64,1,256]{4,2,3,1,0:T(8,128)(2,1)S(1)}, bf16[4,1,64,1,256]{4,2,3,1,0:T(8,128)(2,1)}, u32[]{:S(2)}) copy-start(bf16[4,1,64,1,256]{4,2,3,1,0:T(8,128)(2,1)} %param.13) | copy-start | bytes 393220
  3.4 4.4 %copy-start.4 = (s32[1,2,128]{2,1,0:T(2,128)S(1)}, s32[1,2,128]{2,1,0:T(2,128)}, u32[]{:S(2)}) copy-start(s32[1,2,128]{2,1,0:T(2,128)} %param.10) | copy-start | bytes 3076
  3.4 4.4 %copy-start.3 = (f32[1,2,128]{2,1,0:T(2,128)S(1)}, f32[1,2,128]{2,1,0:T(2,128)}, u32[]{:S(2)}) copy-start(f32[1,2,128]{2,1,0:T(2,128)} %param.9) | copy-start | bytes 3076
  3.7 5.2 %collective-permute-start.1 = (bf16[128,256]{1,0:T(8,128)(2,1)S(1)}, bf16[128,256]{1,0:T(8,128)(2,1)S(1)}, u32[]{:S(2)}, u32[]{:S(2)}) collective-permute-start(bf16[128,256]{1,0:T(8,128)(2,1)S(1)} %fusion.9), channel_id=1, source_target_pairs={{0,2},{2,0},{1,3},{3,1},{4,6},{6,4},{5,7},{7,5},{8,10},{10,8},{9,1... | collective-permute-start | bytes 196616 | tf_op jit(solution)/shard_map/ppermute | solution.py:17
  6.8 2.3 %collective-permute-start = (bf16[4,64,256]{2,1,0:T(8,128)(2,1)S(1)}, bf16[4,64,256]{2,1,0:T(8,128)(2,1)S(1)}, u32[]{:S(2)}, u32[]{:S(2)}) collective-permute-start(bf16[4,64,256]{2,1,0:T(8,128)(2,1)S(1)} %bitcast.92), channel_id=1, source_target_pairs={{0,1},{1,0},{2,3},{3,2},{4,5},{5,4},{6,7},{7,6},{8,9},{9,8},{10,11... | collective-permute-start | bytes 393224 | tf_op jit(solution)/shard_map/ppermute | solution.py:17
  10.0 10.4 %collective-permute-start.2 = (bf16[128,256]{1,0:T(8,128)(2,1)}, bf16[128,256]{1,0:T(8,128)(2,1)}, u32[]{:S(2)}, u32[]{:S(2)}) collective-permute-start(bf16[128,256]{1,0:T(8,128)(2,1)} %get-tuple-element.26), channel_id=1, source_target_pairs={{0,8},{4,12},{8,0},{12,4},{1,9},{5,13},{9,1},{13,5},{2,10},{6,14},... | collective-permute-start | bytes 196616 | tf_op jit(solution)/shard_map/ppermute | solution.py:77
  13.1 7.3 %collective-permute-start.3 = (bf16[128,256]{1,0:T(8,128)(2,1)}, bf16[128,256]{1,0:T(8,128)(2,1)}, u32[]{:S(2)}, u32[]{:S(2)}) collective-permute-start(bf16[128,256]{1,0:T(8,128)(2,1)} %get-tuple-element.28), channel_id=1, source_target_pairs={{0,4},{4,8},{8,12},{12,0},{1,5},{5,9},{9,13},{13,1},{2,6},{6,10},{... | collective-permute-start | bytes 196616 | tf_op jit(solution)/shard_map/ppermute | solution.py:77
  14.7 5.8 %collective-permute-start.4 = (bf16[128,256]{1,0:T(8,128)(2,1)}, bf16[128,256]{1,0:T(8,128)(2,1)}, u32[]{:S(2)}, u32[]{:S(2)}) collective-permute-start(bf16[128,256]{1,0:T(8,128)(2,1)} %get-tuple-element.27), channel_id=1, source_target_pairs={{0,12},{4,0},{8,4},{12,8},{1,13},{5,1},{9,5},{13,9},{2,14},{6,2},{... | collective-permute-start | bytes 196616 | tf_op jit(solution)/shard_map/ppermute | solution.py:77
  22.5 6.7 %collective-permute-start.6 = (bf16[128,900]{1,0:T(8,128)(2,1)S(1)}, bf16[128,900]{1,0:T(8,128)(2,1)S(1)}, u32[]{:S(2)}, u32[]{:S(2)}) collective-permute-start(bf16[128,900]{1,0:T(8,128)(2,1)S(1)} %concatenate.29), channel_id=1, source_target_pairs={{0,2},{2,0},{1,3},{3,1},{4,6},{6,4},{5,7},{7,5},{8,10},{10,8},{9,1... | collective-permute-start | bytes 691208 | tf_op jit(solution)/shard_map/ppermute | solution.py:17
  24.0 2.0 %collective-permute-start.5 = (bf16[128,256]{1,0:T(8,128)(2,1)}, bf16[128,256]{1,0:T(8,128)(2,1)S(1)}, u32[]{:S(2)}, u32[]{:S(2)}) collective-permute-start(bf16[128,256]{1,0:T(8,128)(2,1)} %get-tuple-element.34), channel_id=1, source_target_pairs={{2,4},{4,2},{6,8},{8,6},{10,12},{12,10},{3,5},{5,3},{7,9},{9,7},{1... | collective-permute-start | bytes 196616 | tf_op jit(solution)/shard_map/ppermute | solution.py:165
  24.7 7.6 %collective-permute-start.7 = (bf16[128,256]{1,0:T(8,128)(2,1)}, bf16[128,256]{1,0:T(8,128)(2,1)S(1)}, u32[]{:S(2)}, u32[]{:S(2)}) collective-permute-start(bf16[128,256]{1,0:T(8,128)(2,1)} %get-tuple-element.34), channel_id=1, source_target_pairs={{2,6},{4,0},{6,10},{8,4},{10,14},{12,8},{3,7},{5,1},{7,11},{9,5},{... | collective-permute-start | bytes 196616 | tf_op jit(solution)/shard_map/ppermute | solution.py:166
  33.0 4.8 %collective-permute-start.10 = (bf16[128,256]{1,0:T(8,128)(2,1)S(1)}, bf16[128,256]{1,0:T(8,128)(2,1)S(1)}, u32[]{:S(2)}, u32[]{:S(2)}) collective-permute-start(bf16[128,256]{1,0:T(8,128)(2,1)S(1)} %get-tuple-element.24), channel_id=1, source_target_pairs={{0,12},{4,0},{8,4},{12,8},{1,13},{5,1},{9,5},{13,9},{2,14},{6,2},{... | collective-permute-start | bytes 196616 | tf_op jit(solution)/shard_map/ppermute | solution.py:77
  35.9 5.2 %collective-permute-start.8 = (bf16[128,256]{1,0:T(8,128)(2,1)S(1)}, bf16[128,256]{1,0:T(8,128)(2,1)S(1)}, u32[]{:S(2)}, u32[]{:S(2)}) collective-permute-start(bf16[128,256]{1,0:T(8,128)(2,1)S(1)} %get-tuple-element.23), channel_id=1, source_target_pairs={{0,8},{4,12},{8,0},{12,4},{1,9},{5,13},{9,1},{13,5},{2,10},{6,14},... | collective-permute-start | bytes 196616 | tf_op jit(solution)/shard_map/ppermute | solution.py:77
  36.5 6.1 %collective-permute-start.9 = (bf16[128,256]{1,0:T(8,128)(2,1)S(1)}, bf16[128,256]{1,0:T(8,128)(2,1)S(1)}, u32[]{:S(2)}, u32[]{:S(2)}) collective-permute-start(bf16[128,256]{1,0:T(8,128)(2,1)S(1)} %get-tuple-element.25), channel_id=1, source_target_pairs={{0,4},{4,8},{8,12},{12,0},{1,5},{5,9},{9,13},{13,1},{2,6},{6,10},{... | collective-permute-start | bytes 196616 | tf_op jit(solution)/shard_map/ppermute | solution.py:77
